TPU v7x, 32 devices: a whole 2x2x4 slice. The times are simulated.
32 devices in a mesh: dp: 8 (over y, x, core), space: 4 (over z).
Axes of the slice: x: 2, y: 2, z: 4, core: 2. Of those that a mesh axis runs over, the one named last changes fastest.
Arguments:
- latents: bfloat16 [8, 33, 4, 8, 256], P('dp', None, 'space'), may hold values from -6 to 6
- lengths: int32 [8], P('dp'), may hold values from 9 to 33, as said below
- spatial_weight: bfloat16 [3, 3, 256, 256], replicated, may hold values from -0.125 to 0.125
- temporal_weight: bfloat16 [3, 256, 256], replicated, may hold values from -0.21875 to 0.21875
- critic_weight: bfloat16 [256, 256], replicated, may hold values from -0.375 to 0.375
- critic_head: float32 [256], replicated, may hold values from -5 to 5
- critic_frames: int32 [8, 8], P('dp'), may hold values from 0 to 32, as said below
- recon_grad: bfloat16 [8, 33, 8, 16, 256], P('dp', None, 'space'), may hold values from -6 to 6
Outputs:
- decoded: bfloat16 [8, 33, 8, 16, 256], P('dp', None, 'space')
- grad_spatial: float32 [589824], P(('dp', 'space'))
- grad_temporal: float32 [196608], P(('dp', 'space'))
Inputs may be any that keep to these rules, and one draw needn't show every extreme that they name: `lengths`: some clip has exactly 33 live frames and some exactly 9. `critic_frames`: each entry names a live frame of its clip (below that clip's length); a frame may be named by several slots.
All inputs are finite; a program needn't handle non-finite values.
Results may differ from a plain program's by a relative error of at most 0.0055.
Values may be sent and summed in bfloat16 or wider, within the bound.
No kernel may reach another device: no remote copies, remote signals or barrier semaphores. Data moves between devices by JAX's collectives and lax.ppermute only.
A program may use at most 64 MiB of HBM per device.

v0:
```python
import math

import jax
import jax.numpy as jnp
from jax import lax
from jax.sharding import PartitionSpec as P


def _log2(n):
    b = n.bit_length() - 1
    return b if (1 << b) == n else None


def exchange_rows(cells, axis, dim):
    count = lax.axis_size(axis)
    ends = count - 1
    head = lax.slice_in_dim(cells, 0, 1, axis=dim)
    tail = lax.slice_in_dim(cells, cells.shape[dim] - 1, cells.shape[dim], axis=dim)
    above = lax.ppermute(tail, axis, [(i, i + 1) for i in range(ends)])
    below = lax.ppermute(head, axis, [(i + 1, i) for i in range(ends)])
    return above, below


def upsample(values):
    doubled = jnp.repeat(values, 2, axis=-3)
    return jnp.repeat(doubled, 2, axis=-2)


def silu_slope(pre_act):
    sigmoid_val = jax.nn.sigmoid(pre_act)
    return sigmoid_val * (1.0 + pre_act * (1.0 - sigmoid_val))


def delayed(values, offset):
    if offset == 0:
        return values
    widths = [(0, 0)] * values.ndim
    widths[1] = (offset, 0)
    return jnp.pad(values, widths)[:, : values.shape[1]]


def advanced(values, offset):
    if offset == 0:
        return values
    widths = [(0, 0)] * values.ndim
    widths[1] = (0, offset)
    return jnp.pad(values, widths)[:, offset:]


def space_sum(values):
    count = lax.axis_size("space")
    bits = _log2(count)
    if bits is None:
        return lax.psum(values, "space")
    for bit in range(bits):
        step = 1 << bit
        values = values + lax.ppermute(values, "space", [(i, i ^ step) for i in range(count)])
    return values


def _halve(cur, left, axis, bit):
    size = lax.axis_size(axis)
    pos = left.index((axis, bit))
    hi, lo = 1 << pos, 1 << (len(left) - 1 - pos)
    mine = (lax.axis_index(axis) // (1 << bit)) % 2
    v = cur.reshape(hi, 2, lo * cur.shape[1])
    low, high = v[:, 0].reshape(hi * lo, -1), v[:, 1].reshape(hi * lo, -1)
    upper = mine == 1
    keep = jnp.where(upper, high, low)
    send = jnp.where(upper, low, high)
    left.remove((axis, bit))
    return keep + lax.ppermute(send, axis, [(i, i ^ (1 << bit)) for i in range(size)])


def halving_scatter(blocks, orders):
    nd, ns = lax.axis_size("dp"), lax.axis_size("space")
    bd, bs = _log2(nd), _log2(ns)
    if bd is None or bs is None:
        flat = lax.psum_scatter(blocks.reshape(-1), "dp", scatter_dimension=0, tiled=True)
        return lax.psum_scatter(flat, "space", scatter_dimension=0, tiled=True)
    natural = [("dp", i) for i in reversed(range(bd))] + [("space", i) for i in reversed(range(bs))]
    shared = 0
    while shared < len(natural) and all(o[shared] == orders[0][shared] for o in orders):
        shared += 1
    left = list(natural)
    cur = blocks
    for axis, bit in orders[0][:shared]:
        cur = _halve(cur, left, axis, bit)
    width = cur.shape[1] // len(orders)
    outs = []
    for p, order in enumerate(orders):
        part, part_left = cur[:, p * width : (p + 1) * width], list(left)
        for axis, bit in order[shared:]:
            part = _halve(part, part_left, axis, bit)
        outs.append(part.reshape(-1))
    return jnp.concatenate(outs)


def on_device(
    latents,
    lengths,
    spatial_weight,
    temporal_weight,
    critic_weight,
    critic_head,
    critic_frames,
    recon_grad,
):
    groups = lax.axis_size("space")
    devices = lax.axis_size("dp") * groups
    clip_count = latents.shape[0] * lax.axis_size("dp")
    frame_count = latents.shape[1]
    upsampled = upsample(latents)
    above, below = exchange_rows(latents, "space", 2)
    extended = jnp.concatenate(
        [upsample(above)[:, :, 1:], upsampled, upsample(below)[:, :, :1]], axis=2
    )
    padded = jnp.pad(extended, ((0, 0), (0, 0), (0, 0), (1, 1), (0, 0)))
    height = upsampled.shape[2]
    width = upsampled.shape[3]
    pre_act = jnp.zeros(upsampled.shape, jnp.float32)
    for row_tap in range(3):
        for col_tap in range(3):
            window = padded[:, :, row_tap : row_tap + height, col_tap : col_tap + width]
            pre_act = pre_act + jnp.einsum(
                "nfhwc,cd->nfhwd",
                window,
                spatial_weight[row_tap, col_tap],
                preferred_element_type=jnp.float32,
            )
    activated = jax.nn.silu(pre_act).astype(jnp.bfloat16)
    mixing = jnp.zeros(upsampled.shape, jnp.float32)
    for offset in range(3):
        mixing = mixing + jnp.einsum(
            "nfhwc,cd->nfhwd",
            delayed(activated, offset),
            temporal_weight[offset],
            preferred_element_type=jnp.float32,
        )
    alive_mask = (jnp.arange(frame_count)[None, :] < lengths[:, None]).astype(jnp.float32)[
        :, :, None, None, None
    ]
    decoded = (alive_mask * (upsampled.astype(jnp.float32) + mixing)).astype(jnp.bfloat16)
    chosen = jax.vmap(lambda clip_frames, indices: jnp.take(clip_frames, indices, axis=0))(
        decoded, critic_frames
    )
    hidden = jnp.einsum(
        "nqhwc,ce->nqhwe", chosen, critic_weight, preferred_element_type=jnp.float32
    )
    feature = space_sum(jnp.sum(jax.nn.gelu(hidden), axis=(2, 3))) / (height * groups * width)
    score_val = jnp.sum(feature * critic_head, axis=-1)
    factor = -jax.nn.sigmoid(-score_val)[..., None] * critic_head
    unused, pullback = jax.vjp(jax.nn.gelu, hidden)
    gelu_slope = pullback(jnp.broadcast_to(factor[..., None, None, :], hidden.shape))[0].astype(
        jnp.bfloat16
    )
    slope_rows = jnp.einsum(
        "nqhwe,ce->nqhwc", gelu_slope, critic_weight, preferred_element_type=jnp.float32
    )
    selector = (critic_frames[:, :, None] == jnp.arange(frame_count)[None, None, :]).astype(
        jnp.float32
    )
    adverse_frames = jnp.einsum(
        "nqf,nqhwc->nfhwc", selector, slope_rows, precision=lax.Precision.HIGHEST
    )
    loss_scale = 1.0 / math.sqrt(clip_count * frame_count * height * groups * width)
    cotangent = (
        alive_mask * loss_scale * (recon_grad.astype(jnp.float32) + adverse_frames)
    ).astype(jnp.bfloat16)
    temporal_grad = jnp.stack(
        [
            jnp.einsum(
                "nfhwc,nfhwd->cd",
                delayed(activated, offset),
                cotangent,
                preferred_element_type=jnp.float32,
            )
            for offset in range(3)
        ]
    )
    act_grad = jnp.zeros(upsampled.shape, jnp.float32)
    for offset in range(3):
        act_grad = act_grad + jnp.einsum(
            "nfhwd,cd->nfhwc",
            advanced(cotangent, offset),
            temporal_weight[offset],
            preferred_element_type=jnp.float32,
        )
    pre_slope = (act_grad * silu_slope(pre_act)).astype(jnp.bfloat16)
    tap_grads = []
    for row_tap in range(3):
        for col_tap in range(3):
            window = padded[:, :, row_tap : row_tap + height, col_tap : col_tap + width]
            tap_grads.append(
                jnp.einsum("nfhwc,nfhwd->cd", window, pre_slope, preferred_element_type=jnp.float32)
            )
    spatial_grad = jnp.stack(tap_grads).reshape(devices, -1)
    temporal_grad = temporal_grad.reshape(devices, -1)
    core, x_bit, y_bit = ("dp", 0), ("dp", 1), ("dp", 2)
    z_lo, z_hi = ("space", 0), ("space", 1)
    nd = lax.axis_size("dp")
    if nd == 8 and groups == 4:
        orders = ([core, x_bit, y_bit, z_lo, z_hi], [core, y_bit, x_bit, z_hi, z_lo])
    else:
        plain = [("dp", i) for i in range(nd.bit_length() - 1)]
        orders = (plain + [("space", i) for i in range(groups.bit_length() - 1)],)
    share = halving_scatter(jnp.concatenate([spatial_grad, temporal_grad], axis=1), orders)
    spatial_width = spatial_grad.shape[1]
    return (decoded, share[:spatial_width], share[spatial_width:])


def solution(mesh):
    placed = (
        P("dp", None, "space", None, None),
        P("dp"),
        P(),
        P(),
        P(),
        P(),
        P("dp", None),
        P("dp", None, "space", None, None),
    )
    return jax.shard_map(
        on_device,
        mesh=mesh,
        in_specs=placed,
        out_specs=(P("dp", None, "space", None, None), P(("dp", "space")), P(("dp", "space"))),
        check_vma=False,
    )
```

profile of v0, /device:TPU:0, one launch (start us, length us, event | category | flops | bytes accessed | tf_op | source)
XLA Modules:
  0.0 126.5 jit_solution(14719592256686865451)
XLA Ops:
  0.6 1.4 %collective-permute-start.1 = (bf16[1,33,1,8,256]{4,3,2,1,0:T(8,128)(2,1)}, bf16[1,33,1,8,256]{4,3,2,1,0:T(8,128)(2,1)S(1)}, u32[]{:S(2)}, u32[]{:S(2)}) collective-permute-start(bf16[1,33,1,8,256]{4,3,2,1,0:T(8,128)(2,1)} %param.8), channel_id=1, source_target_pairs={{1,0},{2,1},{3,2},{5,4},{6,5},{7,6},{9,8},{10,9},{11,10},{13,12},{... | collective-permute-start | bytes 405512 | tf_op jit(solution)/shard_map/ppermute | solution.py:20
  2.1 5.6 %collective-permute-start = (bf16[1,33,1,8,256]{4,3,2,1,0:T(8,128)(2,1)}, bf16[1,33,1,8,256]{4,3,2,1,0:T(8,128)(2,1)S(1)}, u32[]{:S(2)}, u32[]{:S(2)}) collective-permute-start(bf16[1,33,1,8,256]{4,3,2,1,0:T(8,128)(2,1)} %param.8), channel_id=1, source_target_pairs={{0,1},{1,2},{2,3},{4,5},{5,6},{6,7},{8,9},{9,10},{10,11},{12,13},{... | collective-permute-start | bytes 405512 | tf_op jit(solution)/shard_map/ppermute | solution.py:19
  9.7 1.1 broadcast_in_dim.46
  16.2 1.4 %multiply_convert_fusion = (bf16[33,2,16,256]{3,2,1,0:T(8,128)(2,1)S(1)}, f32[33,2,16,256]{3,2,1,0:T(8,128)}) fusion(f32[33,2,16,256]{3,2,1,0:T(8,128)S(1)} %convolution_add_fusion.5, bf16[3,3,256,256]{3,2,1,0:T(8,128)(2,1)S(1)} %copy-done.8, bf16[1,33,4,18,256]{4,3,2,1,0:T(8,128)(2,1)S(1)} %fusion.5), kind=kOutput, calls=%fused_computation.57 | convolution fusion | flops 140034048 | bytes 3375104 | tf_op jit(solution)/shard_map/nfhwc,cd->nfhwd/dot_general | solution.py:125
  18.9 1.1 fusion.16
  20.0 2.3 %gather_fusion = bf16[8,2,16,256]{3,2,1,0:T(8,128)(2,1)} fusion(bf16[1,33,2,16,256]{4,3,2,1,0:T(8,128)(2,1)} %fusion.16, s32[8]{0:T(128)S(1)} %or_bitcast_fusion), kind=kCustom, calls=%fused_computation | custom fusion | bytes 262208 | tf_op jit(solution)/shard_map/vmap(jit(_take))/gather | solution.py:144
  22.3 1.9 %fusion.55 = (f32[8,256]{1,0:T(8,128)S(1)}, f32[8,2,16,256]{3,2,1,0:T(8,128)}) fusion(bf16[256,256]{1,0:T(8,128)(2,1)S(1)} %copy-done, bf16[8,2,16,256]{3,2,1,0:T(8,128)(2,1)} %gather_fusion, pred[8]{0:T(512)(128)(4,1)S(1)} %and_bitcast_fusion), kind=kOutput, calls=%fused_computation.104 | convolution fusion | flops 34207744 | bytes 532488 | tf_op jit(solution)/shard_map/nqhwc,ce->nqhwe/dot_general | solution.py:147
  24.1 2.0 %collective-permute-start.2 = (f32[1,8,256]{2,1,0:T(8,128)S(1)}, f32[1,8,256]{2,1,0:T(8,128)S(1)}, u32[]{:S(2)}, u32[]{:S(2)}) collective-permute-start(f32[1,8,256]{2,1,0:T(8,128)S(1)} %bitcast.326), channel_id=1, source_target_pairs={{0,1},{1,0},{2,3},{3,2},{4,5},{5,4},{6,7},{7,6},{8,9},{9,8},{10,11... | collective-permute-start | bytes 24584 | tf_op jit(solution)/shard_map/ppermute | solution.py:57
  26.2 1.6 %collective-permute-done.2 = f32[1,8,256]{2,1,0:T(8,128)S(1)} collective-permute-done((f32[1,8,256]{2,1,0:T(8,128)S(1)}, f32[1,8,256]{2,1,0:T(8,128)S(1)}, u32[]{:S(2)}, u32[]{:S(2)}) %collective-permute-start.2) | collective-permute-done | bytes 8224 | tf_op jit(solution)/shard_map/ppermute | solution.py:57
  27.8 3.0 %collective-permute-start.3 = (f32[1,8,256]{2,1,0:T(8,128)S(1)}, f32[1,8,256]{2,1,0:T(8,128)S(1)}, u32[]{:S(2)}, u32[]{:S(2)}) collective-permute-start(f32[1,8,256]{2,1,0:T(8,128)S(1)} %bitcast_add_fusion), channel_id=1, source_target_pairs={{0,2},{1,3},{2,0},{3,1},{4,6},{5,7},{6,4},{7,5},{8,10},{9,11},{10,... | collective-permute-start | bytes 24584 | tf_op jit(solution)/shard_map/ppermute | solution.py:57
  30.8 1.6 %collective-permute-done.3 = f32[1,8,256]{2,1,0:T(8,128)S(1)} collective-permute-done((f32[1,8,256]{2,1,0:T(8,128)S(1)}, f32[1,8,256]{2,1,0:T(8,128)S(1)}, u32[]{:S(2)}, u32[]{:S(2)}) %collective-permute-start.3) | collective-permute-done | bytes 8224 | tf_op jit(solution)/shard_map/ppermute | solution.py:57
  32.7 1.1 fusion.53
  36.2 1.4 %fusion.63 = f32[33,2,16,256]{3,2,1,0:T(8,128)} fusion(bf16[33,2,16,256]{3,0,2,1:T(8,128)(2,1)S(1)} %bitcast.314, bf16[3,256,256]{2,1,0:T(8,128)(2,1)S(1)} %copy-done.7), kind=kOutput, calls=%fused_computation.115 | convolution fusion | flops 138412032 | bytes 1867776 | tf_op jit(solution)/shard_map/nfhwd,cd->nfhwc/dot_general | solution.py:183
  37.6 1.5 %slice_bitcast_fusion = (bf16[33,2,16,256]{3,0,2,1:T(8,128)(2,1)}, bf16[33,2,16,256]{3,0,2,1:T(8,128)(2,1)}) fusion(bf16[1,33,2,16,256]{4,1,3,2,0:T(8,128)(2,1)S(1)} %fusion.13), kind=kLoop, calls=%fused_computation.64 | loop fusion | bytes 1622016 | tf_op jit(solution)/shard_map/reshape.71
  40.0 1.3 reshape.459
  41.3 2.0 %convolution_add_fusion.1 = f32[33,2,16,256]{3,2,1,0:T(8,128)S(1)} fusion(f32[33,2,16,256]{3,2,1,0:T(8,128)} %fusion.63, bf16[33,2,16,256]{3,0,2,1:T(8,128)(2,1)} %get-tuple-element.18, bf16[3,256,256]{2,1,0:T(8,128)(2,1)} %param.11), kind=kOutput, calls=%fused_computation.17 | convolution fusion | flops 138682368 | bytes 2949120 | tf_op jit(solution)/shard_map/nfhwd,cd->nfhwc/dot_general | solution.py:183
  43.3 1.5 %fusion.14 = bf16[33,2,16,256]{3,2,1,0:T(8,128)(2,1)S(1)} fusion(f32[33,2,16,256]{3,2,1,0:T(8,128)S(1)} %convolution_add_fusion.1, f32[33,2,16,256]{3,2,1,0:T(8,128)S(1)} %copy-done.13, bf16[33,2,16,256]{3,0,2,1:T(8,128)(2,1)S(1)} %copy-done.10, bf16[3,256,256]{2,1,0:T(8,128)(2,1)} %param.11), kind=kOutput, calls=%fused_computation.33 | convolution fusion | flops 141115392 | bytes 3375104 | tf_op jit(solution)/shard_map/nfhwd,cd->nfhwc/dot_general | solution.py:183
  44.8 1.1 fusion.25
  45.9 1.1 fusion.24
  47.0 1.1 fusion.23
  48.1 1.1 fusion.22
  49.2 1.1 fusion.21
  50.3 1.1 fusion.20
  51.4 1.1 fusion.19
  52.5 1.1 fusion.18
  53.6 1.1 fusion.17
  54.7 1.8 %reshape.458 = f32[32,18432]{1,0:T(8,128)S(1)} reshape(f32[9,256,256]{2,1,0:T(8,128)} %fusion.17) | data formatting | bytes 4718592 | tf_op jit(solution)/shard_map/reshape | solution.py:197
  56.5 1.9 %pad_maximum_fusion = f32[32,24576]{1,0:T(8,128)} fusion(f32[32,6144]{1,0:T(8,128)S(1)} %reshape.459, f32[32,18432]{1,0:T(8,128)S(1)} %reshape.458), kind=kLoop, calls=%fused_computation.4 | loop fusion | flops 786432 | bytes 6291456 | tf_op jit(solution)/shard_map/concatenate | solution.py:207
  58.4 4.2 %reshape.460 = f32[4,2,98304]{2,1,0:T(2,128)S(1)} reshape(f32[32,24576]{1,0:T(8,128)} %pad_maximum_fusion) | data formatting | bytes 6291456 | tf_op jit(solution)/shard_map/reshape | solution.py:66
  62.6 11.7 %fusion.7 = (f32[4,98304]{1,0:T(4,128)}, f32[4,98304]{1,0:T(4,128)}) fusion(pred[]{:T(512)S(6)} %eq.55, f32[4,2,98304]{2,1,0:T(2,128)S(1)} %reshape.460), kind=kLoop, calls=%fused_computation.13 | loop fusion | flops 786432 | bytes 6291457 | tf_op jit(solution)/shard_map/jit(_where)/select_n | solution.py:70
  74.3 3.5 %select_n.263 = f32[16,24576]{1,0:T(8,128)} reshape(f32[4,98304]{1,0:T(4,128)} %get-tuple-element.3) | data formatting | bytes 3145728 | tf_op jit(solution)/shard_map/jit(_where)/select_n | solution.py:70
  78.6 2.9 %collective-permute-done.4 = f32[16,24576]{1,0:T(8,128)} collective-permute-done((f32[16,24576]{1,0:T(8,128)}, f32[16,24576]{1,0:T(8,128)}, u32[]{:S(2)}, u32[]{:S(2)}) %collective-permute-start.4) | collective-permute-done | bytes 1572896 | tf_op jit(solution)/shard_map/ppermute | solution.py:72
  81.5 1.6 %add.185 = f32[16,24576]{1,0:T(8,128)S(1)} add(f32[16,24576]{1,0:T(8,128)S(1)} %select_n.261, f32[16,24576]{1,0:T(8,128)} %collective-permute-done.4) | non-fusion elementwise | flops 393216 | bytes 4718592 | tf_op jit(solution)/shard_map/add | solution.py:72
  83.8 2.6 %fusion.42 = (f32[2,49152]{1,0:T(2,128)S(1)}, f32[2,49152]{1,0:T(2,128)S(1)}) fusion(pred[]{:T(512)S(6)} %eq.54, f32[2,2,49152]{2,1,0:T(2,128)S(1)} %reshape.461), kind=kLoop, calls=%fused_computation.84 | loop fusion | flops 196608 | bytes 1572865 | tf_op jit(solution)/shard_map/jit(_where)/select_n | solution.py:70
  86.8 1.9 %collective-permute-start.5 = (f32[8,12288]{1,0:T(8,128)S(1)}, f32[8,12288]{1,0:T(8,128)S(1)}, u32[]{:S(2)}, u32[]{:S(2)}) collective-permute-start(f32[8,12288]{1,0:T(8,128)S(1)} %select_n.267), channel_id=1, source_target_pairs={{0,8},{4,12},{8,0},{12,4},{16,24},{20,28},{24,16},{28,20},{1,9},{5... | collective-permute-start | bytes 1179656 | tf_op jit(solution)/shard_map/ppermute | solution.py:72
  89.4 2.2 %fusion.44 = (f32[98304]{0:T(1024)S(1)}, f32[98304]{0:T(1024)S(1)}) fusion(pred[]{:T(512)S(6)} %eq.53, f32[1,2,98304]{2,1,0:T(2,128)S(1)} %reshape.466), kind=kLoop, calls=%fused_computation.86 | loop fusion | flops 196608 | bytes 1572865 | tf_op jit(solution)/shard_map/jit(_where)/select_n | solution.py:70
  91.7 1.6 %collective-permute-start.9 = (f32[8,12288]{1,0:T(8,128)S(1)}, f32[8,12288]{1,0:T(8,128)S(1)}, u32[]{:S(2)}, u32[]{:S(2)}) collective-permute-start(f32[8,12288]{1,0:T(8,128)S(1)} %select_n.287), channel_id=1, source_target_pairs={{0,16},{4,20},{8,24},{12,28},{16,0},{20,4},{24,8},{28,12},{1,17},{... | collective-permute-start | bytes 1179656 | tf_op jit(solution)/shard_map/ppermute | solution.py:72
  93.6 4.5 %collective-permute-done.5 = f32[8,12288]{1,0:T(8,128)S(1)} collective-permute-done((f32[8,12288]{1,0:T(8,128)S(1)}, f32[8,12288]{1,0:T(8,128)S(1)}, u32[]{:S(2)}, u32[]{:S(2)}) %collective-permute-start.5) | collective-permute-done | bytes 393248 | tf_op jit(solution)/shard_map/ppermute | solution.py:72
  98.5 1.1 fusion.57
  99.7 1.8 %collective-permute-start.6 = (f32[4,12288]{1,0:T(4,128)S(1)}, f32[4,12288]{1,0:T(4,128)S(1)}, u32[]{:S(2)}, u32[]{:S(2)}) collective-permute-start(f32[4,12288]{1,0:T(4,128)S(1)} %select_n.271), channel_id=1, source_target_pairs={{0,16},{4,20},{8,24},{12,28},{16,0},{20,4},{24,8},{28,12},{1,17},{... | collective-permute-start | bytes 589832 | tf_op jit(solution)/shard_map/ppermute | solution.py:72
  101.5 2.0 %collective-permute-done.9 = f32[8,12288]{1,0:T(8,128)S(1)} collective-permute-done((f32[8,12288]{1,0:T(8,128)S(1)}, f32[8,12288]{1,0:T(8,128)S(1)}, u32[]{:S(2)}, u32[]{:S(2)}) %collective-permute-start.9) | collective-permute-done | bytes 393248 | tf_op jit(solution)/shard_map/ppermute | solution.py:72
  104.1 1.1 fusion.59
  105.6 1.3 collective-permute-done.6
  107.0 4.0 %collective-permute-done.10 = f32[4,12288]{1,0:T(4,128)S(1)} collective-permute-done((f32[4,12288]{1,0:T(4,128)S(1)}, f32[4,12288]{1,0:T(4,128)S(1)}, u32[]{:S(2)}, u32[]{:S(2)}) %collective-permute-start.10) | collective-permute-done | bytes 196640 | tf_op jit(solution)/shard_map/ppermute | solution.py:72
  111.9 2.5 %collective-permute-start.11 = (f32[2,12288]{1,0:T(2,128)S(1)}, f32[2,12288]{1,0:T(2,128)S(1)}, u32[]{:S(2)}, u32[]{:S(2)}) collective-permute-start(f32[2,12288]{1,0:T(2,128)S(1)} %select_n.295), channel_id=1, source_target_pairs={{0,2},{1,3},{2,0},{3,1},{4,6},{5,7},{6,4},{7,5},{8,10},{9,11},{10,... | collective-permute-start | bytes 294920 | tf_op jit(solution)/shard_map/ppermute | solution.py:72
  115.7 2.9 %collective-permute-done.11 = f32[2,12288]{1,0:T(2,128)S(1)} collective-permute-done((f32[2,12288]{1,0:T(2,128)S(1)}, f32[2,12288]{1,0:T(2,128)S(1)}, u32[]{:S(2)}, u32[]{:S(2)}) %collective-permute-start.11) | collective-permute-done | bytes 98336 | tf_op jit(solution)/shard_map/ppermute | solution.py:72
  120.2 2.3 %collective-permute-start.8 = (f32[1,12288]{1,0:T(1,128)S(1)}, f32[1,12288]{1,0:T(1,128)S(1)}, u32[]{:S(2)}, u32[]{:S(2)}) collective-permute-start(f32[1,12288]{1,0:T(1,128)S(1)} %fusion.111), channel_id=1, source_target_pairs={{0,2},{1,3},{2,0},{3,1},{4,6},{5,7},{6,4},{7,5},{8,10},{9,11},{10,... | collective-permute-start | bytes 147464 | tf_op jit(solution)/shard_map/ppermute | solution.py:72
  123.6 2.2 %collective-permute-done.8 = f32[1,12288]{1,0:T(1,128)S(1)} collective-permute-done((f32[1,12288]{1,0:T(1,128)S(1)}, f32[1,12288]{1,0:T(1,128)S(1)}, u32[]{:S(2)}, u32[]{:S(2)}) %collective-permute-start.8) | collective-permute-done | bytes 49184 | tf_op jit(solution)/shard_map/ppermute | solution.py:72
  (104 shorter events, 21.5 us)
Async XLA Ops:
  0.6 21.7 %copy-start = (bf16[256,256]{1,0:T(8,128)(2,1)S(1)}, bf16[256,256]{1,0:T(8,128)(2,1)}, u32[]{:S(2)}) copy-start(bf16[256,256]{1,0:T(8,128)(2,1)} %param.12) | copy-start | bytes 393220
  0.6 11.1 %collective-permute-start.1 = (bf16[1,33,1,8,256]{4,3,2,1,0:T(8,128)(2,1)}, bf16[1,33,1,8,256]{4,3,2,1,0:T(8,128)(2,1)S(1)}, u32[]{:S(2)}, u32[]{:S(2)}) collective-permute-start(bf16[1,33,1,8,256]{4,3,2,1,0:T(8,128)(2,1)} %param.8), channel_id=1, source_target_pairs={{1,0},{2,1},{3,2},{5,4},{6,5},{7,6},{9,8},{10,9},{11,10},{13,12},{... | collective-permute-start | bytes 405512 | tf_op jit(solution)/shard_map/ppermute | solution.py:20
  2.1 9.9 %collective-permute-start = (bf16[1,33,1,8,256]{4,3,2,1,0:T(8,128)(2,1)}, bf16[1,33,1,8,256]{4,3,2,1,0:T(8,128)(2,1)S(1)}, u32[]{:S(2)}, u32[]{:S(2)}) collective-permute-start(bf16[1,33,1,8,256]{4,3,2,1,0:T(8,128)(2,1)} %param.8), channel_id=1, source_target_pairs={{0,1},{1,2},{2,3},{4,5},{5,6},{6,7},{8,9},{9,10},{10,11},{12,13},{... | collective-permute-start | bytes 405512 | tf_op jit(solution)/shard_map/ppermute | solution.py:19
  12.0 3.9 %copy-start.2 = (bf16[1,33,1,16,256]{4,3,2,1,0:T(8,128)(2,1)}, bf16[1,33,1,16,256]{4,3,2,1,0:T(8,128)(2,1)S(1)}, u32[]{:S(2)}) copy-start(bf16[1,33,1,16,256]{4,3,2,1,0:T(8,128)(2,1)S(1)} %slice.168) | copy-start | bytes 811012
  12.3 1.7 %copy-start.4 = (bf16[1,33,1,16,256]{4,3,2,1,0:T(8,128)(2,1)}, bf16[1,33,1,16,256]{4,3,2,1,0:T(8,128)(2,1)S(1)}, u32[]{:S(2)}) copy-start(bf16[1,33,1,16,256]{4,3,2,1,0:T(8,128)(2,1)S(1)} %slice.167) | copy-start | bytes 811012
  12.3 1.3 %copy-start.8 = (bf16[3,3,256,256]{3,2,1,0:T(8,128)(2,1)S(1)}, bf16[3,3,256,256]{3,2,1,0:T(8,128)(2,1)}, u32[]{:S(2)}) copy-start(bf16[3,3,256,256]{3,2,1,0:T(8,128)(2,1)} %param.10) | copy-start | bytes 3538948
  16.2 1.4 %copy-start.7 = (bf16[3,256,256]{2,1,0:T(8,128)(2,1)S(1)}, bf16[3,256,256]{2,1,0:T(8,128)(2,1)}, u32[]{:S(2)}) copy-start(bf16[3,256,256]{2,1,0:T(8,128)(2,1)} %param.11) | copy-start | bytes 1179652
  17.9 1.1 copy-start.6
  18.9 7.2 %copy-start.11 = (f32[256]{0:T(256)S(1)}, f32[256]{0:T(256)}, u32[]{:S(2)}) copy-start(f32[256]{0:T(256)} %param.13) | copy-start | bytes 3076
  20.0 14.0 %copy-start.12 = (s32[1,8]{1,0:T(1,128)S(1)}, s32[1,8]{1,0:T(1,128)}, u32[]{:S(2)}) copy-start(s32[1,8]{1,0:T(1,128)} %param.14) | copy-start | bytes 100
  24.1 3.7 %collective-permute-start.2 = (f32[1,8,256]{2,1,0:T(8,128)S(1)}, f32[1,8,256]{2,1,0:T(8,128)S(1)}, u32[]{:S(2)}, u32[]{:S(2)}) collective-permute-start(f32[1,8,256]{2,1,0:T(8,128)S(1)} %bitcast.326), channel_id=1, source_target_pairs={{0,1},{1,0},{2,3},{3,2},{4,5},{5,4},{6,7},{7,6},{8,9},{9,8},{10,11... | collective-permute-start | bytes 24584 | tf_op jit(solution)/shard_map/ppermute | solution.py:57
  27.8 4.7 %collective-permute-start.3 = (f32[1,8,256]{2,1,0:T(8,128)S(1)}, f32[1,8,256]{2,1,0:T(8,128)S(1)}, u32[]{:S(2)}, u32[]{:S(2)}) collective-permute-start(f32[1,8,256]{2,1,0:T(8,128)S(1)} %bitcast_add_fusion), channel_id=1, source_target_pairs={{0,2},{1,3},{2,0},{3,1},{4,6},{5,7},{6,4},{7,5},{8,10},{9,11},{10,... | collective-permute-start | bytes 24584 | tf_op jit(solution)/shard_map/ppermute | solution.py:57
  30.8 3.2 %copy-start.9 = (bf16[1,33,2,16,256]{4,3,2,1,0:T(8,128)(2,1)S(1)}, bf16[1,33,2,16,256]{4,3,2,1,0:T(8,128)(2,1)}, u32[]{:S(2)}) copy-start(bf16[1,33,2,16,256]{4,3,2,1,0:T(8,128)(2,1)} %param.15) | copy-start | bytes 1622020
  41.3 2.0 %copy-start.10 = (bf16[33,2,16,256]{3,0,2,1:T(8,128)(2,1)S(1)}, bf16[33,2,16,256]{3,0,2,1:T(8,128)(2,1)}, u32[]{:S(2)}) copy-start(bf16[33,2,16,256]{3,0,2,1:T(8,128)(2,1)} %get-tuple-element.17) | copy-start | bytes 1622020
  41.3 2.0 %copy-start.13 = (f32[33,2,16,256]{3,2,1,0:T(8,128)S(1)}, f32[33,2,16,256]{3,2,1,0:T(8,128)}, u32[]{:S(2)}) copy-start(f32[33,2,16,256]{3,2,1,0:T(8,128)} %get-tuple-element.25) | copy-start | bytes 3244036
  44.8 1.1 copy-start.5
  51.4 1.1 copy-start.3
  74.3 3.5 %copy-start.1 = (f32[4,98304]{1,0:T(4,128)S(1)}, f32[4,98304]{1,0:T(4,128)}, u32[]{:S(2)}) copy-start(f32[4,98304]{1,0:T(4,128)} %get-tuple-element.4) | copy-start | bytes 4718596
  77.7 3.8 %collective-permute-start.4 = (f32[16,24576]{1,0:T(8,128)}, f32[16,24576]{1,0:T(8,128)}, u32[]{:S(2)}, u32[]{:S(2)}) collective-permute-start(f32[16,24576]{1,0:T(8,128)} %select_n.263), channel_id=1, source_target_pairs={{0,4},{4,0},{8,12},{12,8},{16,20},{20,16},{24,28},{28,24},{1,5},{5... | collective-permute-start | bytes 4718600 | tf_op jit(solution)/shard_map/ppermute | solution.py:72
  86.8 11.3 %collective-permute-start.5 = (f32[8,12288]{1,0:T(8,128)S(1)}, f32[8,12288]{1,0:T(8,128)S(1)}, u32[]{:S(2)}, u32[]{:S(2)}) collective-permute-start(f32[8,12288]{1,0:T(8,128)S(1)} %select_n.267), channel_id=1, source_target_pairs={{0,8},{4,12},{8,0},{12,4},{16,24},{20,28},{24,16},{28,20},{1,9},{5... | collective-permute-start | bytes 1179656 | tf_op jit(solution)/shard_map/ppermute | solution.py:72
  91.7 11.8 %collective-permute-start.9 = (f32[8,12288]{1,0:T(8,128)S(1)}, f32[8,12288]{1,0:T(8,128)S(1)}, u32[]{:S(2)}, u32[]{:S(2)}) collective-permute-start(f32[8,12288]{1,0:T(8,128)S(1)} %select_n.287), channel_id=1, source_target_pairs={{0,16},{4,20},{8,24},{12,28},{16,0},{20,4},{24,8},{28,12},{1,17},{... | collective-permute-start | bytes 1179656 | tf_op jit(solution)/shard_map/ppermute | solution.py:72
  99.7 7.2 %collective-permute-start.6 = (f32[4,12288]{1,0:T(4,128)S(1)}, f32[4,12288]{1,0:T(4,128)S(1)}, u32[]{:S(2)}, u32[]{:S(2)}) collective-permute-start(f32[4,12288]{1,0:T(4,128)S(1)} %select_n.271), channel_id=1, source_target_pairs={{0,16},{4,20},{8,24},{12,28},{16,0},{20,4},{24,8},{28,12},{1,17},{... | collective-permute-start | bytes 589832 | tf_op jit(solution)/shard_map/ppermute | solution.py:72
  105.3 5.7 %collective-permute-start.10 = (f32[4,12288]{1,0:T(4,128)S(1)}, f32[4,12288]{1,0:T(4,128)S(1)}, u32[]{:S(2)}, u32[]{:S(2)}) collective-permute-start(f32[4,12288]{1,0:T(4,128)S(1)} %select_n.291), channel_id=1, source_target_pairs={{0,8},{4,12},{8,0},{12,4},{16,24},{20,28},{24,16},{28,20},{1,9},{5... | collective-permute-start | bytes 589832 | tf_op jit(solution)/shard_map/ppermute | solution.py:72
  111.9 6.7 %collective-permute-start.11 = (f32[2,12288]{1,0:T(2,128)S(1)}, f32[2,12288]{1,0:T(2,128)S(1)}, u32[]{:S(2)}, u32[]{:S(2)}) collective-permute-start(f32[2,12288]{1,0:T(2,128)S(1)} %select_n.295), channel_id=1, source_target_pairs={{0,2},{1,3},{2,0},{3,1},{4,6},{5,7},{6,4},{7,5},{8,10},{9,11},{10,... | collective-permute-start | bytes 294920 | tf_op jit(solution)/shard_map/ppermute | solution.py:72
  114.7 5.3 %collective-permute-start.7 = (f32[2,12288]{1,0:T(2,128)S(1)}, f32[2,12288]{1,0:T(2,128)S(1)}, u32[]{:S(2)}, u32[]{:S(2)}) collective-permute-start(f32[2,12288]{1,0:T(2,128)S(1)} %bitcast.324), channel_id=1, source_target_pairs={{0,1},{1,0},{2,3},{3,2},{4,5},{5,4},{6,7},{7,6},{8,9},{9,8},{10,11... | collective-permute-start | bytes 294920 | tf_op jit(solution)/shard_map/ppermute | solution.py:72
  118.7 4.2 %collective-permute-start.12 = (f32[1,12288]{1,0:T(1,128)S(1)}, f32[1,12288]{1,0:T(1,128)S(1)}, u32[]{:S(2)}, u32[]{:S(2)}) collective-permute-start(f32[1,12288]{1,0:T(1,128)S(1)} %fusion.114), channel_id=1, source_target_pairs={{0,1},{1,0},{2,3},{3,2},{4,5},{5,4},{6,7},{7,6},{8,9},{9,8},{10,11... | collective-permute-start | bytes 147464 | tf_op jit(solution)/shard_map/ppermute | solution.py:72
  120.2 5.6 %collective-permute-start.8 = (f32[1,12288]{1,0:T(1,128)S(1)}, f32[1,12288]{1,0:T(1,128)S(1)}, u32[]{:S(2)}, u32[]{:S(2)}) collective-permute-start(f32[1,12288]{1,0:T(1,128)S(1)} %fusion.111), channel_id=1, source_target_pairs={{0,2},{1,3},{2,0},{3,1},{4,6},{5,7},{6,4},{7,5},{8,10},{9,11},{10,... | collective-permute-start | bytes 147464 | tf_op jit(solution)/shard_map/ppermute | solution.py:72
where the time goes:
time: 127 us
  other arithmetic  29.6 us (23%)
  matrix products  24.5 us (19%)
  waiting for transfers between devices  24.2 us (19%)
  starting transfers between devices  23.7 us (19%)
  local copies, waits for them, and re-layouts  22.7 us (18%)
  between operations  1.9 us (1%)
    ppermute x9, waiting for transfers between devices, _halve(): lax.ppermute(send, axis, [(i, i ^ 1 << bit) for i in range(size)])  21 us
    select_n x8, other arithmetic, _halve(): send = jnp.where(upper, low, high)  19.4 us
    ppermute x9, starting transfers between devices, _halve(): lax.ppermute(send, axis, [(i, i ^ 1 << bit) for i in range(size)])  11.6 us
    dot_general x9, matrix products, on_device(): jnp.einsum('nfhwc,nfhwd->cd', window, pre_slope, preferred_element_type=j...  9.9 us
    reshape x7, local copies, waits for them, and re-layouts, _halve(): v = cur.reshape(hi, 2, lo * cur.shape[1])  6.64 us
    ppermute x1, starting transfers between devices, exchange_rows(): above = lax.ppermute(tail, axis, [(i, i + 1) for i in range(ends)])  5.6 us
    ppermute x2, starting transfers between devices, space_sum(): lax.ppermute(values, 'space', [(i, i ^ step) for i in range(count)])  5.03 us
    dot_general x3, matrix products, on_device(): jnp.einsum('nfhwd,cd->nfhwc', advanced(cotangent, offset), temporal_weigh...  4.81 us
  transfers between devices with their start and end apart: 13, of which 11 were waited for; matrix products, arithmetic and copies ran while one was open for 10% of the time, Pallas kernels for 0%

commit v1 on v0

--- a/solution.py
+++ b/solution.py
@@ -63,8 +63,8 @@
     pos = left.index((axis, bit))
     hi, lo = 1 << pos, 1 << (len(left) - 1 - pos)
     mine = (lax.axis_index(axis) // (1 << bit)) % 2
-    v = cur.reshape(hi, 2, lo * cur.shape[1])
-    low, high = v[:, 0].reshape(hi * lo, -1), v[:, 1].reshape(hi * lo, -1)
+    v = cur.reshape((hi, 2, lo) + cur.shape[1:])
+    low, high = v[:, 0].reshape((hi * lo,) + cur.shape[1:]), v[:, 1].reshape((hi * lo,) + cur.shape[1:])
     upper = mine == 1
     keep = jnp.where(upper, high, low)
     send = jnp.where(upper, low, high)
@@ -76,8 +76,8 @@
     nd, ns = lax.axis_size("dp"), lax.axis_size("space")
     bd, bs = _log2(nd), _log2(ns)
     if bd is None or bs is None:
-        flat = lax.psum_scatter(blocks.reshape(-1), "dp", scatter_dimension=0, tiled=True)
-        return lax.psum_scatter(flat, "space", scatter_dimension=0, tiled=True)
+        flat = lax.psum_scatter(blocks, "dp", scatter_dimension=0, tiled=True)
+        return lax.psum_scatter(flat, "space", scatter_dimension=0, tiled=True)[0]
     natural = [("dp", i) for i in reversed(range(bd))] + [("space", i) for i in reversed(range(bs))]
     shared = 0
     while shared < len(natural) and all(o[shared] == orders[0][shared] for o in orders):
@@ -92,7 +92,7 @@
         part, part_left = cur[:, p * width : (p + 1) * width], list(left)
         for axis, bit in order[shared:]:
             part = _halve(part, part_left, axis, bit)
-        outs.append(part.reshape(-1))
+        outs.append(part[0])
     return jnp.concatenate(outs)
 
 
@@ -194,8 +194,9 @@
             tap_grads.append(
                 jnp.einsum("nfhwc,nfhwd->cd", window, pre_slope, preferred_element_type=jnp.float32)
             )
-    spatial_grad = jnp.stack(tap_grads).reshape(devices, -1)
-    temporal_grad = temporal_grad.reshape(devices, -1)
+    channels = spatial_weight.shape[-1]
+    spatial_grad = jnp.stack(tap_grads).reshape(devices, -1, channels)
+    temporal_grad = temporal_grad.reshape(devices, -1, channels)
     core, x_bit, y_bit = ("dp", 0), ("dp", 1), ("dp", 2)
     z_lo, z_hi = ("space", 0), ("space", 1)
     nd = lax.axis_size("dp")
@@ -205,8 +206,8 @@
         plain = [("dp", i) for i in range(nd.bit_length() - 1)]
         orders = (plain + [("space", i) for i in range(groups.bit_length() - 1)],)
     share = halving_scatter(jnp.concatenate([spatial_grad, temporal_grad], axis=1), orders)
-    spatial_width = spatial_grad.shape[1]
-    return (decoded, share[:spatial_width], share[spatial_width:])
+    spatial_rows = spatial_grad.shape[1]
+    return (decoded, share[:spatial_rows].reshape(-1), share[spatial_rows:].reshape(-1))
 
 
 def solution(mesh):

time: 127 us -> 79.5 us (0.63)
  other arithmetic: 29.6 us -> 6.99 us
  local copies, waits for them, and re-layouts: 22.7 us -> 8.36 us
  matrix products: 24.5 us -> 13.7 us
  starting transfers between devices: 23.7 us -> 27.4 us
  waiting for transfers between devices: 24.2 us -> 20.8 us
    select_n x8 -> x7, other arithmetic: 19.4 us -> 0.15 us  [_halve(): send = jnp.where(upper, low, high)]
    reshape x9 -> x0, local copies, waits for them, and re-layouts: 9.71 us -> none  [the longest x7 6.64 us: _halve(): v = cur.reshape(hi, 2, lo * cur.shape[1])]
    dot_general x9, matrix products: 9.9 us -> 3.54 us  [on_device(): jnp.einsum('nfhwc,nfhwd->cd', window, pre_slope, preferred_element_type=j...]
    select_n x12 -> x0, local copies, waits for them, and re-layouts: 5.5 us -> none  [the longest x6 4.08 us: _halve(): send = jnp.where(upper, low, high)]
    ppermute x9, starting transfers between devices: 11.6 us -> 15.3 us  [_halve(): lax.ppermute(send, axis, [(i, i ^ 1 << bit) for i in range(size)])]
    dot_general x3, matrix products: 4.81 us -> 1.28 us  [on_device(): jnp.einsum('nfhwd,cd->nfhwc', advanced(cotangent, offset), temporal_weigh...]
    ppermute x9, waiting for transfers between devices: 21 us -> 17.5 us  [_halve(): lax.ppermute(send, axis, [(i, i ^ 1 << bit) for i in range(size)])]
    unnamed x29 -> x25, local copies, waits for them, and re-layouts: 1.31 us -> 4.53 us
  transfers between devices with their start and end apart: 13 -> 13, of which waited for: 11 -> 8; matrix products, arithmetic and copies ran while one was open for 10% -> 6% of each run, Pallas kernels for 0% -> 0%
where the time goes in v1:
time: 79.5 us; the launch traced here: 79.1 us
  starting transfers between devices  27.4 us (34%)
  waiting for transfers between devices  20.8 us (26%)
  matrix products  13.7 us (17%)
  local copies, waits for them, and re-layouts  8.36 us (11%)
  other arithmetic  6.99 us (9%)
  between operations  1.84 us (2%)
    ppermute x9, waiting for transfers between devices, _halve(): lax.ppermute(send, axis, [(i, i ^ 1 << bit) for i in range(size)])  17.5 us
    ppermute x9, starting transfers between devices, _halve(): lax.ppermute(send, axis, [(i, i ^ 1 << bit) for i in range(size)])  15.3 us
    ppermute x1, starting transfers between devices, exchange_rows(): above = lax.ppermute(tail, axis, [(i, i + 1) for i in range(ends)])  5.6 us
    ppermute x2, starting transfers between devices, space_sum(): lax.ppermute(values, 'space', [(i, i ^ step) for i in range(count)])  5.04 us
    unnamed x25, local copies, waits for them, and re-layouts  4.53 us
    dot_general x9, matrix products, on_device(): jnp.einsum('nfhwc,cd->nfhwd', window, spatial_weight[row_tap, col_tap], p...  3.89 us
    dot_general x9, matrix products, on_device(): jnp.einsum('nfhwc,nfhwd->cd', window, pre_slope, preferred_element_type=j...  3.54 us
    ppermute x2, waiting for transfers between devices, space_sum(): lax.ppermute(values, 'space', [(i, i ^ step) for i in range(count)])  3.26 us
  transfers between devices with their start and end apart: 13, of which 8 were waited for; matrix products, arithmetic and copies ran while one was open for 6% of the time, Pallas kernels for 0%

profile of v1, /device:TPU:0, one launch (start us, length us, event | category | flops | bytes accessed | tf_op | source)
XLA Modules:
  0.0 79.1 jit_solution(5356102169575093827)
XLA Ops:
  0.6 1.4 %collective-permute-start.1 = (bf16[1,33,1,8,256]{4,3,2,1,0:T(8,128)(2,1)}, bf16[1,33,1,8,256]{4,3,2,1,0:T(8,128)(2,1)S(1)}, u32[]{:S(2)}, u32[]{:S(2)}) collective-permute-start(bf16[1,33,1,8,256]{4,3,2,1,0:T(8,128)(2,1)} %param.8), channel_id=1, source_target_pairs={{1,0},{2,1},{3,2},{5,4},{6,5},{7,6},{9,8},{10,9},{11,10},{13,12},{... | collective-permute-start | bytes 405512 | tf_op jit(solution)/shard_map/ppermute | solution.py:20
  2.1 5.6 %collective-permute-start = (bf16[1,33,1,8,256]{4,3,2,1,0:T(8,128)(2,1)}, bf16[1,33,1,8,256]{4,3,2,1,0:T(8,128)(2,1)S(1)}, u32[]{:S(2)}, u32[]{:S(2)}) collective-permute-start(bf16[1,33,1,8,256]{4,3,2,1,0:T(8,128)(2,1)} %param.8), channel_id=1, source_target_pairs={{0,1},{1,2},{2,3},{4,5},{5,6},{6,7},{8,9},{9,10},{10,11},{12,13},{... | collective-permute-start | bytes 405512 | tf_op jit(solution)/shard_map/ppermute | solution.py:19
  7.7 0.7 fusion.115
  8.4 0.7 and_bitcast_fusion
  9.7 1.1 %broadcast_in_dim.46 = bf16[33,8,2,256]{3,2,1,0:T(2,128)(2,1)S(1)} broadcast(bf16[33,8,256]{2,1,0:T(8,128)(2,1)} %bitcast.408), dimensions={0,1,3} | broadcast | bytes 405504 | tf_op jit(solution)/shard_map/broadcast_in_dim | solution.py:26
  10.8 0.9 %convert_element_type.56 = f32[33,16,256]{2,1,0:T(8,128)} convert(bf16[33,16,256]{2,1,0:T(8,128)(2,1)S(1)} %broadcast_in_dim.47) | non-fusion elementwise | flops 135168 | bytes 811008 | tf_op jit(solution)/shard_map/convert_element_type | solution.py:143
  12.3 0.9 %fusion.5 = bf16[1,33,4,18,256]{4,3,2,1,0:T(8,128)(2,1)S(1)} fusion(bf16[1,33,1,16,256]{4,3,2,1,0:T(8,128)(2,1)S(1)} %slice.166, bf16[1,33,2,16,256]{4,3,2,1,0:T(8,128)(2,1)S(1)} %broadcast_in_dim.50, bf16[1,33,1,16,256]{4,3,2,1,0:T(8,128)(2,1)S(1)} %slice.165), kind=kLoop, calls=%fused_computation.10 | loop fusion | flops 7299072 | bytes 2297856 | tf_op jit(solution)/shard_map/concatenate | solution.py:115
  13.2 0.4 copy-done.6
  16.2 1.4 %multiply_convert_fusion = (bf16[33,2,16,256]{3,2,1,0:T(8,128)(2,1)S(1)}, f32[33,2,16,256]{3,2,1,0:T(8,128)}) fusion(f32[33,2,16,256]{3,2,1,0:T(8,128)S(1)} %convolution_add_fusion.5, bf16[3,3,256,256]{3,2,1,0:T(8,128)(2,1)S(1)} %copy-done.6, bf16[1,33,4,18,256]{4,3,2,1,0:T(8,128)(2,1)S(1)} %fusion.5), kind=kOutput, calls=%fused_computation.57 | convolution fusion | flops 140034048 | bytes 3375104 | tf_op jit(solution)/shard_map/nfhwc,cd->nfhwd/dot_general | solution.py:125
  18.2 0.7 copy-done.3
  18.9 1.1 %fusion.15 = bf16[1,33,2,16,256]{4,3,2,1,0:T(8,128)(2,1)} fusion(f32[33,2,16,256]{3,2,1,0:T(8,128)S(1)} %convolution_add_fusion.3, f32[33,16,256]{2,1,0:T(8,128)S(1)} %copy-done.3, f32[33]{0:T(128)S(1)} %compare_convert_fusion, bf16[1,33,2,16,256]{4,3,2,1,0:T(8,128)(2,1)S(1)} %bitcast.387, bf16[3,256,256]{2,1,0:T(8,128)(2,1)S(1)} %copy-done.4), kind=kOutput, calls=%fused_computation.35 | convolution fusion | flops 139493376 | bytes 2834944 | tf_op jit(solution)/shard_map/nfhwc,cd->nfhwd/dot_general | solution.py:134
  20.1 1.6 %gather_fusion = bf16[8,2,16,256]{3,2,1,0:T(8,128)(2,1)S(1)} fusion(bf16[1,33,2,16,256]{4,3,2,1,0:T(8,128)(2,1)} %fusion.15, s32[8]{0:T(128)S(1)} %or_bitcast_fusion), kind=kCustom, calls=%fused_computation | custom fusion | bytes 262208 | tf_op jit(solution)/shard_map/vmap(jit(_take))/gather | solution.py:144
  21.7 0.9 %fusion.52 = (f32[8,256]{1,0:T(8,128)S(1)}, f32[8,2,16,256]{3,2,1,0:T(8,128)}) fusion(bf16[256,256]{1,0:T(8,128)(2,1)S(1)} %copy-done, bf16[8,2,16,256]{3,2,1,0:T(8,128)(2,1)S(1)} %gather_fusion, pred[8]{0:T(512)(128)(4,1)S(1)} %and_bitcast_fusion), kind=kOutput, calls=%fused_computation.101 | convolution fusion | flops 34207744 | bytes 532488 | tf_op jit(solution)/shard_map/nqhwc,ce->nqhwe/dot_general | solution.py:147
  22.6 2.0 %collective-permute-start.2 = (f32[1,8,256]{2,1,0:T(8,128)S(1)}, f32[1,8,256]{2,1,0:T(8,128)S(1)}, u32[]{:S(2)}, u32[]{:S(2)}) collective-permute-start(f32[1,8,256]{2,1,0:T(8,128)S(1)} %bitcast.413), channel_id=1, source_target_pairs={{0,1},{1,0},{2,3},{3,2},{4,5},{5,4},{6,7},{7,6},{8,9},{9,8},{10,11... | collective-permute-start | bytes 24584 | tf_op jit(solution)/shard_map/ppermute | solution.py:57
  24.7 1.6 %collective-permute-done.2 = f32[1,8,256]{2,1,0:T(8,128)S(1)} collective-permute-done((f32[1,8,256]{2,1,0:T(8,128)S(1)}, f32[1,8,256]{2,1,0:T(8,128)S(1)}, u32[]{:S(2)}, u32[]{:S(2)}) %collective-permute-start.2) | collective-permute-done | bytes 8224 | tf_op jit(solution)/shard_map/ppermute | solution.py:57
  26.3 3.0 %collective-permute-start.3 = (f32[1,8,256]{2,1,0:T(8,128)S(1)}, f32[1,8,256]{2,1,0:T(8,128)S(1)}, u32[]{:S(2)}, u32[]{:S(2)}) collective-permute-start(f32[1,8,256]{2,1,0:T(8,128)S(1)} %bitcast_add_fusion.8), channel_id=1, source_target_pairs={{0,2},{1,3},{2,0},{3,1},{4,6},{5,7},{6,4},{7,5},{8,10},{9,11},{10,... | collective-permute-start | bytes 24584 | tf_op jit(solution)/shard_map/ppermute | solution.py:57
  29.3 1.6 %collective-permute-done.3 = f32[1,8,256]{2,1,0:T(8,128)S(1)} collective-permute-done((f32[1,8,256]{2,1,0:T(8,128)S(1)}, f32[1,8,256]{2,1,0:T(8,128)S(1)}, u32[]{:S(2)}, u32[]{:S(2)}) %collective-permute-start.3) | collective-permute-done | bytes 8224 | tf_op jit(solution)/shard_map/ppermute | solution.py:57
  31.2 1.1 %fusion.50 = bf16[8,2,16,256]{3,2,1,0:T(8,128)(2,1)S(1)} fusion(f32[8,2,16,256]{3,2,1,0:T(8,128)} %get-tuple-element.16, f32[8,256]{1,0:T(8,128)S(1)} %get-tuple-element.12, f32[8,256]{1,0:T(8,128)S(1)} %get-tuple-element.11), kind=kLoop, calls=%fused_computation.98 | loop fusion | flops 1245184 | bytes 409600 | tf_op jit(solution)/shard_map/convert_element_type | solution.py:154
  32.5 1.0 %fusion.12 = bf16[1,33,2,16,256]{4,1,3,2,0:T(8,128)(2,1)S(1)} fusion(f32[8,2,16,256]{3,0,2,1:T(8,128)S(1)} %fusion.58, bf16[1,33,2,16,256]{4,3,2,1,0:T(8,128)(2,1)S(1)} %copy-done.7, f32[33]{0:T(128)S(1)} %compare_select_fusion.1, s32[8]{0:T(128)S(1)} %bitcast.414), kind=kOutput, calls=%fused_computation.32 | convolution fusion | flops 27033864 | bytes 1343652 | tf_op jit(solution)/shard_map/nqf,nqhwc->nfhwc/dot_general | solution.py:163
  34.7 0.6 copy-done.5
  35.7 0.4 slice_bitcast_fusion
  36.5 0.9 %copy-done.10 = f32[33,2,16,256]{3,2,1,0:T(8,128)S(1)} copy-done((f32[33,2,16,256]{3,2,1,0:T(8,128)S(1)}, f32[33,2,16,256]{3,2,1,0:T(8,128)}, u32[]{:S(2)}) %copy-start.10) | copy-done | bytes 1081368
  37.4 0.6 fusion.13
  38.0 0.4 fusion.24
  38.3 0.6 copy-done.2
  38.9 0.4 fusion.23
  39.3 0.4 fusion.22
  40.1 0.4 fusion.20
  40.5 0.4 fusion.19
  41.3 0.4 fusion.17
  41.7 0.4 fusion.16
  42.2 0.4 broadcast_select_fusion.1
  42.7 3.5 %collective-permute-done.4 = f32[16,96,256]{2,1,0:T(8,128)} collective-permute-done((f32[16,96,256]{2,1,0:T(8,128)S(1)}, f32[16,96,256]{2,1,0:T(8,128)}, u32[]{:S(2)}, u32[]{:S(2)}) %collective-permute-start.4) | collective-permute-done | bytes 1572896 | tf_op jit(solution)/shard_map/ppermute | solution.py:72
  46.2 1.6 %bitcast_add_fusion = f32[16,96,256]{2,1,0:T(8,128)S(1)} fusion(f32[16,96,256]{2,1,0:T(8,128)} %collective-permute-done.4, f32[4,1,4,96,256]{4,3,2,1,0:T(8,128)S(1)} %get-tuple-element.3), kind=kLoop, calls=%fused_computation.13 | loop fusion | flops 393216 | bytes 4718592 | tf_op jit(solution)/shard_map/add | solution.py:72
  48.0 1.9 %collective-permute-start.9 = (f32[8,48,256]{2,1,0:T(8,128)S(1)}, f32[8,48,256]{2,1,0:T(8,128)S(1)}, u32[]{:S(2)}, u32[]{:S(2)}) collective-permute-start(f32[8,48,256]{2,1,0:T(8,128)S(1)} %select_bitcast_fusion), channel_id=1, source_target_pairs={{0,16},{4,20},{8,24},{12,28},{16,0},{20,4},{24,8},{28,12},{1,17},{... | collective-permute-start | bytes 1179656 | tf_op jit(solution)/shard_map/ppermute | solution.py:72
  49.9 1.6 %collective-permute-start.5 = (f32[8,48,256]{2,1,0:T(8,128)S(1)}, f32[8,48,256]{2,1,0:T(8,128)S(1)}, u32[]{:S(2)}, u32[]{:S(2)}) collective-permute-start(f32[8,48,256]{2,1,0:T(8,128)S(1)} %bitcast.406), channel_id=1, source_target_pairs={{0,8},{4,12},{8,0},{12,4},{16,24},{20,28},{24,16},{28,20},{1,9},{5... | collective-permute-start | bytes 1179656 | tf_op jit(solution)/shard_map/ppermute | solution.py:72
  51.5 7.8 %collective-permute-done.9 = f32[8,48,256]{2,1,0:T(8,128)S(1)} collective-permute-done((f32[8,48,256]{2,1,0:T(8,128)S(1)}, f32[8,48,256]{2,1,0:T(8,128)S(1)}, u32[]{:S(2)}, u32[]{:S(2)}) %collective-permute-start.9) | collective-permute-done | bytes 393248 | tf_op jit(solution)/shard_map/ppermute | solution.py:72
  59.4 1.8 %collective-permute-start.10 = (f32[4,48,256]{2,1,0:T(8,128)S(1)}, f32[4,48,256]{2,1,0:T(8,128)S(1)}, u32[]{:S(2)}, u32[]{:S(2)}) collective-permute-start(f32[4,48,256]{2,1,0:T(8,128)S(1)} %select_bitcast_fusion.1), channel_id=1, source_target_pairs={{0,8},{4,12},{8,0},{12,4},{16,24},{20,28},{24,16},{28,20},{1,9},{5... | collective-permute-start | bytes 589832 | tf_op jit(solution)/shard_map/ppermute | solution.py:72
  61.3 1.6 %collective-permute-start.6 = (f32[4,48,256]{2,1,0:T(8,128)S(1)}, f32[4,48,256]{2,1,0:T(8,128)S(1)}, u32[]{:S(2)}, u32[]{:S(2)}) collective-permute-start(f32[4,48,256]{2,1,0:T(8,128)S(1)} %select_bitcast_fusion.2), channel_id=1, source_target_pairs={{0,16},{4,20},{8,24},{12,28},{16,0},{20,4},{24,8},{28,12},{1,17},{... | collective-permute-start | bytes 589832 | tf_op jit(solution)/shard_map/ppermute | solution.py:72
  62.9 2.8 %collective-permute-done.10 = f32[4,48,256]{2,1,0:T(8,128)S(1)} collective-permute-done((f32[4,48,256]{2,1,0:T(8,128)S(1)}, f32[4,48,256]{2,1,0:T(8,128)S(1)}, u32[]{:S(2)}, u32[]{:S(2)}) %collective-permute-start.10) | collective-permute-done | bytes 196640 | tf_op jit(solution)/shard_map/ppermute | solution.py:72
  65.7 2.8 %collective-permute-start.11 = (f32[2,48,256]{2,1,0:T(8,128)S(1)}, f32[2,48,256]{2,1,0:T(8,128)S(1)}, u32[]{:S(2)}, u32[]{:S(2)}) collective-permute-start(f32[2,48,256]{2,1,0:T(8,128)S(1)} %select_bitcast_fusion.3), channel_id=1, source_target_pairs={{0,2},{1,3},{2,0},{3,1},{4,6},{5,7},{6,4},{7,5},{8,10},{9,11},{10,... | collective-permute-start | bytes 294920 | tf_op jit(solution)/shard_map/ppermute | solution.py:72
  68.6 1.0 %collective-permute-start.7 = (f32[2,48,256]{2,1,0:T(8,128)S(1)}, f32[2,48,256]{2,1,0:T(8,128)S(1)}, u32[]{:S(2)}, u32[]{:S(2)}) collective-permute-start(f32[2,48,256]{2,1,0:T(8,128)S(1)} %select_bitcast_fusion.4), channel_id=1, source_target_pairs={{0,1},{1,0},{2,3},{3,2},{4,5},{5,4},{6,7},{7,6},{8,9},{9,8},{10,11... | collective-permute-start | bytes 294920 | tf_op jit(solution)/shard_map/ppermute | solution.py:72
  69.6 1.8 %collective-permute-done.11 = f32[2,48,256]{2,1,0:T(8,128)S(1)} collective-permute-done((f32[2,48,256]{2,1,0:T(8,128)S(1)}, f32[2,48,256]{2,1,0:T(8,128)S(1)}, u32[]{:S(2)}, u32[]{:S(2)}) %collective-permute-start.11) | collective-permute-done | bytes 98336 | tf_op jit(solution)/shard_map/ppermute | solution.py:72
  71.4 1.7 %collective-permute-start.12 = (f32[1,48,256]{2,1,0:T(8,128)S(1)}, f32[1,48,256]{2,1,0:T(8,128)S(1)}, u32[]{:S(2)}, u32[]{:S(2)}) collective-permute-start(f32[1,48,256]{2,1,0:T(8,128)S(1)} %select_bitcast_fusion.5), channel_id=1, source_target_pairs={{0,1},{1,0},{2,3},{3,2},{4,5},{5,4},{6,7},{7,6},{8,9},{9,8},{10,11... | collective-permute-start | bytes 147464 | tf_op jit(solution)/shard_map/ppermute | solution.py:72
  73.3 2.9 %collective-permute-start.8 = (f32[1,48,256]{2,1,0:T(8,128)S(1)}, f32[1,48,256]{2,1,0:T(8,128)S(1)}, u32[]{:S(2)}, u32[]{:S(2)}) collective-permute-start(f32[1,48,256]{2,1,0:T(8,128)S(1)} %fusion.101), channel_id=1, source_target_pairs={{0,2},{1,3},{2,0},{3,1},{4,6},{5,7},{6,4},{7,5},{8,10},{9,11},{10,... | collective-permute-start | bytes 147464 | tf_op jit(solution)/shard_map/ppermute | solution.py:72
  76.3 0.6 copy.125
  76.9 1.5 %collective-permute-done.8 = f32[1,48,256]{2,1,0:T(8,128)S(1)} collective-permute-done((f32[1,48,256]{2,1,0:T(8,128)S(1)}, f32[1,48,256]{2,1,0:T(8,128)S(1)}, u32[]{:S(2)}, u32[]{:S(2)}) %collective-permute-start.8) | collective-permute-done | bytes 49184 | tf_op jit(solution)/shard_map/ppermute | solution.py:72
  78.4 0.7 copy.124
  (77 shorter events, 7.7 us)
Async XLA Ops:
  0.6 21.1 %copy-start = (bf16[256,256]{1,0:T(8,128)(2,1)S(1)}, bf16[256,256]{1,0:T(8,128)(2,1)}, u32[]{:S(2)}) copy-start(bf16[256,256]{1,0:T(8,128)(2,1)} %param.12) | copy-start | bytes 393220
  0.6 11.1 %collective-permute-start.1 = (bf16[1,33,1,8,256]{4,3,2,1,0:T(8,128)(2,1)}, bf16[1,33,1,8,256]{4,3,2,1,0:T(8,128)(2,1)S(1)}, u32[]{:S(2)}, u32[]{:S(2)}) collective-permute-start(bf16[1,33,1,8,256]{4,3,2,1,0:T(8,128)(2,1)} %param.8), channel_id=1, source_target_pairs={{1,0},{2,1},{3,2},{5,4},{6,5},{7,6},{9,8},{10,9},{11,10},{13,12},{... | collective-permute-start | bytes 405512 | tf_op jit(solution)/shard_map/ppermute | solution.py:20
  2.1 9.9 %collective-permute-start = (bf16[1,33,1,8,256]{4,3,2,1,0:T(8,128)(2,1)}, bf16[1,33,1,8,256]{4,3,2,1,0:T(8,128)(2,1)S(1)}, u32[]{:S(2)}, u32[]{:S(2)}) collective-permute-start(bf16[1,33,1,8,256]{4,3,2,1,0:T(8,128)(2,1)} %param.8), channel_id=1, source_target_pairs={{0,1},{1,2},{2,3},{4,5},{5,6},{6,7},{8,9},{9,10},{10,11},{12,13},{... | collective-permute-start | bytes 405512 | tf_op jit(solution)/shard_map/ppermute | solution.py:19
  12.2 1.7 %copy-start.1 = (bf16[1,33,1,16,256]{4,3,2,1,0:T(8,128)(2,1)}, bf16[1,33,1,16,256]{4,3,2,1,0:T(8,128)(2,1)S(1)}, u32[]{:S(2)}) copy-start(bf16[1,33,1,16,256]{4,3,2,1,0:T(8,128)(2,1)S(1)} %slice.165) | copy-start | bytes 811012
  12.3 1.3 %copy-start.6 = (bf16[3,3,256,256]{3,2,1,0:T(8,128)(2,1)S(1)}, bf16[3,3,256,256]{3,2,1,0:T(8,128)(2,1)}, u32[]{:S(2)}) copy-start(bf16[3,3,256,256]{3,2,1,0:T(8,128)(2,1)} %param.10) | copy-start | bytes 3538948
  16.1 1.4 %copy-start.4 = (bf16[3,256,256]{2,1,0:T(8,128)(2,1)S(1)}, bf16[3,256,256]{2,1,0:T(8,128)(2,1)}, u32[]{:S(2)}) copy-start(bf16[3,256,256]{2,1,0:T(8,128)(2,1)} %param.11) | copy-start | bytes 1179652
  17.9 1.1 %copy-start.3 = (f32[33,16,256]{2,1,0:T(8,128)S(1)}, f32[33,16,256]{2,1,0:T(8,128)}, u32[]{:S(2)}) copy-start(f32[33,16,256]{2,1,0:T(8,128)} %convert_element_type.56) | copy-start | bytes 1622020
  18.9 5.7 %copy-start.8 = (f32[256]{0:T(256)S(1)}, f32[256]{0:T(256)}, u32[]{:S(2)}) copy-start(f32[256]{0:T(256)} %param.13) | copy-start | bytes 3076
  20.1 12.5 %copy-start.9 = (s32[1,8]{1,0:T(1,128)S(1)}, s32[1,8]{1,0:T(1,128)}, u32[]{:S(2)}) copy-start(s32[1,8]{1,0:T(1,128)} %param.14) | copy-start | bytes 100
  22.6 3.7 %collective-permute-start.2 = (f32[1,8,256]{2,1,0:T(8,128)S(1)}, f32[1,8,256]{2,1,0:T(8,128)S(1)}, u32[]{:S(2)}, u32[]{:S(2)}) collective-permute-start(f32[1,8,256]{2,1,0:T(8,128)S(1)} %bitcast.413), channel_id=1, source_target_pairs={{0,1},{1,0},{2,3},{3,2},{4,5},{5,4},{6,7},{7,6},{8,9},{9,8},{10,11... | collective-permute-start | bytes 24584 | tf_op jit(solution)/shard_map/ppermute | solution.py:57
  26.3 4.7 %collective-permute-start.3 = (f32[1,8,256]{2,1,0:T(8,128)S(1)}, f32[1,8,256]{2,1,0:T(8,128)S(1)}, u32[]{:S(2)}, u32[]{:S(2)}) collective-permute-start(f32[1,8,256]{2,1,0:T(8,128)S(1)} %bitcast_add_fusion.8), channel_id=1, source_target_pairs={{0,2},{1,3},{2,0},{3,1},{4,6},{5,7},{6,4},{7,5},{8,10},{9,11},{10,... | collective-permute-start | bytes 24584 | tf_op jit(solution)/shard_map/ppermute | solution.py:57
  29.3 3.2 %copy-start.7 = (bf16[1,33,2,16,256]{4,3,2,1,0:T(8,128)(2,1)S(1)}, bf16[1,33,2,16,256]{4,3,2,1,0:T(8,128)(2,1)}, u32[]{:S(2)}) copy-start(bf16[1,33,2,16,256]{4,3,2,1,0:T(8,128)(2,1)} %param.15) | copy-start | bytes 1622020
  34.3 1.0 %copy-start.5 = (bf16[3,256,256]{2,1,0:T(8,128)(2,1)S(1)}, bf16[3,256,256]{2,1,0:T(8,128)(2,1)}, u32[]{:S(2)}) copy-start(bf16[3,256,256]{2,1,0:T(8,128)(2,1)} %param.11) | copy-start | bytes 1179652
  36.1 1.2 %copy-start.10 = (f32[33,2,16,256]{3,2,1,0:T(8,128)S(1)}, f32[33,2,16,256]{3,2,1,0:T(8,128)}, u32[]{:S(2)}) copy-start(f32[33,2,16,256]{3,2,1,0:T(8,128)} %get-tuple-element.14) | copy-start | bytes 3244036
  37.9 1.0 %copy-start.2 = (bf16[1,33,1,16,256]{4,3,2,1,0:T(8,128)(2,1)S(1)}, bf16[1,33,1,16,256]{4,3,2,1,0:T(8,128)(2,1)}, u32[]{:S(2)}) copy-start(bf16[1,33,1,16,256]{4,3,2,1,0:T(8,128)(2,1)} %copy-done.1) | copy-start | bytes 811012
  42.6 3.6 %collective-permute-start.4 = (f32[16,96,256]{2,1,0:T(8,128)S(1)}, f32[16,96,256]{2,1,0:T(8,128)}, u32[]{:S(2)}, u32[]{:S(2)}) collective-permute-start(f32[16,96,256]{2,1,0:T(8,128)S(1)} %bitcast.401), channel_id=1, source_target_pairs={{0,4},{4,0},{8,12},{12,8},{16,20},{20,16},{24,28},{28,24},{1,5},{5... | collective-permute-start | bytes 4718600 | tf_op jit(solution)/shard_map/ppermute | solution.py:72
  48.0 11.3 %collective-permute-start.9 = (f32[8,48,256]{2,1,0:T(8,128)S(1)}, f32[8,48,256]{2,1,0:T(8,128)S(1)}, u32[]{:S(2)}, u32[]{:S(2)}) collective-permute-start(f32[8,48,256]{2,1,0:T(8,128)S(1)} %select_bitcast_fusion), channel_id=1, source_target_pairs={{0,16},{4,20},{8,24},{12,28},{16,0},{20,4},{24,8},{28,12},{1,17},{... | collective-permute-start | bytes 1179656 | tf_op jit(solution)/shard_map/ppermute | solution.py:72
  49.9 11.2 %collective-permute-start.5 = (f32[8,48,256]{2,1,0:T(8,128)S(1)}, f32[8,48,256]{2,1,0:T(8,128)S(1)}, u32[]{:S(2)}, u32[]{:S(2)}) collective-permute-start(f32[8,48,256]{2,1,0:T(8,128)S(1)} %bitcast.406), channel_id=1, source_target_pairs={{0,8},{4,12},{8,0},{12,4},{16,24},{20,28},{24,16},{28,20},{1,9},{5... | collective-permute-start | bytes 1179656 | tf_op jit(solution)/shard_map/ppermute | solution.py:72
  59.4 6.2 %collective-permute-start.10 = (f32[4,48,256]{2,1,0:T(8,128)S(1)}, f32[4,48,256]{2,1,0:T(8,128)S(1)}, u32[]{:S(2)}, u32[]{:S(2)}) collective-permute-start(f32[4,48,256]{2,1,0:T(8,128)S(1)} %select_bitcast_fusion.1), channel_id=1, source_target_pairs={{0,8},{4,12},{8,0},{12,4},{16,24},{20,28},{24,16},{28,20},{1,9},{5... | collective-permute-start | bytes 589832 | tf_op jit(solution)/shard_map/ppermute | solution.py:72
  61.3 7.2 %collective-permute-start.6 = (f32[4,48,256]{2,1,0:T(8,128)S(1)}, f32[4,48,256]{2,1,0:T(8,128)S(1)}, u32[]{:S(2)}, u32[]{:S(2)}) collective-permute-start(f32[4,48,256]{2,1,0:T(8,128)S(1)} %select_bitcast_fusion.2), channel_id=1, source_target_pairs={{0,16},{4,20},{8,24},{12,28},{16,0},{20,4},{24,8},{28,12},{1,17},{... | collective-permute-start | bytes 589832 | tf_op jit(solution)/shard_map/ppermute | solution.py:72
  65.7 5.7 %collective-permute-start.11 = (f32[2,48,256]{2,1,0:T(8,128)S(1)}, f32[2,48,256]{2,1,0:T(8,128)S(1)}, u32[]{:S(2)}, u32[]{:S(2)}) collective-permute-start(f32[2,48,256]{2,1,0:T(8,128)S(1)} %select_bitcast_fusion.3), channel_id=1, source_target_pairs={{0,2},{1,3},{2,0},{3,1},{4,6},{5,7},{6,4},{7,5},{8,10},{9,11},{10,... | collective-permute-start | bytes 294920 | tf_op jit(solution)/shard_map/ppermute | solution.py:72
  68.6 4.7 %collective-permute-start.7 = (f32[2,48,256]{2,1,0:T(8,128)S(1)}, f32[2,48,256]{2,1,0:T(8,128)S(1)}, u32[]{:S(2)}, u32[]{:S(2)}) collective-permute-start(f32[2,48,256]{2,1,0:T(8,128)S(1)} %select_bitcast_fusion.4), channel_id=1, source_target_pairs={{0,1},{1,0},{2,3},{3,2},{4,5},{5,4},{6,7},{7,6},{8,9},{9,8},{10,11... | collective-permute-start | bytes 294920 | tf_op jit(solution)/shard_map/ppermute | solution.py:72
  71.4 4.8 %collective-permute-start.12 = (f32[1,48,256]{2,1,0:T(8,128)S(1)}, f32[1,48,256]{2,1,0:T(8,128)S(1)}, u32[]{:S(2)}, u32[]{:S(2)}) collective-permute-start(f32[1,48,256]{2,1,0:T(8,128)S(1)} %select_bitcast_fusion.5), channel_id=1, source_target_pairs={{0,1},{1,0},{2,3},{3,2},{4,5},{5,4},{6,7},{7,6},{8,9},{9,8},{10,11... | collective-permute-start | bytes 147464 | tf_op jit(solution)/shard_map/ppermute | solution.py:72
  73.3 5.1 %collective-permute-start.8 = (f32[1,48,256]{2,1,0:T(8,128)S(1)}, f32[1,48,256]{2,1,0:T(8,128)S(1)}, u32[]{:S(2)}, u32[]{:S(2)}) collective-permute-start(f32[1,48,256]{2,1,0:T(8,128)S(1)} %fusion.101), channel_id=1, source_target_pairs={{0,2},{1,3},{2,0},{3,1},{4,6},{5,7},{6,4},{7,5},{8,10},{9,11},{10,... | collective-permute-start | bytes 147464 | tf_op jit(solution)/shard_map/ppermute | solution.py:72

commit v2 on v1

--- a/solution.py
+++ b/solution.py
@@ -86,14 +86,20 @@
     cur = blocks
     for axis, bit in orders[0][:shared]:
         cur = _halve(cur, left, axis, bit)
+    tail = len(natural)
+    while tail > shared and all(o[tail - 1] == orders[0][tail - 1] for o in orders):
+        tail -= 1
     width = cur.shape[1] // len(orders)
     outs = []
     for p, order in enumerate(orders):
         part, part_left = cur[:, p * width : (p + 1) * width], list(left)
-        for axis, bit in order[shared:]:
+        for axis, bit in order[shared:tail]:
             part = _halve(part, part_left, axis, bit)
-        outs.append(part[0])
-    return jnp.concatenate(outs)
+        outs.append(part)
+    cur = jnp.concatenate(outs, axis=1)
+    for axis, bit in orders[0][tail:]:
+        cur = _halve(cur, part_left, axis, bit)
+    return cur[0]
 
 
 def on_device(
@@ -201,7 +207,7 @@
     z_lo, z_hi = ("space", 0), ("space", 1)
     nd = lax.axis_size("dp")
     if nd == 8 and groups == 4:
-        orders = ([core, x_bit, y_bit, z_lo, z_hi], [core, y_bit, x_bit, z_hi, z_lo])
+        orders = ([core, x_bit, y_bit, z_lo, z_hi], [core, y_bit, x_bit, z_lo, z_hi])
     else:
         plain = [("dp", i) for i in range(nd.bit_length() - 1)]
         orders = (plain + [("space", i) for i in range(groups.bit_length() - 1)],)

time: 79.5 us -> 80.5 us (1.013)
  waiting for transfers between devices: 20.8 us -> 25.4 us
  starting transfers between devices: 27.4 us -> 23.7 us
    ppermute x9 -> x7, waiting for transfers between devices: 17.5 us -> 22.2 us  [_halve(): lax.ppermute(send, axis, [(i, i ^ 1 << bit) for i in range(size)])]
    ppermute x9 -> x7, starting transfers between devices: 15.3 us -> 11.6 us  [_halve(): lax.ppermute(send, axis, [(i, i ^ 1 << bit) for i in range(size)])]
    unnamed x25 -> x26, local copies, waits for them, and re-layouts: 4.53 us -> 4.53 us
  transfers between devices with their start and end apart: 13 -> 11, of which waited for: 8 -> 8; matrix products, arithmetic and copies ran while one was open for 6% -> 5% of each run, Pallas kernels for 0% -> 0%
where the time goes in v2:
time: 80.5 us; the launch traced here: 80.1 us
  waiting for transfers between devices  25.4 us (32%)
  starting transfers between devices  23.7 us (29%)
  matrix products  13.7 us (17%)
  local copies, waits for them, and re-layouts  8.37 us (10%)
  other arithmetic  7 us (9%)
  between operations  1.83 us (2%)
    ppermute x7, waiting for transfers between devices, _halve(): lax.ppermute(send, axis, [(i, i ^ 1 << bit) for i in range(size)])  22.2 us
    ppermute x7, starting transfers between devices, _halve(): lax.ppermute(send, axis, [(i, i ^ 1 << bit) for i in range(size)])  11.6 us
    ppermute x1, starting transfers between devices, exchange_rows(): above = lax.ppermute(tail, axis, [(i, i + 1) for i in range(ends)])  5.6 us
    ppermute x2, starting transfers between devices, space_sum(): lax.ppermute(values, 'space', [(i, i ^ step) for i in range(count)])  5.04 us
    unnamed x26, local copies, waits for them, and re-layouts  4.53 us
    dot_general x9, matrix products, on_device(): jnp.einsum('nfhwc,cd->nfhwd', window, spatial_weight[row_tap, col_tap], p...  3.88 us
    dot_general x9, matrix products, on_device(): jnp.einsum('nfhwc,nfhwd->cd', window, pre_slope, preferred_element_type=j...  3.54 us
    ppermute x2, waiting for transfers between devices, space_sum(): lax.ppermute(values, 'space', [(i, i ^ step) for i in range(count)])  3.26 us
  transfers between devices with their start and end apart: 11, of which 8 were waited for; matrix products, arithmetic and copies ran while one was open for 5% of the time, Pallas kernels for 0%

profile of v2, /device:TPU:0, one launch (start us, length us, event | category | flops | bytes accessed | tf_op | source)
XLA Modules:
  0.0 80.1 jit_solution(9161134590000658252)
XLA Ops:
  0.6 1.4 %collective-permute-start.1 = (bf16[1,33,1,8,256]{4,3,2,1,0:T(8,128)(2,1)}, bf16[1,33,1,8,256]{4,3,2,1,0:T(8,128)(2,1)S(1)}, u32[]{:S(2)}, u32[]{:S(2)}) collective-permute-start(bf16[1,33,1,8,256]{4,3,2,1,0:T(8,128)(2,1)} %param.8), channel_id=1, source_target_pairs={{1,0},{2,1},{3,2},{5,4},{6,5},{7,6},{9,8},{10,9},{11,10},{13,12},{... | collective-permute-start | bytes 405512 | tf_op jit(solution)/shard_map/ppermute | solution.py:20
  2.1 5.6 %collective-permute-start = (bf16[1,33,1,8,256]{4,3,2,1,0:T(8,128)(2,1)}, bf16[1,33,1,8,256]{4,3,2,1,0:T(8,128)(2,1)S(1)}, u32[]{:S(2)}, u32[]{:S(2)}) collective-permute-start(bf16[1,33,1,8,256]{4,3,2,1,0:T(8,128)(2,1)} %param.8), channel_id=1, source_target_pairs={{0,1},{1,2},{2,3},{4,5},{5,6},{6,7},{8,9},{9,10},{10,11},{12,13},{... | collective-permute-start | bytes 405512 | tf_op jit(solution)/shard_map/ppermute | solution.py:19
  7.7 0.7 fusion.110
  8.4 0.7 and_bitcast_fusion
  9.7 1.1 %broadcast_in_dim.46 = bf16[33,8,2,256]{3,2,1,0:T(2,128)(2,1)S(1)} broadcast(bf16[33,8,256]{2,1,0:T(8,128)(2,1)} %bitcast.375), dimensions={0,1,3} | broadcast | bytes 405504 | tf_op jit(solution)/shard_map/broadcast_in_dim | solution.py:26
  10.8 0.9 %convert_element_type.56 = f32[33,16,256]{2,1,0:T(8,128)} convert(bf16[33,16,256]{2,1,0:T(8,128)(2,1)S(1)} %broadcast_in_dim.47) | non-fusion elementwise | flops 135168 | bytes 811008 | tf_op jit(solution)/shard_map/convert_element_type | solution.py:149
  12.3 0.9 %fusion.5 = bf16[1,33,4,18,256]{4,3,2,1,0:T(8,128)(2,1)S(1)} fusion(bf16[1,33,1,16,256]{4,3,2,1,0:T(8,128)(2,1)S(1)} %slice.155, bf16[1,33,2,16,256]{4,3,2,1,0:T(8,128)(2,1)S(1)} %broadcast_in_dim.50, bf16[1,33,1,16,256]{4,3,2,1,0:T(8,128)(2,1)S(1)} %slice.154), kind=kLoop, calls=%fused_computation.10 | loop fusion | flops 7299072 | bytes 2297856 | tf_op jit(solution)/shard_map/concatenate | solution.py:121
  13.2 0.4 copy-done.6
  16.2 1.4 %multiply_convert_fusion = (bf16[33,2,16,256]{3,2,1,0:T(8,128)(2,1)S(1)}, f32[33,2,16,256]{3,2,1,0:T(8,128)}) fusion(f32[33,2,16,256]{3,2,1,0:T(8,128)S(1)} %convolution_add_fusion.5, bf16[3,3,256,256]{3,2,1,0:T(8,128)(2,1)S(1)} %copy-done.6, bf16[1,33,4,18,256]{4,3,2,1,0:T(8,128)(2,1)S(1)} %fusion.5), kind=kOutput, calls=%fused_computation.57 | convolution fusion | flops 140034048 | bytes 3375104 | tf_op jit(solution)/shard_map/nfhwc,cd->nfhwd/dot_general | solution.py:131
  18.2 0.7 copy-done.3
  18.9 1.1 %fusion.15 = bf16[1,33,2,16,256]{4,3,2,1,0:T(8,128)(2,1)} fusion(f32[33,2,16,256]{3,2,1,0:T(8,128)S(1)} %convolution_add_fusion.3, f32[33,16,256]{2,1,0:T(8,128)S(1)} %copy-done.3, f32[33]{0:T(128)S(1)} %compare_convert_fusion, bf16[1,33,2,16,256]{4,3,2,1,0:T(8,128)(2,1)S(1)} %bitcast.357, bf16[3,256,256]{2,1,0:T(8,128)(2,1)S(1)} %copy-done.4), kind=kOutput, calls=%fused_computation.35 | convolution fusion | flops 139493376 | bytes 2834944 | tf_op jit(solution)/shard_map/nfhwc,cd->nfhwd/dot_general | solution.py:140
  20.1 1.6 %gather_fusion = bf16[8,2,16,256]{3,2,1,0:T(8,128)(2,1)S(1)} fusion(bf16[1,33,2,16,256]{4,3,2,1,0:T(8,128)(2,1)} %fusion.15, s32[8]{0:T(128)S(1)} %or_bitcast_fusion), kind=kCustom, calls=%fused_computation | custom fusion | bytes 262208 | tf_op jit(solution)/shard_map/vmap(jit(_take))/gather | solution.py:150
  21.7 0.9 %fusion.50 = (f32[8,256]{1,0:T(8,128)S(1)}, f32[8,2,16,256]{3,2,1,0:T(8,128)}) fusion(bf16[256,256]{1,0:T(8,128)(2,1)S(1)} %copy-done, bf16[8,2,16,256]{3,2,1,0:T(8,128)(2,1)S(1)} %gather_fusion, pred[8]{0:T(512)(128)(4,1)S(1)} %and_bitcast_fusion), kind=kOutput, calls=%fused_computation.100 | convolution fusion | flops 34207744 | bytes 532488 | tf_op jit(solution)/shard_map/nqhwc,ce->nqhwe/dot_general | solution.py:153
  22.6 2.0 %collective-permute-start.2 = (f32[1,8,256]{2,1,0:T(8,128)S(1)}, f32[1,8,256]{2,1,0:T(8,128)S(1)}, u32[]{:S(2)}, u32[]{:S(2)}) collective-permute-start(f32[1,8,256]{2,1,0:T(8,128)S(1)} %bitcast.380), channel_id=1, source_target_pairs={{0,1},{1,0},{2,3},{3,2},{4,5},{5,4},{6,7},{7,6},{8,9},{9,8},{10,11... | collective-permute-start | bytes 24584 | tf_op jit(solution)/shard_map/ppermute | solution.py:57
  24.6 1.6 %collective-permute-done.2 = f32[1,8,256]{2,1,0:T(8,128)S(1)} collective-permute-done((f32[1,8,256]{2,1,0:T(8,128)S(1)}, f32[1,8,256]{2,1,0:T(8,128)S(1)}, u32[]{:S(2)}, u32[]{:S(2)}) %collective-permute-start.2) | collective-permute-done | bytes 8224 | tf_op jit(solution)/shard_map/ppermute | solution.py:57
  26.3 3.0 %collective-permute-start.3 = (f32[1,8,256]{2,1,0:T(8,128)S(1)}, f32[1,8,256]{2,1,0:T(8,128)S(1)}, u32[]{:S(2)}, u32[]{:S(2)}) collective-permute-start(f32[1,8,256]{2,1,0:T(8,128)S(1)} %bitcast_add_fusion.6), channel_id=1, source_target_pairs={{0,2},{1,3},{2,0},{3,1},{4,6},{5,7},{6,4},{7,5},{8,10},{9,11},{10,... | collective-permute-start | bytes 24584 | tf_op jit(solution)/shard_map/ppermute | solution.py:57
  29.3 1.6 %collective-permute-done.3 = f32[1,8,256]{2,1,0:T(8,128)S(1)} collective-permute-done((f32[1,8,256]{2,1,0:T(8,128)S(1)}, f32[1,8,256]{2,1,0:T(8,128)S(1)}, u32[]{:S(2)}, u32[]{:S(2)}) %collective-permute-start.3) | collective-permute-done | bytes 8224 | tf_op jit(solution)/shard_map/ppermute | solution.py:57
  31.1 1.1 %fusion.48 = bf16[8,2,16,256]{3,2,1,0:T(8,128)(2,1)S(1)} fusion(f32[8,2,16,256]{3,2,1,0:T(8,128)} %get-tuple-element.16, f32[8,256]{1,0:T(8,128)S(1)} %get-tuple-element.12, f32[8,256]{1,0:T(8,128)S(1)} %get-tuple-element.11), kind=kLoop, calls=%fused_computation.97 | loop fusion | flops 1245184 | bytes 409600 | tf_op jit(solution)/shard_map/convert_element_type | solution.py:160
  32.5 1.0 %fusion.12 = bf16[1,33,2,16,256]{4,1,3,2,0:T(8,128)(2,1)S(1)} fusion(f32[8,2,16,256]{3,0,2,1:T(8,128)S(1)} %fusion.58, bf16[1,33,2,16,256]{4,3,2,1,0:T(8,128)(2,1)S(1)} %copy-done.7, f32[33]{0:T(128)S(1)} %compare_select_fusion.1, s32[8]{0:T(128)S(1)} %bitcast.381), kind=kOutput, calls=%fused_computation.32 | convolution fusion | flops 27033864 | bytes 1343652 | tf_op jit(solution)/shard_map/nqf,nqhwc->nfhwc/dot_general | solution.py:169
  34.7 0.6 copy-done.5
  35.7 0.4 slice_bitcast_fusion
  36.5 0.9 %copy-done.10 = f32[33,2,16,256]{3,2,1,0:T(8,128)S(1)} copy-done((f32[33,2,16,256]{3,2,1,0:T(8,128)S(1)}, f32[33,2,16,256]{3,2,1,0:T(8,128)}, u32[]{:S(2)}) %copy-start.10) | copy-done | bytes 1081368
  37.3 0.6 fusion.13
  37.9 0.4 fusion.24
  38.3 0.6 copy-done.2
  38.9 0.4 fusion.23
  39.3 0.4 fusion.22
  40.1 0.4 fusion.20
  40.5 0.4 fusion.19
  40.9 0.4 fusion.18
  41.3 0.4 fusion.17
  41.7 0.4 fusion.16
  42.2 0.4 broadcast_select_fusion.1
  42.7 3.5 %collective-permute-done.4 = f32[16,96,256]{2,1,0:T(8,128)} collective-permute-done((f32[16,96,256]{2,1,0:T(8,128)S(1)}, f32[16,96,256]{2,1,0:T(8,128)}, u32[]{:S(2)}, u32[]{:S(2)}) %collective-permute-start.4) | collective-permute-done | bytes 1572896 | tf_op jit(solution)/shard_map/ppermute | solution.py:72
  46.2 1.6 %bitcast_add_fusion = f32[16,96,256]{2,1,0:T(8,128)S(1)} fusion(f32[16,96,256]{2,1,0:T(8,128)} %collective-permute-done.4, f32[4,1,4,96,256]{4,3,2,1,0:T(8,128)S(1)} %get-tuple-element.3), kind=kLoop, calls=%fused_computation.13 | loop fusion | flops 393216 | bytes 4718592 | tf_op jit(solution)/shard_map/add | solution.py:72
  48.0 1.9 %collective-permute-start.7 = (f32[8,48,256]{2,1,0:T(8,128)S(1)}, f32[8,48,256]{2,1,0:T(8,128)S(1)}, u32[]{:S(2)}, u32[]{:S(2)}) collective-permute-start(f32[8,48,256]{2,1,0:T(8,128)S(1)} %select_bitcast_fusion), channel_id=1, source_target_pairs={{0,16},{4,20},{8,24},{12,28},{16,0},{20,4},{24,8},{28,12},{1,17},{... | collective-permute-start | bytes 1179656 | tf_op jit(solution)/shard_map/ppermute | solution.py:72
  49.9 1.6 %collective-permute-start.5 = (f32[8,48,256]{2,1,0:T(8,128)S(1)}, f32[8,48,256]{2,1,0:T(8,128)S(1)}, u32[]{:S(2)}, u32[]{:S(2)}) collective-permute-start(f32[8,48,256]{2,1,0:T(8,128)S(1)} %bitcast.374), channel_id=1, source_target_pairs={{0,8},{4,12},{8,0},{12,4},{16,24},{20,28},{24,16},{28,20},{1,9},{5... | collective-permute-start | bytes 1179656 | tf_op jit(solution)/shard_map/ppermute | solution.py:72
  51.5 7.8 %collective-permute-done.7 = f32[8,48,256]{2,1,0:T(8,128)S(1)} collective-permute-done((f32[8,48,256]{2,1,0:T(8,128)S(1)}, f32[8,48,256]{2,1,0:T(8,128)S(1)}, u32[]{:S(2)}, u32[]{:S(2)}) %collective-permute-start.7) | collective-permute-done | bytes 393248 | tf_op jit(solution)/shard_map/ppermute | solution.py:72
  59.4 1.8 %collective-permute-start.8 = (f32[4,48,256]{2,1,0:T(8,128)S(1)}, f32[4,48,256]{2,1,0:T(8,128)S(1)}, u32[]{:S(2)}, u32[]{:S(2)}) collective-permute-start(f32[4,48,256]{2,1,0:T(8,128)S(1)} %select_bitcast_fusion.2), channel_id=1, source_target_pairs={{0,8},{4,12},{8,0},{12,4},{16,24},{20,28},{24,16},{28,20},{1,9},{5... | collective-permute-start | bytes 589832 | tf_op jit(solution)/shard_map/ppermute | solution.py:72
  61.3 1.6 %collective-permute-start.6 = (f32[4,48,256]{2,1,0:T(8,128)S(1)}, f32[4,48,256]{2,1,0:T(8,128)S(1)}, u32[]{:S(2)}, u32[]{:S(2)}) collective-permute-start(f32[4,48,256]{2,1,0:T(8,128)S(1)} %select_bitcast_fusion.3), channel_id=1, source_target_pairs={{0,16},{4,20},{8,24},{12,28},{16,0},{20,4},{24,8},{28,12},{1,17},{... | collective-permute-start | bytes 589832 | tf_op jit(solution)/shard_map/ppermute | solution.py:72
  62.9 2.8 %collective-permute-done.8 = f32[4,48,256]{2,1,0:T(8,128)S(1)} collective-permute-done((f32[4,48,256]{2,1,0:T(8,128)S(1)}, f32[4,48,256]{2,1,0:T(8,128)S(1)}, u32[]{:S(2)}, u32[]{:S(2)}) %collective-permute-start.8) | collective-permute-done | bytes 196640 | tf_op jit(solution)/shard_map/ppermute | solution.py:72
  65.7 1.4 %collective-permute-done.6 = f32[4,48,256]{2,1,0:T(8,128)S(1)} collective-permute-done((f32[4,48,256]{2,1,0:T(8,128)S(1)}, f32[4,48,256]{2,1,0:T(8,128)S(1)}, u32[]{:S(2)}, u32[]{:S(2)}) %collective-permute-start.6) | collective-permute-done | bytes 196640 | tf_op jit(solution)/shard_map/ppermute | solution.py:72
  67.3 1.7 %collective-permute-start.9 = (f32[2,96,256]{2,1,0:T(8,128)S(1)}, f32[2,96,256]{2,1,0:T(8,128)S(1)}, u32[]{:S(2)}, u32[]{:S(2)}) collective-permute-start(f32[2,96,256]{2,1,0:T(8,128)S(1)} %select_bitcast_fusion.1), channel_id=1, source_target_pairs={{0,1},{1,0},{2,3},{3,2},{4,5},{5,4},{6,7},{7,6},{8,9},{9,8},{10,11... | collective-permute-start | bytes 589832 | tf_op jit(solution)/shard_map/ppermute | solution.py:72
  68.9 4.1 %collective-permute-done.9 = f32[2,96,256]{2,1,0:T(8,128)S(1)} collective-permute-done((f32[2,96,256]{2,1,0:T(8,128)S(1)}, f32[2,96,256]{2,1,0:T(8,128)S(1)}, u32[]{:S(2)}, u32[]{:S(2)}) %collective-permute-start.9) | collective-permute-done | bytes 196640 | tf_op jit(solution)/shard_map/ppermute | solution.py:72
  73.1 3.0 %collective-permute-start.10 = (f32[1,96,256]{2,1,0:T(8,128)S(1)}, f32[1,96,256]{2,1,0:T(8,128)S(1)}, u32[]{:S(2)}, u32[]{:S(2)}) collective-permute-start(f32[1,96,256]{2,1,0:T(8,128)S(1)} %fusion.96), channel_id=1, source_target_pairs={{0,2},{1,3},{2,0},{3,1},{4,6},{5,7},{6,4},{7,5},{8,10},{9,11},{10,... | collective-permute-start | bytes 294920 | tf_op jit(solution)/shard_map/ppermute | solution.py:72
  76.1 2.6 %collective-permute-done.10 = f32[1,96,256]{2,1,0:T(8,128)S(1)} collective-permute-done((f32[1,96,256]{2,1,0:T(8,128)S(1)}, f32[1,96,256]{2,1,0:T(8,128)S(1)}, u32[]{:S(2)}, u32[]{:S(2)}) %collective-permute-start.10) | collective-permute-done | bytes 98336 | tf_op jit(solution)/shard_map/ppermute | solution.py:72
  78.8 0.7 copy.128
  79.4 0.6 copy.129
  (70 shorter events, 7.1 us)
Async XLA Ops:
  0.6 21.0 %copy-start = (bf16[256,256]{1,0:T(8,128)(2,1)S(1)}, bf16[256,256]{1,0:T(8,128)(2,1)}, u32[]{:S(2)}) copy-start(bf16[256,256]{1,0:T(8,128)(2,1)} %param.12) | copy-start | bytes 393220
  0.6 11.1 %collective-permute-start.1 = (bf16[1,33,1,8,256]{4,3,2,1,0:T(8,128)(2,1)}, bf16[1,33,1,8,256]{4,3,2,1,0:T(8,128)(2,1)S(1)}, u32[]{:S(2)}, u32[]{:S(2)}) collective-permute-start(bf16[1,33,1,8,256]{4,3,2,1,0:T(8,128)(2,1)} %param.8), channel_id=1, source_target_pairs={{1,0},{2,1},{3,2},{5,4},{6,5},{7,6},{9,8},{10,9},{11,10},{13,12},{... | collective-permute-start | bytes 405512 | tf_op jit(solution)/shard_map/ppermute | solution.py:20
  2.1 9.9 %collective-permute-start = (bf16[1,33,1,8,256]{4,3,2,1,0:T(8,128)(2,1)}, bf16[1,33,1,8,256]{4,3,2,1,0:T(8,128)(2,1)S(1)}, u32[]{:S(2)}, u32[]{:S(2)}) collective-permute-start(bf16[1,33,1,8,256]{4,3,2,1,0:T(8,128)(2,1)} %param.8), channel_id=1, source_target_pairs={{0,1},{1,2},{2,3},{4,5},{5,6},{6,7},{8,9},{9,10},{10,11},{12,13},{... | collective-permute-start | bytes 405512 | tf_op jit(solution)/shard_map/ppermute | solution.py:19
  12.2 1.7 %copy-start.1 = (bf16[1,33,1,16,256]{4,3,2,1,0:T(8,128)(2,1)}, bf16[1,33,1,16,256]{4,3,2,1,0:T(8,128)(2,1)S(1)}, u32[]{:S(2)}) copy-start(bf16[1,33,1,16,256]{4,3,2,1,0:T(8,128)(2,1)S(1)} %slice.154) | copy-start | bytes 811012
  12.3 1.3 %copy-start.6 = (bf16[3,3,256,256]{3,2,1,0:T(8,128)(2,1)S(1)}, bf16[3,3,256,256]{3,2,1,0:T(8,128)(2,1)}, u32[]{:S(2)}) copy-start(bf16[3,3,256,256]{3,2,1,0:T(8,128)(2,1)} %param.10) | copy-start | bytes 3538948
  16.1 1.4 %copy-start.4 = (bf16[3,256,256]{2,1,0:T(8,128)(2,1)S(1)}, bf16[3,256,256]{2,1,0:T(8,128)(2,1)}, u32[]{:S(2)}) copy-start(bf16[3,256,256]{2,1,0:T(8,128)(2,1)} %param.11) | copy-start | bytes 1179652
  17.9 1.1 %copy-start.3 = (f32[33,16,256]{2,1,0:T(8,128)S(1)}, f32[33,16,256]{2,1,0:T(8,128)}, u32[]{:S(2)}) copy-start(f32[33,16,256]{2,1,0:T(8,128)} %convert_element_type.56) | copy-start | bytes 1622020
  18.9 5.7 %copy-start.8 = (f32[256]{0:T(256)S(1)}, f32[256]{0:T(256)}, u32[]{:S(2)}) copy-start(f32[256]{0:T(256)} %param.13) | copy-start | bytes 3076
  20.1 12.5 %copy-start.9 = (s32[1,8]{1,0:T(1,128)S(1)}, s32[1,8]{1,0:T(1,128)}, u32[]{:S(2)}) copy-start(s32[1,8]{1,0:T(1,128)} %param.14) | copy-start | bytes 100
  22.6 3.7 %collective-permute-start.2 = (f32[1,8,256]{2,1,0:T(8,128)S(1)}, f32[1,8,256]{2,1,0:T(8,128)S(1)}, u32[]{:S(2)}, u32[]{:S(2)}) collective-permute-start(f32[1,8,256]{2,1,0:T(8,128)S(1)} %bitcast.380), channel_id=1, source_target_pairs={{0,1},{1,0},{2,3},{3,2},{4,5},{5,4},{6,7},{7,6},{8,9},{9,8},{10,11... | collective-permute-start | bytes 24584 | tf_op jit(solution)/shard_map/ppermute | solution.py:57
  26.3 4.7 %collective-permute-start.3 = (f32[1,8,256]{2,1,0:T(8,128)S(1)}, f32[1,8,256]{2,1,0:T(8,128)S(1)}, u32[]{:S(2)}, u32[]{:S(2)}) collective-permute-start(f32[1,8,256]{2,1,0:T(8,128)S(1)} %bitcast_add_fusion.6), channel_id=1, source_target_pairs={{0,2},{1,3},{2,0},{3,1},{4,6},{5,7},{6,4},{7,5},{8,10},{9,11},{10,... | collective-permute-start | bytes 24584 | tf_op jit(solution)/shard_map/ppermute | solution.py:57
  29.3 3.2 %copy-start.7 = (bf16[1,33,2,16,256]{4,3,2,1,0:T(8,128)(2,1)S(1)}, bf16[1,33,2,16,256]{4,3,2,1,0:T(8,128)(2,1)}, u32[]{:S(2)}) copy-start(bf16[1,33,2,16,256]{4,3,2,1,0:T(8,128)(2,1)} %param.15) | copy-start | bytes 1622020
  34.3 1.0 %copy-start.5 = (bf16[3,256,256]{2,1,0:T(8,128)(2,1)S(1)}, bf16[3,256,256]{2,1,0:T(8,128)(2,1)}, u32[]{:S(2)}) copy-start(bf16[3,256,256]{2,1,0:T(8,128)(2,1)} %param.11) | copy-start | bytes 1179652
  36.1 1.2 %copy-start.10 = (f32[33,2,16,256]{3,2,1,0:T(8,128)S(1)}, f32[33,2,16,256]{3,2,1,0:T(8,128)}, u32[]{:S(2)}) copy-start(f32[33,2,16,256]{3,2,1,0:T(8,128)} %get-tuple-element.14) | copy-start | bytes 3244036
  37.9 1.0 %copy-start.2 = (bf16[1,33,1,16,256]{4,3,2,1,0:T(8,128)(2,1)S(1)}, bf16[1,33,1,16,256]{4,3,2,1,0:T(8,128)(2,1)}, u32[]{:S(2)}) copy-start(bf16[1,33,1,16,256]{4,3,2,1,0:T(8,128)(2,1)} %copy-done.1) | copy-start | bytes 811012
  42.6 3.6 %collective-permute-start.4 = (f32[16,96,256]{2,1,0:T(8,128)S(1)}, f32[16,96,256]{2,1,0:T(8,128)}, u32[]{:S(2)}, u32[]{:S(2)}) collective-permute-start(f32[16,96,256]{2,1,0:T(8,128)S(1)} %bitcast.373), channel_id=1, source_target_pairs={{0,4},{4,0},{8,12},{12,8},{16,20},{20,16},{24,28},{28,24},{1,5},{5... | collective-permute-start | bytes 4718600 | tf_op jit(solution)/shard_map/ppermute | solution.py:72
  48.0 11.3 %collective-permute-start.7 = (f32[8,48,256]{2,1,0:T(8,128)S(1)}, f32[8,48,256]{2,1,0:T(8,128)S(1)}, u32[]{:S(2)}, u32[]{:S(2)}) collective-permute-start(f32[8,48,256]{2,1,0:T(8,128)S(1)} %select_bitcast_fusion), channel_id=1, source_target_pairs={{0,16},{4,20},{8,24},{12,28},{16,0},{20,4},{24,8},{28,12},{1,17},{... | collective-permute-start | bytes 1179656 | tf_op jit(solution)/shard_map/ppermute | solution.py:72
  49.9 11.2 %collective-permute-start.5 = (f32[8,48,256]{2,1,0:T(8,128)S(1)}, f32[8,48,256]{2,1,0:T(8,128)S(1)}, u32[]{:S(2)}, u32[]{:S(2)}) collective-permute-start(f32[8,48,256]{2,1,0:T(8,128)S(1)} %bitcast.374), channel_id=1, source_target_pairs={{0,8},{4,12},{8,0},{12,4},{16,24},{20,28},{24,16},{28,20},{1,9},{5... | collective-permute-start | bytes 1179656 | tf_op jit(solution)/shard_map/ppermute | solution.py:72
  59.4 6.3 %collective-permute-start.8 = (f32[4,48,256]{2,1,0:T(8,128)S(1)}, f32[4,48,256]{2,1,0:T(8,128)S(1)}, u32[]{:S(2)}, u32[]{:S(2)}) collective-permute-start(f32[4,48,256]{2,1,0:T(8,128)S(1)} %select_bitcast_fusion.2), channel_id=1, source_target_pairs={{0,8},{4,12},{8,0},{12,4},{16,24},{20,28},{24,16},{28,20},{1,9},{5... | collective-permute-start | bytes 589832 | tf_op jit(solution)/shard_map/ppermute | solution.py:72
  61.3 5.9 %collective-permute-start.6 = (f32[4,48,256]{2,1,0:T(8,128)S(1)}, f32[4,48,256]{2,1,0:T(8,128)S(1)}, u32[]{:S(2)}, u32[]{:S(2)}) collective-permute-start(f32[4,48,256]{2,1,0:T(8,128)S(1)} %select_bitcast_fusion.3), channel_id=1, source_target_pairs={{0,16},{4,20},{8,24},{12,28},{16,0},{20,4},{24,8},{28,12},{1,17},{... | collective-permute-start | bytes 589832 | tf_op jit(solution)/shard_map/ppermute | solution.py:72
  67.3 5.7 %collective-permute-start.9 = (f32[2,96,256]{2,1,0:T(8,128)S(1)}, f32[2,96,256]{2,1,0:T(8,128)S(1)}, u32[]{:S(2)}, u32[]{:S(2)}) collective-permute-start(f32[2,96,256]{2,1,0:T(8,128)S(1)} %select_bitcast_fusion.1), channel_id=1, source_target_pairs={{0,1},{1,0},{2,3},{3,2},{4,5},{5,4},{6,7},{7,6},{8,9},{9,8},{10,11... | collective-permute-start | bytes 589832 | tf_op jit(solution)/shard_map/ppermute | solution.py:72
  73.1 5.7 %collective-permute-start.10 = (f32[1,96,256]{2,1,0:T(8,128)S(1)}, f32[1,96,256]{2,1,0:T(8,128)S(1)}, u32[]{:S(2)}, u32[]{:S(2)}) collective-permute-start(f32[1,96,256]{2,1,0:T(8,128)S(1)} %fusion.96), channel_id=1, source_target_pairs={{0,2},{1,3},{2,0},{3,1},{4,6},{5,7},{6,4},{7,5},{8,10},{9,11},{10,... | collective-permute-start | bytes 294920 | tf_op jit(solution)/shard_map/ppermute | solution.py:72

commit v3 on v2

--- a/solution.py
+++ b/solution.py
@@ -58,7 +58,7 @@
     return values
 
 
-def _halve(cur, left, axis, bit):
+def _halve(cur, left, axis, bit, wire=None):
     size = lax.axis_size(axis)
     pos = left.index((axis, bit))
     hi, lo = 1 << pos, 1 << (len(left) - 1 - pos)
@@ -69,7 +69,10 @@
     keep = jnp.where(upper, high, low)
     send = jnp.where(upper, low, high)
     left.remove((axis, bit))
-    return keep + lax.ppermute(send, axis, [(i, i ^ (1 << bit)) for i in range(size)])
+    if wire is not None:
+        send = send.astype(wire)
+    got = lax.ppermute(send, axis, [(i, i ^ (1 << bit)) for i in range(size)])
+    return keep + got.astype(keep.dtype)
 
 
 def halving_scatter(blocks, orders):
@@ -94,7 +97,7 @@
     for p, order in enumerate(orders):
         part, part_left = cur[:, p * width : (p + 1) * width], list(left)
         for axis, bit in order[shared:tail]:
-            part = _halve(part, part_left, axis, bit)
+            part = _halve(part, part_left, axis, bit, jnp.bfloat16)
         outs.append(part)
     cur = jnp.concatenate(outs, axis=1)
     for axis, bit in orders[0][tail:]:

time: 80.5 us -> 75.1 us (0.933)
  waiting for transfers between devices: 25.4 us -> 20 us
    ppermute x7, waiting for transfers between devices: 22.2 us -> 16.7 us  [_halve(): got = lax.ppermute(send, axis, [(i, i ^ 1 << bit) for i in range(size)])]
where the time goes in v3:
time: 75.1 us; the launch traced here: 74.6 us
  starting transfers between devices  23.7 us (32%)
  waiting for transfers between devices  20 us (27%)
  matrix products  13.7 us (18%)
  local copies, waits for them, and re-layouts  8.38 us (11%)
  other arithmetic  6.97 us (9%)
  between operations  1.86 us (2%)
    ppermute x7, waiting for transfers between devices, _halve(): got = lax.ppermute(send, axis, [(i, i ^ 1 << bit) for i in range(size)])  16.7 us
    ppermute x7, starting transfers between devices, _halve(): got = lax.ppermute(send, axis, [(i, i ^ 1 << bit) for i in range(size)])  11.7 us
    ppermute x1, starting transfers between devices, exchange_rows(): above = lax.ppermute(tail, axis, [(i, i + 1) for i in range(ends)])  5.6 us
    ppermute x2, starting transfers between devices, space_sum(): lax.ppermute(values, 'space', [(i, i ^ step) for i in range(count)])  5.04 us
    unnamed x26, local copies, waits for them, and re-layouts  4.54 us
    dot_general x9, matrix products, on_device(): jnp.einsum('nfhwc,cd->nfhwd', window, spatial_weight[row_tap, col_tap], p...  3.87 us
    dot_general x9, matrix products, on_device(): jnp.einsum('nfhwc,nfhwd->cd', window, pre_slope, preferred_element_type=j...  3.54 us
    ppermute x2, waiting for transfers between devices, space_sum(): lax.ppermute(values, 'space', [(i, i ^ step) for i in range(count)])  3.26 us
  transfers between devices with their start and end apart: 11, of which 8 were waited for; matrix products, arithmetic and copies ran while one was open for 5% of the time, Pallas kernels for 0%

profile of v3, /device:TPU:0, one launch (start us, length us, event | category | flops | bytes accessed | tf_op | source)
XLA Modules:
  0.0 74.6 jit_solution(184945519032002285)
XLA Ops:
  0.6 1.4 %collective-permute-start.1 = (bf16[1,33,1,8,256]{4,3,2,1,0:T(8,128)(2,1)}, bf16[1,33,1,8,256]{4,3,2,1,0:T(8,128)(2,1)S(1)}, u32[]{:S(2)}, u32[]{:S(2)}) collective-permute-start(bf16[1,33,1,8,256]{4,3,2,1,0:T(8,128)(2,1)} %param.8), channel_id=1, source_target_pairs={{1,0},{2,1},{3,2},{5,4},{6,5},{7,6},{9,8},{10,9},{11,10},{13,12},{... | collective-permute-start | bytes 405512 | tf_op jit(solution)/shard_map/ppermute | solution.py:20
  2.1 5.6 %collective-permute-start = (bf16[1,33,1,8,256]{4,3,2,1,0:T(8,128)(2,1)}, bf16[1,33,1,8,256]{4,3,2,1,0:T(8,128)(2,1)S(1)}, u32[]{:S(2)}, u32[]{:S(2)}) collective-permute-start(bf16[1,33,1,8,256]{4,3,2,1,0:T(8,128)(2,1)} %param.8), channel_id=1, source_target_pairs={{0,1},{1,2},{2,3},{4,5},{5,6},{6,7},{8,9},{9,10},{10,11},{12,13},{... | collective-permute-start | bytes 405512 | tf_op jit(solution)/shard_map/ppermute | solution.py:19
  7.7 0.7 fusion.113
  8.4 0.7 and_bitcast_fusion
  9.7 1.1 %broadcast_in_dim.46 = bf16[33,8,2,256]{3,2,1,0:T(2,128)(2,1)S(1)} broadcast(bf16[33,8,256]{2,1,0:T(8,128)(2,1)} %bitcast.376), dimensions={0,1,3} | broadcast | bytes 405504 | tf_op jit(solution)/shard_map/broadcast_in_dim | solution.py:26
  10.8 0.9 %convert_element_type.92 = f32[33,16,256]{2,1,0:T(8,128)} convert(bf16[33,16,256]{2,1,0:T(8,128)(2,1)S(1)} %broadcast_in_dim.47) | non-fusion elementwise | flops 135168 | bytes 811008 | tf_op jit(solution)/shard_map/convert_element_type | solution.py:152
  12.3 0.9 %fusion.5 = bf16[1,33,4,18,256]{4,3,2,1,0:T(8,128)(2,1)S(1)} fusion(bf16[1,33,1,16,256]{4,3,2,1,0:T(8,128)(2,1)S(1)} %slice.155, bf16[1,33,2,16,256]{4,3,2,1,0:T(8,128)(2,1)S(1)} %broadcast_in_dim.50, bf16[1,33,1,16,256]{4,3,2,1,0:T(8,128)(2,1)S(1)} %slice.154), kind=kLoop, calls=%fused_computation.10 | loop fusion | flops 7299072 | bytes 2297856 | tf_op jit(solution)/shard_map/concatenate | solution.py:124
  13.2 0.4 copy-done.6
  16.2 1.4 %multiply_convert_fusion = (bf16[33,2,16,256]{3,2,1,0:T(8,128)(2,1)S(1)}, f32[33,2,16,256]{3,2,1,0:T(8,128)}) fusion(f32[33,2,16,256]{3,2,1,0:T(8,128)S(1)} %convolution_add_fusion.5, bf16[3,3,256,256]{3,2,1,0:T(8,128)(2,1)S(1)} %copy-done.6, bf16[1,33,4,18,256]{4,3,2,1,0:T(8,128)(2,1)S(1)} %fusion.5), kind=kOutput, calls=%fused_computation.57 | convolution fusion | flops 140034048 | bytes 3375104 | tf_op jit(solution)/shard_map/nfhwc,cd->nfhwd/dot_general | solution.py:134
  18.2 0.7 copy-done.3
  18.9 1.1 %fusion.15 = bf16[1,33,2,16,256]{4,3,2,1,0:T(8,128)(2,1)} fusion(f32[33,2,16,256]{3,2,1,0:T(8,128)S(1)} %convolution_add_fusion.3, f32[33,16,256]{2,1,0:T(8,128)S(1)} %copy-done.3, f32[33]{0:T(128)S(1)} %compare_convert_fusion, bf16[1,33,2,16,256]{4,3,2,1,0:T(8,128)(2,1)S(1)} %bitcast.359, bf16[3,256,256]{2,1,0:T(8,128)(2,1)S(1)} %copy-done.4), kind=kOutput, calls=%fused_computation.35 | convolution fusion | flops 139493376 | bytes 2834944 | tf_op jit(solution)/shard_map/nfhwc,cd->nfhwd/dot_general | solution.py:143
  20.0 1.6 %gather_fusion = bf16[8,2,16,256]{3,2,1,0:T(8,128)(2,1)S(1)} fusion(bf16[1,33,2,16,256]{4,3,2,1,0:T(8,128)(2,1)} %fusion.15, s32[8]{0:T(128)S(1)} %or_bitcast_fusion), kind=kCustom, calls=%fused_computation | custom fusion | bytes 262208 | tf_op jit(solution)/shard_map/vmap(jit(_take))/gather | solution.py:153
  21.7 0.9 %fusion.50 = (f32[8,256]{1,0:T(8,128)S(1)}, f32[8,2,16,256]{3,2,1,0:T(8,128)}) fusion(bf16[256,256]{1,0:T(8,128)(2,1)S(1)} %copy-done, bf16[8,2,16,256]{3,2,1,0:T(8,128)(2,1)S(1)} %gather_fusion, pred[8]{0:T(512)(128)(4,1)S(1)} %and_bitcast_fusion), kind=kOutput, calls=%fused_computation.100 | convolution fusion | flops 34207744 | bytes 532488 | tf_op jit(solution)/shard_map/nqhwc,ce->nqhwe/dot_general | solution.py:156
  22.6 2.0 %collective-permute-start.2 = (f32[1,8,256]{2,1,0:T(8,128)S(1)}, f32[1,8,256]{2,1,0:T(8,128)S(1)}, u32[]{:S(2)}, u32[]{:S(2)}) collective-permute-start(f32[1,8,256]{2,1,0:T(8,128)S(1)} %bitcast.381), channel_id=1, source_target_pairs={{0,1},{1,0},{2,3},{3,2},{4,5},{5,4},{6,7},{7,6},{8,9},{9,8},{10,11... | collective-permute-start | bytes 24584 | tf_op jit(solution)/shard_map/ppermute | solution.py:57
  24.6 1.6 %collective-permute-done.2 = f32[1,8,256]{2,1,0:T(8,128)S(1)} collective-permute-done((f32[1,8,256]{2,1,0:T(8,128)S(1)}, f32[1,8,256]{2,1,0:T(8,128)S(1)}, u32[]{:S(2)}, u32[]{:S(2)}) %collective-permute-start.2) | collective-permute-done | bytes 8224 | tf_op jit(solution)/shard_map/ppermute | solution.py:57
  26.2 3.0 %collective-permute-start.3 = (f32[1,8,256]{2,1,0:T(8,128)S(1)}, f32[1,8,256]{2,1,0:T(8,128)S(1)}, u32[]{:S(2)}, u32[]{:S(2)}) collective-permute-start(f32[1,8,256]{2,1,0:T(8,128)S(1)} %bitcast_add_fusion.6), channel_id=1, source_target_pairs={{0,2},{1,3},{2,0},{3,1},{4,6},{5,7},{6,4},{7,5},{8,10},{9,11},{10,... | collective-permute-start | bytes 24584 | tf_op jit(solution)/shard_map/ppermute | solution.py:57
  29.3 1.6 %collective-permute-done.3 = f32[1,8,256]{2,1,0:T(8,128)S(1)} collective-permute-done((f32[1,8,256]{2,1,0:T(8,128)S(1)}, f32[1,8,256]{2,1,0:T(8,128)S(1)}, u32[]{:S(2)}, u32[]{:S(2)}) %collective-permute-start.3) | collective-permute-done | bytes 8224 | tf_op jit(solution)/shard_map/ppermute | solution.py:57
  31.1 1.1 %fusion.48 = bf16[8,2,16,256]{3,2,1,0:T(8,128)(2,1)S(1)} fusion(f32[8,2,16,256]{3,2,1,0:T(8,128)} %get-tuple-element.14, f32[8,256]{1,0:T(8,128)S(1)} %get-tuple-element.10, f32[8,256]{1,0:T(8,128)S(1)} %get-tuple-element.9), kind=kLoop, calls=%fused_computation.97 | loop fusion | flops 1245184 | bytes 409600 | tf_op jit(solution)/shard_map/convert_element_type | solution.py:163
  32.5 1.0 %fusion.12 = bf16[1,33,2,16,256]{4,1,3,2,0:T(8,128)(2,1)S(1)} fusion(f32[8,2,16,256]{3,0,2,1:T(8,128)S(1)} %fusion.59, bf16[1,33,2,16,256]{4,3,2,1,0:T(8,128)(2,1)S(1)} %copy-done.7, f32[33]{0:T(128)S(1)} %compare_select_fusion.1, s32[8]{0:T(128)S(1)} %bitcast.382), kind=kOutput, calls=%fused_computation.32 | convolution fusion | flops 27033864 | bytes 1343652 | tf_op jit(solution)/shard_map/nqf,nqhwc->nfhwc/dot_general | solution.py:172
  34.7 0.6 copy-done.5
  35.7 0.4 slice_bitcast_fusion
  36.4 0.9 %copy-done.10 = f32[33,2,16,256]{3,2,1,0:T(8,128)S(1)} copy-done((f32[33,2,16,256]{3,2,1,0:T(8,128)S(1)}, f32[33,2,16,256]{3,2,1,0:T(8,128)}, u32[]{:S(2)}) %copy-start.10) | copy-done | bytes 1081368
  37.3 0.6 fusion.13
  38.3 0.6 copy-done.2
  38.9 0.4 fusion.23
  39.3 0.4 fusion.22
  39.7 0.4 fusion.21
  40.1 0.4 fusion.20
  40.5 0.4 fusion.19
  40.9 0.4 fusion.18
  41.3 0.4 fusion.17
  41.7 0.4 fusion.16
  42.1 0.4 broadcast_select_fusion.1
  42.7 3.5 %collective-permute-done.4 = f32[16,96,256]{2,1,0:T(8,128)} collective-permute-done((f32[16,96,256]{2,1,0:T(8,128)S(1)}, f32[16,96,256]{2,1,0:T(8,128)}, u32[]{:S(2)}, u32[]{:S(2)}) %collective-permute-start.4) | collective-permute-done | bytes 1572896 | tf_op jit(solution)/shard_map/ppermute | solution.py:74
  46.2 1.6 %bitcast_add_fusion = f32[16,96,256]{2,1,0:T(8,128)S(1)} fusion(f32[16,96,256]{2,1,0:T(8,128)} %collective-permute-done.4, f32[4,1,4,96,256]{4,3,2,1,0:T(8,128)S(1)} %get-tuple-element.3), kind=kLoop, calls=%fused_computation.13 | loop fusion | flops 393216 | bytes 4718592 | tf_op jit(solution)/shard_map/add | solution.py:75
  47.9 1.9 %collective-permute-start.5 = (bf16[8,48,256]{2,1,0:T(8,128)(2,1)S(1)}, bf16[8,48,256]{2,1,0:T(8,128)(2,1)S(1)}, u32[]{:S(2)}, u32[]{:S(2)}) collective-permute-start(bf16[8,48,256]{2,1,0:T(8,128)(2,1)S(1)} %bitcast.375), channel_id=1, source_target_pairs={{0,8},{4,12},{8,0},{12,4},{16,24},{20,28},{24,16},{28,20},{1,9},{5... | collective-permute-start | bytes 589832 | tf_op jit(solution)/shard_map/ppermute | solution.py:74
  49.8 1.6 %collective-permute-start.7 = (bf16[8,48,256]{2,1,0:T(8,128)(2,1)S(1)}, bf16[8,48,256]{2,1,0:T(8,128)(2,1)S(1)}, u32[]{:S(2)}, u32[]{:S(2)}) collective-permute-start(bf16[8,48,256]{2,1,0:T(8,128)(2,1)S(1)} %fusion.51), channel_id=1, source_target_pairs={{0,16},{4,20},{8,24},{12,28},{16,0},{20,4},{24,8},{28,12},{1,17},{... | collective-permute-start | bytes 589832 | tf_op jit(solution)/shard_map/ppermute | solution.py:74
  51.5 3.5 %collective-permute-done.5 = bf16[8,48,256]{2,1,0:T(8,128)(2,1)S(1)} collective-permute-done((bf16[8,48,256]{2,1,0:T(8,128)(2,1)S(1)}, bf16[8,48,256]{2,1,0:T(8,128)(2,1)S(1)}, u32[]{:S(2)}, u32[]{:S(2)}) %collective-permute-start.5) | collective-permute-done | bytes 196640 | tf_op jit(solution)/shard_map/ppermute | solution.py:74
  55.1 1.8 %collective-permute-start.6 = (bf16[4,48,256]{2,1,0:T(8,128)(2,1)S(1)}, bf16[4,48,256]{2,1,0:T(8,128)(2,1)S(1)}, u32[]{:S(2)}, u32[]{:S(2)}) collective-permute-start(bf16[4,48,256]{2,1,0:T(8,128)(2,1)S(1)} %fusion.97), channel_id=1, source_target_pairs={{0,16},{4,20},{8,24},{12,28},{16,0},{20,4},{24,8},{28,12},{1,17},{... | collective-permute-start | bytes 294920 | tf_op jit(solution)/shard_map/ppermute | solution.py:74
  57.0 1.6 %collective-permute-start.8 = (bf16[4,48,256]{2,1,0:T(8,128)(2,1)S(1)}, bf16[4,48,256]{2,1,0:T(8,128)(2,1)S(1)}, u32[]{:S(2)}, u32[]{:S(2)}) collective-permute-start(bf16[4,48,256]{2,1,0:T(8,128)(2,1)S(1)} %fusion.98), channel_id=1, source_target_pairs={{0,8},{4,12},{8,0},{12,4},{16,24},{20,28},{24,16},{28,20},{1,9},{5... | collective-permute-start | bytes 294920 | tf_op jit(solution)/shard_map/ppermute | solution.py:74
  58.6 1.2 %collective-permute-done.6 = bf16[4,48,256]{2,1,0:T(8,128)(2,1)S(1)} collective-permute-done((bf16[4,48,256]{2,1,0:T(8,128)(2,1)S(1)}, bf16[4,48,256]{2,1,0:T(8,128)(2,1)S(1)}, u32[]{:S(2)}, u32[]{:S(2)}) %collective-permute-start.6) | collective-permute-done | bytes 98336 | tf_op jit(solution)/shard_map/ppermute | solution.py:74
  59.8 1.9 %collective-permute-done.8 = bf16[4,48,256]{2,1,0:T(8,128)(2,1)S(1)} collective-permute-done((bf16[4,48,256]{2,1,0:T(8,128)(2,1)S(1)}, bf16[4,48,256]{2,1,0:T(8,128)(2,1)S(1)}, u32[]{:S(2)}, u32[]{:S(2)}) %collective-permute-start.8) | collective-permute-done | bytes 98336 | tf_op jit(solution)/shard_map/ppermute | solution.py:74
  61.8 1.7 %collective-permute-start.9 = (f32[2,96,256]{2,1,0:T(8,128)S(1)}, f32[2,96,256]{2,1,0:T(8,128)S(1)}, u32[]{:S(2)}, u32[]{:S(2)}) collective-permute-start(f32[2,96,256]{2,1,0:T(8,128)S(1)} %select_bitcast_fusion), channel_id=1, source_target_pairs={{0,1},{1,0},{2,3},{3,2},{4,5},{5,4},{6,7},{7,6},{8,9},{9,8},{10,11... | collective-permute-start | bytes 589832 | tf_op jit(solution)/shard_map/ppermute | solution.py:74
  63.5 4.1 %collective-permute-done.9 = f32[2,96,256]{2,1,0:T(8,128)S(1)} collective-permute-done((f32[2,96,256]{2,1,0:T(8,128)S(1)}, f32[2,96,256]{2,1,0:T(8,128)S(1)}, u32[]{:S(2)}, u32[]{:S(2)}) %collective-permute-start.9) | collective-permute-done | bytes 196640 | tf_op jit(solution)/shard_map/ppermute | solution.py:74
  67.6 3.0 %collective-permute-start.10 = (f32[1,96,256]{2,1,0:T(8,128)S(1)}, f32[1,96,256]{2,1,0:T(8,128)S(1)}, u32[]{:S(2)}, u32[]{:S(2)}) collective-permute-start(f32[1,96,256]{2,1,0:T(8,128)S(1)} %fusion.99), channel_id=1, source_target_pairs={{0,2},{1,3},{2,0},{3,1},{4,6},{5,7},{6,4},{7,5},{8,10},{9,11},{10,... | collective-permute-start | bytes 294920 | tf_op jit(solution)/shard_map/ppermute | solution.py:74
  70.6 2.6 %collective-permute-done.10 = f32[1,96,256]{2,1,0:T(8,128)S(1)} collective-permute-done((f32[1,96,256]{2,1,0:T(8,128)S(1)}, f32[1,96,256]{2,1,0:T(8,128)S(1)}, u32[]{:S(2)}, u32[]{:S(2)}) %collective-permute-start.10) | collective-permute-done | bytes 98336 | tf_op jit(solution)/shard_map/ppermute | solution.py:74
  73.3 0.7 copy.128
  74.0 0.6 copy.129
  (71 shorter events, 7.1 us)
Async XLA Ops:
  0.6 21.0 %copy-start = (bf16[256,256]{1,0:T(8,128)(2,1)S(1)}, bf16[256,256]{1,0:T(8,128)(2,1)}, u32[]{:S(2)}) copy-start(bf16[256,256]{1,0:T(8,128)(2,1)} %param.12) | copy-start | bytes 393220
  0.6 11.1 %collective-permute-start.1 = (bf16[1,33,1,8,256]{4,3,2,1,0:T(8,128)(2,1)}, bf16[1,33,1,8,256]{4,3,2,1,0:T(8,128)(2,1)S(1)}, u32[]{:S(2)}, u32[]{:S(2)}) collective-permute-start(bf16[1,33,1,8,256]{4,3,2,1,0:T(8,128)(2,1)} %param.8), channel_id=1, source_target_pairs={{1,0},{2,1},{3,2},{5,4},{6,5},{7,6},{9,8},{10,9},{11,10},{13,12},{... | collective-permute-start | bytes 405512 | tf_op jit(solution)/shard_map/ppermute | solution.py:20
  2.1 9.9 %collective-permute-start = (bf16[1,33,1,8,256]{4,3,2,1,0:T(8,128)(2,1)}, bf16[1,33,1,8,256]{4,3,2,1,0:T(8,128)(2,1)S(1)}, u32[]{:S(2)}, u32[]{:S(2)}) collective-permute-start(bf16[1,33,1,8,256]{4,3,2,1,0:T(8,128)(2,1)} %param.8), channel_id=1, source_target_pairs={{0,1},{1,2},{2,3},{4,5},{5,6},{6,7},{8,9},{9,10},{10,11},{12,13},{... | collective-permute-start | bytes 405512 | tf_op jit(solution)/shard_map/ppermute | solution.py:19
  12.2 1.7 %copy-start.1 = (bf16[1,33,1,16,256]{4,3,2,1,0:T(8,128)(2,1)}, bf16[1,33,1,16,256]{4,3,2,1,0:T(8,128)(2,1)S(1)}, u32[]{:S(2)}) copy-start(bf16[1,33,1,16,256]{4,3,2,1,0:T(8,128)(2,1)S(1)} %slice.154) | copy-start | bytes 811012
  12.3 1.3 %copy-start.6 = (bf16[3,3,256,256]{3,2,1,0:T(8,128)(2,1)S(1)}, bf16[3,3,256,256]{3,2,1,0:T(8,128)(2,1)}, u32[]{:S(2)}) copy-start(bf16[3,3,256,256]{3,2,1,0:T(8,128)(2,1)} %param.10) | copy-start | bytes 3538948
  16.1 1.4 %copy-start.4 = (bf16[3,256,256]{2,1,0:T(8,128)(2,1)S(1)}, bf16[3,256,256]{2,1,0:T(8,128)(2,1)}, u32[]{:S(2)}) copy-start(bf16[3,256,256]{2,1,0:T(8,128)(2,1)} %param.11) | copy-start | bytes 1179652
  17.9 1.1 %copy-start.3 = (f32[33,16,256]{2,1,0:T(8,128)S(1)}, f32[33,16,256]{2,1,0:T(8,128)}, u32[]{:S(2)}) copy-start(f32[33,16,256]{2,1,0:T(8,128)} %convert_element_type.92) | copy-start | bytes 1622020
  18.9 5.7 %copy-start.8 = (f32[256]{0:T(256)S(1)}, f32[256]{0:T(256)}, u32[]{:S(2)}) copy-start(f32[256]{0:T(256)} %param.13) | copy-start | bytes 3076
  20.0 12.5 %copy-start.9 = (s32[1,8]{1,0:T(1,128)S(1)}, s32[1,8]{1,0:T(1,128)}, u32[]{:S(2)}) copy-start(s32[1,8]{1,0:T(1,128)} %param.14) | copy-start | bytes 100
  22.6 3.7 %collective-permute-start.2 = (f32[1,8,256]{2,1,0:T(8,128)S(1)}, f32[1,8,256]{2,1,0:T(8,128)S(1)}, u32[]{:S(2)}, u32[]{:S(2)}) collective-permute-start(f32[1,8,256]{2,1,0:T(8,128)S(1)} %bitcast.381), channel_id=1, source_target_pairs={{0,1},{1,0},{2,3},{3,2},{4,5},{5,4},{6,7},{7,6},{8,9},{9,8},{10,11... | collective-permute-start | bytes 24584 | tf_op jit(solution)/shard_map/ppermute | solution.py:57
  26.2 4.7 %collective-permute-start.3 = (f32[1,8,256]{2,1,0:T(8,128)S(1)}, f32[1,8,256]{2,1,0:T(8,128)S(1)}, u32[]{:S(2)}, u32[]{:S(2)}) collective-permute-start(f32[1,8,256]{2,1,0:T(8,128)S(1)} %bitcast_add_fusion.6), channel_id=1, source_target_pairs={{0,2},{1,3},{2,0},{3,1},{4,6},{5,7},{6,4},{7,5},{8,10},{9,11},{10,... | collective-permute-start | bytes 24584 | tf_op jit(solution)/shard_map/ppermute | solution.py:57
  29.3 3.2 %copy-start.7 = (bf16[1,33,2,16,256]{4,3,2,1,0:T(8,128)(2,1)S(1)}, bf16[1,33,2,16,256]{4,3,2,1,0:T(8,128)(2,1)}, u32[]{:S(2)}) copy-start(bf16[1,33,2,16,256]{4,3,2,1,0:T(8,128)(2,1)} %param.15) | copy-start | bytes 1622020
  34.3 1.0 %copy-start.5 = (bf16[3,256,256]{2,1,0:T(8,128)(2,1)S(1)}, bf16[3,256,256]{2,1,0:T(8,128)(2,1)}, u32[]{:S(2)}) copy-start(bf16[3,256,256]{2,1,0:T(8,128)(2,1)} %param.11) | copy-start | bytes 1179652
  36.1 1.2 %copy-start.10 = (f32[33,2,16,256]{3,2,1,0:T(8,128)S(1)}, f32[33,2,16,256]{3,2,1,0:T(8,128)}, u32[]{:S(2)}) copy-start(f32[33,2,16,256]{3,2,1,0:T(8,128)} %get-tuple-element.12) | copy-start | bytes 3244036
  37.9 1.0 %copy-start.2 = (bf16[1,33,1,16,256]{4,3,2,1,0:T(8,128)(2,1)S(1)}, bf16[1,33,1,16,256]{4,3,2,1,0:T(8,128)(2,1)}, u32[]{:S(2)}) copy-start(bf16[1,33,1,16,256]{4,3,2,1,0:T(8,128)(2,1)} %copy-done.1) | copy-start | bytes 811012
  42.6 3.6 %collective-permute-start.4 = (f32[16,96,256]{2,1,0:T(8,128)S(1)}, f32[16,96,256]{2,1,0:T(8,128)}, u32[]{:S(2)}, u32[]{:S(2)}) collective-permute-start(f32[16,96,256]{2,1,0:T(8,128)S(1)} %bitcast.374), channel_id=1, source_target_pairs={{0,4},{4,0},{8,12},{12,8},{16,20},{20,16},{24,28},{28,24},{1,5},{5... | collective-permute-start | bytes 4718600 | tf_op jit(solution)/shard_map/ppermute | solution.py:74
  47.9 7.1 %collective-permute-start.5 = (bf16[8,48,256]{2,1,0:T(8,128)(2,1)S(1)}, bf16[8,48,256]{2,1,0:T(8,128)(2,1)S(1)}, u32[]{:S(2)}, u32[]{:S(2)}) collective-permute-start(bf16[8,48,256]{2,1,0:T(8,128)(2,1)S(1)} %bitcast.375), channel_id=1, source_target_pairs={{0,8},{4,12},{8,0},{12,4},{16,24},{20,28},{24,16},{28,20},{1,9},{5... | collective-permute-start | bytes 589832 | tf_op jit(solution)/shard_map/ppermute | solution.py:74
  49.8 7.1 %collective-permute-start.7 = (bf16[8,48,256]{2,1,0:T(8,128)(2,1)S(1)}, bf16[8,48,256]{2,1,0:T(8,128)(2,1)S(1)}, u32[]{:S(2)}, u32[]{:S(2)}) collective-permute-start(bf16[8,48,256]{2,1,0:T(8,128)(2,1)S(1)} %fusion.51), channel_id=1, source_target_pairs={{0,16},{4,20},{8,24},{12,28},{16,0},{20,4},{24,8},{28,12},{1,17},{... | collective-permute-start | bytes 589832 | tf_op jit(solution)/shard_map/ppermute | solution.py:74
  55.1 4.7 %collective-permute-start.6 = (bf16[4,48,256]{2,1,0:T(8,128)(2,1)S(1)}, bf16[4,48,256]{2,1,0:T(8,128)(2,1)S(1)}, u32[]{:S(2)}, u32[]{:S(2)}) collective-permute-start(bf16[4,48,256]{2,1,0:T(8,128)(2,1)S(1)} %fusion.97), channel_id=1, source_target_pairs={{0,16},{4,20},{8,24},{12,28},{16,0},{20,4},{24,8},{28,12},{1,17},{... | collective-permute-start | bytes 294920 | tf_op jit(solution)/shard_map/ppermute | solution.py:74
  57.0 4.7 %collective-permute-start.8 = (bf16[4,48,256]{2,1,0:T(8,128)(2,1)S(1)}, bf16[4,48,256]{2,1,0:T(8,128)(2,1)S(1)}, u32[]{:S(2)}, u32[]{:S(2)}) collective-permute-start(bf16[4,48,256]{2,1,0:T(8,128)(2,1)S(1)} %fusion.98), channel_id=1, source_target_pairs={{0,8},{4,12},{8,0},{12,4},{16,24},{20,28},{24,16},{28,20},{1,9},{5... | collective-permute-start | bytes 294920 | tf_op jit(solution)/shard_map/ppermute | solution.py:74
  61.8 5.7 %collective-permute-start.9 = (f32[2,96,256]{2,1,0:T(8,128)S(1)}, f32[2,96,256]{2,1,0:T(8,128)S(1)}, u32[]{:S(2)}, u32[]{:S(2)}) collective-permute-start(f32[2,96,256]{2,1,0:T(8,128)S(1)} %select_bitcast_fusion), channel_id=1, source_target_pairs={{0,1},{1,0},{2,3},{3,2},{4,5},{5,4},{6,7},{7,6},{8,9},{9,8},{10,11... | collective-permute-start | bytes 589832 | tf_op jit(solution)/shard_map/ppermute | solution.py:74
  67.6 5.6 %collective-permute-start.10 = (f32[1,96,256]{2,1,0:T(8,128)S(1)}, f32[1,96,256]{2,1,0:T(8,128)S(1)}, u32[]{:S(2)}, u32[]{:S(2)}) collective-permute-start(f32[1,96,256]{2,1,0:T(8,128)S(1)} %fusion.99), channel_id=1, source_target_pairs={{0,2},{1,3},{2,0},{3,1},{4,6},{5,7},{6,4},{7,5},{8,10},{9,11},{10,... | collective-permute-start | bytes 294920 | tf_op jit(solution)/shard_map/ppermute | solution.py:74

commit v4 on v3

--- a/solution.py
+++ b/solution.py
@@ -100,7 +100,15 @@
             part = _halve(part, part_left, axis, bit, jnp.bfloat16)
         outs.append(part)
     cur = jnp.concatenate(outs, axis=1)
-    for axis, bit in orders[0][tail:]:
+    rest = orders[0][tail:]
+    if sorted(rest) == [("space", i) for i in range(bs)] and part_left == rest[::-1] == natural[bd:]:
+        me = lax.axis_index("space")
+        total = lax.dynamic_index_in_dim(cur, me, 0, keepdims=False)
+        for shift in range(1, ns):
+            send = lax.dynamic_index_in_dim(cur, (me + shift) % ns, 0, keepdims=False)
+            total = total + lax.ppermute(send, "space", [(i, (i + shift) % ns) for i in range(ns)])
+        return total
+    for axis, bit in rest:
         cur = _halve(cur, part_left, axis, bit)
     return cur[0]
 

time: 75.1 us -> 73.6 us (0.980)
  waiting for transfers between devices: 20 us -> 17.7 us
  starting transfers between devices: 23.7 us -> 24.5 us
    ppermute x7 -> x5, waiting for transfers between devices: 16.7 us -> 10 us  [_halve(): got = lax.ppermute(send, axis, [(i, i ^ 1 << bit) for i in range(size)])]
    ppermute x0 -> x3, starting transfers between devices: none -> 5.58 us  [halving_scatter(): lax.ppermute(send, 'space', [(i, (i + shift) % ns) for i in range(ns)])]
    ppermute x7 -> x5, starting transfers between devices: 11.7 us -> 6.91 us  [_halve(): got = lax.ppermute(send, axis, [(i, i ^ 1 << bit) for i in range(size)])]
    ppermute x0 -> x3, waiting for transfers between devices: none -> 4.39 us  [halving_scatter(): lax.ppermute(send, 'space', [(i, (i + shift) % ns) for i in range(ns)])]
    add x7 -> x5, other arithmetic: 1.82 us -> 1.76 us  [_halve(): return keep + got.astype(keep.dtype)]
  transfers between devices with their start and end apart: 11 -> 12, of which waited for: 8 -> 8; matrix products, arithmetic and copies ran while one was open for 5% -> 5% of each run, Pallas kernels for 0% -> 0%
where the time goes in v4:
time: 73.6 us; the launch traced here: 73.1 us
  starting transfers between devices  24.5 us (33%)
  waiting for transfers between devices  17.7 us (24%)
  matrix products  13.7 us (19%)
  local copies, waits for them, and re-layouts  8.36 us (11%)
  other arithmetic  6.91 us (9%)
  between operations  1.87 us (3%)
    ppermute x5, waiting for transfers between devices, _halve(): got = lax.ppermute(send, axis, [(i, i ^ 1 << bit) for i in range(size)])  10 us
    ppermute x5, starting transfers between devices, _halve(): got = lax.ppermute(send, axis, [(i, i ^ 1 << bit) for i in range(size)])  6.91 us
    ppermute x1, starting transfers between devices, exchange_rows(): above = lax.ppermute(tail, axis, [(i, i + 1) for i in range(ends)])  5.6 us
    ppermute x3, starting transfers between devices, halving_scatter(): lax.ppermute(send, 'space', [(i, (i + shift) % ns) for i in range(ns)])  5.58 us
    ppermute x2, starting transfers between devices, space_sum(): lax.ppermute(values, 'space', [(i, i ^ step) for i in range(count)])  5.04 us
    unnamed x26, local copies, waits for them, and re-layouts  4.53 us
    ppermute x3, waiting for transfers between devices, halving_scatter(): lax.ppermute(send, 'space', [(i, (i + shift) % ns) for i in range(ns)])  4.39 us
    dot_general x9, matrix products, on_device(): jnp.einsum('nfhwc,cd->nfhwd', window, spatial_weight[row_tap, col_tap], p...  3.89 us
  transfers between devices with their start and end apart: 12, of which 8 were waited for; matrix products, arithmetic and copies ran while one was open for 5% of the time, Pallas kernels for 0%

profile of v4, /device:TPU:0, one launch (start us, length us, event | category | flops | bytes accessed | tf_op | source)
XLA Modules:
  0.0 73.1 jit_solution(10193178739941983442)
XLA Ops:
  0.6 1.4 %collective-permute-start.1 = (bf16[1,33,1,8,256]{4,3,2,1,0:T(8,128)(2,1)}, bf16[1,33,1,8,256]{4,3,2,1,0:T(8,128)(2,1)S(1)}, u32[]{:S(2)}, u32[]{:S(2)}) collective-permute-start(bf16[1,33,1,8,256]{4,3,2,1,0:T(8,128)(2,1)} %param.8), channel_id=1, source_target_pairs={{1,0},{2,1},{3,2},{5,4},{6,5},{7,6},{9,8},{10,9},{11,10},{13,12},{... | collective-permute-start | bytes 405512 | tf_op jit(solution)/shard_map/ppermute | solution.py:20
  2.1 5.6 %collective-permute-start = (bf16[1,33,1,8,256]{4,3,2,1,0:T(8,128)(2,1)}, bf16[1,33,1,8,256]{4,3,2,1,0:T(8,128)(2,1)S(1)}, u32[]{:S(2)}, u32[]{:S(2)}) collective-permute-start(bf16[1,33,1,8,256]{4,3,2,1,0:T(8,128)(2,1)} %param.8), channel_id=1, source_target_pairs={{0,1},{1,2},{2,3},{4,5},{5,6},{6,7},{8,9},{9,10},{10,11},{12,13},{... | collective-permute-start | bytes 405512 | tf_op jit(solution)/shard_map/ppermute | solution.py:19
  7.7 0.7 fusion.121
  8.4 0.7 and_bitcast_fusion
  9.7 1.1 %broadcast_in_dim.46 = bf16[33,8,2,256]{3,2,1,0:T(2,128)(2,1)S(1)} broadcast(bf16[33,8,256]{2,1,0:T(8,128)(2,1)} %bitcast.349), dimensions={0,1,3} | broadcast | bytes 405504 | tf_op jit(solution)/shard_map/broadcast_in_dim | solution.py:26
  10.8 0.9 %convert_element_type.92 = f32[33,16,256]{2,1,0:T(8,128)} convert(bf16[33,16,256]{2,1,0:T(8,128)(2,1)S(1)} %broadcast_in_dim.47) | non-fusion elementwise | flops 135168 | bytes 811008 | tf_op jit(solution)/shard_map/convert_element_type | solution.py:160
  12.3 0.9 %fusion.5 = bf16[1,33,4,18,256]{4,3,2,1,0:T(8,128)(2,1)S(1)} fusion(bf16[1,33,1,16,256]{4,3,2,1,0:T(8,128)(2,1)S(1)} %slice.141, bf16[1,33,2,16,256]{4,3,2,1,0:T(8,128)(2,1)S(1)} %broadcast_in_dim.50, bf16[1,33,1,16,256]{4,3,2,1,0:T(8,128)(2,1)S(1)} %slice.140), kind=kLoop, calls=%fused_computation.10 | loop fusion | flops 7299072 | bytes 2297856 | tf_op jit(solution)/shard_map/concatenate | solution.py:132
  13.2 0.4 copy-done.6
  16.2 1.4 %multiply_convert_fusion = (bf16[33,2,16,256]{3,2,1,0:T(8,128)(2,1)S(1)}, f32[33,2,16,256]{3,2,1,0:T(8,128)}) fusion(f32[33,2,16,256]{3,2,1,0:T(8,128)S(1)} %convolution_add_fusion.5, bf16[3,3,256,256]{3,2,1,0:T(8,128)(2,1)S(1)} %copy-done.6, bf16[1,33,4,18,256]{4,3,2,1,0:T(8,128)(2,1)S(1)} %fusion.5), kind=kOutput, calls=%fused_computation.57 | convolution fusion | flops 140034048 | bytes 3375104 | tf_op jit(solution)/shard_map/nfhwc,cd->nfhwd/dot_general | solution.py:142
  18.2 0.7 %copy-done.3 = f32[33,16,256]{2,1,0:T(8,128)S(1)} copy-done((f32[33,16,256]{2,1,0:T(8,128)S(1)}, f32[33,16,256]{2,1,0:T(8,128)}, u32[]{:S(2)}) %copy-start.3) | copy-done | bytes 540696
  18.9 1.1 %fusion.15 = bf16[1,33,2,16,256]{4,3,2,1,0:T(8,128)(2,1)} fusion(f32[33,2,16,256]{3,2,1,0:T(8,128)S(1)} %convolution_add_fusion.3, f32[33,16,256]{2,1,0:T(8,128)S(1)} %copy-done.3, f32[33]{0:T(128)S(1)} %compare_convert_fusion, bf16[1,33,2,16,256]{4,3,2,1,0:T(8,128)(2,1)S(1)} %bitcast.338, bf16[3,256,256]{2,1,0:T(8,128)(2,1)S(1)} %copy-done.4), kind=kOutput, calls=%fused_computation.35 | convolution fusion | flops 139493376 | bytes 2834944 | tf_op jit(solution)/shard_map/nfhwc,cd->nfhwd/dot_general | solution.py:151
  20.1 1.6 %gather_fusion = bf16[8,2,16,256]{3,2,1,0:T(8,128)(2,1)S(1)} fusion(bf16[1,33,2,16,256]{4,3,2,1,0:T(8,128)(2,1)} %fusion.15, s32[8]{0:T(128)S(1)} %or_bitcast_fusion), kind=kCustom, calls=%fused_computation | custom fusion | bytes 262208 | tf_op jit(solution)/shard_map/vmap(jit(_take))/gather | solution.py:161
  21.7 0.9 %fusion.50 = (f32[8,256]{1,0:T(8,128)S(1)}, f32[8,2,16,256]{3,2,1,0:T(8,128)}) fusion(bf16[256,256]{1,0:T(8,128)(2,1)S(1)} %copy-done, bf16[8,2,16,256]{3,2,1,0:T(8,128)(2,1)S(1)} %gather_fusion, pred[8]{0:T(512)(128)(4,1)S(1)} %and_bitcast_fusion), kind=kOutput, calls=%fused_computation.107 | convolution fusion | flops 34207744 | bytes 532488 | tf_op jit(solution)/shard_map/nqhwc,ce->nqhwe/dot_general | solution.py:164
  22.6 2.0 %collective-permute-start.2 = (f32[1,8,256]{2,1,0:T(8,128)S(1)}, f32[1,8,256]{2,1,0:T(8,128)S(1)}, u32[]{:S(2)}, u32[]{:S(2)}) collective-permute-start(f32[1,8,256]{2,1,0:T(8,128)S(1)} %bitcast.354), channel_id=1, source_target_pairs={{0,1},{1,0},{2,3},{3,2},{4,5},{5,4},{6,7},{7,6},{8,9},{9,8},{10,11... | collective-permute-start | bytes 24584 | tf_op jit(solution)/shard_map/ppermute | solution.py:57
  24.6 1.6 %collective-permute-done.2 = f32[1,8,256]{2,1,0:T(8,128)S(1)} collective-permute-done((f32[1,8,256]{2,1,0:T(8,128)S(1)}, f32[1,8,256]{2,1,0:T(8,128)S(1)}, u32[]{:S(2)}, u32[]{:S(2)}) %collective-permute-start.2) | collective-permute-done | bytes 8224 | tf_op jit(solution)/shard_map/ppermute | solution.py:57
  26.3 3.0 %collective-permute-start.3 = (f32[1,8,256]{2,1,0:T(8,128)S(1)}, f32[1,8,256]{2,1,0:T(8,128)S(1)}, u32[]{:S(2)}, u32[]{:S(2)}) collective-permute-start(f32[1,8,256]{2,1,0:T(8,128)S(1)} %bitcast_add_fusion.5), channel_id=1, source_target_pairs={{0,2},{1,3},{2,0},{3,1},{4,6},{5,7},{6,4},{7,5},{8,10},{9,11},{10,... | collective-permute-start | bytes 24584 | tf_op jit(solution)/shard_map/ppermute | solution.py:57
  29.3 1.6 %collective-permute-done.3 = f32[1,8,256]{2,1,0:T(8,128)S(1)} collective-permute-done((f32[1,8,256]{2,1,0:T(8,128)S(1)}, f32[1,8,256]{2,1,0:T(8,128)S(1)}, u32[]{:S(2)}, u32[]{:S(2)}) %collective-permute-start.3) | collective-permute-done | bytes 8224 | tf_op jit(solution)/shard_map/ppermute | solution.py:57
  31.2 1.1 %fusion.48 = bf16[8,2,16,256]{3,2,1,0:T(8,128)(2,1)S(1)} fusion(f32[8,2,16,256]{3,2,1,0:T(8,128)} %get-tuple-element.17, f32[8,256]{1,0:T(8,128)S(1)} %get-tuple-element.13, f32[8,256]{1,0:T(8,128)S(1)} %get-tuple-element.12), kind=kLoop, calls=%fused_computation.104 | loop fusion | flops 1245184 | bytes 409600 | tf_op jit(solution)/shard_map/convert_element_type | solution.py:171
  32.5 1.0 %fusion.12 = bf16[1,33,2,16,256]{4,1,3,2,0:T(8,128)(2,1)S(1)} fusion(f32[8,2,16,256]{3,0,2,1:T(8,128)S(1)} %fusion.57, bf16[1,33,2,16,256]{4,3,2,1,0:T(8,128)(2,1)S(1)} %copy-done.7, f32[33]{0:T(128)S(1)} %compare_select_fusion.1, s32[8]{0:T(128)S(1)} %bitcast.355), kind=kOutput, calls=%fused_computation.32 | convolution fusion | flops 27033864 | bytes 1343652 | tf_op jit(solution)/shard_map/nqf,nqhwc->nfhwc/dot_general | solution.py:180
  34.7 0.6 copy-done.5
  35.7 0.4 slice_bitcast_fusion
  36.5 0.9 %copy-done.10 = f32[33,2,16,256]{3,2,1,0:T(8,128)S(1)} copy-done((f32[33,2,16,256]{3,2,1,0:T(8,128)S(1)}, f32[33,2,16,256]{3,2,1,0:T(8,128)}, u32[]{:S(2)}) %copy-start.10) | copy-done | bytes 1081368
  37.4 0.6 fusion.13
  37.9 0.4 fusion.24
  38.3 0.6 copy-done.2
  38.9 0.4 fusion.23
  39.3 0.4 fusion.22
  40.1 0.4 fusion.20
  40.5 0.4 fusion.19
  41.3 0.4 fusion.17
  41.7 0.4 fusion.16
  42.2 0.4 broadcast_select_fusion.1
  42.8 3.4 %collective-permute-done.4 = f32[16,96,256]{2,1,0:T(8,128)} collective-permute-done((f32[16,96,256]{2,1,0:T(8,128)S(1)}, f32[16,96,256]{2,1,0:T(8,128)}, u32[]{:S(2)}, u32[]{:S(2)}) %collective-permute-start.4) | collective-permute-done | bytes 1572896 | tf_op jit(solution)/shard_map/ppermute | solution.py:74
  46.2 1.6 %bitcast_add_fusion = f32[16,96,256]{2,1,0:T(8,128)S(1)} fusion(f32[16,96,256]{2,1,0:T(8,128)} %collective-permute-done.4, f32[4,1,4,96,256]{4,3,2,1,0:T(8,128)S(1)} %get-tuple-element.3), kind=kLoop, calls=%fused_computation.13 | loop fusion | flops 393216 | bytes 4718592 | tf_op jit(solution)/shard_map/add | solution.py:75
  48.0 1.9 %collective-permute-start.7 = (bf16[8,48,256]{2,1,0:T(8,128)(2,1)S(1)}, bf16[8,48,256]{2,1,0:T(8,128)(2,1)S(1)}, u32[]{:S(2)}, u32[]{:S(2)}) collective-permute-start(bf16[8,48,256]{2,1,0:T(8,128)(2,1)S(1)} %fusion.51), channel_id=1, source_target_pairs={{0,16},{4,20},{8,24},{12,28},{16,0},{20,4},{24,8},{28,12},{1,17},{... | collective-permute-start | bytes 589832 | tf_op jit(solution)/shard_map/ppermute | solution.py:74
  49.9 1.6 %collective-permute-start.5 = (bf16[8,48,256]{2,1,0:T(8,128)(2,1)S(1)}, bf16[8,48,256]{2,1,0:T(8,128)(2,1)S(1)}, u32[]{:S(2)}, u32[]{:S(2)}) collective-permute-start(bf16[8,48,256]{2,1,0:T(8,128)(2,1)S(1)} %bitcast.348), channel_id=1, source_target_pairs={{0,8},{4,12},{8,0},{12,4},{16,24},{20,28},{24,16},{28,20},{1,9},{5... | collective-permute-start | bytes 589832 | tf_op jit(solution)/shard_map/ppermute | solution.py:74
  51.5 3.5 %collective-permute-done.7 = bf16[8,48,256]{2,1,0:T(8,128)(2,1)S(1)} collective-permute-done((bf16[8,48,256]{2,1,0:T(8,128)(2,1)S(1)}, bf16[8,48,256]{2,1,0:T(8,128)(2,1)S(1)}, u32[]{:S(2)}, u32[]{:S(2)}) %collective-permute-start.7) | collective-permute-done | bytes 196640 | tf_op jit(solution)/shard_map/ppermute | solution.py:74
  55.2 1.8 %collective-permute-start.8 = (bf16[4,48,256]{2,1,0:T(8,128)(2,1)S(1)}, bf16[4,48,256]{2,1,0:T(8,128)(2,1)S(1)}, u32[]{:S(2)}, u32[]{:S(2)}) collective-permute-start(bf16[4,48,256]{2,1,0:T(8,128)(2,1)S(1)} %fusion.96), channel_id=1, source_target_pairs={{0,8},{4,12},{8,0},{12,4},{16,24},{20,28},{24,16},{28,20},{1,9},{5... | collective-permute-start | bytes 294920 | tf_op jit(solution)/shard_map/ppermute | solution.py:74
  57.0 1.6 %collective-permute-start.6 = (bf16[4,48,256]{2,1,0:T(8,128)(2,1)S(1)}, bf16[4,48,256]{2,1,0:T(8,128)(2,1)S(1)}, u32[]{:S(2)}, u32[]{:S(2)}) collective-permute-start(bf16[4,48,256]{2,1,0:T(8,128)(2,1)S(1)} %fusion.95), channel_id=1, source_target_pairs={{0,16},{4,20},{8,24},{12,28},{16,0},{20,4},{24,8},{28,12},{1,17},{... | collective-permute-start | bytes 294920 | tf_op jit(solution)/shard_map/ppermute | solution.py:74
  58.6 1.2 %collective-permute-done.8 = bf16[4,48,256]{2,1,0:T(8,128)(2,1)S(1)} collective-permute-done((bf16[4,48,256]{2,1,0:T(8,128)(2,1)S(1)}, bf16[4,48,256]{2,1,0:T(8,128)(2,1)S(1)}, u32[]{:S(2)}, u32[]{:S(2)}) %collective-permute-start.8) | collective-permute-done | bytes 98336 | tf_op jit(solution)/shard_map/ppermute | solution.py:74
  59.9 1.8 %collective-permute-done.6 = bf16[4,48,256]{2,1,0:T(8,128)(2,1)S(1)} collective-permute-done((bf16[4,48,256]{2,1,0:T(8,128)(2,1)S(1)}, bf16[4,48,256]{2,1,0:T(8,128)(2,1)S(1)}, u32[]{:S(2)}, u32[]{:S(2)}) %collective-permute-start.6) | collective-permute-done | bytes 98336 | tf_op jit(solution)/shard_map/ppermute | solution.py:74
  61.8 1.6 %collective-permute-start.9 = (f32[96,256]{1,0:T(8,128)S(1)}, f32[96,256]{1,0:T(8,128)S(1)}, u32[]{:S(2)}, u32[]{:S(2)}) collective-permute-start(f32[96,256]{1,0:T(8,128)S(1)} %get-tuple-element.9), channel_id=1, source_target_pairs={{0,1},{1,2},{2,3},{3,0},{4,5},{5,6},{6,7},{7,4},{8,9},{9,10},{10,1... | collective-permute-start | bytes 294920 | tf_op jit(solution)/shard_map/ppermute | solution.py:109
  63.4 1.9 %collective-permute-start.10 = (f32[96,256]{1,0:T(8,128)S(1)}, f32[96,256]{1,0:T(8,128)S(1)}, u32[]{:S(2)}, u32[]{:S(2)}) collective-permute-start(f32[96,256]{1,0:T(8,128)S(1)} %get-tuple-element.10), channel_id=1, source_target_pairs={{0,2},{1,3},{2,0},{3,1},{4,6},{5,7},{6,4},{7,5},{8,10},{9,11},{10,... | collective-permute-start | bytes 294920 | tf_op jit(solution)/shard_map/ppermute | solution.py:109
  65.3 2.0 %collective-permute-start.11 = (f32[96,256]{1,0:T(8,128)S(1)}, f32[96,256]{1,0:T(8,128)S(1)}, u32[]{:S(2)}, u32[]{:S(2)}) collective-permute-start(f32[96,256]{1,0:T(8,128)S(1)} %get-tuple-element.11), channel_id=1, source_target_pairs={{0,3},{1,0},{2,1},{3,2},{4,7},{5,4},{6,5},{7,6},{8,11},{9,8},{10,9... | collective-permute-start | bytes 294920 | tf_op jit(solution)/shard_map/ppermute | solution.py:109
  67.3 1.6 %collective-permute-done.9 = f32[96,256]{1,0:T(8,128)S(1)} collective-permute-done((f32[96,256]{1,0:T(8,128)S(1)}, f32[96,256]{1,0:T(8,128)S(1)}, u32[]{:S(2)}, u32[]{:S(2)}) %collective-permute-start.9) | collective-permute-done | bytes 98336 | tf_op jit(solution)/shard_map/ppermute | solution.py:109
  68.9 2.8 %collective-permute-done.10 = f32[96,256]{1,0:T(8,128)S(1)} collective-permute-done((f32[96,256]{1,0:T(8,128)S(1)}, f32[96,256]{1,0:T(8,128)S(1)}, u32[]{:S(2)}, u32[]{:S(2)}) %collective-permute-start.10) | collective-permute-done | bytes 98336 | tf_op jit(solution)/shard_map/ppermute | solution.py:109
  71.8 0.7 copy.111
  72.5 0.6 copy.112
  (70 shorter events, 7.4 us)
Async XLA Ops:
  0.6 21.1 %copy-start = (bf16[256,256]{1,0:T(8,128)(2,1)S(1)}, bf16[256,256]{1,0:T(8,128)(2,1)}, u32[]{:S(2)}) copy-start(bf16[256,256]{1,0:T(8,128)(2,1)} %param.12) | copy-start | bytes 393220
  0.6 11.1 %collective-permute-start.1 = (bf16[1,33,1,8,256]{4,3,2,1,0:T(8,128)(2,1)}, bf16[1,33,1,8,256]{4,3,2,1,0:T(8,128)(2,1)S(1)}, u32[]{:S(2)}, u32[]{:S(2)}) collective-permute-start(bf16[1,33,1,8,256]{4,3,2,1,0:T(8,128)(2,1)} %param.8), channel_id=1, source_target_pairs={{1,0},{2,1},{3,2},{5,4},{6,5},{7,6},{9,8},{10,9},{11,10},{13,12},{... | collective-permute-start | bytes 405512 | tf_op jit(solution)/shard_map/ppermute | solution.py:20
  2.1 9.9 %collective-permute-start = (bf16[1,33,1,8,256]{4,3,2,1,0:T(8,128)(2,1)}, bf16[1,33,1,8,256]{4,3,2,1,0:T(8,128)(2,1)S(1)}, u32[]{:S(2)}, u32[]{:S(2)}) collective-permute-start(bf16[1,33,1,8,256]{4,3,2,1,0:T(8,128)(2,1)} %param.8), channel_id=1, source_target_pairs={{0,1},{1,2},{2,3},{4,5},{5,6},{6,7},{8,9},{9,10},{10,11},{12,13},{... | collective-permute-start | bytes 405512 | tf_op jit(solution)/shard_map/ppermute | solution.py:19
  12.2 1.7 %copy-start.1 = (bf16[1,33,1,16,256]{4,3,2,1,0:T(8,128)(2,1)}, bf16[1,33,1,16,256]{4,3,2,1,0:T(8,128)(2,1)S(1)}, u32[]{:S(2)}) copy-start(bf16[1,33,1,16,256]{4,3,2,1,0:T(8,128)(2,1)S(1)} %slice.140) | copy-start | bytes 811012
  12.3 1.3 %copy-start.6 = (bf16[3,3,256,256]{3,2,1,0:T(8,128)(2,1)S(1)}, bf16[3,3,256,256]{3,2,1,0:T(8,128)(2,1)}, u32[]{:S(2)}) copy-start(bf16[3,3,256,256]{3,2,1,0:T(8,128)(2,1)} %param.10) | copy-start | bytes 3538948
  16.1 1.5 %copy-start.4 = (bf16[3,256,256]{2,1,0:T(8,128)(2,1)S(1)}, bf16[3,256,256]{2,1,0:T(8,128)(2,1)}, u32[]{:S(2)}) copy-start(bf16[3,256,256]{2,1,0:T(8,128)(2,1)} %param.11) | copy-start | bytes 1179652
  17.9 1.1 %copy-start.3 = (f32[33,16,256]{2,1,0:T(8,128)S(1)}, f32[33,16,256]{2,1,0:T(8,128)}, u32[]{:S(2)}) copy-start(f32[33,16,256]{2,1,0:T(8,128)} %convert_element_type.92) | copy-start | bytes 1622020
  18.9 5.7 %copy-start.8 = (f32[256]{0:T(256)S(1)}, f32[256]{0:T(256)}, u32[]{:S(2)}) copy-start(f32[256]{0:T(256)} %param.13) | copy-start | bytes 3076
  20.1 12.5 %copy-start.9 = (s32[1,8]{1,0:T(1,128)S(1)}, s32[1,8]{1,0:T(1,128)}, u32[]{:S(2)}) copy-start(s32[1,8]{1,0:T(1,128)} %param.14) | copy-start | bytes 100
  22.6 3.7 %collective-permute-start.2 = (f32[1,8,256]{2,1,0:T(8,128)S(1)}, f32[1,8,256]{2,1,0:T(8,128)S(1)}, u32[]{:S(2)}, u32[]{:S(2)}) collective-permute-start(f32[1,8,256]{2,1,0:T(8,128)S(1)} %bitcast.354), channel_id=1, source_target_pairs={{0,1},{1,0},{2,3},{3,2},{4,5},{5,4},{6,7},{7,6},{8,9},{9,8},{10,11... | collective-permute-start | bytes 24584 | tf_op jit(solution)/shard_map/ppermute | solution.py:57
  26.3 4.7 %collective-permute-start.3 = (f32[1,8,256]{2,1,0:T(8,128)S(1)}, f32[1,8,256]{2,1,0:T(8,128)S(1)}, u32[]{:S(2)}, u32[]{:S(2)}) collective-permute-start(f32[1,8,256]{2,1,0:T(8,128)S(1)} %bitcast_add_fusion.5), channel_id=1, source_target_pairs={{0,2},{1,3},{2,0},{3,1},{4,6},{5,7},{6,4},{7,5},{8,10},{9,11},{10,... | collective-permute-start | bytes 24584 | tf_op jit(solution)/shard_map/ppermute | solution.py:57
  29.3 3.2 %copy-start.7 = (bf16[1,33,2,16,256]{4,3,2,1,0:T(8,128)(2,1)S(1)}, bf16[1,33,2,16,256]{4,3,2,1,0:T(8,128)(2,1)}, u32[]{:S(2)}) copy-start(bf16[1,33,2,16,256]{4,3,2,1,0:T(8,128)(2,1)} %param.15) | copy-start | bytes 1622020
  34.3 1.0 %copy-start.5 = (bf16[3,256,256]{2,1,0:T(8,128)(2,1)S(1)}, bf16[3,256,256]{2,1,0:T(8,128)(2,1)}, u32[]{:S(2)}) copy-start(bf16[3,256,256]{2,1,0:T(8,128)(2,1)} %param.11) | copy-start | bytes 1179652
  36.1 1.2 %copy-start.10 = (f32[33,2,16,256]{3,2,1,0:T(8,128)S(1)}, f32[33,2,16,256]{3,2,1,0:T(8,128)}, u32[]{:S(2)}) copy-start(f32[33,2,16,256]{3,2,1,0:T(8,128)} %get-tuple-element.15) | copy-start | bytes 3244036
  37.9 1.0 %copy-start.2 = (bf16[1,33,1,16,256]{4,3,2,1,0:T(8,128)(2,1)S(1)}, bf16[1,33,1,16,256]{4,3,2,1,0:T(8,128)(2,1)}, u32[]{:S(2)}) copy-start(bf16[1,33,1,16,256]{4,3,2,1,0:T(8,128)(2,1)} %copy-done.1) | copy-start | bytes 811012
  42.6 3.6 %collective-permute-start.4 = (f32[16,96,256]{2,1,0:T(8,128)S(1)}, f32[16,96,256]{2,1,0:T(8,128)}, u32[]{:S(2)}, u32[]{:S(2)}) collective-permute-start(f32[16,96,256]{2,1,0:T(8,128)S(1)} %bitcast.347), channel_id=1, source_target_pairs={{0,4},{4,0},{8,12},{12,8},{16,20},{20,16},{24,28},{28,24},{1,5},{5... | collective-permute-start | bytes 4718600 | tf_op jit(solution)/shard_map/ppermute | solution.py:74
  48.0 7.1 %collective-permute-start.7 = (bf16[8,48,256]{2,1,0:T(8,128)(2,1)S(1)}, bf16[8,48,256]{2,1,0:T(8,128)(2,1)S(1)}, u32[]{:S(2)}, u32[]{:S(2)}) collective-permute-start(bf16[8,48,256]{2,1,0:T(8,128)(2,1)S(1)} %fusion.51), channel_id=1, source_target_pairs={{0,16},{4,20},{8,24},{12,28},{16,0},{20,4},{24,8},{28,12},{1,17},{... | collective-permute-start | bytes 589832 | tf_op jit(solution)/shard_map/ppermute | solution.py:74
  49.9 7.0 %collective-permute-start.5 = (bf16[8,48,256]{2,1,0:T(8,128)(2,1)S(1)}, bf16[8,48,256]{2,1,0:T(8,128)(2,1)S(1)}, u32[]{:S(2)}, u32[]{:S(2)}) collective-permute-start(bf16[8,48,256]{2,1,0:T(8,128)(2,1)S(1)} %bitcast.348), channel_id=1, source_target_pairs={{0,8},{4,12},{8,0},{12,4},{16,24},{20,28},{24,16},{28,20},{1,9},{5... | collective-permute-start | bytes 589832 | tf_op jit(solution)/shard_map/ppermute | solution.py:74
  55.2 4.7 %collective-permute-start.8 = (bf16[4,48,256]{2,1,0:T(8,128)(2,1)S(1)}, bf16[4,48,256]{2,1,0:T(8,128)(2,1)S(1)}, u32[]{:S(2)}, u32[]{:S(2)}) collective-permute-start(bf16[4,48,256]{2,1,0:T(8,128)(2,1)S(1)} %fusion.96), channel_id=1, source_target_pairs={{0,8},{4,12},{8,0},{12,4},{16,24},{20,28},{24,16},{28,20},{1,9},{5... | collective-permute-start | bytes 294920 | tf_op jit(solution)/shard_map/ppermute | solution.py:74
  57.0 4.7 %collective-permute-start.6 = (bf16[4,48,256]{2,1,0:T(8,128)(2,1)S(1)}, bf16[4,48,256]{2,1,0:T(8,128)(2,1)S(1)}, u32[]{:S(2)}, u32[]{:S(2)}) collective-permute-start(bf16[4,48,256]{2,1,0:T(8,128)(2,1)S(1)} %fusion.95), channel_id=1, source_target_pairs={{0,16},{4,20},{8,24},{12,28},{16,0},{20,4},{24,8},{28,12},{1,17},{... | collective-permute-start | bytes 294920 | tf_op jit(solution)/shard_map/ppermute | solution.py:74
  61.8 7.2 %collective-permute-start.9 = (f32[96,256]{1,0:T(8,128)S(1)}, f32[96,256]{1,0:T(8,128)S(1)}, u32[]{:S(2)}, u32[]{:S(2)}) collective-permute-start(f32[96,256]{1,0:T(8,128)S(1)} %get-tuple-element.9), channel_id=1, source_target_pairs={{0,1},{1,2},{2,3},{3,0},{4,5},{5,6},{6,7},{7,4},{8,9},{9,10},{10,1... | collective-permute-start | bytes 294920 | tf_op jit(solution)/shard_map/ppermute | solution.py:109
  63.4 8.3 %collective-permute-start.10 = (f32[96,256]{1,0:T(8,128)S(1)}, f32[96,256]{1,0:T(8,128)S(1)}, u32[]{:S(2)}, u32[]{:S(2)}) collective-permute-start(f32[96,256]{1,0:T(8,128)S(1)} %get-tuple-element.10), channel_id=1, source_target_pairs={{0,2},{1,3},{2,0},{3,1},{4,6},{5,7},{6,4},{7,5},{8,10},{9,11},{10,... | collective-permute-start | bytes 294920 | tf_op jit(solution)/shard_map/ppermute | solution.py:109
  65.3 6.4 %collective-permute-start.11 = (f32[96,256]{1,0:T(8,128)S(1)}, f32[96,256]{1,0:T(8,128)S(1)}, u32[]{:S(2)}, u32[]{:S(2)}) collective-permute-start(f32[96,256]{1,0:T(8,128)S(1)} %get-tuple-element.11), channel_id=1, source_target_pairs={{0,3},{1,0},{2,1},{3,2},{4,7},{5,4},{6,5},{7,6},{8,11},{9,8},{10,9... | collective-permute-start | bytes 294920 | tf_op jit(solution)/shard_map/ppermute | solution.py:109

commit v5 on v4

--- a/solution.py
+++ b/solution.py
@@ -80,7 +80,7 @@
     bd, bs = _log2(nd), _log2(ns)
     if bd is None or bs is None:
         flat = lax.psum_scatter(blocks, "dp", scatter_dimension=0, tiled=True)
-        return lax.psum_scatter(flat, "space", scatter_dimension=0, tiled=True)[0]
+        return [lax.psum_scatter(flat, "space", scatter_dimension=0, tiled=True)[0]]
     natural = [("dp", i) for i in reversed(range(bd))] + [("space", i) for i in reversed(range(bs))]
     shared = 0
     while shared < len(natural) and all(o[shared] == orders[0][shared] for o in orders):
@@ -103,14 +103,14 @@
     rest = orders[0][tail:]
     if sorted(rest) == [("space", i) for i in range(bs)] and part_left == rest[::-1] == natural[bd:]:
         me = lax.axis_index("space")
-        total = lax.dynamic_index_in_dim(cur, me, 0, keepdims=False)
+        terms = [lax.dynamic_index_in_dim(cur, me, 0, keepdims=False)]
         for shift in range(1, ns):
             send = lax.dynamic_index_in_dim(cur, (me + shift) % ns, 0, keepdims=False)
-            total = total + lax.ppermute(send, "space", [(i, (i + shift) % ns) for i in range(ns)])
-        return total
+            terms.append(lax.ppermute(send, "space", [(i, (i + shift) % ns) for i in range(ns)]))
+        return terms
     for axis, bit in rest:
         cur = _halve(cur, part_left, axis, bit)
-    return cur[0]
+    return [cur[0]]
 
 
 def on_device(
@@ -158,9 +158,12 @@
         :, :, None, None, None
     ]
     decoded = (alive_mask * (upsampled.astype(jnp.float32) + mixing)).astype(jnp.bfloat16)
-    chosen = jax.vmap(lambda clip_frames, indices: jnp.take(clip_frames, indices, axis=0))(
-        decoded, critic_frames
-    )
+    picker = (critic_frames[:, :, None] == jnp.arange(frame_count)[None, None, :]).astype(
+        jnp.bfloat16
+    )
+    chosen = jnp.einsum(
+        "nqf,nfhwc->nqhwc", picker, decoded, preferred_element_type=jnp.float32
+    ).astype(jnp.bfloat16)
     hidden = jnp.einsum(
         "nqhwc,ce->nqhwe", chosen, critic_weight, preferred_element_type=jnp.float32
     )
@@ -224,7 +227,12 @@
         orders = (plain + [("space", i) for i in range(groups.bit_length() - 1)],)
     share = halving_scatter(jnp.concatenate([spatial_grad, temporal_grad], axis=1), orders)
     spatial_rows = spatial_grad.shape[1]
-    return (decoded, share[:spatial_rows].reshape(-1), share[spatial_rows:].reshape(-1))
+    spatial_share = share[0][:spatial_rows].reshape(-1)
+    temporal_share = share[0][spatial_rows:].reshape(-1)
+    for term in share[1:]:
+        spatial_share = spatial_share + term[:spatial_rows].reshape(-1)
+        temporal_share = temporal_share + term[spatial_rows:].reshape(-1)
+    return (decoded, spatial_share, temporal_share)
 
 
 def solution(mesh):

time: 73.6 us -> 71.8 us (0.976)
  local copies, waits for them, and re-layouts: 8.36 us -> 6.47 us
    gather x2 -> x0, local copies, waits for them, and re-layouts: 1.62 us -> none  [on_device(): jnp.take(clip_frames, indices, axis=0)]
    add x1 -> x2, other arithmetic: 0.03 us -> 1.27 us  [the longest x1 0.65 us: on_device(): spatial_share = spatial_share + term[:spatial_rows].reshape(-1)]
    dot_general x3, matrix products: 1.7 us -> 0.89 us  [on_device(): jnp.einsum('nfhwc,cd->nfhwd', delayed(activated, offset), temporal_weight...]
    unnamed x26 -> x40, local copies, waits for them, and re-layouts: 4.53 us -> 4.26 us
  transfers between devices with their start and end apart: 12 -> 12, of which waited for: 8 -> 9; matrix products, arithmetic and copies ran while one was open for 5% -> 4% of each run, Pallas kernels for 0% -> 0%
where the time goes in v5:
time: 71.8 us; the launch traced here: 71.4 us
  starting transfers between devices  24.9 us (35%)
  waiting for transfers between devices  17.9 us (25%)
  matrix products  13.3 us (19%)
  other arithmetic  6.83 us (10%)
  local copies, waits for them, and re-layouts  6.47 us (9%)
  between operations  1.94 us (3%)
    ppermute x5, waiting for transfers between devices, _halve(): got = lax.ppermute(send, axis, [(i, i ^ 1 << bit) for i in range(size)])  10.3 us
    ppermute x5, starting transfers between devices, _halve(): got = lax.ppermute(send, axis, [(i, i ^ 1 << bit) for i in range(size)])  6.33 us
    ppermute x3, starting transfers between devices, halving_scatter(): lax.ppermute(send, 'space', [(i, (i + shift) % ns) for i in range(ns)])  5.96 us
    ppermute x1, starting transfers between devices, exchange_rows(): above = lax.ppermute(tail, axis, [(i, i + 1) for i in range(ends)])  5.59 us
    ppermute x2, starting transfers between devices, space_sum(): lax.ppermute(values, 'space', [(i, i ^ step) for i in range(count)])  5.59 us
    unnamed x40, local copies, waits for them, and re-layouts  4.26 us
    ppermute x3, waiting for transfers between devices, halving_scatter(): lax.ppermute(send, 'space', [(i, (i + shift) % ns) for i in range(ns)])  4.21 us
    dot_general x9, matrix products, on_device(): jnp.einsum('nfhwc,cd->nfhwd', window, spatial_weight[row_tap, col_tap], p...  3.88 us
  transfers between devices with their start and end apart: 12, of which 9 were waited for; matrix products, arithmetic and copies ran while one was open for 4% of the time, Pallas kernels for 0%

profile of v5, /device:TPU:0, one launch (start us, length us, event | category | flops | bytes accessed | tf_op | source)
XLA Modules:
  0.0 71.4 jit_solution(14443600488544559349)
XLA Ops:
  0.6 1.4 %collective-permute-start.1 = (bf16[1,33,1,8,256]{4,3,2,1,0:T(8,128)(2,1)}, bf16[1,33,1,8,256]{4,3,2,1,0:T(8,128)(2,1)S(1)}, u32[]{:S(2)}, u32[]{:S(2)}) collective-permute-start(bf16[1,33,1,8,256]{4,3,2,1,0:T(8,128)(2,1)} %param.8), channel_id=1, source_target_pairs={{1,0},{2,1},{3,2},{5,4},{6,5},{7,6},{9,8},{10,9},{11,10},{13,12},{... | collective-permute-start | bytes 405512 | tf_op jit(solution)/shard_map/ppermute | solution.py:20
  2.1 5.6 %collective-permute-start = (bf16[1,33,1,8,256]{4,3,2,1,0:T(8,128)(2,1)}, bf16[1,33,1,8,256]{4,3,2,1,0:T(8,128)(2,1)S(1)}, u32[]{:S(2)}, u32[]{:S(2)}) collective-permute-start(bf16[1,33,1,8,256]{4,3,2,1,0:T(8,128)(2,1)} %param.8), channel_id=1, source_target_pairs={{0,1},{1,2},{2,3},{4,5},{5,6},{6,7},{8,9},{9,10},{10,11},{12,13},{... | collective-permute-start | bytes 405512 | tf_op jit(solution)/shard_map/ppermute | solution.py:19
  8.3 1.1 %broadcast_in_dim.16 = bf16[33,8,2,256]{3,2,1,0:T(2,128)(2,1)S(1)} broadcast(bf16[33,8,256]{2,1,0:T(8,128)(2,1)} %bitcast.356), dimensions={0,1,3} | broadcast | bytes 405504 | tf_op jit(solution)/shard_map/broadcast_in_dim | solution.py:26
  9.5 0.9 %convert_element_type.97 = f32[33,16,256]{2,1,0:T(8,128)} convert(bf16[33,16,256]{2,1,0:T(8,128)(2,1)S(1)} %broadcast_in_dim.17) | non-fusion elementwise | flops 135168 | bytes 811008 | tf_op jit(solution)/shard_map/convert_element_type | solution.py:160
  11.1 0.9 %fusion.5 = bf16[1,33,4,18,256]{4,3,2,1,0:T(8,128)(2,1)S(1)} fusion(bf16[1,33,1,16,256]{4,3,2,1,0:T(8,128)(2,1)S(1)} %slice.161, bf16[1,33,2,16,256]{4,3,2,1,0:T(8,128)(2,1)S(1)} %broadcast_in_dim.40, bf16[1,33,1,16,256]{4,3,2,1,0:T(8,128)(2,1)S(1)} %slice.160), kind=kLoop, calls=%fused_computation.9 | loop fusion | flops 7299072 | bytes 2297856 | tf_op jit(solution)/shard_map/concatenate | solution.py:132
  12.0 0.4 copy-done.7
  15.0 1.4 %multiply_convert_fusion = (bf16[33,2,16,256]{3,2,1,0:T(8,128)(2,1)S(1)}, f32[33,2,16,256]{3,2,1,0:T(8,128)}) fusion(f32[33,2,16,256]{3,2,1,0:T(8,128)S(1)} %convolution_add_fusion.5, bf16[3,3,256,256]{3,2,1,0:T(8,128)(2,1)S(1)} %copy-done.7, bf16[1,33,4,18,256]{4,3,2,1,0:T(8,128)(2,1)S(1)} %fusion.5), kind=kOutput, calls=%fused_computation.55 | convolution fusion | flops 140034048 | bytes 3375104 | tf_op jit(solution)/shard_map/nfhwc,cd->nfhwd/dot_general | solution.py:142
  17.0 0.7 %copy-done.4 = f32[33,16,256]{2,1,0:T(8,128)S(1)} copy-done((f32[33,16,256]{2,1,0:T(8,128)S(1)}, f32[33,16,256]{2,1,0:T(8,128)}, u32[]{:S(2)}) %copy-start.4) | copy-done | bytes 540696
  18.1 0.8 %copy-done.1 = bf16[33,2,16,256]{3,2,1,0:T(8,128)(2,1)} copy-done((bf16[33,2,16,256]{3,2,1,0:T(8,128)(2,1)}, bf16[33,2,16,256]{3,2,1,0:T(8,128)(2,1)S(1)}, u32[]{:S(2)}) %copy-start.1) | copy-done | bytes 540696
  18.9 0.4 fusion.24
  19.3 0.9 %fusion.51 = (f32[8,256]{1,0:T(8,128)S(1)}, f32[8,2,16,256]{3,2,1,0:T(8,128)}) fusion(bf16[256,256]{1,0:T(8,128)(2,1)S(1)} %copy-done, bf16[8,2,16,256]{3,0,2,1:T(8,128)(2,1)S(1)} %fusion.24), kind=kOutput, calls=%fused_computation.108 | convolution fusion | flops 34142208 | bytes 532480 | tf_op jit(solution)/shard_map/nqhwc,ce->nqhwe/dot_general | solution.py:167
  20.2 2.4 %collective-permute-start.2 = (f32[1,8,256]{2,1,0:T(8,128)S(1)}, f32[1,8,256]{2,1,0:T(8,128)S(1)}, u32[]{:S(2)}, u32[]{:S(2)}) collective-permute-start(f32[1,8,256]{2,1,0:T(8,128)S(1)} %bitcast.363), channel_id=1, source_target_pairs={{0,1},{1,0},{2,3},{3,2},{4,5},{5,4},{6,7},{7,6},{8,9},{9,8},{10,11... | collective-permute-start | bytes 24584 | tf_op jit(solution)/shard_map/ppermute | solution.py:57
  22.6 1.6 %collective-permute-done.2 = f32[1,8,256]{2,1,0:T(8,128)S(1)} collective-permute-done((f32[1,8,256]{2,1,0:T(8,128)S(1)}, f32[1,8,256]{2,1,0:T(8,128)S(1)}, u32[]{:S(2)}, u32[]{:S(2)}) %collective-permute-start.2) | collective-permute-done | bytes 8224 | tf_op jit(solution)/shard_map/ppermute | solution.py:57
  24.3 3.2 %collective-permute-start.3 = (f32[1,8,256]{2,1,0:T(8,128)S(1)}, f32[1,8,256]{2,1,0:T(8,128)S(1)}, u32[]{:S(2)}, u32[]{:S(2)}) collective-permute-start(f32[1,8,256]{2,1,0:T(8,128)S(1)} %bitcast_add_fusion.5), channel_id=1, source_target_pairs={{0,2},{1,3},{2,0},{3,1},{4,6},{5,7},{6,4},{7,5},{8,10},{9,11},{10,... | collective-permute-start | bytes 24584 | tf_op jit(solution)/shard_map/ppermute | solution.py:57
  27.5 1.6 %collective-permute-done.3 = f32[1,8,256]{2,1,0:T(8,128)S(1)} collective-permute-done((f32[1,8,256]{2,1,0:T(8,128)S(1)}, f32[1,8,256]{2,1,0:T(8,128)S(1)}, u32[]{:S(2)}, u32[]{:S(2)}) %collective-permute-start.3) | collective-permute-done | bytes 8224 | tf_op jit(solution)/shard_map/ppermute | solution.py:57
  29.3 1.1 %fusion.49 = bf16[8,2,16,256]{3,2,1,0:T(8,128)(2,1)S(1)} fusion(f32[8,2,16,256]{3,2,1,0:T(8,128)} %get-tuple-element.18, f32[8,256]{1,0:T(8,128)S(1)} %get-tuple-element.14, f32[8,256]{1,0:T(8,128)S(1)} %get-tuple-element.13), kind=kLoop, calls=%fused_computation.104 | loop fusion | flops 1245184 | bytes 409600 | tf_op jit(solution)/shard_map/convert_element_type | solution.py:174
  30.7 1.0 %fusion.12 = bf16[1,33,2,16,256]{4,1,3,2,0:T(8,128)(2,1)S(1)} fusion(f32[8,2,16,256]{3,0,2,1:T(8,128)S(1)} %fusion.59, bf16[1,33,2,16,256]{4,3,2,1,0:T(8,128)(2,1)S(1)} %copy-done.8, f32[33]{0:T(128)S(1)} %compare_select_fusion, s32[8]{0:T(128)S(1)} %bitcast.365), kind=kOutput, calls=%fused_computation.31 | convolution fusion | flops 27033864 | bytes 1343652 | tf_op jit(solution)/shard_map/nqf,nqhwc->nfhwc/dot_general | solution.py:183
  32.9 0.6 copy-done.6
  33.8 0.4 slice_bitcast_fusion
  34.6 0.9 %copy-done.11 = f32[33,2,16,256]{3,2,1,0:T(8,128)S(1)} copy-done((f32[33,2,16,256]{3,2,1,0:T(8,128)S(1)}, f32[33,2,16,256]{3,2,1,0:T(8,128)}, u32[]{:S(2)}) %copy-start.11) | copy-done | bytes 1081368
  35.5 0.6 fusion.13
  36.1 0.4 fusion.23
  36.5 0.6 copy-done.3
  37.0 0.4 fusion.22
  37.4 0.4 fusion.21
  37.9 0.4 fusion.20
  38.2 0.4 fusion.19
  38.6 0.4 fusion.18
  39.0 0.4 fusion.17
  39.4 0.4 fusion.16
  39.8 0.4 fusion.15
  40.3 0.4 broadcast_select_fusion.1
  40.9 3.4 %collective-permute-done.4 = f32[16,96,256]{2,1,0:T(8,128)} collective-permute-done((f32[16,96,256]{2,1,0:T(8,128)S(1)}, f32[16,96,256]{2,1,0:T(8,128)}, u32[]{:S(2)}, u32[]{:S(2)}) %collective-permute-start.4) | collective-permute-done | bytes 1572896 | tf_op jit(solution)/shard_map/ppermute | solution.py:74
  44.4 1.6 %bitcast_add_fusion = f32[16,96,256]{2,1,0:T(8,128)S(1)} fusion(f32[16,96,256]{2,1,0:T(8,128)} %collective-permute-done.4, f32[4,1,4,96,256]{4,3,2,1,0:T(8,128)S(1)} %get-tuple-element.3), kind=kLoop, calls=%fused_computation.12 | loop fusion | flops 393216 | bytes 4718592 | tf_op jit(solution)/shard_map/add | solution.py:75
  46.1 1.6 %collective-permute-start.7 = (bf16[8,48,256]{2,1,0:T(8,128)(2,1)S(1)}, bf16[8,48,256]{2,1,0:T(8,128)(2,1)S(1)}, u32[]{:S(2)}, u32[]{:S(2)}) collective-permute-start(bf16[8,48,256]{2,1,0:T(8,128)(2,1)S(1)} %fusion.52), channel_id=1, source_target_pairs={{0,16},{4,20},{8,24},{12,28},{16,0},{20,4},{24,8},{28,12},{1,17},{... | collective-permute-start | bytes 589832 | tf_op jit(solution)/shard_map/ppermute | solution.py:74
  47.7 1.6 %collective-permute-start.5 = (bf16[8,48,256]{2,1,0:T(8,128)(2,1)S(1)}, bf16[8,48,256]{2,1,0:T(8,128)(2,1)S(1)}, u32[]{:S(2)}, u32[]{:S(2)}) collective-permute-start(bf16[8,48,256]{2,1,0:T(8,128)(2,1)S(1)} %bitcast.355), channel_id=1, source_target_pairs={{0,8},{4,12},{8,0},{12,4},{16,24},{20,28},{24,16},{28,20},{1,9},{5... | collective-permute-start | bytes 589832 | tf_op jit(solution)/shard_map/ppermute | solution.py:74
  49.3 3.8 %collective-permute-done.7 = bf16[8,48,256]{2,1,0:T(8,128)(2,1)S(1)} collective-permute-done((bf16[8,48,256]{2,1,0:T(8,128)(2,1)S(1)}, bf16[8,48,256]{2,1,0:T(8,128)(2,1)S(1)}, u32[]{:S(2)}, u32[]{:S(2)}) %collective-permute-start.7) | collective-permute-done | bytes 196640 | tf_op jit(solution)/shard_map/ppermute | solution.py:74
  53.2 1.5 %collective-permute-start.8 = (bf16[4,48,256]{2,1,0:T(8,128)(2,1)S(1)}, bf16[4,48,256]{2,1,0:T(8,128)(2,1)S(1)}, u32[]{:S(2)}, u32[]{:S(2)}) collective-permute-start(bf16[4,48,256]{2,1,0:T(8,128)(2,1)S(1)} %fusion.95), channel_id=1, source_target_pairs={{0,8},{4,12},{8,0},{12,4},{16,24},{20,28},{24,16},{28,20},{1,9},{5... | collective-permute-start | bytes 294920 | tf_op jit(solution)/shard_map/ppermute | solution.py:74
  54.8 1.6 %collective-permute-start.6 = (bf16[4,48,256]{2,1,0:T(8,128)(2,1)S(1)}, bf16[4,48,256]{2,1,0:T(8,128)(2,1)S(1)}, u32[]{:S(2)}, u32[]{:S(2)}) collective-permute-start(bf16[4,48,256]{2,1,0:T(8,128)(2,1)S(1)} %fusion.94), channel_id=1, source_target_pairs={{0,16},{4,20},{8,24},{12,28},{16,0},{20,4},{24,8},{28,12},{1,17},{... | collective-permute-start | bytes 294920 | tf_op jit(solution)/shard_map/ppermute | solution.py:74
  56.4 1.5 %collective-permute-done.8 = bf16[4,48,256]{2,1,0:T(8,128)(2,1)S(1)} collective-permute-done((bf16[4,48,256]{2,1,0:T(8,128)(2,1)S(1)}, bf16[4,48,256]{2,1,0:T(8,128)(2,1)S(1)}, u32[]{:S(2)}, u32[]{:S(2)}) %collective-permute-start.8) | collective-permute-done | bytes 98336 | tf_op jit(solution)/shard_map/ppermute | solution.py:74
  57.9 1.6 %collective-permute-done.6 = bf16[4,48,256]{2,1,0:T(8,128)(2,1)S(1)} collective-permute-done((bf16[4,48,256]{2,1,0:T(8,128)(2,1)S(1)}, bf16[4,48,256]{2,1,0:T(8,128)(2,1)S(1)}, u32[]{:S(2)}, u32[]{:S(2)}) %collective-permute-start.6) | collective-permute-done | bytes 98336 | tf_op jit(solution)/shard_map/ppermute | solution.py:74
  59.6 2.0 %collective-permute-start.9 = (f32[96,256]{1,0:T(8,128)S(1)}, f32[96,256]{1,0:T(8,128)S(1)}, u32[]{:S(2)}, u32[]{:S(2)}) collective-permute-start(f32[96,256]{1,0:T(8,128)S(1)} %get-tuple-element.9), channel_id=1, source_target_pairs={{0,1},{1,2},{2,3},{3,0},{4,5},{5,6},{6,7},{7,4},{8,9},{9,10},{10,1... | collective-permute-start | bytes 294920 | tf_op jit(solution)/shard_map/ppermute | solution.py:109
  61.6 2.6 %collective-permute-start.10 = (f32[96,256]{1,0:T(8,128)S(1)}, f32[96,256]{1,0:T(8,128)S(1)}, u32[]{:S(2)}, u32[]{:S(2)}) collective-permute-start(f32[96,256]{1,0:T(8,128)S(1)} %get-tuple-element.11), channel_id=1, source_target_pairs={{0,2},{1,3},{2,0},{3,1},{4,6},{5,7},{6,4},{7,5},{8,10},{9,11},{10,... | collective-permute-start | bytes 294920 | tf_op jit(solution)/shard_map/ppermute | solution.py:109
  64.3 1.4 %collective-permute-start.11 = (f32[96,256]{1,0:T(8,128)S(1)}, f32[96,256]{1,0:T(8,128)S(1)}, u32[]{:S(2)}, u32[]{:S(2)}) collective-permute-start(f32[96,256]{1,0:T(8,128)S(1)} %get-tuple-element.12), channel_id=1, source_target_pairs={{0,3},{1,0},{2,1},{3,2},{4,7},{5,4},{6,5},{7,6},{8,11},{9,8},{10,9... | collective-permute-start | bytes 294920 | tf_op jit(solution)/shard_map/ppermute | solution.py:109
  65.7 1.6 %collective-permute-done.9 = f32[96,256]{1,0:T(8,128)S(1)} collective-permute-done((f32[96,256]{1,0:T(8,128)S(1)}, f32[96,256]{1,0:T(8,128)S(1)}, u32[]{:S(2)}, u32[]{:S(2)}) %collective-permute-start.9) | collective-permute-done | bytes 98336 | tf_op jit(solution)/shard_map/ppermute | solution.py:109
  67.3 2.6 %collective-permute-done.10 = f32[96,256]{1,0:T(8,128)S(1)} collective-permute-done((f32[96,256]{1,0:T(8,128)S(1)}, f32[96,256]{1,0:T(8,128)S(1)}, u32[]{:S(2)}, u32[]{:S(2)}) %collective-permute-start.10) | collective-permute-done | bytes 98336 | tf_op jit(solution)/shard_map/ppermute | solution.py:109
  70.1 0.7 add_add_fusion
  70.8 0.6 add_add_fusion.1
  (81 shorter events, 7.4 us)
Async XLA Ops:
  0.6 18.7 %copy-start = (bf16[256,256]{1,0:T(8,128)(2,1)S(1)}, bf16[256,256]{1,0:T(8,128)(2,1)}, u32[]{:S(2)}) copy-start(bf16[256,256]{1,0:T(8,128)(2,1)} %param.12) | copy-start | bytes 393220
  0.6 9.7 %collective-permute-start.1 = (bf16[1,33,1,8,256]{4,3,2,1,0:T(8,128)(2,1)}, bf16[1,33,1,8,256]{4,3,2,1,0:T(8,128)(2,1)S(1)}, u32[]{:S(2)}, u32[]{:S(2)}) collective-permute-start(bf16[1,33,1,8,256]{4,3,2,1,0:T(8,128)(2,1)} %param.8), channel_id=1, source_target_pairs={{1,0},{2,1},{3,2},{5,4},{6,5},{7,6},{9,8},{10,9},{11,10},{13,12},{... | collective-permute-start | bytes 405512 | tf_op jit(solution)/shard_map/ppermute | solution.py:20
  2.1 8.7 %collective-permute-start = (bf16[1,33,1,8,256]{4,3,2,1,0:T(8,128)(2,1)}, bf16[1,33,1,8,256]{4,3,2,1,0:T(8,128)(2,1)S(1)}, u32[]{:S(2)}, u32[]{:S(2)}) collective-permute-start(bf16[1,33,1,8,256]{4,3,2,1,0:T(8,128)(2,1)} %param.8), channel_id=1, source_target_pairs={{0,1},{1,2},{2,3},{4,5},{5,6},{6,7},{8,9},{9,10},{10,11},{12,13},{... | collective-permute-start | bytes 405512 | tf_op jit(solution)/shard_map/ppermute | solution.py:19
  11.1 1.7 %copy-start.2 = (bf16[1,33,1,16,256]{4,3,2,1,0:T(8,128)(2,1)}, bf16[1,33,1,16,256]{4,3,2,1,0:T(8,128)(2,1)S(1)}, u32[]{:S(2)}) copy-start(bf16[1,33,1,16,256]{4,3,2,1,0:T(8,128)(2,1)S(1)} %slice.160) | copy-start | bytes 811012
  11.1 1.3 %copy-start.7 = (bf16[3,3,256,256]{3,2,1,0:T(8,128)(2,1)S(1)}, bf16[3,3,256,256]{3,2,1,0:T(8,128)(2,1)}, u32[]{:S(2)}) copy-start(bf16[3,3,256,256]{3,2,1,0:T(8,128)(2,1)} %param.10) | copy-start | bytes 3538948
  15.0 1.4 %copy-start.5 = (bf16[3,256,256]{2,1,0:T(8,128)(2,1)S(1)}, bf16[3,256,256]{2,1,0:T(8,128)(2,1)}, u32[]{:S(2)}) copy-start(bf16[3,256,256]{2,1,0:T(8,128)(2,1)} %param.11) | copy-start | bytes 1179652
  16.7 1.1 %copy-start.4 = (f32[33,16,256]{2,1,0:T(8,128)S(1)}, f32[33,16,256]{2,1,0:T(8,128)}, u32[]{:S(2)}) copy-start(f32[33,16,256]{2,1,0:T(8,128)} %convert_element_type.97) | copy-start | bytes 1622020
  17.8 1.1 %copy-start.10 = (s32[1,8]{1,0:T(1,128)S(1)}, s32[1,8]{1,0:T(1,128)}, u32[]{:S(2)}) copy-start(s32[1,8]{1,0:T(1,128)} %param.14) | copy-start | bytes 100
  18.1 0.8 %copy-start.1 = (bf16[33,2,16,256]{3,2,1,0:T(8,128)(2,1)}, bf16[33,2,16,256]{3,2,1,0:T(8,128)(2,1)S(1)}, u32[]{:S(2)}) copy-start(bf16[33,2,16,256]{3,2,1,0:T(8,128)(2,1)S(1)} %fusion.14) | copy-start | bytes 1622020
  18.1 4.5 %copy-start.9 = (f32[256]{0:T(256)S(1)}, f32[256]{0:T(256)}, u32[]{:S(2)}) copy-start(f32[256]{0:T(256)} %param.13) | copy-start | bytes 3076
  20.2 4.0 %collective-permute-start.2 = (f32[1,8,256]{2,1,0:T(8,128)S(1)}, f32[1,8,256]{2,1,0:T(8,128)S(1)}, u32[]{:S(2)}, u32[]{:S(2)}) collective-permute-start(f32[1,8,256]{2,1,0:T(8,128)S(1)} %bitcast.363), channel_id=1, source_target_pairs={{0,1},{1,0},{2,3},{3,2},{4,5},{5,4},{6,7},{7,6},{8,9},{9,8},{10,11... | collective-permute-start | bytes 24584 | tf_op jit(solution)/shard_map/ppermute | solution.py:57
  24.3 4.8 %collective-permute-start.3 = (f32[1,8,256]{2,1,0:T(8,128)S(1)}, f32[1,8,256]{2,1,0:T(8,128)S(1)}, u32[]{:S(2)}, u32[]{:S(2)}) collective-permute-start(f32[1,8,256]{2,1,0:T(8,128)S(1)} %bitcast_add_fusion.5), channel_id=1, source_target_pairs={{0,2},{1,3},{2,0},{3,1},{4,6},{5,7},{6,4},{7,5},{8,10},{9,11},{10,... | collective-permute-start | bytes 24584 | tf_op jit(solution)/shard_map/ppermute | solution.py:57
  27.5 3.2 %copy-start.8 = (bf16[1,33,2,16,256]{4,3,2,1,0:T(8,128)(2,1)S(1)}, bf16[1,33,2,16,256]{4,3,2,1,0:T(8,128)(2,1)}, u32[]{:S(2)}) copy-start(bf16[1,33,2,16,256]{4,3,2,1,0:T(8,128)(2,1)} %param.15) | copy-start | bytes 1622020
  32.5 1.0 %copy-start.6 = (bf16[3,256,256]{2,1,0:T(8,128)(2,1)S(1)}, bf16[3,256,256]{2,1,0:T(8,128)(2,1)}, u32[]{:S(2)}) copy-start(bf16[3,256,256]{2,1,0:T(8,128)(2,1)} %param.11) | copy-start | bytes 1179652
  34.3 1.2 %copy-start.11 = (f32[33,2,16,256]{3,2,1,0:T(8,128)S(1)}, f32[33,2,16,256]{3,2,1,0:T(8,128)}, u32[]{:S(2)}) copy-start(f32[33,2,16,256]{3,2,1,0:T(8,128)} %get-tuple-element.16) | copy-start | bytes 3244036
  36.1 1.0 %copy-start.3 = (bf16[1,33,1,16,256]{4,3,2,1,0:T(8,128)(2,1)S(1)}, bf16[1,33,1,16,256]{4,3,2,1,0:T(8,128)(2,1)}, u32[]{:S(2)}) copy-start(bf16[1,33,1,16,256]{4,3,2,1,0:T(8,128)(2,1)} %copy-done.2) | copy-start | bytes 811012
  40.7 3.6 %collective-permute-start.4 = (f32[16,96,256]{2,1,0:T(8,128)S(1)}, f32[16,96,256]{2,1,0:T(8,128)}, u32[]{:S(2)}, u32[]{:S(2)}) collective-permute-start(f32[16,96,256]{2,1,0:T(8,128)S(1)} %bitcast.350), channel_id=1, source_target_pairs={{0,4},{4,0},{8,12},{12,8},{16,20},{20,16},{24,28},{28,24},{1,5},{5... | collective-permute-start | bytes 4718600 | tf_op jit(solution)/shard_map/ppermute | solution.py:74
  46.1 7.0 %collective-permute-start.7 = (bf16[8,48,256]{2,1,0:T(8,128)(2,1)S(1)}, bf16[8,48,256]{2,1,0:T(8,128)(2,1)S(1)}, u32[]{:S(2)}, u32[]{:S(2)}) collective-permute-start(bf16[8,48,256]{2,1,0:T(8,128)(2,1)S(1)} %fusion.52), channel_id=1, source_target_pairs={{0,16},{4,20},{8,24},{12,28},{16,0},{20,4},{24,8},{28,12},{1,17},{... | collective-permute-start | bytes 589832 | tf_op jit(solution)/shard_map/ppermute | solution.py:74
  47.7 7.1 %collective-permute-start.5 = (bf16[8,48,256]{2,1,0:T(8,128)(2,1)S(1)}, bf16[8,48,256]{2,1,0:T(8,128)(2,1)S(1)}, u32[]{:S(2)}, u32[]{:S(2)}) collective-permute-start(bf16[8,48,256]{2,1,0:T(8,128)(2,1)S(1)} %bitcast.355), channel_id=1, source_target_pairs={{0,8},{4,12},{8,0},{12,4},{16,24},{20,28},{24,16},{28,20},{1,9},{5... | collective-permute-start | bytes 589832 | tf_op jit(solution)/shard_map/ppermute | solution.py:74
  53.2 4.7 %collective-permute-start.8 = (bf16[4,48,256]{2,1,0:T(8,128)(2,1)S(1)}, bf16[4,48,256]{2,1,0:T(8,128)(2,1)S(1)}, u32[]{:S(2)}, u32[]{:S(2)}) collective-permute-start(bf16[4,48,256]{2,1,0:T(8,128)(2,1)S(1)} %fusion.95), channel_id=1, source_target_pairs={{0,8},{4,12},{8,0},{12,4},{16,24},{20,28},{24,16},{28,20},{1,9},{5... | collective-permute-start | bytes 294920 | tf_op jit(solution)/shard_map/ppermute | solution.py:74
  54.8 4.7 %collective-permute-start.6 = (bf16[4,48,256]{2,1,0:T(8,128)(2,1)S(1)}, bf16[4,48,256]{2,1,0:T(8,128)(2,1)S(1)}, u32[]{:S(2)}, u32[]{:S(2)}) collective-permute-start(bf16[4,48,256]{2,1,0:T(8,128)(2,1)S(1)} %fusion.94), channel_id=1, source_target_pairs={{0,16},{4,20},{8,24},{12,28},{16,0},{20,4},{24,8},{28,12},{1,17},{... | collective-permute-start | bytes 294920 | tf_op jit(solution)/shard_map/ppermute | solution.py:74
  59.6 7.6 %collective-permute-start.9 = (f32[96,256]{1,0:T(8,128)S(1)}, f32[96,256]{1,0:T(8,128)S(1)}, u32[]{:S(2)}, u32[]{:S(2)}) collective-permute-start(f32[96,256]{1,0:T(8,128)S(1)} %get-tuple-element.9), channel_id=1, source_target_pairs={{0,1},{1,2},{2,3},{3,0},{4,5},{5,6},{6,7},{7,4},{8,9},{9,10},{10,1... | collective-permute-start | bytes 294920 | tf_op jit(solution)/shard_map/ppermute | solution.py:109
  61.6 8.2 %collective-permute-start.10 = (f32[96,256]{1,0:T(8,128)S(1)}, f32[96,256]{1,0:T(8,128)S(1)}, u32[]{:S(2)}, u32[]{:S(2)}) collective-permute-start(f32[96,256]{1,0:T(8,128)S(1)} %get-tuple-element.11), channel_id=1, source_target_pairs={{0,2},{1,3},{2,0},{3,1},{4,6},{5,7},{6,4},{7,5},{8,10},{9,11},{10,... | collective-permute-start | bytes 294920 | tf_op jit(solution)/shard_map/ppermute | solution.py:109
  64.3 5.7 %collective-permute-start.11 = (f32[96,256]{1,0:T(8,128)S(1)}, f32[96,256]{1,0:T(8,128)S(1)}, u32[]{:S(2)}, u32[]{:S(2)}) collective-permute-start(f32[96,256]{1,0:T(8,128)S(1)} %get-tuple-element.12), channel_id=1, source_target_pairs={{0,3},{1,0},{2,1},{3,2},{4,7},{5,4},{6,5},{7,6},{8,11},{9,8},{10,9... | collective-permute-start | bytes 294920 | tf_op jit(solution)/shard_map/ppermute | solution.py:109

commit v6 on v5

--- a/solution.py
+++ b/solution.py
@@ -128,23 +128,41 @@
     clip_count = latents.shape[0] * lax.axis_size("dp")
     frame_count = latents.shape[1]
     upsampled = upsample(latents)
-    above, below = exchange_rows(latents, "space", 2)
-    extended = jnp.concatenate(
-        [upsample(above)[:, :, 1:], upsampled, upsample(below)[:, :, :1]], axis=2
-    )
-    padded = jnp.pad(extended, ((0, 0), (0, 0), (0, 0), (1, 1), (0, 0)))
     height = upsampled.shape[2]
     width = upsampled.shape[3]
-    pre_act = jnp.zeros(upsampled.shape, jnp.float32)
+    own = jnp.pad(upsampled, ((0, 0), (0, 0), (1, 1), (1, 1), (0, 0)))
+    local = jnp.zeros(upsampled.shape, jnp.float32)
     for row_tap in range(3):
         for col_tap in range(3):
-            window = padded[:, :, row_tap : row_tap + height, col_tap : col_tap + width]
-            pre_act = pre_act + jnp.einsum(
+            window = own[:, :, row_tap : row_tap + height, col_tap : col_tap + width]
+            local = local + jnp.einsum(
                 "nfhwc,cd->nfhwd",
                 window,
                 spatial_weight[row_tap, col_tap],
                 preferred_element_type=jnp.float32,
             )
+    local, ready = lax.optimization_barrier((local, latents))
+    above, below = exchange_rows(ready, "space", 2)
+    above_row = jnp.pad(upsample(above)[:, :, 1:], ((0, 0), (0, 0), (0, 0), (1, 1), (0, 0)))
+    below_row = jnp.pad(upsample(below)[:, :, :1], ((0, 0), (0, 0), (0, 0), (1, 1), (0, 0)))
+    top = jnp.zeros(above_row.shape[:3] + (width, local.shape[-1]), jnp.float32)
+    bottom = jnp.zeros(top.shape, jnp.float32)
+    for col_tap in range(3):
+        top = top + jnp.einsum(
+            "nfhwc,cd->nfhwd",
+            above_row[:, :, :, col_tap : col_tap + width],
+            spatial_weight[0, col_tap],
+            preferred_element_type=jnp.float32,
+        )
+        bottom = bottom + jnp.einsum(
+            "nfhwc,cd->nfhwd",
+            below_row[:, :, :, col_tap : col_tap + width],
+            spatial_weight[2, col_tap],
+            preferred_element_type=jnp.float32,
+        )
+    edge = ((0, 0), (0, 0), (0, height - 1), (0, 0), (0, 0))
+    pre_act = local + jnp.pad(top, edge) + jnp.pad(bottom, edge[:2] + ((height - 1, 0),) + edge[3:])
+    padded = jnp.concatenate([above_row, own[:, :, 1:-1], below_row], axis=2)
     activated = jax.nn.silu(pre_act).astype(jnp.bfloat16)
     mixing = jnp.zeros(upsampled.shape, jnp.float32)
     for offset in range(3):

time: 71.8 us -> 79.7 us (1.11)
  matrix products: 13.3 us -> 19.6 us
  local copies, waits for them, and re-layouts: 6.47 us -> 8.97 us
  other arithmetic: 6.83 us -> 5.38 us
  waiting for transfers between devices: 17.9 us -> 19 us
    dot_general x0 -> x6, matrix products: none -> 7.01 us  [the longest x3 3.56 us: on_device(): jnp.einsum('nfhwc,cd->nfhwd', above_row[:, :, :, col_tap:col_tap + width]...]
    ppermute x3, waiting for transfers between devices: 4.21 us -> 6.38 us  [halving_scatter(): lax.ppermute(send, 'space', [(i, (i + shift) % ns) for i in range(ns)])]
    ppermute x2, waiting for transfers between devices: 3.24 us -> 1.62 us  [space_sum(): lax.ppermute(values, 'space', [(i, i ^ step) for i in range(count)])]
    slice x0 -> x1, local copies, waits for them, and re-layouts: none -> 1.34 us  [on_device(): padded = jnp.concatenate([above_row, own[:, :, 1:-1], below_row], axis=2)]
    dot_general x9, matrix products: 3.88 us -> 2.76 us  [on_device(): jnp.einsum('nfhwc,cd->nfhwd', window, spatial_weight[row_tap, col_tap], p...]
    broadcast_in_dim x5 -> x7, local copies, waits for them, and re-layouts: 1.48 us -> 2.51 us  [upsample(): return jnp.repeat(doubled, 2, axis=-2)]
    convert_element_type x1, other arithmetic: 1.14 us -> 0.18 us  [on_device(): pullback(jnp.broadcast_to(factor[..., None, None, :], hidden.shape))[0]]
    concatenate x1 -> x0, other arithmetic: 0.9 us -> none  [on_device(): jnp.concatenate([upsample(above)[:, :, 1:], upsampled, upsample(below)[:,...]
where the time goes in v6:
time: 79.7 us; the launch traced here: 79.2 us
  starting transfers between devices  24.2 us (30%)
  matrix products  19.6 us (25%)
  waiting for transfers between devices  19 us (24%)
  local copies, waits for them, and re-layouts  8.97 us (11%)
  other arithmetic  5.38 us (7%)
  between operations  2.08 us (3%)
    ppermute x5, waiting for transfers between devices, _halve(): got = lax.ppermute(send, axis, [(i, i ^ 1 << bit) for i in range(size)])  10.3 us
    ppermute x3, waiting for transfers between devices, halving_scatter(): lax.ppermute(send, 'space', [(i, (i + shift) % ns) for i in range(ns)])  6.38 us
    ppermute x5, starting transfers between devices, _halve(): got = lax.ppermute(send, axis, [(i, i ^ 1 << bit) for i in range(size)])  6.37 us
    ppermute x1, starting transfers between devices, exchange_rows(): above = lax.ppermute(tail, axis, [(i, i + 1) for i in range(ends)])  5.77 us
    ppermute x2, starting transfers between devices, space_sum(): lax.ppermute(values, 'space', [(i, i ^ step) for i in range(count)])  5.68 us
    ppermute x3, starting transfers between devices, halving_scatter(): lax.ppermute(send, 'space', [(i, (i + shift) % ns) for i in range(ns)])  5.11 us
    unnamed x48, local copies, waits for them, and re-layouts  4.12 us
    dot_general x9, matrix products, on_device(): jnp.einsum('nfhwc,nfhwd->cd', window, pre_slope, preferred_element_type=j...  3.83 us
  transfers between devices with their start and end apart: 12, of which 9 were waited for; matrix products, arithmetic and copies ran while one was open for 4% of the time, Pallas kernels for 0%

profile of v6, /device:TPU:0, one launch (start us, length us, event | category | flops | bytes accessed | tf_op | source)
XLA Modules:
  0.0 79.2 jit_solution(9849198543824594873)
XLA Ops:
  0.7 1.2 %broadcast_in_dim.40 = bf16[33,8,2,256]{3,2,1,0:T(2,128)(2,1)S(1)} broadcast(bf16[33,8,256]{2,1,0:T(8,128)(2,1)} %bitcast.416), dimensions={0,1,3} | broadcast | bytes 405504 | tf_op jit(solution)/shard_map/broadcast_in_dim | solution.py:26
  4.9 0.6 copy-done.13
  5.4 1.3 %collective-permute-start.1 = (bf16[1,33,1,8,256]{4,3,2,1,0:T(8,128)(2,1)S(1)}, bf16[1,33,1,8,256]{4,3,2,1,0:T(8,128)(2,1)S(1)}, u32[]{:S(2)}, u32[]{:S(2)}) collective-permute-start(bf16[1,33,1,8,256]{4,3,2,1,0:T(8,128)(2,1)S(1)} %copy-done.13), channel_id=1, source_target_pairs={{1,0},{2,1},{3,2},{5,4},{6,5},{7,6},{9,8},{10,9},{11,10},{13,12},{... | collective-permute-start | bytes 405512 | tf_op jit(solution)/shard_map/ppermute | solution.py:20
  6.7 5.8 %collective-permute-start = (bf16[1,33,1,8,256]{4,3,2,1,0:T(8,128)(2,1)S(1)}, bf16[1,33,1,8,256]{4,3,2,1,0:T(8,128)(2,1)S(1)}, u32[]{:S(2)}, u32[]{:S(2)}) collective-permute-start(bf16[1,33,1,8,256]{4,3,2,1,0:T(8,128)(2,1)S(1)} %copy-done.13), channel_id=1, source_target_pairs={{0,1},{1,2},{2,3},{4,5},{5,6},{6,7},{8,9},{9,10},{10,11},{12,13},{... | collective-permute-start | bytes 405512 | tf_op jit(solution)/shard_map/ppermute | solution.py:19
  12.5 0.9 %convert_element_type.100 = f32[33,16,256]{2,1,0:T(8,128)} convert(bf16[33,16,256]{2,1,0:T(8,128)(2,1)S(1)} %broadcast_in_dim.41) | non-fusion elementwise | flops 135168 | bytes 811008 | tf_op jit(solution)/shard_map/convert_element_type | solution.py:178
  14.4 0.7 collective-permute-done
  15.4 0.8 %broadcast_in_dim.46 = bf16[33,16,256]{2,1,0:T(8,128)(2,1)} reshape(bf16[33,8,2,256]{3,2,1,0:T(2,128)(2,1)S(1)} %broadcast_in_dim.45) | data formatting | bytes 540672 | tf_op jit(solution)/shard_map/broadcast_in_dim | solution.py:26
  16.2 1.1 %fusion.76 = f32[33,16,256]{2,1,0:T(8,128)S(1)} fusion(bf16[3,3,256,256]{3,2,1,0:T(8,128)(2,1)} %param.10, bf16[1,33,1,16,256]{4,3,2,1,0:T(8,128)(2,1)S(1)} %slice.219), kind=kOutput, calls=%fused_computation.133 | convolution fusion | flops 69206016 | bytes 942080 | tf_op jit(solution)/shard_map/nfhwc,cd->nfhwd/dot_general | solution.py:157
  17.4 1.1 %convolution_add_fusion.13 = f32[33,16,256]{2,1,0:T(8,128)S(1)} fusion(f32[33,16,256]{2,1,0:T(8,128)S(1)} %fusion.76, bf16[33,16,256]{2,1,0:T(8,128)(2,1)S(1)} %broadcast_in_dim.48, bf16[3,3,256,256]{3,2,1,0:T(8,128)(2,1)} %param.10), kind=kOutput, calls=%fused_computation.48 | convolution fusion | flops 69341184 | bytes 1482752 | tf_op jit(solution)/shard_map/nfhwc,cd->nfhwd/dot_general | solution.py:157
  18.5 1.2 %fusion.12 = f32[1,33,1,16,256]{4,3,2,1,0:T(8,128)S(1)} fusion(f32[33,16,256]{2,1,0:T(8,128)S(1)} %convolution_add_fusion.13, bf16[3,3,256,256]{3,2,1,0:T(8,128)(2,1)} %param.10, bf16[1,33,1,16,256]{4,3,2,1,0:T(8,128)(2,1)S(1)} %slice.219), kind=kOutput, calls=%fused_computation.47 | convolution fusion | flops 69341184 | bytes 1482752 | tf_op jit(solution)/shard_map/nfhwc,cd->nfhwd/dot_general | solution.py:157
  19.7 1.3 %fusion.79 = f32[33,16,256]{2,1,0:T(8,128)S(1)} fusion(bf16[3,3,256,256]{3,2,1,0:T(8,128)(2,1)} %param.10, bf16[1,33,1,16,256]{4,3,2,1,0:T(8,128)(2,1)S(1)} %slice.216), kind=kOutput, calls=%fused_computation.136 | convolution fusion | flops 69206016 | bytes 942080 | tf_op jit(solution)/shard_map/nfhwc,cd->nfhwd/dot_general | solution.py:151
  21.0 1.1 %convolution_add_fusion.15 = f32[33,16,256]{2,1,0:T(8,128)S(1)} fusion(f32[33,16,256]{2,1,0:T(8,128)S(1)} %fusion.79, bf16[33,16,256]{2,1,0:T(8,128)(2,1)S(1)} %copy-done.9, bf16[3,3,256,256]{3,2,1,0:T(8,128)(2,1)} %param.10), kind=kOutput, calls=%fused_computation.51 | convolution fusion | flops 69341184 | bytes 1482752 | tf_op jit(solution)/shard_map/nfhwc,cd->nfhwd/dot_general | solution.py:151
  22.2 1.1 %fusion.13 = f32[1,33,1,16,256]{4,3,2,1,0:T(8,128)S(1)} fusion(f32[33,16,256]{2,1,0:T(8,128)S(1)} %convolution_add_fusion.15, bf16[3,3,256,256]{3,2,1,0:T(8,128)(2,1)} %param.10, bf16[1,33,1,16,256]{4,3,2,1,0:T(8,128)(2,1)S(1)} %slice.216), kind=kOutput, calls=%fused_computation.50 | convolution fusion | flops 69341184 | bytes 1482752 | tf_op jit(solution)/shard_map/nfhwc,cd->nfhwd/dot_general | solution.py:151
  23.3 0.4 multiply_convert_fusion
  25.1 0.7 copy-done.3
  26.5 0.4 fusion.23
  27.0 0.9 %fusion.93 = (f32[8,256]{1,0:T(8,128)S(1)}, f32[8,2,16,256]{3,2,1,0:T(8,128)}) fusion(bf16[256,256]{1,0:T(8,128)(2,1)S(1)} %copy-done, bf16[8,2,16,256]{3,0,2,1:T(8,128)(2,1)S(1)} %fusion.23), kind=kOutput, calls=%fused_computation.152 | convolution fusion | flops 34142208 | bytes 532480 | tf_op jit(solution)/shard_map/nqhwc,ce->nqhwe/dot_general | solution.py:185
  27.9 2.5 %collective-permute-start.2 = (f32[1,8,256]{2,1,0:T(8,128)S(1)}, f32[1,8,256]{2,1,0:T(8,128)S(1)}, u32[]{:S(2)}, u32[]{:S(2)}) collective-permute-start(f32[1,8,256]{2,1,0:T(8,128)S(1)} %bitcast.423), channel_id=1, source_target_pairs={{0,1},{1,0},{2,3},{3,2},{4,5},{5,4},{6,7},{7,6},{8,9},{9,8},{10,11... | collective-permute-start | bytes 24584 | tf_op jit(solution)/shard_map/ppermute | solution.py:57
  30.4 1.3 %pad_slice_fusion = bf16[1,33,2,18,256]{4,3,2,1,0:T(8,128)(2,1)} fusion(bf16[1,33,2,16,256]{4,3,2,1,0:T(8,128)(2,1)S(1)} %broadcast_in_dim.43), kind=kLoop, calls=%fused_computation | loop fusion | bytes 1148928 | tf_op jit(solution)/shard_map/slice | solution.py:165
  32.0 3.2 %collective-permute-start.3 = (f32[1,8,256]{2,1,0:T(8,128)S(1)}, f32[1,8,256]{2,1,0:T(8,128)S(1)}, u32[]{:S(2)}, u32[]{:S(2)}) collective-permute-start(f32[1,8,256]{2,1,0:T(8,128)S(1)} %bitcast_add_fusion.5), channel_id=1, source_target_pairs={{0,2},{1,3},{2,0},{3,1},{4,6},{5,7},{6,4},{7,5},{8,10},{9,11},{10,... | collective-permute-start | bytes 24584 | tf_op jit(solution)/shard_map/ppermute | solution.py:57
  35.5 1.3 %collective-permute-done.3 = f32[1,8,256]{2,1,0:T(8,128)S(1)} collective-permute-done((f32[1,8,256]{2,1,0:T(8,128)S(1)}, f32[1,8,256]{2,1,0:T(8,128)S(1)}, u32[]{:S(2)}, u32[]{:S(2)}) %collective-permute-start.3) | collective-permute-done | bytes 8224 | tf_op jit(solution)/shard_map/ppermute | solution.py:57
  37.5 1.0 %fusion.8 = bf16[1,33,2,16,256]{4,1,3,2,0:T(8,128)(2,1)S(1)} fusion(f32[8,2,16,256]{3,0,2,1:T(8,128)S(1)} %fusion.101, bf16[1,33,2,16,256]{4,3,2,1,0:T(8,128)(2,1)S(1)} %copy-done.11, f32[33]{0:T(128)S(1)} %compare_select_fusion, s32[8]{0:T(128)S(1)} %bitcast.425), kind=kOutput, calls=%fused_computation.38 | convolution fusion | flops 27033864 | bytes 1343652 | tf_op jit(solution)/shard_map/nqf,nqhwc->nfhwc/dot_general | solution.py:201
  40.0 0.4 slice_bitcast_fusion
  40.8 0.7 copy-done.5
  41.6 0.6 fusion.11
  42.3 0.5 copy-done.10
  42.8 0.4 fusion.22
  43.2 0.5 fusion.21
  43.7 0.4 fusion.20
  45.3 0.4 fusion.16
  45.7 0.5 fusion.15
  46.3 0.4 fusion.14
  46.7 0.4 broadcast_select_fusion.1
  47.4 3.4 %collective-permute-done.4 = f32[16,96,256]{2,1,0:T(8,128)} collective-permute-done((f32[16,96,256]{2,1,0:T(8,128)S(1)}, f32[16,96,256]{2,1,0:T(8,128)}, u32[]{:S(2)}, u32[]{:S(2)}) %collective-permute-start.4) | collective-permute-done | bytes 1572896 | tf_op jit(solution)/shard_map/ppermute | solution.py:74
  50.8 1.6 %bitcast_add_fusion = f32[16,96,256]{2,1,0:T(8,128)S(1)} fusion(f32[16,96,256]{2,1,0:T(8,128)} %collective-permute-done.4, f32[4,1,4,96,256]{4,3,2,1,0:T(8,128)S(1)} %get-tuple-element.7), kind=kLoop, calls=%fused_computation.13 | loop fusion | flops 393216 | bytes 4718592 | tf_op jit(solution)/shard_map/add | solution.py:75
  52.5 1.6 %collective-permute-start.5 = (bf16[8,48,256]{2,1,0:T(8,128)(2,1)S(1)}, bf16[8,48,256]{2,1,0:T(8,128)(2,1)S(1)}, u32[]{:S(2)}, u32[]{:S(2)}) collective-permute-start(bf16[8,48,256]{2,1,0:T(8,128)(2,1)S(1)} %bitcast.415), channel_id=1, source_target_pairs={{0,8},{4,12},{8,0},{12,4},{16,24},{20,28},{24,16},{28,20},{1,9},{5... | collective-permute-start | bytes 589832 | tf_op jit(solution)/shard_map/ppermute | solution.py:74
  54.1 1.6 %collective-permute-start.7 = (bf16[8,48,256]{2,1,0:T(8,128)(2,1)S(1)}, bf16[8,48,256]{2,1,0:T(8,128)(2,1)S(1)}, u32[]{:S(2)}, u32[]{:S(2)}) collective-permute-start(bf16[8,48,256]{2,1,0:T(8,128)(2,1)S(1)} %fusion.94), channel_id=1, source_target_pairs={{0,16},{4,20},{8,24},{12,28},{16,0},{20,4},{24,8},{28,12},{1,17},{... | collective-permute-start | bytes 589832 | tf_op jit(solution)/shard_map/ppermute | solution.py:74
  55.8 3.8 %collective-permute-done.5 = bf16[8,48,256]{2,1,0:T(8,128)(2,1)S(1)} collective-permute-done((bf16[8,48,256]{2,1,0:T(8,128)(2,1)S(1)}, bf16[8,48,256]{2,1,0:T(8,128)(2,1)S(1)}, u32[]{:S(2)}, u32[]{:S(2)}) %collective-permute-start.5) | collective-permute-done | bytes 196640 | tf_op jit(solution)/shard_map/ppermute | solution.py:74
  59.6 1.6 %collective-permute-start.6 = (bf16[4,48,256]{2,1,0:T(8,128)(2,1)S(1)}, bf16[4,48,256]{2,1,0:T(8,128)(2,1)S(1)}, u32[]{:S(2)}, u32[]{:S(2)}) collective-permute-start(bf16[4,48,256]{2,1,0:T(8,128)(2,1)S(1)} %fusion.147), channel_id=1, source_target_pairs={{0,16},{4,20},{8,24},{12,28},{16,0},{20,4},{24,8},{28,12},{1,17},{... | collective-permute-start | bytes 294920 | tf_op jit(solution)/shard_map/ppermute | solution.py:74
  61.3 1.6 %collective-permute-start.8 = (bf16[4,48,256]{2,1,0:T(8,128)(2,1)S(1)}, bf16[4,48,256]{2,1,0:T(8,128)(2,1)S(1)}, u32[]{:S(2)}, u32[]{:S(2)}) collective-permute-start(bf16[4,48,256]{2,1,0:T(8,128)(2,1)S(1)} %fusion.148), channel_id=1, source_target_pairs={{0,8},{4,12},{8,0},{12,4},{16,24},{20,28},{24,16},{28,20},{1,9},{5... | collective-permute-start | bytes 294920 | tf_op jit(solution)/shard_map/ppermute | solution.py:74
  62.9 1.4 %collective-permute-done.6 = bf16[4,48,256]{2,1,0:T(8,128)(2,1)S(1)} collective-permute-done((bf16[4,48,256]{2,1,0:T(8,128)(2,1)S(1)}, bf16[4,48,256]{2,1,0:T(8,128)(2,1)S(1)}, u32[]{:S(2)}, u32[]{:S(2)}) %collective-permute-start.6) | collective-permute-done | bytes 98336 | tf_op jit(solution)/shard_map/ppermute | solution.py:74
  64.3 1.7 %collective-permute-done.8 = bf16[4,48,256]{2,1,0:T(8,128)(2,1)S(1)} collective-permute-done((bf16[4,48,256]{2,1,0:T(8,128)(2,1)S(1)}, bf16[4,48,256]{2,1,0:T(8,128)(2,1)S(1)}, u32[]{:S(2)}, u32[]{:S(2)}) %collective-permute-start.8) | collective-permute-done | bytes 98336 | tf_op jit(solution)/shard_map/ppermute | solution.py:74
  66.1 4.0 %collective-permute-start.11 = (f32[96,256]{1,0:T(8,128)S(1)}, f32[96,256]{1,0:T(8,128)S(1)}, u32[]{:S(2)}, u32[]{:S(2)}) collective-permute-start(f32[96,256]{1,0:T(8,128)S(1)} %get-tuple-element.16), channel_id=1, source_target_pairs={{0,3},{1,0},{2,1},{3,2},{4,7},{5,4},{6,5},{7,6},{8,11},{9,8},{10,9... | collective-permute-start | bytes 294920 | tf_op jit(solution)/shard_map/ppermute | solution.py:109
  70.2 1.1 %collective-permute-start.9 = (f32[96,256]{1,0:T(8,128)S(1)}, f32[96,256]{1,0:T(8,128)S(1)}, u32[]{:S(2)}, u32[]{:S(2)}) collective-permute-start(f32[96,256]{1,0:T(8,128)S(1)} %get-tuple-element.13), channel_id=1, source_target_pairs={{0,1},{1,2},{2,3},{3,0},{4,5},{5,6},{6,7},{7,4},{8,9},{9,10},{10,1... | collective-permute-start | bytes 294920 | tf_op jit(solution)/shard_map/ppermute | solution.py:109
  71.3 1.3 %collective-permute-done.11 = f32[96,256]{1,0:T(8,128)S(1)} collective-permute-done((f32[96,256]{1,0:T(8,128)S(1)}, f32[96,256]{1,0:T(8,128)S(1)}, u32[]{:S(2)}, u32[]{:S(2)}) %collective-permute-start.11) | collective-permute-done | bytes 98336 | tf_op jit(solution)/shard_map/ppermute | solution.py:109
  72.6 5.1 %collective-permute-done.10 = f32[96,256]{1,0:T(8,128)S(1)} collective-permute-done((f32[96,256]{1,0:T(8,128)S(1)}, f32[96,256]{1,0:T(8,128)S(1)}, u32[]{:S(2)}, u32[]{:S(2)}) %collective-permute-start.10) | collective-permute-done | bytes 98336 | tf_op jit(solution)/shard_map/ppermute | solution.py:109
  77.9 0.7 add_add_fusion
  78.6 0.6 add_add_fusion.1
  (100 shorter events, 10.9 us)
Async XLA Ops:
  0.6 26.3 %copy-start = (bf16[256,256]{1,0:T(8,128)(2,1)S(1)}, bf16[256,256]{1,0:T(8,128)(2,1)}, u32[]{:S(2)}) copy-start(bf16[256,256]{1,0:T(8,128)(2,1)} %param.12) | copy-start | bytes 393220
  0.6 1.4 %copy-start.1 = (bf16[3,3,256,256]{3,2,1,0:T(8,128)(2,1)S(1)}, bf16[3,3,256,256]{3,2,1,0:T(8,128)(2,1)}, u32[]{:S(2)}) copy-start(bf16[3,3,256,256]{3,2,1,0:T(8,128)(2,1)} %param.10) | copy-start | bytes 3538948
  4.5 0.9 %copy-start.13 = (bf16[1,33,1,8,256]{4,3,2,1,0:T(8,128)(2,1)S(1)}, bf16[1,33,1,8,256]{4,3,2,1,0:T(8,128)(2,1)}, u32[]{:S(2)}) copy-start(bf16[1,33,1,8,256]{4,3,2,1,0:T(8,128)(2,1)} %param.8) | copy-start | bytes 405508
  4.5 8.0 %copy-start.14 = (f32[256]{0:T(256)S(1)}, f32[256]{0:T(256)}, u32[]{:S(2)}) copy-start(f32[256]{0:T(256)} %param.13) | copy-start | bytes 3076
  5.4 8.6 %collective-permute-start.1 = (bf16[1,33,1,8,256]{4,3,2,1,0:T(8,128)(2,1)S(1)}, bf16[1,33,1,8,256]{4,3,2,1,0:T(8,128)(2,1)S(1)}, u32[]{:S(2)}, u32[]{:S(2)}) collective-permute-start(bf16[1,33,1,8,256]{4,3,2,1,0:T(8,128)(2,1)S(1)} %copy-done.13), channel_id=1, source_target_pairs={{1,0},{2,1},{3,2},{5,4},{6,5},{7,6},{9,8},{10,9},{11,10},{13,12},{... | collective-permute-start | bytes 405512 | tf_op jit(solution)/shard_map/ppermute | solution.py:20
  6.7 8.4 %collective-permute-start = (bf16[1,33,1,8,256]{4,3,2,1,0:T(8,128)(2,1)S(1)}, bf16[1,33,1,8,256]{4,3,2,1,0:T(8,128)(2,1)S(1)}, u32[]{:S(2)}, u32[]{:S(2)}) collective-permute-start(bf16[1,33,1,8,256]{4,3,2,1,0:T(8,128)(2,1)S(1)} %copy-done.13), channel_id=1, source_target_pairs={{0,1},{1,2},{2,3},{4,5},{5,6},{6,7},{8,9},{9,10},{10,11},{12,13},{... | collective-permute-start | bytes 405512 | tf_op jit(solution)/shard_map/ppermute | solution.py:19
  18.5 2.5 %copy-start.9 = (bf16[33,16,256]{2,1,0:T(8,128)(2,1)S(1)}, bf16[33,16,256]{2,1,0:T(8,128)(2,1)}, u32[]{:S(2)}) copy-start(bf16[33,16,256]{2,1,0:T(8,128)(2,1)} %broadcast_in_dim.46) | copy-start | bytes 811012
  19.7 3.6 %copy-start.4 = (f32[1,33,1,16,256]{4,3,2,1,0:T(8,128)}, f32[1,33,1,16,256]{4,3,2,1,0:T(8,128)S(1)}, u32[]{:S(2)}) copy-start(f32[1,33,1,16,256]{4,3,2,1,0:T(8,128)S(1)} %fusion.12) | copy-start | bytes 1622020
  23.3 0.8 %copy-start.6 = (f32[1,33,1,16,256]{4,3,2,1,0:T(8,128)}, f32[1,33,1,16,256]{4,3,2,1,0:T(8,128)S(1)}, u32[]{:S(2)}) copy-start(f32[1,33,1,16,256]{4,3,2,1,0:T(8,128)S(1)} %fusion.13) | copy-start | bytes 1622020
  23.3 1.2 %copy-start.8 = (bf16[3,256,256]{2,1,0:T(8,128)(2,1)S(1)}, bf16[3,256,256]{2,1,0:T(8,128)(2,1)}, u32[]{:S(2)}) copy-start(bf16[3,256,256]{2,1,0:T(8,128)(2,1)} %param.11) | copy-start | bytes 1179652
  24.8 1.1 %copy-start.3 = (f32[33,16,256]{2,1,0:T(8,128)S(1)}, f32[33,16,256]{2,1,0:T(8,128)}, u32[]{:S(2)}) copy-start(f32[33,16,256]{2,1,0:T(8,128)} %convert_element_type.100) | copy-start | bytes 1622020
  25.9 0.7 copy-start.15
  26.2 5.5 %copy-start.2 = (bf16[33,2,16,256]{3,2,1,0:T(8,128)(2,1)}, bf16[33,2,16,256]{3,2,1,0:T(8,128)(2,1)S(1)}, u32[]{:S(2)}) copy-start(bf16[33,2,16,256]{3,2,1,0:T(8,128)(2,1)S(1)} %fusion.10) | copy-start | bytes 1622020
  27.9 4.1 %collective-permute-start.2 = (f32[1,8,256]{2,1,0:T(8,128)S(1)}, f32[1,8,256]{2,1,0:T(8,128)S(1)}, u32[]{:S(2)}, u32[]{:S(2)}) collective-permute-start(f32[1,8,256]{2,1,0:T(8,128)S(1)} %bitcast.423), channel_id=1, source_target_pairs={{0,1},{1,0},{2,3},{3,2},{4,5},{5,4},{6,7},{7,6},{8,9},{9,8},{10,11... | collective-permute-start | bytes 24584 | tf_op jit(solution)/shard_map/ppermute | solution.py:57
  32.0 4.8 %collective-permute-start.3 = (f32[1,8,256]{2,1,0:T(8,128)S(1)}, f32[1,8,256]{2,1,0:T(8,128)S(1)}, u32[]{:S(2)}, u32[]{:S(2)}) collective-permute-start(f32[1,8,256]{2,1,0:T(8,128)S(1)} %bitcast_add_fusion.5), channel_id=1, source_target_pairs={{0,2},{1,3},{2,0},{3,1},{4,6},{5,7},{6,4},{7,5},{8,10},{9,11},{10,... | collective-permute-start | bytes 24584 | tf_op jit(solution)/shard_map/ppermute | solution.py:57
  35.2 1.8 %copy-start.12 = (f32[8,2,16,256]{3,2,1,0:T(8,128)S(1)}, f32[8,2,16,256]{3,2,1,0:T(8,128)}, u32[]{:S(2)}) copy-start(f32[8,2,16,256]{3,2,1,0:T(8,128)} %get-tuple-element.20) | copy-start | bytes 786436
  35.2 2.2 %copy-start.11 = (bf16[1,33,2,16,256]{4,3,2,1,0:T(8,128)(2,1)S(1)}, bf16[1,33,2,16,256]{4,3,2,1,0:T(8,128)(2,1)}, u32[]{:S(2)}) copy-start(bf16[1,33,2,16,256]{4,3,2,1,0:T(8,128)(2,1)} %param.15) | copy-start | bytes 1622020
  40.4 1.0 %copy-start.5 = (f32[1,33,1,16,256]{4,3,2,1,0:T(8,128)S(1)}, f32[1,33,1,16,256]{4,3,2,1,0:T(8,128)}, u32[]{:S(2)}) copy-start(f32[1,33,1,16,256]{4,3,2,1,0:T(8,128)} %copy-done.4) | copy-start | bytes 1622020
  40.4 1.2 %copy-start.7 = (f32[1,33,1,16,256]{4,3,2,1,0:T(8,128)S(1)}, f32[1,33,1,16,256]{4,3,2,1,0:T(8,128)}, u32[]{:S(2)}) copy-start(f32[1,33,1,16,256]{4,3,2,1,0:T(8,128)} %copy-done.6) | copy-start | bytes 1622020
  41.6 1.1 %copy-start.10 = (bf16[1,33,2,18,256]{4,3,2,1,0:T(8,128)(2,1)S(1)}, bf16[1,33,2,18,256]{4,3,2,1,0:T(8,128)(2,1)}, u32[]{:S(2)}) copy-start(bf16[1,33,2,18,256]{4,3,2,1,0:T(8,128)(2,1)} %pad_slice_fusion) | copy-start | bytes 1824772
  47.2 3.6 %collective-permute-start.4 = (f32[16,96,256]{2,1,0:T(8,128)S(1)}, f32[16,96,256]{2,1,0:T(8,128)}, u32[]{:S(2)}, u32[]{:S(2)}) collective-permute-start(f32[16,96,256]{2,1,0:T(8,128)S(1)} %bitcast.410), channel_id=1, source_target_pairs={{0,4},{4,0},{8,12},{12,8},{16,20},{20,16},{24,28},{28,24},{1,5},{5... | collective-permute-start | bytes 4718600 | tf_op jit(solution)/shard_map/ppermute | solution.py:74
  52.5 7.0 %collective-permute-start.5 = (bf16[8,48,256]{2,1,0:T(8,128)(2,1)S(1)}, bf16[8,48,256]{2,1,0:T(8,128)(2,1)S(1)}, u32[]{:S(2)}, u32[]{:S(2)}) collective-permute-start(bf16[8,48,256]{2,1,0:T(8,128)(2,1)S(1)} %bitcast.415), channel_id=1, source_target_pairs={{0,8},{4,12},{8,0},{12,4},{16,24},{20,28},{24,16},{28,20},{1,9},{5... | collective-permute-start | bytes 589832 | tf_op jit(solution)/shard_map/ppermute | solution.py:74
  54.1 7.1 %collective-permute-start.7 = (bf16[8,48,256]{2,1,0:T(8,128)(2,1)S(1)}, bf16[8,48,256]{2,1,0:T(8,128)(2,1)S(1)}, u32[]{:S(2)}, u32[]{:S(2)}) collective-permute-start(bf16[8,48,256]{2,1,0:T(8,128)(2,1)S(1)} %fusion.94), channel_id=1, source_target_pairs={{0,16},{4,20},{8,24},{12,28},{16,0},{20,4},{24,8},{28,12},{1,17},{... | collective-permute-start | bytes 589832 | tf_op jit(solution)/shard_map/ppermute | solution.py:74
  59.6 4.7 %collective-permute-start.6 = (bf16[4,48,256]{2,1,0:T(8,128)(2,1)S(1)}, bf16[4,48,256]{2,1,0:T(8,128)(2,1)S(1)}, u32[]{:S(2)}, u32[]{:S(2)}) collective-permute-start(bf16[4,48,256]{2,1,0:T(8,128)(2,1)S(1)} %fusion.147), channel_id=1, source_target_pairs={{0,16},{4,20},{8,24},{12,28},{16,0},{20,4},{24,8},{28,12},{1,17},{... | collective-permute-start | bytes 294920 | tf_op jit(solution)/shard_map/ppermute | solution.py:74
  61.3 4.7 %collective-permute-start.8 = (bf16[4,48,256]{2,1,0:T(8,128)(2,1)S(1)}, bf16[4,48,256]{2,1,0:T(8,128)(2,1)S(1)}, u32[]{:S(2)}, u32[]{:S(2)}) collective-permute-start(bf16[4,48,256]{2,1,0:T(8,128)(2,1)S(1)} %fusion.148), channel_id=1, source_target_pairs={{0,8},{4,12},{8,0},{12,4},{16,24},{20,28},{24,16},{28,20},{1,9},{5... | collective-permute-start | bytes 294920 | tf_op jit(solution)/shard_map/ppermute | solution.py:74
  66.1 6.5 %collective-permute-start.11 = (f32[96,256]{1,0:T(8,128)S(1)}, f32[96,256]{1,0:T(8,128)S(1)}, u32[]{:S(2)}, u32[]{:S(2)}) collective-permute-start(f32[96,256]{1,0:T(8,128)S(1)} %get-tuple-element.16), channel_id=1, source_target_pairs={{0,3},{1,0},{2,1},{3,2},{4,7},{5,4},{6,5},{7,6},{8,11},{9,8},{10,9... | collective-permute-start | bytes 294920 | tf_op jit(solution)/shard_map/ppermute | solution.py:109
  70.1 7.6 %collective-permute-start.10 = (f32[96,256]{1,0:T(8,128)S(1)}, f32[96,256]{1,0:T(8,128)S(1)}, u32[]{:S(2)}, u32[]{:S(2)}) collective-permute-start(f32[96,256]{1,0:T(8,128)S(1)} %get-tuple-element.15), channel_id=1, source_target_pairs={{0,2},{1,3},{2,0},{3,1},{4,6},{5,7},{6,4},{7,5},{8,10},{9,11},{10,... | collective-permute-start | bytes 294920 | tf_op jit(solution)/shard_map/ppermute | solution.py:109
  70.2 7.6 %collective-permute-start.9 = (f32[96,256]{1,0:T(8,128)S(1)}, f32[96,256]{1,0:T(8,128)S(1)}, u32[]{:S(2)}, u32[]{:S(2)}) collective-permute-start(f32[96,256]{1,0:T(8,128)S(1)} %get-tuple-element.13), channel_id=1, source_target_pairs={{0,1},{1,2},{2,3},{3,0},{4,5},{5,6},{6,7},{7,4},{8,9},{9,10},{10,1... | collective-permute-start | bytes 294920 | tf_op jit(solution)/shard_map/ppermute | solution.py:109

commit v7 on v5

--- a/solution.py
+++ b/solution.py
@@ -49,13 +49,19 @@
 
 def space_sum(values):
     count = lax.axis_size("space")
-    bits = _log2(count)
-    if bits is None:
+    if count > 4:
         return lax.psum(values, "space")
-    for bit in range(bits):
-        step = 1 << bit
-        values = values + lax.ppermute(values, "space", [(i, i ^ step) for i in range(count)])
-    return values
+    me = lax.axis_index("space")
+    terms = [values] + [
+        lax.ppermute(values, "space", [(i, (i + shift) % count) for i in range(count)])
+        for shift in range(1, count)
+    ]
+    stacked = jnp.stack(terms)
+    ordered = jnp.take(stacked, (me - jnp.arange(count)) % count, axis=0)
+    total = ordered[0]
+    for t in range(1, count):
+        total = total + ordered[t]
+    return total
 
 
 def _halve(cur, left, axis, bit, wire=None):

time: 71.8 us -> 72.4 us (level)
  starting transfers between devices: 24.9 us -> 22.5 us
  waiting for transfers between devices: 17.9 us -> 19.5 us
  other arithmetic: 6.83 us -> 7.61 us
    ppermute x3, starting transfers between devices: 5.96 us -> 4.14 us  [halving_scatter(): lax.ppermute(send, 'space', [(i, (i + shift) % ns) for i in range(ns)])]
    ppermute x2 -> x3, waiting for transfers between devices: 3.24 us -> 4.4 us  [space_sum(): lax.ppermute(values, 'space', [(i, (i + shift) % count) for i in range(co...]
    ppermute x2 -> x3, starting transfers between devices: 5.59 us -> 5.03 us  [space_sum(): lax.ppermute(values, 'space', [(i, (i + shift) % count) for i in range(co...]
  transfers between devices with their start and end apart: 12 -> 13, of which waited for: 9 -> 9; matrix products, arithmetic and copies ran while one was open for 4% -> 5% of each run, Pallas kernels for 0% -> 0%
where the time goes in v7:
time: 72.4 us; the launch traced here: 72 us
  starting transfers between devices  22.5 us (31%)
  waiting for transfers between devices  19.5 us (27%)
  matrix products  13.3 us (18%)
  other arithmetic  7.61 us (11%)
  local copies, waits for them, and re-layouts  7.03 us (10%)
  between operations  2.01 us (3%)
    ppermute x5, waiting for transfers between devices, _halve(): got = lax.ppermute(send, axis, [(i, i ^ 1 << bit) for i in range(size)])  10.3 us
    ppermute x5, starting transfers between devices, _halve(): got = lax.ppermute(send, axis, [(i, i ^ 1 << bit) for i in range(size)])  6.33 us
    ppermute x1, starting transfers between devices, exchange_rows(): above = lax.ppermute(tail, axis, [(i, i + 1) for i in range(ends)])  5.6 us
    ppermute x3, starting transfers between devices, space_sum(): lax.ppermute(values, 'space', [(i, (i + shift) % count) for i in range(co...  5.03 us
    ppermute x3, waiting for transfers between devices, halving_scatter(): lax.ppermute(send, 'space', [(i, (i + shift) % ns) for i in range(ns)])  4.77 us
    ppermute x3, waiting for transfers between devices, space_sum(): lax.ppermute(values, 'space', [(i, (i + shift) % count) for i in range(co...  4.4 us
    unnamed x40, local copies, waits for them, and re-layouts  4.27 us
    ppermute x3, starting transfers between devices, halving_scatter(): lax.ppermute(send, 'space', [(i, (i + shift) % ns) for i in range(ns)])  4.14 us
  transfers between devices with their start and end apart: 13, of which 9 were waited for; matrix products, arithmetic and copies ran while one was open for 5% of the time, Pallas kernels for 0%

profile of v7, /device:TPU:0, one launch (start us, length us, event | category | flops | bytes accessed | tf_op | source)
XLA Modules:
  0.0 72.0 jit_solution(6876690726910141176)
XLA Ops:
  0.6 1.4 %collective-permute-start.1 = (bf16[1,33,1,8,256]{4,3,2,1,0:T(8,128)(2,1)}, bf16[1,33,1,8,256]{4,3,2,1,0:T(8,128)(2,1)S(1)}, u32[]{:S(2)}, u32[]{:S(2)}) collective-permute-start(bf16[1,33,1,8,256]{4,3,2,1,0:T(8,128)(2,1)} %param.8), channel_id=1, source_target_pairs={{1,0},{2,1},{3,2},{5,4},{6,5},{7,6},{9,8},{10,9},{11,10},{13,12},{... | collective-permute-start | bytes 405512 | tf_op jit(solution)/shard_map/ppermute | solution.py:20
  2.1 5.6 %collective-permute-start = (bf16[1,33,1,8,256]{4,3,2,1,0:T(8,128)(2,1)}, bf16[1,33,1,8,256]{4,3,2,1,0:T(8,128)(2,1)S(1)}, u32[]{:S(2)}, u32[]{:S(2)}) collective-permute-start(bf16[1,33,1,8,256]{4,3,2,1,0:T(8,128)(2,1)} %param.8), channel_id=1, source_target_pairs={{0,1},{1,2},{2,3},{4,5},{5,6},{6,7},{8,9},{9,10},{10,11},{12,13},{... | collective-permute-start | bytes 405512 | tf_op jit(solution)/shard_map/ppermute | solution.py:19
  8.4 0.7 broadcast_multiply_fusion.2
  9.1 1.0 %broadcast_in_dim.46 = bf16[33,8,2,256]{3,2,1,0:T(2,128)(2,1)S(1)} broadcast(bf16[33,8,256]{2,1,0:T(8,128)(2,1)} %bitcast.371), dimensions={0,1,3} | broadcast | bytes 405504 | tf_op jit(solution)/shard_map/broadcast_in_dim | solution.py:26
  10.2 0.9 %convert_element_type.97 = f32[33,16,256]{2,1,0:T(8,128)} convert(bf16[33,16,256]{2,1,0:T(8,128)(2,1)S(1)} %broadcast_in_dim.47) | non-fusion elementwise | flops 135168 | bytes 811008 | tf_op jit(solution)/shard_map/convert_element_type | solution.py:166
  11.7 0.9 %fusion.5 = bf16[1,33,4,18,256]{4,3,2,1,0:T(8,128)(2,1)S(1)} fusion(bf16[1,33,1,16,256]{4,3,2,1,0:T(8,128)(2,1)S(1)} %slice.173, bf16[1,33,2,16,256]{4,3,2,1,0:T(8,128)(2,1)S(1)} %broadcast_in_dim.50, bf16[1,33,1,16,256]{4,3,2,1,0:T(8,128)(2,1)S(1)} %slice.172), kind=kLoop, calls=%fused_computation.10 | loop fusion | flops 7299072 | bytes 2297856 | tf_op jit(solution)/shard_map/concatenate | solution.py:138
  12.6 0.4 copy-done.7
  15.6 1.4 %multiply_convert_fusion = (bf16[33,2,16,256]{3,2,1,0:T(8,128)(2,1)S(1)}, f32[33,2,16,256]{3,2,1,0:T(8,128)}) fusion(f32[33,2,16,256]{3,2,1,0:T(8,128)S(1)} %convolution_add_fusion.5, bf16[3,3,256,256]{3,2,1,0:T(8,128)(2,1)S(1)} %copy-done.7, bf16[1,33,4,18,256]{4,3,2,1,0:T(8,128)(2,1)S(1)} %fusion.5), kind=kOutput, calls=%fused_computation.56 | convolution fusion | flops 140034048 | bytes 3375104 | tf_op jit(solution)/shard_map/nfhwc,cd->nfhwd/dot_general | solution.py:148
  17.6 0.7 %copy-done.4 = f32[33,16,256]{2,1,0:T(8,128)S(1)} copy-done((f32[33,16,256]{2,1,0:T(8,128)S(1)}, f32[33,16,256]{2,1,0:T(8,128)}, u32[]{:S(2)}) %copy-start.4) | copy-done | bytes 540696
  18.7 0.8 %copy-done.1 = bf16[33,2,16,256]{3,2,1,0:T(8,128)(2,1)} copy-done((bf16[33,2,16,256]{3,2,1,0:T(8,128)(2,1)}, bf16[33,2,16,256]{3,2,1,0:T(8,128)(2,1)S(1)}, u32[]{:S(2)}) %copy-start.1) | copy-done | bytes 540696
  19.5 0.4 fusion.24
  19.9 0.9 %fusion.51 = (f32[8,256]{1,0:T(8,128)S(1)}, f32[8,2,16,256]{3,2,1,0:T(8,128)}) fusion(bf16[256,256]{1,0:T(8,128)(2,1)S(1)} %copy-done, bf16[8,2,16,256]{3,0,2,1:T(8,128)(2,1)S(1)} %fusion.24), kind=kOutput, calls=%fused_computation.109 | convolution fusion | flops 34142208 | bytes 532480 | tf_op jit(solution)/shard_map/nqhwc,ce->nqhwe/dot_general | solution.py:173
  20.8 4.0 %collective-permute-start.4 = (f32[1,8,256]{2,1,0:T(8,128)S(1)}, f32[1,8,256]{2,1,0:T(8,128)S(1)}, u32[]{:S(2)}, u32[]{:S(2)}) collective-permute-start(f32[1,8,256]{2,1,0:T(8,128)S(1)} %bitcast.378), channel_id=1, source_target_pairs={{0,3},{1,0},{2,1},{3,2},{4,7},{5,4},{6,5},{7,6},{8,11},{9,8},{10,9... | collective-permute-start | bytes 24584 | tf_op jit(solution)/shard_map/ppermute | solution.py:56
  24.8 1.0 %collective-permute-start.2 = (f32[1,8,256]{2,1,0:T(8,128)S(1)}, f32[1,8,256]{2,1,0:T(8,128)S(1)}, u32[]{:S(2)}, u32[]{:S(2)}) collective-permute-start(f32[1,8,256]{2,1,0:T(8,128)S(1)} %bitcast.380), channel_id=1, source_target_pairs={{0,1},{1,2},{2,3},{3,0},{4,5},{5,6},{6,7},{7,4},{8,9},{9,10},{10,1... | collective-permute-start | bytes 24584 | tf_op jit(solution)/shard_map/ppermute | solution.py:56
  26.2 3.2 %collective-permute-done.3 = f32[1,8,256]{2,1,0:T(8,128)S(1)} collective-permute-done((f32[1,8,256]{2,1,0:T(8,128)S(1)}, f32[1,8,256]{2,1,0:T(8,128)S(1)}, u32[]{:S(2)}, u32[]{:S(2)}) %collective-permute-start.3) | collective-permute-done | bytes 8224 | tf_op jit(solution)/shard_map/ppermute | solution.py:56
  29.4 0.9 %collective-permute-done.2 = f32[1,8,256]{2,1,0:T(8,128)S(1)} collective-permute-done((f32[1,8,256]{2,1,0:T(8,128)S(1)}, f32[1,8,256]{2,1,0:T(8,128)S(1)}, u32[]{:S(2)}, u32[]{:S(2)}) %collective-permute-start.2) | collective-permute-done | bytes 8224 | tf_op jit(solution)/shard_map/ppermute | solution.py:56
  30.3 0.5 gather_fusion
  31.1 1.1 %fusion.49 = bf16[8,2,16,256]{3,2,1,0:T(8,128)(2,1)S(1)} fusion(f32[8,2,16,256]{3,2,1,0:T(8,128)} %get-tuple-element.18, f32[8,256]{1,0:T(8,128)S(1)} %get-tuple-element.14, f32[8,256]{1,0:T(8,128)S(1)} %get-tuple-element.13), kind=kLoop, calls=%fused_computation.105 | loop fusion | flops 1245184 | bytes 409600 | tf_op jit(solution)/shard_map/convert_element_type | solution.py:180
  32.5 1.0 %fusion.12 = bf16[1,33,2,16,256]{4,1,3,2,0:T(8,128)(2,1)S(1)} fusion(f32[8,2,16,256]{3,0,2,1:T(8,128)S(1)} %fusion.59, bf16[1,33,2,16,256]{4,3,2,1,0:T(8,128)(2,1)S(1)} %copy-done.8, f32[33]{0:T(128)S(1)} %compare_select_fusion.6, s32[8]{0:T(128)S(1)} %bitcast.386), kind=kOutput, calls=%fused_computation.32 | convolution fusion | flops 27033864 | bytes 1343652 | tf_op jit(solution)/shard_map/nqf,nqhwc->nfhwc/dot_general | solution.py:189
  34.7 0.6 copy-done.6
  35.7 0.4 slice_bitcast_fusion
  36.4 0.9 %copy-done.11 = f32[33,2,16,256]{3,2,1,0:T(8,128)S(1)} copy-done((f32[33,2,16,256]{3,2,1,0:T(8,128)S(1)}, f32[33,2,16,256]{3,2,1,0:T(8,128)}, u32[]{:S(2)}) %copy-start.11) | copy-done | bytes 1081368
  37.3 0.6 fusion.13
  38.3 0.6 copy-done.3
  38.9 0.4 fusion.22
  39.3 0.4 fusion.21
  39.7 0.4 fusion.20
  40.1 0.4 fusion.19
  40.5 0.4 fusion.18
  40.9 0.4 fusion.17
  41.2 0.4 fusion.16
  41.7 0.4 fusion.15
  42.1 0.4 broadcast_select_fusion.1
  42.7 3.4 %collective-permute-done.5 = f32[16,96,256]{2,1,0:T(8,128)} collective-permute-done((f32[16,96,256]{2,1,0:T(8,128)S(1)}, f32[16,96,256]{2,1,0:T(8,128)}, u32[]{:S(2)}, u32[]{:S(2)}) %collective-permute-start.5) | collective-permute-done | bytes 1572896 | tf_op jit(solution)/shard_map/ppermute | solution.py:80
  46.2 1.6 %bitcast_add_fusion = f32[16,96,256]{2,1,0:T(8,128)S(1)} fusion(f32[16,96,256]{2,1,0:T(8,128)} %collective-permute-done.5, f32[4,1,4,96,256]{4,3,2,1,0:T(8,128)S(1)} %get-tuple-element.3), kind=kLoop, calls=%fused_computation.13 | loop fusion | flops 393216 | bytes 4718592 | tf_op jit(solution)/shard_map/add | solution.py:81
  47.9 1.6 %collective-permute-start.8 = (bf16[8,48,256]{2,1,0:T(8,128)(2,1)S(1)}, bf16[8,48,256]{2,1,0:T(8,128)(2,1)S(1)}, u32[]{:S(2)}, u32[]{:S(2)}) collective-permute-start(bf16[8,48,256]{2,1,0:T(8,128)(2,1)S(1)} %fusion.52), channel_id=1, source_target_pairs={{0,16},{4,20},{8,24},{12,28},{16,0},{20,4},{24,8},{28,12},{1,17},{... | collective-permute-start | bytes 589832 | tf_op jit(solution)/shard_map/ppermute | solution.py:80
  49.5 1.5 %collective-permute-start.6 = (bf16[8,48,256]{2,1,0:T(8,128)(2,1)S(1)}, bf16[8,48,256]{2,1,0:T(8,128)(2,1)S(1)}, u32[]{:S(2)}, u32[]{:S(2)}) collective-permute-start(bf16[8,48,256]{2,1,0:T(8,128)(2,1)S(1)} %bitcast.370), channel_id=1, source_target_pairs={{0,8},{4,12},{8,0},{12,4},{16,24},{20,28},{24,16},{28,20},{1,9},{5... | collective-permute-start | bytes 589832 | tf_op jit(solution)/shard_map/ppermute | solution.py:80
  51.1 3.8 %collective-permute-done.8 = bf16[8,48,256]{2,1,0:T(8,128)(2,1)S(1)} collective-permute-done((bf16[8,48,256]{2,1,0:T(8,128)(2,1)S(1)}, bf16[8,48,256]{2,1,0:T(8,128)(2,1)S(1)}, u32[]{:S(2)}, u32[]{:S(2)}) %collective-permute-start.8) | collective-permute-done | bytes 196640 | tf_op jit(solution)/shard_map/ppermute | solution.py:80
  55.0 1.6 %collective-permute-start.9 = (bf16[4,48,256]{2,1,0:T(8,128)(2,1)S(1)}, bf16[4,48,256]{2,1,0:T(8,128)(2,1)S(1)}, u32[]{:S(2)}, u32[]{:S(2)}) collective-permute-start(bf16[4,48,256]{2,1,0:T(8,128)(2,1)S(1)} %fusion.95), channel_id=1, source_target_pairs={{0,8},{4,12},{8,0},{12,4},{16,24},{20,28},{24,16},{28,20},{1,9},{5... | collective-permute-start | bytes 294920 | tf_op jit(solution)/shard_map/ppermute | solution.py:80
  56.7 1.6 %collective-permute-start.7 = (bf16[4,48,256]{2,1,0:T(8,128)(2,1)S(1)}, bf16[4,48,256]{2,1,0:T(8,128)(2,1)S(1)}, u32[]{:S(2)}, u32[]{:S(2)}) collective-permute-start(bf16[4,48,256]{2,1,0:T(8,128)(2,1)S(1)} %fusion.94), channel_id=1, source_target_pairs={{0,16},{4,20},{8,24},{12,28},{16,0},{20,4},{24,8},{28,12},{1,17},{... | collective-permute-start | bytes 294920 | tf_op jit(solution)/shard_map/ppermute | solution.py:80
  58.2 1.5 %collective-permute-done.9 = bf16[4,48,256]{2,1,0:T(8,128)(2,1)S(1)} collective-permute-done((bf16[4,48,256]{2,1,0:T(8,128)(2,1)S(1)}, bf16[4,48,256]{2,1,0:T(8,128)(2,1)S(1)}, u32[]{:S(2)}, u32[]{:S(2)}) %collective-permute-start.9) | collective-permute-done | bytes 98336 | tf_op jit(solution)/shard_map/ppermute | solution.py:80
  59.8 1.6 %collective-permute-done.7 = bf16[4,48,256]{2,1,0:T(8,128)(2,1)S(1)} collective-permute-done((bf16[4,48,256]{2,1,0:T(8,128)(2,1)S(1)}, bf16[4,48,256]{2,1,0:T(8,128)(2,1)S(1)}, u32[]{:S(2)}, u32[]{:S(2)}) %collective-permute-start.7) | collective-permute-done | bytes 98336 | tf_op jit(solution)/shard_map/ppermute | solution.py:80
  61.6 1.2 %collective-permute-start.11 = (f32[96,256]{1,0:T(8,128)S(1)}, f32[96,256]{1,0:T(8,128)S(1)}, u32[]{:S(2)}, u32[]{:S(2)}) collective-permute-start(f32[96,256]{1,0:T(8,128)S(1)} %get-tuple-element.11), channel_id=1, source_target_pairs={{0,2},{1,3},{2,0},{3,1},{4,6},{5,7},{6,4},{7,5},{8,10},{9,11},{10,... | collective-permute-start | bytes 294920 | tf_op jit(solution)/shard_map/ppermute | solution.py:115
  62.8 2.9 %collective-permute-start.12 = (f32[96,256]{1,0:T(8,128)S(1)}, f32[96,256]{1,0:T(8,128)S(1)}, u32[]{:S(2)}, u32[]{:S(2)}) collective-permute-start(f32[96,256]{1,0:T(8,128)S(1)} %get-tuple-element.12), channel_id=1, source_target_pairs={{0,3},{1,0},{2,1},{3,2},{4,7},{5,4},{6,5},{7,6},{8,11},{9,8},{10,9... | collective-permute-start | bytes 294920 | tf_op jit(solution)/shard_map/ppermute | solution.py:115
  65.7 2.8 %collective-permute-done.10 = f32[96,256]{1,0:T(8,128)S(1)} collective-permute-done((f32[96,256]{1,0:T(8,128)S(1)}, f32[96,256]{1,0:T(8,128)S(1)}, u32[]{:S(2)}, u32[]{:S(2)}) %collective-permute-start.10) | collective-permute-done | bytes 98336 | tf_op jit(solution)/shard_map/ppermute | solution.py:115
  68.4 2.0 %collective-permute-done.11 = f32[96,256]{1,0:T(8,128)S(1)} collective-permute-done((f32[96,256]{1,0:T(8,128)S(1)}, f32[96,256]{1,0:T(8,128)S(1)}, u32[]{:S(2)}, u32[]{:S(2)}) %collective-permute-start.11) | collective-permute-done | bytes 98336 | tf_op jit(solution)/shard_map/ppermute | solution.py:115
  70.7 0.7 add_add_fusion
  71.4 0.6 add_add_fusion.1
  (88 shorter events, 8.1 us)
Async XLA Ops:
  0.6 19.3 %copy-start = (bf16[256,256]{1,0:T(8,128)(2,1)S(1)}, bf16[256,256]{1,0:T(8,128)(2,1)}, u32[]{:S(2)}) copy-start(bf16[256,256]{1,0:T(8,128)(2,1)} %param.12) | copy-start | bytes 393220
  0.6 10.4 %collective-permute-start.1 = (bf16[1,33,1,8,256]{4,3,2,1,0:T(8,128)(2,1)}, bf16[1,33,1,8,256]{4,3,2,1,0:T(8,128)(2,1)S(1)}, u32[]{:S(2)}, u32[]{:S(2)}) collective-permute-start(bf16[1,33,1,8,256]{4,3,2,1,0:T(8,128)(2,1)} %param.8), channel_id=1, source_target_pairs={{1,0},{2,1},{3,2},{5,4},{6,5},{7,6},{9,8},{10,9},{11,10},{13,12},{... | collective-permute-start | bytes 405512 | tf_op jit(solution)/shard_map/ppermute | solution.py:20
  2.1 9.3 %collective-permute-start = (bf16[1,33,1,8,256]{4,3,2,1,0:T(8,128)(2,1)}, bf16[1,33,1,8,256]{4,3,2,1,0:T(8,128)(2,1)S(1)}, u32[]{:S(2)}, u32[]{:S(2)}) collective-permute-start(bf16[1,33,1,8,256]{4,3,2,1,0:T(8,128)(2,1)} %param.8), channel_id=1, source_target_pairs={{0,1},{1,2},{2,3},{4,5},{5,6},{6,7},{8,9},{9,10},{10,11},{12,13},{... | collective-permute-start | bytes 405512 | tf_op jit(solution)/shard_map/ppermute | solution.py:19
  11.6 1.7 %copy-start.2 = (bf16[1,33,1,16,256]{4,3,2,1,0:T(8,128)(2,1)}, bf16[1,33,1,16,256]{4,3,2,1,0:T(8,128)(2,1)S(1)}, u32[]{:S(2)}) copy-start(bf16[1,33,1,16,256]{4,3,2,1,0:T(8,128)(2,1)S(1)} %slice.172) | copy-start | bytes 811012
  11.7 1.3 %copy-start.7 = (bf16[3,3,256,256]{3,2,1,0:T(8,128)(2,1)S(1)}, bf16[3,3,256,256]{3,2,1,0:T(8,128)(2,1)}, u32[]{:S(2)}) copy-start(bf16[3,3,256,256]{3,2,1,0:T(8,128)(2,1)} %param.10) | copy-start | bytes 3538948
  15.6 1.4 %copy-start.5 = (bf16[3,256,256]{2,1,0:T(8,128)(2,1)S(1)}, bf16[3,256,256]{2,1,0:T(8,128)(2,1)}, u32[]{:S(2)}) copy-start(bf16[3,256,256]{2,1,0:T(8,128)(2,1)} %param.11) | copy-start | bytes 1179652
  17.3 1.1 %copy-start.4 = (f32[33,16,256]{2,1,0:T(8,128)S(1)}, f32[33,16,256]{2,1,0:T(8,128)}, u32[]{:S(2)}) copy-start(f32[33,16,256]{2,1,0:T(8,128)} %convert_element_type.97) | copy-start | bytes 1622020
  18.4 1.1 %copy-start.10 = (s32[1,8]{1,0:T(1,128)S(1)}, s32[1,8]{1,0:T(1,128)}, u32[]{:S(2)}) copy-start(s32[1,8]{1,0:T(1,128)} %param.14) | copy-start | bytes 100
  18.7 0.8 %copy-start.1 = (bf16[33,2,16,256]{3,2,1,0:T(8,128)(2,1)}, bf16[33,2,16,256]{3,2,1,0:T(8,128)(2,1)S(1)}, u32[]{:S(2)}) copy-start(bf16[33,2,16,256]{3,2,1,0:T(8,128)(2,1)S(1)} %fusion.14) | copy-start | bytes 1622020
  18.7 12.4 %copy-start.9 = (f32[256]{0:T(256)S(1)}, f32[256]{0:T(256)}, u32[]{:S(2)}) copy-start(f32[256]{0:T(256)} %param.13) | copy-start | bytes 3076
  20.8 5.4 %collective-permute-start.4 = (f32[1,8,256]{2,1,0:T(8,128)S(1)}, f32[1,8,256]{2,1,0:T(8,128)S(1)}, u32[]{:S(2)}, u32[]{:S(2)}) collective-permute-start(f32[1,8,256]{2,1,0:T(8,128)S(1)} %bitcast.378), channel_id=1, source_target_pairs={{0,3},{1,0},{2,1},{3,2},{4,7},{5,4},{6,5},{7,6},{8,11},{9,8},{10,9... | collective-permute-start | bytes 24584 | tf_op jit(solution)/shard_map/ppermute | solution.py:56
  24.8 4.5 %collective-permute-start.3 = (f32[1,8,256]{2,1,0:T(8,128)S(1)}, f32[1,8,256]{2,1,0:T(8,128)S(1)}, u32[]{:S(2)}, u32[]{:S(2)}) collective-permute-start(f32[1,8,256]{2,1,0:T(8,128)S(1)} %bitcast.379), channel_id=1, source_target_pairs={{0,2},{1,3},{2,0},{3,1},{4,6},{5,7},{6,4},{7,5},{8,10},{9,11},{10,... | collective-permute-start | bytes 24584 | tf_op jit(solution)/shard_map/ppermute | solution.py:56
  24.8 5.4 %collective-permute-start.2 = (f32[1,8,256]{2,1,0:T(8,128)S(1)}, f32[1,8,256]{2,1,0:T(8,128)S(1)}, u32[]{:S(2)}, u32[]{:S(2)}) collective-permute-start(f32[1,8,256]{2,1,0:T(8,128)S(1)} %bitcast.380), channel_id=1, source_target_pairs={{0,1},{1,2},{2,3},{3,0},{4,5},{5,6},{6,7},{7,4},{8,9},{9,10},{10,1... | collective-permute-start | bytes 24584 | tf_op jit(solution)/shard_map/ppermute | solution.py:56
  30.8 1.7 %copy-start.8 = (bf16[1,33,2,16,256]{4,3,2,1,0:T(8,128)(2,1)S(1)}, bf16[1,33,2,16,256]{4,3,2,1,0:T(8,128)(2,1)}, u32[]{:S(2)}) copy-start(bf16[1,33,2,16,256]{4,3,2,1,0:T(8,128)(2,1)} %param.15) | copy-start | bytes 1622020
  34.3 1.0 %copy-start.6 = (bf16[3,256,256]{2,1,0:T(8,128)(2,1)S(1)}, bf16[3,256,256]{2,1,0:T(8,128)(2,1)}, u32[]{:S(2)}) copy-start(bf16[3,256,256]{2,1,0:T(8,128)(2,1)} %param.11) | copy-start | bytes 1179652
  36.1 1.2 %copy-start.11 = (f32[33,2,16,256]{3,2,1,0:T(8,128)S(1)}, f32[33,2,16,256]{3,2,1,0:T(8,128)}, u32[]{:S(2)}) copy-start(f32[33,2,16,256]{3,2,1,0:T(8,128)} %get-tuple-element.16) | copy-start | bytes 3244036
  37.9 1.0 %copy-start.3 = (bf16[1,33,1,16,256]{4,3,2,1,0:T(8,128)(2,1)S(1)}, bf16[1,33,1,16,256]{4,3,2,1,0:T(8,128)(2,1)}, u32[]{:S(2)}) copy-start(bf16[1,33,1,16,256]{4,3,2,1,0:T(8,128)(2,1)} %copy-done.2) | copy-start | bytes 811012
  42.6 3.6 %collective-permute-start.5 = (f32[16,96,256]{2,1,0:T(8,128)S(1)}, f32[16,96,256]{2,1,0:T(8,128)}, u32[]{:S(2)}, u32[]{:S(2)}) collective-permute-start(f32[16,96,256]{2,1,0:T(8,128)S(1)} %bitcast.365), channel_id=1, source_target_pairs={{0,4},{4,0},{8,12},{12,8},{16,20},{20,16},{24,28},{28,24},{1,5},{5... | collective-permute-start | bytes 4718600 | tf_op jit(solution)/shard_map/ppermute | solution.py:80
  47.9 7.0 %collective-permute-start.8 = (bf16[8,48,256]{2,1,0:T(8,128)(2,1)S(1)}, bf16[8,48,256]{2,1,0:T(8,128)(2,1)S(1)}, u32[]{:S(2)}, u32[]{:S(2)}) collective-permute-start(bf16[8,48,256]{2,1,0:T(8,128)(2,1)S(1)} %fusion.52), channel_id=1, source_target_pairs={{0,16},{4,20},{8,24},{12,28},{16,0},{20,4},{24,8},{28,12},{1,17},{... | collective-permute-start | bytes 589832 | tf_op jit(solution)/shard_map/ppermute | solution.py:80
  49.5 7.1 %collective-permute-start.6 = (bf16[8,48,256]{2,1,0:T(8,128)(2,1)S(1)}, bf16[8,48,256]{2,1,0:T(8,128)(2,1)S(1)}, u32[]{:S(2)}, u32[]{:S(2)}) collective-permute-start(bf16[8,48,256]{2,1,0:T(8,128)(2,1)S(1)} %bitcast.370), channel_id=1, source_target_pairs={{0,8},{4,12},{8,0},{12,4},{16,24},{20,28},{24,16},{28,20},{1,9},{5... | collective-permute-start | bytes 589832 | tf_op jit(solution)/shard_map/ppermute | solution.py:80
  55.0 4.7 %collective-permute-start.9 = (bf16[4,48,256]{2,1,0:T(8,128)(2,1)S(1)}, bf16[4,48,256]{2,1,0:T(8,128)(2,1)S(1)}, u32[]{:S(2)}, u32[]{:S(2)}) collective-permute-start(bf16[4,48,256]{2,1,0:T(8,128)(2,1)S(1)} %fusion.95), channel_id=1, source_target_pairs={{0,8},{4,12},{8,0},{12,4},{16,24},{20,28},{24,16},{28,20},{1,9},{5... | collective-permute-start | bytes 294920 | tf_op jit(solution)/shard_map/ppermute | solution.py:80
  56.7 4.7 %collective-permute-start.7 = (bf16[4,48,256]{2,1,0:T(8,128)(2,1)S(1)}, bf16[4,48,256]{2,1,0:T(8,128)(2,1)S(1)}, u32[]{:S(2)}, u32[]{:S(2)}) collective-permute-start(bf16[4,48,256]{2,1,0:T(8,128)(2,1)S(1)} %fusion.94), channel_id=1, source_target_pairs={{0,16},{4,20},{8,24},{12,28},{16,0},{20,4},{24,8},{28,12},{1,17},{... | collective-permute-start | bytes 294920 | tf_op jit(solution)/shard_map/ppermute | solution.py:80
  61.4 7.0 %collective-permute-start.10 = (f32[96,256]{1,0:T(8,128)S(1)}, f32[96,256]{1,0:T(8,128)S(1)}, u32[]{:S(2)}, u32[]{:S(2)}) collective-permute-start(f32[96,256]{1,0:T(8,128)S(1)} %get-tuple-element.9), channel_id=1, source_target_pairs={{0,1},{1,2},{2,3},{3,0},{4,5},{5,6},{6,7},{7,4},{8,9},{9,10},{10,1... | collective-permute-start | bytes 294920 | tf_op jit(solution)/shard_map/ppermute | solution.py:115
  61.6 8.9 %collective-permute-start.11 = (f32[96,256]{1,0:T(8,128)S(1)}, f32[96,256]{1,0:T(8,128)S(1)}, u32[]{:S(2)}, u32[]{:S(2)}) collective-permute-start(f32[96,256]{1,0:T(8,128)S(1)} %get-tuple-element.11), channel_id=1, source_target_pairs={{0,2},{1,3},{2,0},{3,1},{4,6},{5,7},{6,4},{7,5},{8,10},{9,11},{10,... | collective-permute-start | bytes 294920 | tf_op jit(solution)/shard_map/ppermute | solution.py:115
  62.8 7.8 %collective-permute-start.12 = (f32[96,256]{1,0:T(8,128)S(1)}, f32[96,256]{1,0:T(8,128)S(1)}, u32[]{:S(2)}, u32[]{:S(2)}) collective-permute-start(f32[96,256]{1,0:T(8,128)S(1)} %get-tuple-element.12), channel_id=1, source_target_pairs={{0,3},{1,0},{2,1},{3,2},{4,7},{5,4},{6,5},{7,6},{8,11},{9,8},{10,9... | collective-permute-start | bytes 294920 | tf_op jit(solution)/shard_map/ppermute | solution.py:115

commit v8 on v5

--- a/solution.py
+++ b/solution.py
@@ -88,7 +88,7 @@
     left = list(natural)
     cur = blocks
     for axis, bit in orders[0][:shared]:
-        cur = _halve(cur, left, axis, bit)
+        cur = _halve(cur, left, axis, bit, jnp.bfloat16)
     tail = len(natural)
     while tail > shared and all(o[tail - 1] == orders[0][tail - 1] for o in orders):
         tail -= 1

time: 71.8 us -> 70.1 us (0.976)
  waiting for transfers between devices: 17.9 us -> 14.9 us
  local copies, waits for them, and re-layouts: 6.47 us -> 7.63 us
    ppermute x5, waiting for transfers between devices: 10.3 us -> 7.29 us  [_halve(): got = lax.ppermute(send, axis, [(i, i ^ 1 << bit) for i in range(size)])]
    select_n x2, other arithmetic: 0.48 us -> 1.88 us  [_halve(): keep = jnp.where(upper, high, low)]
    add x5, other arithmetic: 1.76 us -> 0.4 us  [_halve(): return keep + got.astype(keep.dtype)]
    unnamed x40 -> x42, local copies, waits for them, and re-layouts: 4.26 us -> 5.42 us
  transfers between devices with their start and end apart: 12 -> 12, of which waited for: 9 -> 9; matrix products, arithmetic and copies ran while one was open for 4% -> 7% of each run, Pallas kernels for 0% -> 0%
where the time goes in v8:
time: 70.1 us; the launch traced here: 69.7 us
  starting transfers between devices  24.8 us (35%)
  waiting for transfers between devices  14.9 us (21%)
  matrix products  13.3 us (19%)
  local copies, waits for them, and re-layouts  7.63 us (11%)
  other arithmetic  7.06 us (10%)
  between operations  1.85 us (3%)
    ppermute x5, waiting for transfers between devices, _halve(): got = lax.ppermute(send, axis, [(i, i ^ 1 << bit) for i in range(size)])  7.29 us
    ppermute x5, starting transfers between devices, _halve(): got = lax.ppermute(send, axis, [(i, i ^ 1 << bit) for i in range(size)])  6.26 us
    ppermute x3, starting transfers between devices, halving_scatter(): lax.ppermute(send, 'space', [(i, (i + shift) % ns) for i in range(ns)])  5.96 us
    ppermute x1, starting transfers between devices, exchange_rows(): above = lax.ppermute(tail, axis, [(i, i + 1) for i in range(ends)])  5.59 us
    ppermute x2, starting transfers between devices, space_sum(): lax.ppermute(values, 'space', [(i, i ^ step) for i in range(count)])  5.59 us
    unnamed x42, local copies, waits for them, and re-layouts  5.42 us
    ppermute x3, waiting for transfers between devices, halving_scatter(): lax.ppermute(send, 'space', [(i, (i + shift) % ns) for i in range(ns)])  4.21 us
    dot_general x9, matrix products, on_device(): jnp.einsum('nfhwc,cd->nfhwd', window, spatial_weight[row_tap, col_tap], p...  3.88 us
  transfers between devices with their start and end apart: 12, of which 9 were waited for; matrix products, arithmetic and copies ran while one was open for 7% of the time, Pallas kernels for 0%

profile of v8, /device:TPU:0, one launch (start us, length us, event | category | flops | bytes accessed | tf_op | source)
XLA Modules:
  0.0 69.7 jit_solution(17713761815412087363)
XLA Ops:
  0.6 1.4 %collective-permute-start.1 = (bf16[1,33,1,8,256]{4,3,2,1,0:T(8,128)(2,1)}, bf16[1,33,1,8,256]{4,3,2,1,0:T(8,128)(2,1)S(1)}, u32[]{:S(2)}, u32[]{:S(2)}) collective-permute-start(bf16[1,33,1,8,256]{4,3,2,1,0:T(8,128)(2,1)} %param.8), channel_id=1, source_target_pairs={{1,0},{2,1},{3,2},{5,4},{6,5},{7,6},{9,8},{10,9},{11,10},{13,12},{... | collective-permute-start | bytes 405512 | tf_op jit(solution)/shard_map/ppermute | solution.py:20
  2.1 5.6 %collective-permute-start = (bf16[1,33,1,8,256]{4,3,2,1,0:T(8,128)(2,1)}, bf16[1,33,1,8,256]{4,3,2,1,0:T(8,128)(2,1)S(1)}, u32[]{:S(2)}, u32[]{:S(2)}) collective-permute-start(bf16[1,33,1,8,256]{4,3,2,1,0:T(8,128)(2,1)} %param.8), channel_id=1, source_target_pairs={{0,1},{1,2},{2,3},{4,5},{5,6},{6,7},{8,9},{9,10},{10,11},{12,13},{... | collective-permute-start | bytes 405512 | tf_op jit(solution)/shard_map/ppermute | solution.py:19
  8.3 1.1 %broadcast_in_dim.16 = bf16[33,8,2,256]{3,2,1,0:T(2,128)(2,1)S(1)} broadcast(bf16[33,8,256]{2,1,0:T(8,128)(2,1)} %bitcast.358), dimensions={0,1,3} | broadcast | bytes 405504 | tf_op jit(solution)/shard_map/broadcast_in_dim | solution.py:26
  9.5 0.9 %convert_element_type.106 = f32[33,16,256]{2,1,0:T(8,128)} convert(bf16[33,16,256]{2,1,0:T(8,128)(2,1)S(1)} %broadcast_in_dim.17) | non-fusion elementwise | flops 135168 | bytes 811008 | tf_op jit(solution)/shard_map/convert_element_type | solution.py:160
  11.1 0.9 %fusion.5 = bf16[1,33,4,18,256]{4,3,2,1,0:T(8,128)(2,1)S(1)} fusion(bf16[1,33,1,16,256]{4,3,2,1,0:T(8,128)(2,1)S(1)} %slice.161, bf16[1,33,2,16,256]{4,3,2,1,0:T(8,128)(2,1)S(1)} %broadcast_in_dim.40, bf16[1,33,1,16,256]{4,3,2,1,0:T(8,128)(2,1)S(1)} %slice.160), kind=kLoop, calls=%fused_computation.9 | loop fusion | flops 7299072 | bytes 2297856 | tf_op jit(solution)/shard_map/concatenate | solution.py:132
  12.0 0.4 copy-done.8
  15.0 1.4 %multiply_convert_fusion = (bf16[33,2,16,256]{3,2,1,0:T(8,128)(2,1)S(1)}, f32[33,2,16,256]{3,2,1,0:T(8,128)}) fusion(f32[33,2,16,256]{3,2,1,0:T(8,128)S(1)} %convolution_add_fusion.5, bf16[3,3,256,256]{3,2,1,0:T(8,128)(2,1)S(1)} %copy-done.8, bf16[1,33,4,18,256]{4,3,2,1,0:T(8,128)(2,1)S(1)} %fusion.5), kind=kOutput, calls=%fused_computation.56 | convolution fusion | flops 140034048 | bytes 3375104 | tf_op jit(solution)/shard_map/nfhwc,cd->nfhwd/dot_general | solution.py:142
  17.0 0.7 %copy-done.5 = f32[33,16,256]{2,1,0:T(8,128)S(1)} copy-done((f32[33,16,256]{2,1,0:T(8,128)S(1)}, f32[33,16,256]{2,1,0:T(8,128)}, u32[]{:S(2)}) %copy-start.5) | copy-done | bytes 540696
  18.1 0.8 %copy-done.2 = bf16[33,2,16,256]{3,2,1,0:T(8,128)(2,1)} copy-done((bf16[33,2,16,256]{3,2,1,0:T(8,128)(2,1)}, bf16[33,2,16,256]{3,2,1,0:T(8,128)(2,1)S(1)}, u32[]{:S(2)}) %copy-start.2) | copy-done | bytes 540696
  18.9 0.4 fusion.24
  19.3 0.9 %fusion.51 = (f32[8,256]{1,0:T(8,128)S(1)}, f32[8,2,16,256]{3,2,1,0:T(8,128)}) fusion(bf16[256,256]{1,0:T(8,128)(2,1)S(1)} %copy-done, bf16[8,2,16,256]{3,0,2,1:T(8,128)(2,1)S(1)} %fusion.24), kind=kOutput, calls=%fused_computation.108 | convolution fusion | flops 34142208 | bytes 532480 | tf_op jit(solution)/shard_map/nqhwc,ce->nqhwe/dot_general | solution.py:167
  20.2 2.4 %collective-permute-start.2 = (f32[1,8,256]{2,1,0:T(8,128)S(1)}, f32[1,8,256]{2,1,0:T(8,128)S(1)}, u32[]{:S(2)}, u32[]{:S(2)}) collective-permute-start(f32[1,8,256]{2,1,0:T(8,128)S(1)} %bitcast.365), channel_id=1, source_target_pairs={{0,1},{1,0},{2,3},{3,2},{4,5},{5,4},{6,7},{7,6},{8,9},{9,8},{10,11... | collective-permute-start | bytes 24584 | tf_op jit(solution)/shard_map/ppermute | solution.py:57
  22.6 1.6 %collective-permute-done.2 = f32[1,8,256]{2,1,0:T(8,128)S(1)} collective-permute-done((f32[1,8,256]{2,1,0:T(8,128)S(1)}, f32[1,8,256]{2,1,0:T(8,128)S(1)}, u32[]{:S(2)}, u32[]{:S(2)}) %collective-permute-start.2) | collective-permute-done | bytes 8224 | tf_op jit(solution)/shard_map/ppermute | solution.py:57
  24.3 3.2 %collective-permute-start.3 = (f32[1,8,256]{2,1,0:T(8,128)S(1)}, f32[1,8,256]{2,1,0:T(8,128)S(1)}, u32[]{:S(2)}, u32[]{:S(2)}) collective-permute-start(f32[1,8,256]{2,1,0:T(8,128)S(1)} %bitcast_add_fusion.5), channel_id=1, source_target_pairs={{0,2},{1,3},{2,0},{3,1},{4,6},{5,7},{6,4},{7,5},{8,10},{9,11},{10,... | collective-permute-start | bytes 24584 | tf_op jit(solution)/shard_map/ppermute | solution.py:57
  27.5 1.6 %collective-permute-done.3 = f32[1,8,256]{2,1,0:T(8,128)S(1)} collective-permute-done((f32[1,8,256]{2,1,0:T(8,128)S(1)}, f32[1,8,256]{2,1,0:T(8,128)S(1)}, u32[]{:S(2)}, u32[]{:S(2)}) %collective-permute-start.3) | collective-permute-done | bytes 8224 | tf_op jit(solution)/shard_map/ppermute | solution.py:57
  29.3 1.1 %fusion.49 = bf16[8,2,16,256]{3,2,1,0:T(8,128)(2,1)S(1)} fusion(f32[8,2,16,256]{3,2,1,0:T(8,128)} %get-tuple-element.16, f32[8,256]{1,0:T(8,128)S(1)} %get-tuple-element.12, f32[8,256]{1,0:T(8,128)S(1)} %get-tuple-element.11), kind=kLoop, calls=%fused_computation.104 | loop fusion | flops 1245184 | bytes 409600 | tf_op jit(solution)/shard_map/convert_element_type | solution.py:174
  30.7 1.0 %fusion.12 = bf16[1,33,2,16,256]{4,1,3,2,0:T(8,128)(2,1)S(1)} fusion(f32[8,2,16,256]{3,0,2,1:T(8,128)S(1)} %fusion.59, bf16[1,33,2,16,256]{4,3,2,1,0:T(8,128)(2,1)S(1)} %copy-done.9, f32[33]{0:T(128)S(1)} %compare_select_fusion, s32[8]{0:T(128)S(1)} %bitcast.367), kind=kOutput, calls=%fused_computation.32 | convolution fusion | flops 27033864 | bytes 1343652 | tf_op jit(solution)/shard_map/nqf,nqhwc->nfhwc/dot_general | solution.py:183
  32.9 0.6 copy-done.7
  33.8 0.4 slice_bitcast_fusion
  34.6 0.9 %copy-done.12 = f32[33,2,16,256]{3,2,1,0:T(8,128)S(1)} copy-done((f32[33,2,16,256]{3,2,1,0:T(8,128)S(1)}, f32[33,2,16,256]{3,2,1,0:T(8,128)}, u32[]{:S(2)}) %copy-start.12) | copy-done | bytes 1081368
  35.5 0.6 fusion.13
  36.1 0.4 fusion.23
  36.5 0.6 copy-done.4
  37.0 0.4 fusion.22
  37.4 0.4 fusion.21
  37.9 0.4 fusion.20
  38.2 0.4 fusion.19
  38.6 0.4 fusion.18
  39.0 0.4 fusion.17
  39.4 0.4 fusion.16
  39.8 0.4 fusion.15
  40.5 1.2 %copy-done.1 = f32[9,256,256]{2,1,0:T(8,128)} copy-done((f32[9,256,256]{2,1,0:T(8,128)}, f32[9,256,256]{2,1,0:T(8,128)S(1)}, u32[]{:S(2)}) %copy-start.1) | copy-done | bytes 2359320
  41.7 1.8 %broadcast_select_fusion = f32[4,1,4,96,256]{4,3,2,1,0:T(8,128)S(1)} fusion(pred[]{:T(512)S(6)} %eq.53, f32[4,2,4,24,256]{4,3,2,1,0:T(8,128)S(1)} %bitcast.334, f32[4,2,4,72,256]{4,3,2,1,0:T(8,128)} %bitcast.332), kind=kLoop, calls=%fused_computation.59 | loop fusion | flops 1179648 | bytes 4718593 | tf_op jit(solution)/shard_map/jit(_where)/select_n | solution.py:69
  43.5 0.4 collective-permute-done.4
  44.4 1.6 %collective-permute-start.7 = (bf16[8,48,256]{2,1,0:T(8,128)(2,1)S(1)}, bf16[8,48,256]{2,1,0:T(8,128)(2,1)S(1)}, u32[]{:S(2)}, u32[]{:S(2)}) collective-permute-start(bf16[8,48,256]{2,1,0:T(8,128)(2,1)S(1)} %fusion.52), channel_id=1, source_target_pairs={{0,16},{4,20},{8,24},{12,28},{16,0},{20,4},{24,8},{28,12},{1,17},{... | collective-permute-start | bytes 589832 | tf_op jit(solution)/shard_map/ppermute | solution.py:74
  46.0 1.6 %collective-permute-start.5 = (bf16[8,48,256]{2,1,0:T(8,128)(2,1)S(1)}, bf16[8,48,256]{2,1,0:T(8,128)(2,1)S(1)}, u32[]{:S(2)}, u32[]{:S(2)}) collective-permute-start(bf16[8,48,256]{2,1,0:T(8,128)(2,1)S(1)} %bitcast.357), channel_id=1, source_target_pairs={{0,8},{4,12},{8,0},{12,4},{16,24},{20,28},{24,16},{28,20},{1,9},{5... | collective-permute-start | bytes 589832 | tf_op jit(solution)/shard_map/ppermute | solution.py:74
  47.6 3.8 %collective-permute-done.7 = bf16[8,48,256]{2,1,0:T(8,128)(2,1)S(1)} collective-permute-done((bf16[8,48,256]{2,1,0:T(8,128)(2,1)S(1)}, bf16[8,48,256]{2,1,0:T(8,128)(2,1)S(1)}, u32[]{:S(2)}, u32[]{:S(2)}) %collective-permute-start.7) | collective-permute-done | bytes 196640 | tf_op jit(solution)/shard_map/ppermute | solution.py:74
  51.5 1.5 %collective-permute-start.8 = (bf16[4,48,256]{2,1,0:T(8,128)(2,1)S(1)}, bf16[4,48,256]{2,1,0:T(8,128)(2,1)S(1)}, u32[]{:S(2)}, u32[]{:S(2)}) collective-permute-start(bf16[4,48,256]{2,1,0:T(8,128)(2,1)S(1)} %fusion.95), channel_id=1, source_target_pairs={{0,8},{4,12},{8,0},{12,4},{16,24},{20,28},{24,16},{28,20},{1,9},{5... | collective-permute-start | bytes 294920 | tf_op jit(solution)/shard_map/ppermute | solution.py:74
  53.1 1.6 %collective-permute-start.6 = (bf16[4,48,256]{2,1,0:T(8,128)(2,1)S(1)}, bf16[4,48,256]{2,1,0:T(8,128)(2,1)S(1)}, u32[]{:S(2)}, u32[]{:S(2)}) collective-permute-start(bf16[4,48,256]{2,1,0:T(8,128)(2,1)S(1)} %fusion.94), channel_id=1, source_target_pairs={{0,16},{4,20},{8,24},{12,28},{16,0},{20,4},{24,8},{28,12},{1,17},{... | collective-permute-start | bytes 294920 | tf_op jit(solution)/shard_map/ppermute | solution.py:74
  54.7 1.5 %collective-permute-done.8 = bf16[4,48,256]{2,1,0:T(8,128)(2,1)S(1)} collective-permute-done((bf16[4,48,256]{2,1,0:T(8,128)(2,1)S(1)}, bf16[4,48,256]{2,1,0:T(8,128)(2,1)S(1)}, u32[]{:S(2)}, u32[]{:S(2)}) %collective-permute-start.8) | collective-permute-done | bytes 98336 | tf_op jit(solution)/shard_map/ppermute | solution.py:74
  56.2 1.6 %collective-permute-done.6 = bf16[4,48,256]{2,1,0:T(8,128)(2,1)S(1)} collective-permute-done((bf16[4,48,256]{2,1,0:T(8,128)(2,1)S(1)}, bf16[4,48,256]{2,1,0:T(8,128)(2,1)S(1)}, u32[]{:S(2)}, u32[]{:S(2)}) %collective-permute-start.6) | collective-permute-done | bytes 98336 | tf_op jit(solution)/shard_map/ppermute | solution.py:74
  57.9 2.0 %collective-permute-start.9 = (f32[96,256]{1,0:T(8,128)S(1)}, f32[96,256]{1,0:T(8,128)S(1)}, u32[]{:S(2)}, u32[]{:S(2)}) collective-permute-start(f32[96,256]{1,0:T(8,128)S(1)} %get-tuple-element.7), channel_id=1, source_target_pairs={{0,1},{1,2},{2,3},{3,0},{4,5},{5,6},{6,7},{7,4},{8,9},{9,10},{10,1... | collective-permute-start | bytes 294920 | tf_op jit(solution)/shard_map/ppermute | solution.py:109
  59.9 2.6 %collective-permute-start.10 = (f32[96,256]{1,0:T(8,128)S(1)}, f32[96,256]{1,0:T(8,128)S(1)}, u32[]{:S(2)}, u32[]{:S(2)}) collective-permute-start(f32[96,256]{1,0:T(8,128)S(1)} %get-tuple-element.9), channel_id=1, source_target_pairs={{0,2},{1,3},{2,0},{3,1},{4,6},{5,7},{6,4},{7,5},{8,10},{9,11},{10,... | collective-permute-start | bytes 294920 | tf_op jit(solution)/shard_map/ppermute | solution.py:109
  62.5 1.4 %collective-permute-start.11 = (f32[96,256]{1,0:T(8,128)S(1)}, f32[96,256]{1,0:T(8,128)S(1)}, u32[]{:S(2)}, u32[]{:S(2)}) collective-permute-start(f32[96,256]{1,0:T(8,128)S(1)} %get-tuple-element.10), channel_id=1, source_target_pairs={{0,3},{1,0},{2,1},{3,2},{4,7},{5,4},{6,5},{7,6},{8,11},{9,8},{10,9... | collective-permute-start | bytes 294920 | tf_op jit(solution)/shard_map/ppermute | solution.py:109
  63.9 1.6 %collective-permute-done.9 = f32[96,256]{1,0:T(8,128)S(1)} collective-permute-done((f32[96,256]{1,0:T(8,128)S(1)}, f32[96,256]{1,0:T(8,128)S(1)}, u32[]{:S(2)}, u32[]{:S(2)}) %collective-permute-start.9) | collective-permute-done | bytes 98336 | tf_op jit(solution)/shard_map/ppermute | solution.py:109
  65.5 2.6 %collective-permute-done.10 = f32[96,256]{1,0:T(8,128)S(1)} collective-permute-done((f32[96,256]{1,0:T(8,128)S(1)}, f32[96,256]{1,0:T(8,128)S(1)}, u32[]{:S(2)}, u32[]{:S(2)}) %collective-permute-start.10) | collective-permute-done | bytes 98336 | tf_op jit(solution)/shard_map/ppermute | solution.py:109
  68.4 0.7 add_add_fusion
  69.0 0.6 add_add_fusion.1
  (84 shorter events, 7.7 us)
Async XLA Ops:
  0.6 18.7 %copy-start = (bf16[256,256]{1,0:T(8,128)(2,1)S(1)}, bf16[256,256]{1,0:T(8,128)(2,1)}, u32[]{:S(2)}) copy-start(bf16[256,256]{1,0:T(8,128)(2,1)} %param.12) | copy-start | bytes 393220
  0.6 9.7 %collective-permute-start.1 = (bf16[1,33,1,8,256]{4,3,2,1,0:T(8,128)(2,1)}, bf16[1,33,1,8,256]{4,3,2,1,0:T(8,128)(2,1)S(1)}, u32[]{:S(2)}, u32[]{:S(2)}) collective-permute-start(bf16[1,33,1,8,256]{4,3,2,1,0:T(8,128)(2,1)} %param.8), channel_id=1, source_target_pairs={{1,0},{2,1},{3,2},{5,4},{6,5},{7,6},{9,8},{10,9},{11,10},{13,12},{... | collective-permute-start | bytes 405512 | tf_op jit(solution)/shard_map/ppermute | solution.py:20
  2.1 8.7 %collective-permute-start = (bf16[1,33,1,8,256]{4,3,2,1,0:T(8,128)(2,1)}, bf16[1,33,1,8,256]{4,3,2,1,0:T(8,128)(2,1)S(1)}, u32[]{:S(2)}, u32[]{:S(2)}) collective-permute-start(bf16[1,33,1,8,256]{4,3,2,1,0:T(8,128)(2,1)} %param.8), channel_id=1, source_target_pairs={{0,1},{1,2},{2,3},{4,5},{5,6},{6,7},{8,9},{9,10},{10,11},{12,13},{... | collective-permute-start | bytes 405512 | tf_op jit(solution)/shard_map/ppermute | solution.py:19
  11.1 1.7 %copy-start.3 = (bf16[1,33,1,16,256]{4,3,2,1,0:T(8,128)(2,1)}, bf16[1,33,1,16,256]{4,3,2,1,0:T(8,128)(2,1)S(1)}, u32[]{:S(2)}) copy-start(bf16[1,33,1,16,256]{4,3,2,1,0:T(8,128)(2,1)S(1)} %slice.160) | copy-start | bytes 811012
  11.1 1.3 %copy-start.8 = (bf16[3,3,256,256]{3,2,1,0:T(8,128)(2,1)S(1)}, bf16[3,3,256,256]{3,2,1,0:T(8,128)(2,1)}, u32[]{:S(2)}) copy-start(bf16[3,3,256,256]{3,2,1,0:T(8,128)(2,1)} %param.10) | copy-start | bytes 3538948
  15.0 1.4 %copy-start.6 = (bf16[3,256,256]{2,1,0:T(8,128)(2,1)S(1)}, bf16[3,256,256]{2,1,0:T(8,128)(2,1)}, u32[]{:S(2)}) copy-start(bf16[3,256,256]{2,1,0:T(8,128)(2,1)} %param.11) | copy-start | bytes 1179652
  16.7 1.1 %copy-start.5 = (f32[33,16,256]{2,1,0:T(8,128)S(1)}, f32[33,16,256]{2,1,0:T(8,128)}, u32[]{:S(2)}) copy-start(f32[33,16,256]{2,1,0:T(8,128)} %convert_element_type.106) | copy-start | bytes 1622020
  17.8 1.1 %copy-start.11 = (s32[1,8]{1,0:T(1,128)S(1)}, s32[1,8]{1,0:T(1,128)}, u32[]{:S(2)}) copy-start(s32[1,8]{1,0:T(1,128)} %param.14) | copy-start | bytes 100
  18.1 0.8 %copy-start.2 = (bf16[33,2,16,256]{3,2,1,0:T(8,128)(2,1)}, bf16[33,2,16,256]{3,2,1,0:T(8,128)(2,1)S(1)}, u32[]{:S(2)}) copy-start(bf16[33,2,16,256]{3,2,1,0:T(8,128)(2,1)S(1)} %fusion.14) | copy-start | bytes 1622020
  18.1 4.5 %copy-start.10 = (f32[256]{0:T(256)S(1)}, f32[256]{0:T(256)}, u32[]{:S(2)}) copy-start(f32[256]{0:T(256)} %param.13) | copy-start | bytes 3076
  20.2 4.0 %collective-permute-start.2 = (f32[1,8,256]{2,1,0:T(8,128)S(1)}, f32[1,8,256]{2,1,0:T(8,128)S(1)}, u32[]{:S(2)}, u32[]{:S(2)}) collective-permute-start(f32[1,8,256]{2,1,0:T(8,128)S(1)} %bitcast.365), channel_id=1, source_target_pairs={{0,1},{1,0},{2,3},{3,2},{4,5},{5,4},{6,7},{7,6},{8,9},{9,8},{10,11... | collective-permute-start | bytes 24584 | tf_op jit(solution)/shard_map/ppermute | solution.py:57
  24.3 4.8 %collective-permute-start.3 = (f32[1,8,256]{2,1,0:T(8,128)S(1)}, f32[1,8,256]{2,1,0:T(8,128)S(1)}, u32[]{:S(2)}, u32[]{:S(2)}) collective-permute-start(f32[1,8,256]{2,1,0:T(8,128)S(1)} %bitcast_add_fusion.5), channel_id=1, source_target_pairs={{0,2},{1,3},{2,0},{3,1},{4,6},{5,7},{6,4},{7,5},{8,10},{9,11},{10,... | collective-permute-start | bytes 24584 | tf_op jit(solution)/shard_map/ppermute | solution.py:57
  27.5 3.2 %copy-start.9 = (bf16[1,33,2,16,256]{4,3,2,1,0:T(8,128)(2,1)S(1)}, bf16[1,33,2,16,256]{4,3,2,1,0:T(8,128)(2,1)}, u32[]{:S(2)}) copy-start(bf16[1,33,2,16,256]{4,3,2,1,0:T(8,128)(2,1)} %param.15) | copy-start | bytes 1622020
  32.5 1.0 %copy-start.7 = (bf16[3,256,256]{2,1,0:T(8,128)(2,1)S(1)}, bf16[3,256,256]{2,1,0:T(8,128)(2,1)}, u32[]{:S(2)}) copy-start(bf16[3,256,256]{2,1,0:T(8,128)(2,1)} %param.11) | copy-start | bytes 1179652
  34.3 1.2 %copy-start.12 = (f32[33,2,16,256]{3,2,1,0:T(8,128)S(1)}, f32[33,2,16,256]{3,2,1,0:T(8,128)}, u32[]{:S(2)}) copy-start(f32[33,2,16,256]{3,2,1,0:T(8,128)} %get-tuple-element.14) | copy-start | bytes 3244036
  36.1 1.0 %copy-start.4 = (bf16[1,33,1,16,256]{4,3,2,1,0:T(8,128)(2,1)S(1)}, bf16[1,33,1,16,256]{4,3,2,1,0:T(8,128)(2,1)}, u32[]{:S(2)}) copy-start(bf16[1,33,1,16,256]{4,3,2,1,0:T(8,128)(2,1)} %copy-done.3) | copy-start | bytes 811012
  40.2 1.4 %copy-start.1 = (f32[9,256,256]{2,1,0:T(8,128)}, f32[9,256,256]{2,1,0:T(8,128)S(1)}, u32[]{:S(2)}) copy-start(f32[9,256,256]{2,1,0:T(8,128)S(1)} %fusion.15) | copy-start | bytes 7077892
  41.7 2.3 %collective-permute-start.4 = (bf16[16,96,256]{2,1,0:T(8,128)(2,1)S(1)}, bf16[16,96,256]{2,1,0:T(8,128)(2,1)S(1)}, u32[]{:S(2)}, u32[]{:S(2)}) collective-permute-start(bf16[16,96,256]{2,1,0:T(8,128)(2,1)S(1)} %bitcast.352), channel_id=1, source_target_pairs={{0,4},{4,0},{8,12},{12,8},{16,20},{20,16},{24,28},{28,24},{1,5},{5... | collective-permute-start | bytes 2359304 | tf_op jit(solution)/shard_map/ppermute | solution.py:74
  44.4 7.0 %collective-permute-start.7 = (bf16[8,48,256]{2,1,0:T(8,128)(2,1)S(1)}, bf16[8,48,256]{2,1,0:T(8,128)(2,1)S(1)}, u32[]{:S(2)}, u32[]{:S(2)}) collective-permute-start(bf16[8,48,256]{2,1,0:T(8,128)(2,1)S(1)} %fusion.52), channel_id=1, source_target_pairs={{0,16},{4,20},{8,24},{12,28},{16,0},{20,4},{24,8},{28,12},{1,17},{... | collective-permute-start | bytes 589832 | tf_op jit(solution)/shard_map/ppermute | solution.py:74
  46.0 7.1 %collective-permute-start.5 = (bf16[8,48,256]{2,1,0:T(8,128)(2,1)S(1)}, bf16[8,48,256]{2,1,0:T(8,128)(2,1)S(1)}, u32[]{:S(2)}, u32[]{:S(2)}) collective-permute-start(bf16[8,48,256]{2,1,0:T(8,128)(2,1)S(1)} %bitcast.357), channel_id=1, source_target_pairs={{0,8},{4,12},{8,0},{12,4},{16,24},{20,28},{24,16},{28,20},{1,9},{5... | collective-permute-start | bytes 589832 | tf_op jit(solution)/shard_map/ppermute | solution.py:74
  51.5 4.7 %collective-permute-start.8 = (bf16[4,48,256]{2,1,0:T(8,128)(2,1)S(1)}, bf16[4,48,256]{2,1,0:T(8,128)(2,1)S(1)}, u32[]{:S(2)}, u32[]{:S(2)}) collective-permute-start(bf16[4,48,256]{2,1,0:T(8,128)(2,1)S(1)} %fusion.95), channel_id=1, source_target_pairs={{0,8},{4,12},{8,0},{12,4},{16,24},{20,28},{24,16},{28,20},{1,9},{5... | collective-permute-start | bytes 294920 | tf_op jit(solution)/shard_map/ppermute | solution.py:74
  53.1 4.7 %collective-permute-start.6 = (bf16[4,48,256]{2,1,0:T(8,128)(2,1)S(1)}, bf16[4,48,256]{2,1,0:T(8,128)(2,1)S(1)}, u32[]{:S(2)}, u32[]{:S(2)}) collective-permute-start(bf16[4,48,256]{2,1,0:T(8,128)(2,1)S(1)} %fusion.94), channel_id=1, source_target_pairs={{0,16},{4,20},{8,24},{12,28},{16,0},{20,4},{24,8},{28,12},{1,17},{... | collective-permute-start | bytes 294920 | tf_op jit(solution)/shard_map/ppermute | solution.py:74
  57.9 7.6 %collective-permute-start.9 = (f32[96,256]{1,0:T(8,128)S(1)}, f32[96,256]{1,0:T(8,128)S(1)}, u32[]{:S(2)}, u32[]{:S(2)}) collective-permute-start(f32[96,256]{1,0:T(8,128)S(1)} %get-tuple-element.7), channel_id=1, source_target_pairs={{0,1},{1,2},{2,3},{3,0},{4,5},{5,6},{6,7},{7,4},{8,9},{9,10},{10,1... | collective-permute-start | bytes 294920 | tf_op jit(solution)/shard_map/ppermute | solution.py:109
  59.9 8.2 %collective-permute-start.10 = (f32[96,256]{1,0:T(8,128)S(1)}, f32[96,256]{1,0:T(8,128)S(1)}, u32[]{:S(2)}, u32[]{:S(2)}) collective-permute-start(f32[96,256]{1,0:T(8,128)S(1)} %get-tuple-element.9), channel_id=1, source_target_pairs={{0,2},{1,3},{2,0},{3,1},{4,6},{5,7},{6,4},{7,5},{8,10},{9,11},{10,... | collective-permute-start | bytes 294920 | tf_op jit(solution)/shard_map/ppermute | solution.py:109
  62.5 5.7 %collective-permute-start.11 = (f32[96,256]{1,0:T(8,128)S(1)}, f32[96,256]{1,0:T(8,128)S(1)}, u32[]{:S(2)}, u32[]{:S(2)}) collective-permute-start(f32[96,256]{1,0:T(8,128)S(1)} %get-tuple-element.10), channel_id=1, source_target_pairs={{0,3},{1,0},{2,1},{3,2},{4,7},{5,4},{6,5},{7,6},{8,11},{9,8},{10,9... | collective-permute-start | bytes 294920 | tf_op jit(solution)/shard_map/ppermute | solution.py:109

commit v9 on v8

--- a/solution.py
+++ b/solution.py
@@ -13,11 +13,13 @@
 
 def exchange_rows(cells, axis, dim):
     count = lax.axis_size(axis)
-    ends = count - 1
+    me = lax.axis_index(axis)
     head = lax.slice_in_dim(cells, 0, 1, axis=dim)
     tail = lax.slice_in_dim(cells, cells.shape[dim] - 1, cells.shape[dim], axis=dim)
-    above = lax.ppermute(tail, axis, [(i, i + 1) for i in range(ends)])
-    below = lax.ppermute(head, axis, [(i + 1, i) for i in range(ends)])
+    above = lax.ppermute(tail, axis, [(i, (i + 1) % count) for i in range(count)])
+    below = lax.ppermute(head, axis, [((i + 1) % count, i) for i in range(count)])
+    above = jnp.where(me == 0, jnp.zeros_like(above), above)
+    below = jnp.where(me == count - 1, jnp.zeros_like(below), below)
     return above, below
 
 

time: 70.1 us -> 71.2 us (1.016)
  waiting for transfers between devices: 14.9 us -> 23.5 us
  starting transfers between devices: 24.8 us -> 17.4 us
    ppermute x2, waiting for transfers between devices: 0.2 us -> 4.09 us  [the longest x1 2.48 us: exchange_rows(): lax.ppermute(tail, axis, [(i, (i + 1) % count) for i in range(count)])]
    ppermute x2, starting transfers between devices: 5.59 us -> 1.99 us  [space_sum(): lax.ppermute(values, 'space', [(i, i ^ step) for i in range(count)])]
    ppermute x2, waiting for transfers between devices: 3.24 us -> 6.2 us  [space_sum(): lax.ppermute(values, 'space', [(i, i ^ step) for i in range(count)])]
    ppermute x3, starting transfers between devices: 5.96 us -> 4.01 us  [halving_scatter(): lax.ppermute(send, 'space', [(i, (i + shift) % ns) for i in range(ns)])]
    ppermute x2, starting transfers between devices: 7.02 us -> 5.13 us  [the longest x1 5.13 us: exchange_rows(): lax.ppermute(head, axis, [((i + 1) % count, i) for i in range(count)])]
    ppermute x3, waiting for transfers between devices: 4.21 us -> 5.87 us  [halving_scatter(): lax.ppermute(send, 'space', [(i, (i + shift) % ns) for i in range(ns)])]
  transfers between devices with their start and end apart: 12 -> 12, of which waited for: 9 -> 10; matrix products, arithmetic and copies ran while one was open for 7% -> 6% of each run, Pallas kernels for 0% -> 0%
where the time goes in v9:
time: 71.2 us; the launch traced here: 70.8 us
  waiting for transfers between devices  23.5 us (33%)
  starting transfers between devices  17.4 us (24%)
  matrix products  13.3 us (19%)
  local copies, waits for them, and re-layouts  7.64 us (11%)
  other arithmetic  7.09 us (10%)
  between operations  1.85 us (3%)
    ppermute x5, waiting for transfers between devices, _halve(): got = lax.ppermute(send, axis, [(i, i ^ 1 << bit) for i in range(size)])  7.3 us
    ppermute x5, starting transfers between devices, _halve(): got = lax.ppermute(send, axis, [(i, i ^ 1 << bit) for i in range(size)])  6.26 us
    ppermute x2, waiting for transfers between devices, space_sum(): lax.ppermute(values, 'space', [(i, i ^ step) for i in range(count)])  6.2 us
    ppermute x3, waiting for transfers between devices, halving_scatter(): lax.ppermute(send, 'space', [(i, (i + shift) % ns) for i in range(ns)])  5.87 us
    unnamed x42, local copies, waits for them, and re-layouts  5.42 us
    ppermute x1, starting transfers between devices, exchange_rows(): lax.ppermute(head, axis, [((i + 1) % count, i) for i in range(count)])  5.13 us
    ppermute x3, starting transfers between devices, halving_scatter(): lax.ppermute(send, 'space', [(i, (i + shift) % ns) for i in range(ns)])  4.01 us
    dot_general x9, matrix products, on_device(): jnp.einsum('nfhwc,cd->nfhwd', window, spatial_weight[row_tap, col_tap], p...  3.89 us
  transfers between devices with their start and end apart: 12, of which 10 were waited for; matrix products, arithmetic and copies ran while one was open for 6% of the time, Pallas kernels for 0%

profile of v9, /device:TPU:0, one launch (start us, length us, event | category | flops | bytes accessed | tf_op | source)
XLA Modules:
  0.0 70.8 jit_solution(7838468884227659777)
XLA Ops:
  0.6 5.1 %collective-permute-start.1 = (bf16[1,33,1,8,256]{4,3,2,1,0:T(8,128)(2,1)}, bf16[1,33,1,8,256]{4,3,2,1,0:T(8,128)(2,1)S(1)}, u32[]{:S(2)}, u32[]{:S(2)}) collective-permute-start(bf16[1,33,1,8,256]{4,3,2,1,0:T(8,128)(2,1)} %param.8), channel_id=1, source_target_pairs={{1,0},{2,1},{3,2},{0,3},{5,4},{6,5},{7,6},{4,7},{9,8},{10,9},{11,1... | collective-permute-start | bytes 405512 | tf_op jit(solution)/shard_map/ppermute | solution.py:20
  6.4 1.1 %broadcast_in_dim.16 = bf16[33,8,2,256]{3,2,1,0:T(2,128)(2,1)S(1)} broadcast(bf16[33,8,256]{2,1,0:T(8,128)(2,1)} %bitcast.360), dimensions={0,1,3} | broadcast | bytes 405504 | tf_op jit(solution)/shard_map/broadcast_in_dim | solution.py:28
  7.6 0.9 %convert_element_type.106 = f32[33,16,256]{2,1,0:T(8,128)} convert(bf16[33,16,256]{2,1,0:T(8,128)(2,1)S(1)} %broadcast_in_dim.17) | non-fusion elementwise | flops 135168 | bytes 811008 | tf_op jit(solution)/shard_map/convert_element_type | solution.py:162
  8.5 1.6 %collective-permute-done.1 = bf16[1,33,1,8,256]{4,3,2,1,0:T(8,128)(2,1)S(1)} collective-permute-done((bf16[1,33,1,8,256]{4,3,2,1,0:T(8,128)(2,1)}, bf16[1,33,1,8,256]{4,3,2,1,0:T(8,128)(2,1)S(1)}, u32[]{:S(2)}, u32[]{:S(2)}) %collective-permute-start.1) | collective-permute-done | bytes 135200 | tf_op jit(solution)/shard_map/ppermute | solution.py:20
  10.3 2.5 %collective-permute-done = bf16[1,33,1,8,256]{4,3,2,1,0:T(8,128)(2,1)S(1)} collective-permute-done((bf16[1,33,1,8,256]{4,3,2,1,0:T(8,128)(2,1)}, bf16[1,33,1,8,256]{4,3,2,1,0:T(8,128)(2,1)S(1)}, u32[]{:S(2)}, u32[]{:S(2)}) %collective-permute-start) | collective-permute-done | bytes 135200 | tf_op jit(solution)/shard_map/ppermute | solution.py:19
  13.2 0.9 %fusion.5 = bf16[1,33,4,18,256]{4,3,2,1,0:T(8,128)(2,1)S(1)} fusion(bf16[1,33,1,16,256]{4,3,2,1,0:T(8,128)(2,1)S(1)} %slice.161, bf16[1,33,2,16,256]{4,3,2,1,0:T(8,128)(2,1)S(1)} %broadcast_in_dim.40, bf16[1,33,1,16,256]{4,3,2,1,0:T(8,128)(2,1)S(1)} %slice.160), kind=kLoop, calls=%fused_computation.9 | loop fusion | flops 7299072 | bytes 2297856 | tf_op jit(solution)/shard_map/concatenate | solution.py:134
  14.1 0.4 copy-done.8
  17.0 1.4 %multiply_convert_fusion = (bf16[33,2,16,256]{3,2,1,0:T(8,128)(2,1)S(1)}, f32[33,2,16,256]{3,2,1,0:T(8,128)}) fusion(f32[33,2,16,256]{3,2,1,0:T(8,128)S(1)} %convolution_add_fusion.5, bf16[3,3,256,256]{3,2,1,0:T(8,128)(2,1)S(1)} %copy-done.8, bf16[1,33,4,18,256]{4,3,2,1,0:T(8,128)(2,1)S(1)} %fusion.5), kind=kOutput, calls=%fused_computation.56 | convolution fusion | flops 140034048 | bytes 3375104 | tf_op jit(solution)/shard_map/nfhwc,cd->nfhwd/dot_general | solution.py:144
  19.1 0.7 %copy-done.5 = f32[33,16,256]{2,1,0:T(8,128)S(1)} copy-done((f32[33,16,256]{2,1,0:T(8,128)S(1)}, f32[33,16,256]{2,1,0:T(8,128)}, u32[]{:S(2)}) %copy-start.5) | copy-done | bytes 540696
  20.2 0.8 %copy-done.2 = bf16[33,2,16,256]{3,2,1,0:T(8,128)(2,1)} copy-done((bf16[33,2,16,256]{3,2,1,0:T(8,128)(2,1)}, bf16[33,2,16,256]{3,2,1,0:T(8,128)(2,1)S(1)}, u32[]{:S(2)}) %copy-start.2) | copy-done | bytes 540696
  20.9 0.4 fusion.24
  21.4 0.9 %fusion.51 = (f32[8,256]{1,0:T(8,128)S(1)}, f32[8,2,16,256]{3,2,1,0:T(8,128)}) fusion(bf16[256,256]{1,0:T(8,128)(2,1)S(1)} %copy-done, bf16[8,2,16,256]{3,0,2,1:T(8,128)(2,1)S(1)} %fusion.24), kind=kOutput, calls=%fused_computation.108 | convolution fusion | flops 34142208 | bytes 532480 | tf_op jit(solution)/shard_map/nqhwc,ce->nqhwe/dot_general | solution.py:169
  22.3 1.4 %collective-permute-start.2 = (f32[1,8,256]{2,1,0:T(8,128)S(1)}, f32[1,8,256]{2,1,0:T(8,128)S(1)}, u32[]{:S(2)}, u32[]{:S(2)}) collective-permute-start(f32[1,8,256]{2,1,0:T(8,128)S(1)} %bitcast.365), channel_id=1, source_target_pairs={{0,1},{1,0},{2,3},{3,2},{4,5},{5,4},{6,7},{7,6},{8,9},{9,8},{10,11... | collective-permute-start | bytes 24584 | tf_op jit(solution)/shard_map/ppermute | solution.py:59
  23.8 2.2 %collective-permute-done.2 = f32[1,8,256]{2,1,0:T(8,128)S(1)} collective-permute-done((f32[1,8,256]{2,1,0:T(8,128)S(1)}, f32[1,8,256]{2,1,0:T(8,128)S(1)}, u32[]{:S(2)}, u32[]{:S(2)}) %collective-permute-start.2) | collective-permute-done | bytes 8224 | tf_op jit(solution)/shard_map/ppermute | solution.py:59
  26.0 0.5 collective-permute-start.3
  26.5 4.0 %collective-permute-done.3 = f32[1,8,256]{2,1,0:T(8,128)S(1)} collective-permute-done((f32[1,8,256]{2,1,0:T(8,128)S(1)}, f32[1,8,256]{2,1,0:T(8,128)S(1)}, u32[]{:S(2)}, u32[]{:S(2)}) %collective-permute-start.3) | collective-permute-done | bytes 8224 | tf_op jit(solution)/shard_map/ppermute | solution.py:59
  30.7 1.1 %fusion.49 = bf16[8,2,16,256]{3,2,1,0:T(8,128)(2,1)S(1)} fusion(f32[8,2,16,256]{3,2,1,0:T(8,128)} %get-tuple-element.16, f32[8,256]{1,0:T(8,128)S(1)} %get-tuple-element.12, f32[8,256]{1,0:T(8,128)S(1)} %get-tuple-element.11), kind=kLoop, calls=%fused_computation.104 | loop fusion | flops 1245184 | bytes 409600 | tf_op jit(solution)/shard_map/convert_element_type | solution.py:176
  32.1 1.0 %fusion.12 = bf16[1,33,2,16,256]{4,1,3,2,0:T(8,128)(2,1)S(1)} fusion(f32[8,2,16,256]{3,0,2,1:T(8,128)S(1)} %fusion.59, bf16[1,33,2,16,256]{4,3,2,1,0:T(8,128)(2,1)S(1)} %copy-done.9, f32[33]{0:T(128)S(1)} %compare_select_fusion, s32[8]{0:T(128)S(1)} %bitcast.367), kind=kOutput, calls=%fused_computation.32 | convolution fusion | flops 27033864 | bytes 1343652 | tf_op jit(solution)/shard_map/nqf,nqhwc->nfhwc/dot_general | solution.py:185
  34.3 0.6 copy-done.7
  35.2 0.4 slice_bitcast_fusion
  36.0 0.9 %copy-done.12 = f32[33,2,16,256]{3,2,1,0:T(8,128)S(1)} copy-done((f32[33,2,16,256]{3,2,1,0:T(8,128)S(1)}, f32[33,2,16,256]{3,2,1,0:T(8,128)}, u32[]{:S(2)}) %copy-start.12) | copy-done | bytes 1081368
  36.9 0.6 fusion.13
  37.5 0.4 fusion.23
  37.9 0.6 copy-done.4
  38.4 0.4 fusion.22
  38.9 0.4 fusion.21
  39.6 0.4 fusion.19
  40.0 0.4 fusion.18
  40.4 0.4 fusion.17
  40.8 0.4 fusion.16
  41.3 0.4 fusion.15
  41.9 1.2 %copy-done.1 = f32[9,256,256]{2,1,0:T(8,128)} copy-done((f32[9,256,256]{2,1,0:T(8,128)}, f32[9,256,256]{2,1,0:T(8,128)S(1)}, u32[]{:S(2)}) %copy-start.1) | copy-done | bytes 2359320
  43.1 1.8 %broadcast_select_fusion = f32[4,1,4,96,256]{4,3,2,1,0:T(8,128)S(1)} fusion(pred[]{:T(512)S(6)} %eq.61, f32[4,2,4,24,256]{4,3,2,1,0:T(8,128)S(1)} %bitcast.336, f32[4,2,4,72,256]{4,3,2,1,0:T(8,128)} %bitcast.334), kind=kLoop, calls=%fused_computation.59 | loop fusion | flops 1179648 | bytes 4718593 | tf_op jit(solution)/shard_map/jit(_where)/select_n | solution.py:71
  44.9 0.4 collective-permute-done.4
  45.8 1.6 %collective-permute-start.7 = (bf16[8,48,256]{2,1,0:T(8,128)(2,1)S(1)}, bf16[8,48,256]{2,1,0:T(8,128)(2,1)S(1)}, u32[]{:S(2)}, u32[]{:S(2)}) collective-permute-start(bf16[8,48,256]{2,1,0:T(8,128)(2,1)S(1)} %fusion.52), channel_id=1, source_target_pairs={{0,16},{4,20},{8,24},{12,28},{16,0},{20,4},{24,8},{28,12},{1,17},{... | collective-permute-start | bytes 589832 | tf_op jit(solution)/shard_map/ppermute | solution.py:76
  47.4 1.5 %collective-permute-start.5 = (bf16[8,48,256]{2,1,0:T(8,128)(2,1)S(1)}, bf16[8,48,256]{2,1,0:T(8,128)(2,1)S(1)}, u32[]{:S(2)}, u32[]{:S(2)}) collective-permute-start(bf16[8,48,256]{2,1,0:T(8,128)(2,1)S(1)} %bitcast.359), channel_id=1, source_target_pairs={{0,8},{4,12},{8,0},{12,4},{16,24},{20,28},{24,16},{28,20},{1,9},{5... | collective-permute-start | bytes 589832 | tf_op jit(solution)/shard_map/ppermute | solution.py:76
  49.0 3.8 %collective-permute-done.7 = bf16[8,48,256]{2,1,0:T(8,128)(2,1)S(1)} collective-permute-done((bf16[8,48,256]{2,1,0:T(8,128)(2,1)S(1)}, bf16[8,48,256]{2,1,0:T(8,128)(2,1)S(1)}, u32[]{:S(2)}, u32[]{:S(2)}) %collective-permute-start.7) | collective-permute-done | bytes 196640 | tf_op jit(solution)/shard_map/ppermute | solution.py:76
  52.9 1.6 %collective-permute-start.8 = (bf16[4,48,256]{2,1,0:T(8,128)(2,1)S(1)}, bf16[4,48,256]{2,1,0:T(8,128)(2,1)S(1)}, u32[]{:S(2)}, u32[]{:S(2)}) collective-permute-start(bf16[4,48,256]{2,1,0:T(8,128)(2,1)S(1)} %fusion.95), channel_id=1, source_target_pairs={{0,8},{4,12},{8,0},{12,4},{16,24},{20,28},{24,16},{28,20},{1,9},{5... | collective-permute-start | bytes 294920 | tf_op jit(solution)/shard_map/ppermute | solution.py:76
  54.5 1.6 %collective-permute-start.6 = (bf16[4,48,256]{2,1,0:T(8,128)(2,1)S(1)}, bf16[4,48,256]{2,1,0:T(8,128)(2,1)S(1)}, u32[]{:S(2)}, u32[]{:S(2)}) collective-permute-start(bf16[4,48,256]{2,1,0:T(8,128)(2,1)S(1)} %fusion.94), channel_id=1, source_target_pairs={{0,16},{4,20},{8,24},{12,28},{16,0},{20,4},{24,8},{28,12},{1,17},{... | collective-permute-start | bytes 294920 | tf_op jit(solution)/shard_map/ppermute | solution.py:76
  56.1 1.5 %collective-permute-done.8 = bf16[4,48,256]{2,1,0:T(8,128)(2,1)S(1)} collective-permute-done((bf16[4,48,256]{2,1,0:T(8,128)(2,1)S(1)}, bf16[4,48,256]{2,1,0:T(8,128)(2,1)S(1)}, u32[]{:S(2)}, u32[]{:S(2)}) %collective-permute-start.8) | collective-permute-done | bytes 98336 | tf_op jit(solution)/shard_map/ppermute | solution.py:76
  57.6 1.6 %collective-permute-done.6 = bf16[4,48,256]{2,1,0:T(8,128)(2,1)S(1)} collective-permute-done((bf16[4,48,256]{2,1,0:T(8,128)(2,1)S(1)}, bf16[4,48,256]{2,1,0:T(8,128)(2,1)S(1)}, u32[]{:S(2)}, u32[]{:S(2)}) %collective-permute-start.6) | collective-permute-done | bytes 98336 | tf_op jit(solution)/shard_map/ppermute | solution.py:76
  59.3 1.5 %collective-permute-start.9 = (f32[96,256]{1,0:T(8,128)S(1)}, f32[96,256]{1,0:T(8,128)S(1)}, u32[]{:S(2)}, u32[]{:S(2)}) collective-permute-start(f32[96,256]{1,0:T(8,128)S(1)} %get-tuple-element.7), channel_id=1, source_target_pairs={{0,1},{1,2},{2,3},{3,0},{4,5},{5,6},{6,7},{7,4},{8,9},{9,10},{10,1... | collective-permute-start | bytes 294920 | tf_op jit(solution)/shard_map/ppermute | solution.py:111
  60.8 0.9 %collective-permute-start.10 = (f32[96,256]{1,0:T(8,128)S(1)}, f32[96,256]{1,0:T(8,128)S(1)}, u32[]{:S(2)}, u32[]{:S(2)}) collective-permute-start(f32[96,256]{1,0:T(8,128)S(1)} %get-tuple-element.9), channel_id=1, source_target_pairs={{0,2},{1,3},{2,0},{3,1},{4,6},{5,7},{6,4},{7,5},{8,10},{9,11},{10,... | collective-permute-start | bytes 294920 | tf_op jit(solution)/shard_map/ppermute | solution.py:111
  61.8 1.6 %collective-permute-start.11 = (f32[96,256]{1,0:T(8,128)S(1)}, f32[96,256]{1,0:T(8,128)S(1)}, u32[]{:S(2)}, u32[]{:S(2)}) collective-permute-start(f32[96,256]{1,0:T(8,128)S(1)} %get-tuple-element.10), channel_id=1, source_target_pairs={{0,3},{1,0},{2,1},{3,2},{4,7},{5,4},{6,5},{7,6},{8,11},{9,8},{10,9... | collective-permute-start | bytes 294920 | tf_op jit(solution)/shard_map/ppermute | solution.py:111
  63.4 2.9 %collective-permute-done.9 = f32[96,256]{1,0:T(8,128)S(1)} collective-permute-done((f32[96,256]{1,0:T(8,128)S(1)}, f32[96,256]{1,0:T(8,128)S(1)}, u32[]{:S(2)}, u32[]{:S(2)}) %collective-permute-start.9) | collective-permute-done | bytes 98336 | tf_op jit(solution)/shard_map/ppermute | solution.py:111
  66.3 3.0 %collective-permute-done.10 = f32[96,256]{1,0:T(8,128)S(1)} collective-permute-done((f32[96,256]{1,0:T(8,128)S(1)}, f32[96,256]{1,0:T(8,128)S(1)}, u32[]{:S(2)}, u32[]{:S(2)}) %collective-permute-start.10) | collective-permute-done | bytes 98336 | tf_op jit(solution)/shard_map/ppermute | solution.py:111
  69.5 0.7 add_add_fusion
  70.2 0.6 add_add_fusion.1
  (86 shorter events, 7.9 us)
Async XLA Ops:
  0.6 20.8 %copy-start = (bf16[256,256]{1,0:T(8,128)(2,1)S(1)}, bf16[256,256]{1,0:T(8,128)(2,1)}, u32[]{:S(2)}) copy-start(bf16[256,256]{1,0:T(8,128)(2,1)} %param.12) | copy-start | bytes 393220
  0.6 9.4 %collective-permute-start.1 = (bf16[1,33,1,8,256]{4,3,2,1,0:T(8,128)(2,1)}, bf16[1,33,1,8,256]{4,3,2,1,0:T(8,128)(2,1)S(1)}, u32[]{:S(2)}, u32[]{:S(2)}) collective-permute-start(bf16[1,33,1,8,256]{4,3,2,1,0:T(8,128)(2,1)} %param.8), channel_id=1, source_target_pairs={{1,0},{2,1},{3,2},{0,3},{5,4},{6,5},{7,6},{4,7},{9,8},{10,9},{11,1... | collective-permute-start | bytes 405512 | tf_op jit(solution)/shard_map/ppermute | solution.py:20
  5.8 7.1 %collective-permute-start = (bf16[1,33,1,8,256]{4,3,2,1,0:T(8,128)(2,1)}, bf16[1,33,1,8,256]{4,3,2,1,0:T(8,128)(2,1)S(1)}, u32[]{:S(2)}, u32[]{:S(2)}) collective-permute-start(bf16[1,33,1,8,256]{4,3,2,1,0:T(8,128)(2,1)} %param.8), channel_id=1, source_target_pairs={{0,1},{1,2},{2,3},{3,0},{4,5},{5,6},{6,7},{7,4},{8,9},{9,10},{10,1... | collective-permute-start | bytes 405512 | tf_op jit(solution)/shard_map/ppermute | solution.py:19
  13.1 1.7 %copy-start.3 = (bf16[1,33,1,16,256]{4,3,2,1,0:T(8,128)(2,1)}, bf16[1,33,1,16,256]{4,3,2,1,0:T(8,128)(2,1)S(1)}, u32[]{:S(2)}) copy-start(bf16[1,33,1,16,256]{4,3,2,1,0:T(8,128)(2,1)S(1)} %slice.160) | copy-start | bytes 811012
  13.2 1.3 %copy-start.8 = (bf16[3,3,256,256]{3,2,1,0:T(8,128)(2,1)S(1)}, bf16[3,3,256,256]{3,2,1,0:T(8,128)(2,1)}, u32[]{:S(2)}) copy-start(bf16[3,3,256,256]{3,2,1,0:T(8,128)(2,1)} %param.10) | copy-start | bytes 3538948
  17.0 1.4 %copy-start.6 = (bf16[3,256,256]{2,1,0:T(8,128)(2,1)S(1)}, bf16[3,256,256]{2,1,0:T(8,128)(2,1)}, u32[]{:S(2)}) copy-start(bf16[3,256,256]{2,1,0:T(8,128)(2,1)} %param.11) | copy-start | bytes 1179652
  18.8 1.1 %copy-start.5 = (f32[33,16,256]{2,1,0:T(8,128)S(1)}, f32[33,16,256]{2,1,0:T(8,128)}, u32[]{:S(2)}) copy-start(f32[33,16,256]{2,1,0:T(8,128)} %convert_element_type.106) | copy-start | bytes 1622020
  19.8 1.1 %copy-start.11 = (s32[1,8]{1,0:T(1,128)S(1)}, s32[1,8]{1,0:T(1,128)}, u32[]{:S(2)}) copy-start(s32[1,8]{1,0:T(1,128)} %param.14) | copy-start | bytes 100
  20.1 0.8 %copy-start.2 = (bf16[33,2,16,256]{3,2,1,0:T(8,128)(2,1)}, bf16[33,2,16,256]{3,2,1,0:T(8,128)(2,1)S(1)}, u32[]{:S(2)}) copy-start(bf16[33,2,16,256]{3,2,1,0:T(8,128)(2,1)S(1)} %fusion.14) | copy-start | bytes 1622020
  20.1 3.6 %copy-start.10 = (f32[256]{0:T(256)S(1)}, f32[256]{0:T(256)}, u32[]{:S(2)}) copy-start(f32[256]{0:T(256)} %param.13) | copy-start | bytes 3076
  22.3 3.7 %collective-permute-start.2 = (f32[1,8,256]{2,1,0:T(8,128)S(1)}, f32[1,8,256]{2,1,0:T(8,128)S(1)}, u32[]{:S(2)}, u32[]{:S(2)}) collective-permute-start(f32[1,8,256]{2,1,0:T(8,128)S(1)} %bitcast.365), channel_id=1, source_target_pairs={{0,1},{1,0},{2,3},{3,2},{4,5},{5,4},{6,7},{7,6},{8,9},{9,8},{10,11... | collective-permute-start | bytes 24584 | tf_op jit(solution)/shard_map/ppermute | solution.py:59
  26.0 4.5 %collective-permute-start.3 = (f32[1,8,256]{2,1,0:T(8,128)S(1)}, f32[1,8,256]{2,1,0:T(8,128)S(1)}, u32[]{:S(2)}, u32[]{:S(2)}) collective-permute-start(f32[1,8,256]{2,1,0:T(8,128)S(1)} %bitcast_add_fusion.5), channel_id=1, source_target_pairs={{0,2},{1,3},{2,0},{3,1},{4,6},{5,7},{6,4},{7,5},{8,10},{9,11},{10,... | collective-permute-start | bytes 24584 | tf_op jit(solution)/shard_map/ppermute | solution.py:59
  26.5 5.6 %copy-start.9 = (bf16[1,33,2,16,256]{4,3,2,1,0:T(8,128)(2,1)S(1)}, bf16[1,33,2,16,256]{4,3,2,1,0:T(8,128)(2,1)}, u32[]{:S(2)}) copy-start(bf16[1,33,2,16,256]{4,3,2,1,0:T(8,128)(2,1)} %param.15) | copy-start | bytes 1622020
  33.9 1.0 %copy-start.7 = (bf16[3,256,256]{2,1,0:T(8,128)(2,1)S(1)}, bf16[3,256,256]{2,1,0:T(8,128)(2,1)}, u32[]{:S(2)}) copy-start(bf16[3,256,256]{2,1,0:T(8,128)(2,1)} %param.11) | copy-start | bytes 1179652
  35.7 1.2 %copy-start.12 = (f32[33,2,16,256]{3,2,1,0:T(8,128)S(1)}, f32[33,2,16,256]{3,2,1,0:T(8,128)}, u32[]{:S(2)}) copy-start(f32[33,2,16,256]{3,2,1,0:T(8,128)} %get-tuple-element.14) | copy-start | bytes 3244036
  37.5 1.0 %copy-start.4 = (bf16[1,33,1,16,256]{4,3,2,1,0:T(8,128)(2,1)S(1)}, bf16[1,33,1,16,256]{4,3,2,1,0:T(8,128)(2,1)}, u32[]{:S(2)}) copy-start(bf16[1,33,1,16,256]{4,3,2,1,0:T(8,128)(2,1)} %copy-done.3) | copy-start | bytes 811012
  41.7 1.4 %copy-start.1 = (f32[9,256,256]{2,1,0:T(8,128)}, f32[9,256,256]{2,1,0:T(8,128)S(1)}, u32[]{:S(2)}) copy-start(f32[9,256,256]{2,1,0:T(8,128)S(1)} %fusion.15) | copy-start | bytes 7077892
  43.1 2.3 %collective-permute-start.4 = (bf16[16,96,256]{2,1,0:T(8,128)(2,1)S(1)}, bf16[16,96,256]{2,1,0:T(8,128)(2,1)S(1)}, u32[]{:S(2)}, u32[]{:S(2)}) collective-permute-start(bf16[16,96,256]{2,1,0:T(8,128)(2,1)S(1)} %bitcast.354), channel_id=1, source_target_pairs={{0,4},{4,0},{8,12},{12,8},{16,20},{20,16},{24,28},{28,24},{1,5},{5... | collective-permute-start | bytes 2359304 | tf_op jit(solution)/shard_map/ppermute | solution.py:76
  45.8 7.0 %collective-permute-start.7 = (bf16[8,48,256]{2,1,0:T(8,128)(2,1)S(1)}, bf16[8,48,256]{2,1,0:T(8,128)(2,1)S(1)}, u32[]{:S(2)}, u32[]{:S(2)}) collective-permute-start(bf16[8,48,256]{2,1,0:T(8,128)(2,1)S(1)} %fusion.52), channel_id=1, source_target_pairs={{0,16},{4,20},{8,24},{12,28},{16,0},{20,4},{24,8},{28,12},{1,17},{... | collective-permute-start | bytes 589832 | tf_op jit(solution)/shard_map/ppermute | solution.py:76
  47.4 7.1 %collective-permute-start.5 = (bf16[8,48,256]{2,1,0:T(8,128)(2,1)S(1)}, bf16[8,48,256]{2,1,0:T(8,128)(2,1)S(1)}, u32[]{:S(2)}, u32[]{:S(2)}) collective-permute-start(bf16[8,48,256]{2,1,0:T(8,128)(2,1)S(1)} %bitcast.359), channel_id=1, source_target_pairs={{0,8},{4,12},{8,0},{12,4},{16,24},{20,28},{24,16},{28,20},{1,9},{5... | collective-permute-start | bytes 589832 | tf_op jit(solution)/shard_map/ppermute | solution.py:76
  52.9 4.7 %collective-permute-start.8 = (bf16[4,48,256]{2,1,0:T(8,128)(2,1)S(1)}, bf16[4,48,256]{2,1,0:T(8,128)(2,1)S(1)}, u32[]{:S(2)}, u32[]{:S(2)}) collective-permute-start(bf16[4,48,256]{2,1,0:T(8,128)(2,1)S(1)} %fusion.95), channel_id=1, source_target_pairs={{0,8},{4,12},{8,0},{12,4},{16,24},{20,28},{24,16},{28,20},{1,9},{5... | collective-permute-start | bytes 294920 | tf_op jit(solution)/shard_map/ppermute | solution.py:76
  54.5 4.7 %collective-permute-start.6 = (bf16[4,48,256]{2,1,0:T(8,128)(2,1)S(1)}, bf16[4,48,256]{2,1,0:T(8,128)(2,1)S(1)}, u32[]{:S(2)}, u32[]{:S(2)}) collective-permute-start(bf16[4,48,256]{2,1,0:T(8,128)(2,1)S(1)} %fusion.94), channel_id=1, source_target_pairs={{0,16},{4,20},{8,24},{12,28},{16,0},{20,4},{24,8},{28,12},{1,17},{... | collective-permute-start | bytes 294920 | tf_op jit(solution)/shard_map/ppermute | solution.py:76
  59.3 7.0 %collective-permute-start.9 = (f32[96,256]{1,0:T(8,128)S(1)}, f32[96,256]{1,0:T(8,128)S(1)}, u32[]{:S(2)}, u32[]{:S(2)}) collective-permute-start(f32[96,256]{1,0:T(8,128)S(1)} %get-tuple-element.7), channel_id=1, source_target_pairs={{0,1},{1,2},{2,3},{3,0},{4,5},{5,6},{6,7},{7,4},{8,9},{9,10},{10,1... | collective-permute-start | bytes 294920 | tf_op jit(solution)/shard_map/ppermute | solution.py:111
  60.8 8.4 %collective-permute-start.10 = (f32[96,256]{1,0:T(8,128)S(1)}, f32[96,256]{1,0:T(8,128)S(1)}, u32[]{:S(2)}, u32[]{:S(2)}) collective-permute-start(f32[96,256]{1,0:T(8,128)S(1)} %get-tuple-element.9), channel_id=1, source_target_pairs={{0,2},{1,3},{2,0},{3,1},{4,6},{5,7},{6,4},{7,5},{8,10},{9,11},{10,... | collective-permute-start | bytes 294920 | tf_op jit(solution)/shard_map/ppermute | solution.py:111
  61.8 7.6 %collective-permute-start.11 = (f32[96,256]{1,0:T(8,128)S(1)}, f32[96,256]{1,0:T(8,128)S(1)}, u32[]{:S(2)}, u32[]{:S(2)}) collective-permute-start(f32[96,256]{1,0:T(8,128)S(1)} %get-tuple-element.10), channel_id=1, source_target_pairs={{0,3},{1,0},{2,1},{3,2},{4,7},{5,4},{6,5},{7,6},{8,11},{9,8},{10,9... | collective-permute-start | bytes 294920 | tf_op jit(solution)/shard_map/ppermute | solution.py:111

commit v10 on v8

--- a/solution.py
+++ b/solution.py
@@ -106,7 +106,8 @@
         terms = [lax.dynamic_index_in_dim(cur, me, 0, keepdims=False)]
         for shift in range(1, ns):
             send = lax.dynamic_index_in_dim(cur, (me + shift) % ns, 0, keepdims=False)
-            terms.append(lax.ppermute(send, "space", [(i, (i + shift) % ns) for i in range(ns)]))
+            got = lax.ppermute(send.astype(jnp.bfloat16), "space", [(i, (i + shift) % ns) for i in range(ns)])
+            terms.append(got.astype(cur.dtype))
         return terms
     for axis, bit in rest:
         cur = _halve(cur, part_left, axis, bit)

time: 70.1 us -> 68.7 us (0.980)
  waiting for transfers between devices: 14.9 us -> 13.4 us
    ppermute x3, waiting for transfers between devices: 4.21 us -> 2.66 us  [halving_scatter(): lax.ppermute(send.astype(jnp.bfloat16), 'space', [(i, (i + shift) % ns) f...]
where the time goes in v10:
time: 68.7 us; the launch traced here: 68.2 us
  starting transfers between devices  24.8 us (36%)
  waiting for transfers between devices  13.4 us (20%)
  matrix products  13.3 us (19%)
  local copies, waits for them, and re-layouts  7.64 us (11%)
  other arithmetic  7.1 us (10%)
  between operations  1.88 us (3%)
    ppermute x5, waiting for transfers between devices, _halve(): got = lax.ppermute(send, axis, [(i, i ^ 1 << bit) for i in range(size)])  7.32 us
    ppermute x5, starting transfers between devices, _halve(): got = lax.ppermute(send, axis, [(i, i ^ 1 << bit) for i in range(size)])  6.26 us
    ppermute x3, starting transfers between devices, halving_scatter(): lax.ppermute(send.astype(jnp.bfloat16), 'space', [(i, (i + shift) % ns) f...  5.96 us
    ppermute x1, starting transfers between devices, exchange_rows(): above = lax.ppermute(tail, axis, [(i, i + 1) for i in range(ends)])  5.59 us
    ppermute x2, starting transfers between devices, space_sum(): lax.ppermute(values, 'space', [(i, i ^ step) for i in range(count)])  5.59 us
    unnamed x42, local copies, waits for them, and re-layouts  5.43 us
    dot_general x9, matrix products, on_device(): jnp.einsum('nfhwc,cd->nfhwd', window, spatial_weight[row_tap, col_tap], p...  3.88 us
    dot_general x9, matrix products, on_device(): jnp.einsum('nfhwc,nfhwd->cd', window, pre_slope, preferred_element_type=j...  3.54 us
  transfers between devices with their start and end apart: 12, of which 9 were waited for; matrix products, arithmetic and copies ran while one was open for 7% of the time, Pallas kernels for 0%

profile of v10, /device:TPU:0, one launch (start us, length us, event | category | flops | bytes accessed | tf_op | source)
XLA Modules:
  0.0 68.2 jit_solution(2282474564804362097)
XLA Ops:
  0.6 1.4 %collective-permute-start.1 = (bf16[1,33,1,8,256]{4,3,2,1,0:T(8,128)(2,1)}, bf16[1,33,1,8,256]{4,3,2,1,0:T(8,128)(2,1)S(1)}, u32[]{:S(2)}, u32[]{:S(2)}) collective-permute-start(bf16[1,33,1,8,256]{4,3,2,1,0:T(8,128)(2,1)} %param.8), channel_id=1, source_target_pairs={{1,0},{2,1},{3,2},{5,4},{6,5},{7,6},{9,8},{10,9},{11,10},{13,12},{... | collective-permute-start | bytes 405512 | tf_op jit(solution)/shard_map/ppermute | solution.py:20
  2.1 5.6 %collective-permute-start = (bf16[1,33,1,8,256]{4,3,2,1,0:T(8,128)(2,1)}, bf16[1,33,1,8,256]{4,3,2,1,0:T(8,128)(2,1)S(1)}, u32[]{:S(2)}, u32[]{:S(2)}) collective-permute-start(bf16[1,33,1,8,256]{4,3,2,1,0:T(8,128)(2,1)} %param.8), channel_id=1, source_target_pairs={{0,1},{1,2},{2,3},{4,5},{5,6},{6,7},{8,9},{9,10},{10,11},{12,13},{... | collective-permute-start | bytes 405512 | tf_op jit(solution)/shard_map/ppermute | solution.py:19
  8.3 1.1 %broadcast_in_dim.16 = bf16[33,8,2,256]{3,2,1,0:T(2,128)(2,1)S(1)} broadcast(bf16[33,8,256]{2,1,0:T(8,128)(2,1)} %bitcast.358), dimensions={0,1,3} | broadcast | bytes 405504 | tf_op jit(solution)/shard_map/broadcast_in_dim | solution.py:26
  9.5 0.9 %convert_element_type.133 = f32[33,16,256]{2,1,0:T(8,128)} convert(bf16[33,16,256]{2,1,0:T(8,128)(2,1)S(1)} %broadcast_in_dim.17) | non-fusion elementwise | flops 135168 | bytes 811008 | tf_op jit(solution)/shard_map/convert_element_type | solution.py:161
  11.1 0.9 %fusion.5 = bf16[1,33,4,18,256]{4,3,2,1,0:T(8,128)(2,1)S(1)} fusion(bf16[1,33,1,16,256]{4,3,2,1,0:T(8,128)(2,1)S(1)} %slice.161, bf16[1,33,2,16,256]{4,3,2,1,0:T(8,128)(2,1)S(1)} %broadcast_in_dim.40, bf16[1,33,1,16,256]{4,3,2,1,0:T(8,128)(2,1)S(1)} %slice.160), kind=kLoop, calls=%fused_computation.9 | loop fusion | flops 7299072 | bytes 2297856 | tf_op jit(solution)/shard_map/concatenate | solution.py:133
  12.0 0.4 copy-done.8
  15.0 1.4 %multiply_convert_fusion = (bf16[33,2,16,256]{3,2,1,0:T(8,128)(2,1)S(1)}, f32[33,2,16,256]{3,2,1,0:T(8,128)}) fusion(f32[33,2,16,256]{3,2,1,0:T(8,128)S(1)} %convolution_add_fusion.5, bf16[3,3,256,256]{3,2,1,0:T(8,128)(2,1)S(1)} %copy-done.8, bf16[1,33,4,18,256]{4,3,2,1,0:T(8,128)(2,1)S(1)} %fusion.5), kind=kOutput, calls=%fused_computation.56 | convolution fusion | flops 140034048 | bytes 3375104 | tf_op jit(solution)/shard_map/nfhwc,cd->nfhwd/dot_general | solution.py:143
  17.0 0.7 %copy-done.5 = f32[33,16,256]{2,1,0:T(8,128)S(1)} copy-done((f32[33,16,256]{2,1,0:T(8,128)S(1)}, f32[33,16,256]{2,1,0:T(8,128)}, u32[]{:S(2)}) %copy-start.5) | copy-done | bytes 540696
  18.1 0.8 %copy-done.2 = bf16[33,2,16,256]{3,2,1,0:T(8,128)(2,1)} copy-done((bf16[33,2,16,256]{3,2,1,0:T(8,128)(2,1)}, bf16[33,2,16,256]{3,2,1,0:T(8,128)(2,1)S(1)}, u32[]{:S(2)}) %copy-start.2) | copy-done | bytes 540696
  18.9 0.4 fusion.24
  19.3 0.9 %fusion.51 = (f32[8,256]{1,0:T(8,128)S(1)}, f32[8,2,16,256]{3,2,1,0:T(8,128)}) fusion(bf16[256,256]{1,0:T(8,128)(2,1)S(1)} %copy-done, bf16[8,2,16,256]{3,0,2,1:T(8,128)(2,1)S(1)} %fusion.24), kind=kOutput, calls=%fused_computation.108 | convolution fusion | flops 34142208 | bytes 532480 | tf_op jit(solution)/shard_map/nqhwc,ce->nqhwe/dot_general | solution.py:168
  20.2 2.4 %collective-permute-start.2 = (f32[1,8,256]{2,1,0:T(8,128)S(1)}, f32[1,8,256]{2,1,0:T(8,128)S(1)}, u32[]{:S(2)}, u32[]{:S(2)}) collective-permute-start(f32[1,8,256]{2,1,0:T(8,128)S(1)} %bitcast.365), channel_id=1, source_target_pairs={{0,1},{1,0},{2,3},{3,2},{4,5},{5,4},{6,7},{7,6},{8,9},{9,8},{10,11... | collective-permute-start | bytes 24584 | tf_op jit(solution)/shard_map/ppermute | solution.py:57
  22.6 1.6 %collective-permute-done.2 = f32[1,8,256]{2,1,0:T(8,128)S(1)} collective-permute-done((f32[1,8,256]{2,1,0:T(8,128)S(1)}, f32[1,8,256]{2,1,0:T(8,128)S(1)}, u32[]{:S(2)}, u32[]{:S(2)}) %collective-permute-start.2) | collective-permute-done | bytes 8224 | tf_op jit(solution)/shard_map/ppermute | solution.py:57
  24.3 3.2 %collective-permute-start.3 = (f32[1,8,256]{2,1,0:T(8,128)S(1)}, f32[1,8,256]{2,1,0:T(8,128)S(1)}, u32[]{:S(2)}, u32[]{:S(2)}) collective-permute-start(f32[1,8,256]{2,1,0:T(8,128)S(1)} %bitcast_add_fusion.5), channel_id=1, source_target_pairs={{0,2},{1,3},{2,0},{3,1},{4,6},{5,7},{6,4},{7,5},{8,10},{9,11},{10,... | collective-permute-start | bytes 24584 | tf_op jit(solution)/shard_map/ppermute | solution.py:57
  27.5 1.6 %collective-permute-done.3 = f32[1,8,256]{2,1,0:T(8,128)S(1)} collective-permute-done((f32[1,8,256]{2,1,0:T(8,128)S(1)}, f32[1,8,256]{2,1,0:T(8,128)S(1)}, u32[]{:S(2)}, u32[]{:S(2)}) %collective-permute-start.3) | collective-permute-done | bytes 8224 | tf_op jit(solution)/shard_map/ppermute | solution.py:57
  29.3 1.1 %fusion.49 = bf16[8,2,16,256]{3,2,1,0:T(8,128)(2,1)S(1)} fusion(f32[8,2,16,256]{3,2,1,0:T(8,128)} %get-tuple-element.15, f32[8,256]{1,0:T(8,128)S(1)} %get-tuple-element.11, f32[8,256]{1,0:T(8,128)S(1)} %get-tuple-element.10), kind=kLoop, calls=%fused_computation.104 | loop fusion | flops 1245184 | bytes 409600 | tf_op jit(solution)/shard_map/convert_element_type | solution.py:175
  30.7 1.0 %fusion.12 = bf16[1,33,2,16,256]{4,1,3,2,0:T(8,128)(2,1)S(1)} fusion(f32[8,2,16,256]{3,0,2,1:T(8,128)S(1)} %fusion.59, bf16[1,33,2,16,256]{4,3,2,1,0:T(8,128)(2,1)S(1)} %copy-done.9, f32[33]{0:T(128)S(1)} %compare_select_fusion, s32[8]{0:T(128)S(1)} %bitcast.367), kind=kOutput, calls=%fused_computation.32 | convolution fusion | flops 27033864 | bytes 1343652 | tf_op jit(solution)/shard_map/nqf,nqhwc->nfhwc/dot_general | solution.py:184
  32.9 0.6 copy-done.7
  33.8 0.4 slice_bitcast_fusion
  34.6 0.9 %copy-done.12 = f32[33,2,16,256]{3,2,1,0:T(8,128)S(1)} copy-done((f32[33,2,16,256]{3,2,1,0:T(8,128)S(1)}, f32[33,2,16,256]{3,2,1,0:T(8,128)}, u32[]{:S(2)}) %copy-start.12) | copy-done | bytes 1081368
  35.5 0.6 fusion.13
  36.1 0.4 fusion.23
  36.5 0.6 copy-done.4
  37.0 0.4 fusion.22
  37.4 0.4 fusion.21
  37.9 0.4 fusion.20
  38.2 0.4 fusion.19
  38.6 0.4 fusion.18
  39.0 0.4 fusion.17
  39.4 0.4 fusion.16
  39.8 0.4 fusion.15
  40.5 1.2 %copy-done.1 = f32[9,256,256]{2,1,0:T(8,128)} copy-done((f32[9,256,256]{2,1,0:T(8,128)}, f32[9,256,256]{2,1,0:T(8,128)S(1)}, u32[]{:S(2)}) %copy-start.1) | copy-done | bytes 2359320
  41.7 1.8 %broadcast_select_fusion = f32[4,1,4,96,256]{4,3,2,1,0:T(8,128)S(1)} fusion(pred[]{:T(512)S(6)} %eq.53, f32[4,2,4,24,256]{4,3,2,1,0:T(8,128)S(1)} %bitcast.334, f32[4,2,4,72,256]{4,3,2,1,0:T(8,128)} %bitcast.332), kind=kLoop, calls=%fused_computation.59 | loop fusion | flops 1179648 | bytes 4718593 | tf_op jit(solution)/shard_map/jit(_where)/select_n | solution.py:69
  43.5 0.4 collective-permute-done.4
  44.4 1.5 %collective-permute-start.5 = (bf16[8,48,256]{2,1,0:T(8,128)(2,1)S(1)}, bf16[8,48,256]{2,1,0:T(8,128)(2,1)S(1)}, u32[]{:S(2)}, u32[]{:S(2)}) collective-permute-start(bf16[8,48,256]{2,1,0:T(8,128)(2,1)S(1)} %bitcast.357), channel_id=1, source_target_pairs={{0,8},{4,12},{8,0},{12,4},{16,24},{20,28},{24,16},{28,20},{1,9},{5... | collective-permute-start | bytes 589832 | tf_op jit(solution)/shard_map/ppermute | solution.py:74
  45.9 1.6 %collective-permute-start.7 = (bf16[8,48,256]{2,1,0:T(8,128)(2,1)S(1)}, bf16[8,48,256]{2,1,0:T(8,128)(2,1)S(1)}, u32[]{:S(2)}, u32[]{:S(2)}) collective-permute-start(bf16[8,48,256]{2,1,0:T(8,128)(2,1)S(1)} %fusion.52), channel_id=1, source_target_pairs={{0,16},{4,20},{8,24},{12,28},{16,0},{20,4},{24,8},{28,12},{1,17},{... | collective-permute-start | bytes 589832 | tf_op jit(solution)/shard_map/ppermute | solution.py:74
  47.6 3.8 %collective-permute-done.5 = bf16[8,48,256]{2,1,0:T(8,128)(2,1)S(1)} collective-permute-done((bf16[8,48,256]{2,1,0:T(8,128)(2,1)S(1)}, bf16[8,48,256]{2,1,0:T(8,128)(2,1)S(1)}, u32[]{:S(2)}, u32[]{:S(2)}) %collective-permute-start.5) | collective-permute-done | bytes 196640 | tf_op jit(solution)/shard_map/ppermute | solution.py:74
  51.4 1.6 %collective-permute-start.6 = (bf16[4,48,256]{2,1,0:T(8,128)(2,1)S(1)}, bf16[4,48,256]{2,1,0:T(8,128)(2,1)S(1)}, u32[]{:S(2)}, u32[]{:S(2)}) collective-permute-start(bf16[4,48,256]{2,1,0:T(8,128)(2,1)S(1)} %fusion.94), channel_id=1, source_target_pairs={{0,16},{4,20},{8,24},{12,28},{16,0},{20,4},{24,8},{28,12},{1,17},{... | collective-permute-start | bytes 294920 | tf_op jit(solution)/shard_map/ppermute | solution.py:74
  53.1 1.6 %collective-permute-start.8 = (bf16[4,48,256]{2,1,0:T(8,128)(2,1)S(1)}, bf16[4,48,256]{2,1,0:T(8,128)(2,1)S(1)}, u32[]{:S(2)}, u32[]{:S(2)}) collective-permute-start(bf16[4,48,256]{2,1,0:T(8,128)(2,1)S(1)} %fusion.95), channel_id=1, source_target_pairs={{0,8},{4,12},{8,0},{12,4},{16,24},{20,28},{24,16},{28,20},{1,9},{5... | collective-permute-start | bytes 294920 | tf_op jit(solution)/shard_map/ppermute | solution.py:74
  54.7 1.4 %collective-permute-done.6 = bf16[4,48,256]{2,1,0:T(8,128)(2,1)S(1)} collective-permute-done((bf16[4,48,256]{2,1,0:T(8,128)(2,1)S(1)}, bf16[4,48,256]{2,1,0:T(8,128)(2,1)S(1)}, u32[]{:S(2)}, u32[]{:S(2)}) %collective-permute-start.6) | collective-permute-done | bytes 98336 | tf_op jit(solution)/shard_map/ppermute | solution.py:74
  56.2 1.7 %collective-permute-done.8 = bf16[4,48,256]{2,1,0:T(8,128)(2,1)S(1)} collective-permute-done((bf16[4,48,256]{2,1,0:T(8,128)(2,1)S(1)}, bf16[4,48,256]{2,1,0:T(8,128)(2,1)S(1)}, u32[]{:S(2)}, u32[]{:S(2)}) %collective-permute-start.8) | collective-permute-done | bytes 98336 | tf_op jit(solution)/shard_map/ppermute | solution.py:74
  57.9 2.0 %collective-permute-start.9 = (bf16[96,256]{1,0:T(8,128)(2,1)S(1)}, bf16[96,256]{1,0:T(8,128)(2,1)S(1)}, u32[]{:S(2)}, u32[]{:S(2)}) collective-permute-start(bf16[96,256]{1,0:T(8,128)(2,1)S(1)} %get-tuple-element.7), channel_id=1, source_target_pairs={{0,1},{1,2},{2,3},{3,0},{4,5},{5,6},{6,7},{7,4},{8,9},{9,10},{10,1... | collective-permute-start | bytes 147464 | tf_op jit(solution)/shard_map/ppermute | solution.py:109
  59.9 2.7 %collective-permute-start.10 = (bf16[96,256]{1,0:T(8,128)(2,1)S(1)}, bf16[96,256]{1,0:T(8,128)(2,1)S(1)}, u32[]{:S(2)}, u32[]{:S(2)}) collective-permute-start(bf16[96,256]{1,0:T(8,128)(2,1)S(1)} %get-tuple-element.8), channel_id=1, source_target_pairs={{0,2},{1,3},{2,0},{3,1},{4,6},{5,7},{6,4},{7,5},{8,10},{9,11},{10,... | collective-permute-start | bytes 147464 | tf_op jit(solution)/shard_map/ppermute | solution.py:109
  62.6 1.3 %collective-permute-start.11 = (bf16[96,256]{1,0:T(8,128)(2,1)S(1)}, bf16[96,256]{1,0:T(8,128)(2,1)S(1)}, u32[]{:S(2)}, u32[]{:S(2)}) collective-permute-start(bf16[96,256]{1,0:T(8,128)(2,1)S(1)} %get-tuple-element.9), channel_id=1, source_target_pairs={{0,3},{1,0},{2,1},{3,2},{4,7},{5,4},{6,5},{7,6},{8,11},{9,8},{10,9... | collective-permute-start | bytes 147464 | tf_op jit(solution)/shard_map/ppermute | solution.py:109
  64.0 1.0 %collective-permute-done.10 = bf16[96,256]{1,0:T(8,128)(2,1)S(1)} collective-permute-done((bf16[96,256]{1,0:T(8,128)(2,1)S(1)}, bf16[96,256]{1,0:T(8,128)(2,1)S(1)}, u32[]{:S(2)}, u32[]{:S(2)}) %collective-permute-start.10) | collective-permute-done | bytes 49184 | tf_op jit(solution)/shard_map/ppermute | solution.py:109
  65.0 1.7 %collective-permute-done.11 = bf16[96,256]{1,0:T(8,128)(2,1)S(1)} collective-permute-done((bf16[96,256]{1,0:T(8,128)(2,1)S(1)}, bf16[96,256]{1,0:T(8,128)(2,1)S(1)}, u32[]{:S(2)}, u32[]{:S(2)}) %collective-permute-start.11) | collective-permute-done | bytes 49184 | tf_op jit(solution)/shard_map/ppermute | solution.py:109
  66.9 0.7 add_add_fusion
  67.6 0.6 add_add_fusion.1
  (88 shorter events, 7.8 us)
Async XLA Ops:
  0.6 18.7 %copy-start = (bf16[256,256]{1,0:T(8,128)(2,1)S(1)}, bf16[256,256]{1,0:T(8,128)(2,1)}, u32[]{:S(2)}) copy-start(bf16[256,256]{1,0:T(8,128)(2,1)} %param.12) | copy-start | bytes 393220
  0.6 9.7 %collective-permute-start.1 = (bf16[1,33,1,8,256]{4,3,2,1,0:T(8,128)(2,1)}, bf16[1,33,1,8,256]{4,3,2,1,0:T(8,128)(2,1)S(1)}, u32[]{:S(2)}, u32[]{:S(2)}) collective-permute-start(bf16[1,33,1,8,256]{4,3,2,1,0:T(8,128)(2,1)} %param.8), channel_id=1, source_target_pairs={{1,0},{2,1},{3,2},{5,4},{6,5},{7,6},{9,8},{10,9},{11,10},{13,12},{... | collective-permute-start | bytes 405512 | tf_op jit(solution)/shard_map/ppermute | solution.py:20
  2.1 8.7 %collective-permute-start = (bf16[1,33,1,8,256]{4,3,2,1,0:T(8,128)(2,1)}, bf16[1,33,1,8,256]{4,3,2,1,0:T(8,128)(2,1)S(1)}, u32[]{:S(2)}, u32[]{:S(2)}) collective-permute-start(bf16[1,33,1,8,256]{4,3,2,1,0:T(8,128)(2,1)} %param.8), channel_id=1, source_target_pairs={{0,1},{1,2},{2,3},{4,5},{5,6},{6,7},{8,9},{9,10},{10,11},{12,13},{... | collective-permute-start | bytes 405512 | tf_op jit(solution)/shard_map/ppermute | solution.py:19
  11.1 1.7 %copy-start.3 = (bf16[1,33,1,16,256]{4,3,2,1,0:T(8,128)(2,1)}, bf16[1,33,1,16,256]{4,3,2,1,0:T(8,128)(2,1)S(1)}, u32[]{:S(2)}) copy-start(bf16[1,33,1,16,256]{4,3,2,1,0:T(8,128)(2,1)S(1)} %slice.160) | copy-start | bytes 811012
  11.1 1.3 %copy-start.8 = (bf16[3,3,256,256]{3,2,1,0:T(8,128)(2,1)S(1)}, bf16[3,3,256,256]{3,2,1,0:T(8,128)(2,1)}, u32[]{:S(2)}) copy-start(bf16[3,3,256,256]{3,2,1,0:T(8,128)(2,1)} %param.10) | copy-start | bytes 3538948
  15.0 1.4 %copy-start.6 = (bf16[3,256,256]{2,1,0:T(8,128)(2,1)S(1)}, bf16[3,256,256]{2,1,0:T(8,128)(2,1)}, u32[]{:S(2)}) copy-start(bf16[3,256,256]{2,1,0:T(8,128)(2,1)} %param.11) | copy-start | bytes 1179652
  16.7 1.1 %copy-start.5 = (f32[33,16,256]{2,1,0:T(8,128)S(1)}, f32[33,16,256]{2,1,0:T(8,128)}, u32[]{:S(2)}) copy-start(f32[33,16,256]{2,1,0:T(8,128)} %convert_element_type.133) | copy-start | bytes 1622020
  17.8 1.1 %copy-start.11 = (s32[1,8]{1,0:T(1,128)S(1)}, s32[1,8]{1,0:T(1,128)}, u32[]{:S(2)}) copy-start(s32[1,8]{1,0:T(1,128)} %param.14) | copy-start | bytes 100
  18.1 0.8 %copy-start.2 = (bf16[33,2,16,256]{3,2,1,0:T(8,128)(2,1)}, bf16[33,2,16,256]{3,2,1,0:T(8,128)(2,1)S(1)}, u32[]{:S(2)}) copy-start(bf16[33,2,16,256]{3,2,1,0:T(8,128)(2,1)S(1)} %fusion.14) | copy-start | bytes 1622020
  18.1 4.5 %copy-start.10 = (f32[256]{0:T(256)S(1)}, f32[256]{0:T(256)}, u32[]{:S(2)}) copy-start(f32[256]{0:T(256)} %param.13) | copy-start | bytes 3076
  20.2 4.0 %collective-permute-start.2 = (f32[1,8,256]{2,1,0:T(8,128)S(1)}, f32[1,8,256]{2,1,0:T(8,128)S(1)}, u32[]{:S(2)}, u32[]{:S(2)}) collective-permute-start(f32[1,8,256]{2,1,0:T(8,128)S(1)} %bitcast.365), channel_id=1, source_target_pairs={{0,1},{1,0},{2,3},{3,2},{4,5},{5,4},{6,7},{7,6},{8,9},{9,8},{10,11... | collective-permute-start | bytes 24584 | tf_op jit(solution)/shard_map/ppermute | solution.py:57
  24.3 4.8 %collective-permute-start.3 = (f32[1,8,256]{2,1,0:T(8,128)S(1)}, f32[1,8,256]{2,1,0:T(8,128)S(1)}, u32[]{:S(2)}, u32[]{:S(2)}) collective-permute-start(f32[1,8,256]{2,1,0:T(8,128)S(1)} %bitcast_add_fusion.5), channel_id=1, source_target_pairs={{0,2},{1,3},{2,0},{3,1},{4,6},{5,7},{6,4},{7,5},{8,10},{9,11},{10,... | collective-permute-start | bytes 24584 | tf_op jit(solution)/shard_map/ppermute | solution.py:57
  27.5 3.2 %copy-start.9 = (bf16[1,33,2,16,256]{4,3,2,1,0:T(8,128)(2,1)S(1)}, bf16[1,33,2,16,256]{4,3,2,1,0:T(8,128)(2,1)}, u32[]{:S(2)}) copy-start(bf16[1,33,2,16,256]{4,3,2,1,0:T(8,128)(2,1)} %param.15) | copy-start | bytes 1622020
  32.5 1.0 %copy-start.7 = (bf16[3,256,256]{2,1,0:T(8,128)(2,1)S(1)}, bf16[3,256,256]{2,1,0:T(8,128)(2,1)}, u32[]{:S(2)}) copy-start(bf16[3,256,256]{2,1,0:T(8,128)(2,1)} %param.11) | copy-start | bytes 1179652
  34.3 1.2 %copy-start.12 = (f32[33,2,16,256]{3,2,1,0:T(8,128)S(1)}, f32[33,2,16,256]{3,2,1,0:T(8,128)}, u32[]{:S(2)}) copy-start(f32[33,2,16,256]{3,2,1,0:T(8,128)} %get-tuple-element.13) | copy-start | bytes 3244036
  36.1 1.0 %copy-start.4 = (bf16[1,33,1,16,256]{4,3,2,1,0:T(8,128)(2,1)S(1)}, bf16[1,33,1,16,256]{4,3,2,1,0:T(8,128)(2,1)}, u32[]{:S(2)}) copy-start(bf16[1,33,1,16,256]{4,3,2,1,0:T(8,128)(2,1)} %copy-done.3) | copy-start | bytes 811012
  40.2 1.4 %copy-start.1 = (f32[9,256,256]{2,1,0:T(8,128)}, f32[9,256,256]{2,1,0:T(8,128)S(1)}, u32[]{:S(2)}) copy-start(f32[9,256,256]{2,1,0:T(8,128)S(1)} %fusion.15) | copy-start | bytes 7077892
  41.7 2.3 %collective-permute-start.4 = (bf16[16,96,256]{2,1,0:T(8,128)(2,1)S(1)}, bf16[16,96,256]{2,1,0:T(8,128)(2,1)S(1)}, u32[]{:S(2)}, u32[]{:S(2)}) collective-permute-start(bf16[16,96,256]{2,1,0:T(8,128)(2,1)S(1)} %bitcast.352), channel_id=1, source_target_pairs={{0,4},{4,0},{8,12},{12,8},{16,20},{20,16},{24,28},{28,24},{1,5},{5... | collective-permute-start | bytes 2359304 | tf_op jit(solution)/shard_map/ppermute | solution.py:74
  44.4 7.0 %collective-permute-start.5 = (bf16[8,48,256]{2,1,0:T(8,128)(2,1)S(1)}, bf16[8,48,256]{2,1,0:T(8,128)(2,1)S(1)}, u32[]{:S(2)}, u32[]{:S(2)}) collective-permute-start(bf16[8,48,256]{2,1,0:T(8,128)(2,1)S(1)} %bitcast.357), channel_id=1, source_target_pairs={{0,8},{4,12},{8,0},{12,4},{16,24},{20,28},{24,16},{28,20},{1,9},{5... | collective-permute-start | bytes 589832 | tf_op jit(solution)/shard_map/ppermute | solution.py:74
  45.9 7.1 %collective-permute-start.7 = (bf16[8,48,256]{2,1,0:T(8,128)(2,1)S(1)}, bf16[8,48,256]{2,1,0:T(8,128)(2,1)S(1)}, u32[]{:S(2)}, u32[]{:S(2)}) collective-permute-start(bf16[8,48,256]{2,1,0:T(8,128)(2,1)S(1)} %fusion.52), channel_id=1, source_target_pairs={{0,16},{4,20},{8,24},{12,28},{16,0},{20,4},{24,8},{28,12},{1,17},{... | collective-permute-start | bytes 589832 | tf_op jit(solution)/shard_map/ppermute | solution.py:74
  51.4 4.7 %collective-permute-start.6 = (bf16[4,48,256]{2,1,0:T(8,128)(2,1)S(1)}, bf16[4,48,256]{2,1,0:T(8,128)(2,1)S(1)}, u32[]{:S(2)}, u32[]{:S(2)}) collective-permute-start(bf16[4,48,256]{2,1,0:T(8,128)(2,1)S(1)} %fusion.94), channel_id=1, source_target_pairs={{0,16},{4,20},{8,24},{12,28},{16,0},{20,4},{24,8},{28,12},{1,17},{... | collective-permute-start | bytes 294920 | tf_op jit(solution)/shard_map/ppermute | solution.py:74
  53.1 4.7 %collective-permute-start.8 = (bf16[4,48,256]{2,1,0:T(8,128)(2,1)S(1)}, bf16[4,48,256]{2,1,0:T(8,128)(2,1)S(1)}, u32[]{:S(2)}, u32[]{:S(2)}) collective-permute-start(bf16[4,48,256]{2,1,0:T(8,128)(2,1)S(1)} %fusion.95), channel_id=1, source_target_pairs={{0,8},{4,12},{8,0},{12,4},{16,24},{20,28},{24,16},{28,20},{1,9},{5... | collective-permute-start | bytes 294920 | tf_op jit(solution)/shard_map/ppermute | solution.py:74
  57.9 6.1 %collective-permute-start.9 = (bf16[96,256]{1,0:T(8,128)(2,1)S(1)}, bf16[96,256]{1,0:T(8,128)(2,1)S(1)}, u32[]{:S(2)}, u32[]{:S(2)}) collective-permute-start(bf16[96,256]{1,0:T(8,128)(2,1)S(1)} %get-tuple-element.7), channel_id=1, source_target_pairs={{0,1},{1,2},{2,3},{3,0},{4,5},{5,6},{6,7},{7,4},{8,9},{9,10},{10,1... | collective-permute-start | bytes 147464 | tf_op jit(solution)/shard_map/ppermute | solution.py:109
  59.9 5.1 %collective-permute-start.10 = (bf16[96,256]{1,0:T(8,128)(2,1)S(1)}, bf16[96,256]{1,0:T(8,128)(2,1)S(1)}, u32[]{:S(2)}, u32[]{:S(2)}) collective-permute-start(bf16[96,256]{1,0:T(8,128)(2,1)S(1)} %get-tuple-element.8), channel_id=1, source_target_pairs={{0,2},{1,3},{2,0},{3,1},{4,6},{5,7},{6,4},{7,5},{8,10},{9,11},{10,... | collective-permute-start | bytes 147464 | tf_op jit(solution)/shard_map/ppermute | solution.py:109
  62.6 4.1 %collective-permute-start.11 = (bf16[96,256]{1,0:T(8,128)(2,1)S(1)}, bf16[96,256]{1,0:T(8,128)(2,1)S(1)}, u32[]{:S(2)}, u32[]{:S(2)}) collective-permute-start(bf16[96,256]{1,0:T(8,128)(2,1)S(1)} %get-tuple-element.9), channel_id=1, source_target_pairs={{0,3},{1,0},{2,1},{3,2},{4,7},{5,4},{6,5},{7,6},{8,11},{9,8},{10,9... | collective-permute-start | bytes 147464 | tf_op jit(solution)/shard_map/ppermute | solution.py:109

commit v11 on v10

--- a/solution.py
+++ b/solution.py
@@ -64,10 +64,8 @@
     hi, lo = 1 << pos, 1 << (len(left) - 1 - pos)
     mine = (lax.axis_index(axis) // (1 << bit)) % 2
     v = cur.reshape((hi, 2, lo) + cur.shape[1:])
-    low, high = v[:, 0].reshape((hi * lo,) + cur.shape[1:]), v[:, 1].reshape((hi * lo,) + cur.shape[1:])
-    upper = mine == 1
-    keep = jnp.where(upper, high, low)
-    send = jnp.where(upper, low, high)
+    keep = lax.dynamic_index_in_dim(v, mine, 1, keepdims=False).reshape((hi * lo,) + cur.shape[1:])
+    send = lax.dynamic_index_in_dim(v, 1 - mine, 1, keepdims=False).reshape((hi * lo,) + cur.shape[1:])
     left.remove((axis, bit))
     if wire is not None:
         send = send.astype(wire)

time: 68.7 us -> 68.5 us (level)
  waiting for transfers between devices: 13.4 us -> 16.4 us
  starting transfers between devices: 24.8 us -> 22.4 us
  other arithmetic: 7.1 us -> 6.36 us
    ppermute x1, waiting for transfers between devices: 0.01 us -> 2.88 us  [exchange_rows(): below = lax.ppermute(head, axis, [(i + 1, i) for i in range(ends)])]
    select_n x2 -> x0, other arithmetic: 1.88 us -> none  [_halve(): keep = jnp.where(upper, high, low)]
    ppermute x2, starting transfers between devices: 5.59 us -> 4.14 us  [space_sum(): lax.ppermute(values, 'space', [(i, i ^ step) for i in range(count)])]
    concatenate x0 -> x1, other arithmetic: none -> 1.42 us  [on_device(): jnp.concatenate([spatial_grad, temporal_grad], axis=1)]
    ppermute x3, waiting for transfers between devices: 2.66 us -> 1.63 us  [halving_scatter(): lax.ppermute(send.astype(jnp.bfloat16), 'space', [(i, (i + shift) % ns) f...]
    ppermute x2, waiting for transfers between devices: 3.24 us -> 4.05 us  [space_sum(): lax.ppermute(values, 'space', [(i, i ^ step) for i in range(count)])]
  transfers between devices with their start and end apart: 12 -> 12, of which waited for: 9 -> 10; matrix products, arithmetic and copies ran while one was open for 7% -> 6% of each run, Pallas kernels for 0% -> 0%
where the time goes in v11:
time: 68.5 us; the launch traced here: 68.1 us
  starting transfers between devices  22.4 us (33%)
  waiting for transfers between devices  16.4 us (24%)
  matrix products  13.3 us (19%)
  local copies, waits for them, and re-layouts  7.77 us (11%)
  other arithmetic  6.36 us (9%)
  between operations  1.9 us (3%)
    ppermute x5, waiting for transfers between devices, _halve(): got = lax.ppermute(send, axis, [(i, i ^ 1 << bit) for i in range(size)])  7.79 us
    ppermute x5, starting transfers between devices, _halve(): got = lax.ppermute(send, axis, [(i, i ^ 1 << bit) for i in range(size)])  6.26 us
    ppermute x3, starting transfers between devices, halving_scatter(): lax.ppermute(send.astype(jnp.bfloat16), 'space', [(i, (i + shift) % ns) f...  5.62 us
    unnamed x42, local copies, waits for them, and re-layouts  5.43 us
    ppermute x1, starting transfers between devices, exchange_rows(): above = lax.ppermute(tail, axis, [(i, i + 1) for i in range(ends)])  5.1 us
    ppermute x2, starting transfers between devices, space_sum(): lax.ppermute(values, 'space', [(i, i ^ step) for i in range(count)])  4.14 us
    ppermute x2, waiting for transfers between devices, space_sum(): lax.ppermute(values, 'space', [(i, i ^ step) for i in range(count)])  4.05 us
    dot_general x9, matrix products, on_device(): jnp.einsum('nfhwc,cd->nfhwd', window, spatial_weight[row_tap, col_tap], p...  3.89 us
  transfers between devices with their start and end apart: 12, of which 10 were waited for; matrix products, arithmetic and copies ran while one was open for 6% of the time, Pallas kernels for 0%

profile of v11, /device:TPU:0, one launch (start us, length us, event | category | flops | bytes accessed | tf_op | source)
XLA Modules:
  0.0 68.1 jit_solution(10299363391452481910)
XLA Ops:
  0.6 5.1 %collective-permute-start = (bf16[1,33,1,8,256]{4,3,2,1,0:T(8,128)(2,1)}, bf16[1,33,1,8,256]{4,3,2,1,0:T(8,128)(2,1)S(1)}, u32[]{:S(2)}, u32[]{:S(2)}) collective-permute-start(bf16[1,33,1,8,256]{4,3,2,1,0:T(8,128)(2,1)} %param.8), channel_id=1, source_target_pairs={{0,1},{1,2},{2,3},{4,5},{5,6},{6,7},{8,9},{9,10},{10,11},{12,13},{... | collective-permute-start | bytes 405512 | tf_op jit(solution)/shard_map/ppermute | solution.py:19
  5.7 1.3 %collective-permute-start.1 = (bf16[1,33,1,8,256]{4,3,2,1,0:T(8,128)(2,1)}, bf16[1,33,1,8,256]{4,3,2,1,0:T(8,128)(2,1)S(1)}, u32[]{:S(2)}, u32[]{:S(2)}) collective-permute-start(bf16[1,33,1,8,256]{4,3,2,1,0:T(8,128)(2,1)} %param.8), channel_id=1, source_target_pairs={{1,0},{2,1},{3,2},{5,4},{6,5},{7,6},{9,8},{10,9},{11,10},{13,12},{... | collective-permute-start | bytes 405512 | tf_op jit(solution)/shard_map/ppermute | solution.py:20
  7.0 1.1 %broadcast_in_dim.16 = bf16[33,8,2,256]{3,2,1,0:T(2,128)(2,1)S(1)} broadcast(bf16[33,8,256]{2,1,0:T(8,128)(2,1)} %bitcast.358), dimensions={0,1,3} | broadcast | bytes 405504 | tf_op jit(solution)/shard_map/broadcast_in_dim | solution.py:26
  8.2 0.9 %convert_element_type.133 = f32[33,16,256]{2,1,0:T(8,128)} convert(bf16[33,16,256]{2,1,0:T(8,128)(2,1)S(1)} %broadcast_in_dim.17) | non-fusion elementwise | flops 135168 | bytes 811008 | tf_op jit(solution)/shard_map/convert_element_type | solution.py:159
  10.0 2.9 %collective-permute-done.1 = bf16[1,33,1,8,256]{4,3,2,1,0:T(8,128)(2,1)S(1)} collective-permute-done((bf16[1,33,1,8,256]{4,3,2,1,0:T(8,128)(2,1)}, bf16[1,33,1,8,256]{4,3,2,1,0:T(8,128)(2,1)S(1)}, u32[]{:S(2)}, u32[]{:S(2)}) %collective-permute-start.1) | collective-permute-done | bytes 135200 | tf_op jit(solution)/shard_map/ppermute | solution.py:20
  13.2 0.9 %fusion.5 = bf16[1,33,4,18,256]{4,3,2,1,0:T(8,128)(2,1)S(1)} fusion(bf16[1,33,1,16,256]{4,3,2,1,0:T(8,128)(2,1)S(1)} %slice.131, bf16[1,33,2,16,256]{4,3,2,1,0:T(8,128)(2,1)S(1)} %broadcast_in_dim.40, bf16[1,33,1,16,256]{4,3,2,1,0:T(8,128)(2,1)S(1)} %slice.130), kind=kLoop, calls=%fused_computation.11 | loop fusion | flops 7299072 | bytes 2297856 | tf_op jit(solution)/shard_map/concatenate | solution.py:131
  17.0 1.4 %multiply_convert_fusion = (bf16[33,2,16,256]{3,2,1,0:T(8,128)(2,1)S(1)}, f32[33,2,16,256]{3,2,1,0:T(8,128)}) fusion(f32[33,2,16,256]{3,2,1,0:T(8,128)S(1)} %convolution_add_fusion.5, bf16[3,3,256,256]{3,2,1,0:T(8,128)(2,1)S(1)} %copy-done.8, bf16[1,33,4,18,256]{4,3,2,1,0:T(8,128)(2,1)S(1)} %fusion.5), kind=kOutput, calls=%fused_computation.58 | convolution fusion | flops 140034048 | bytes 3375104 | tf_op jit(solution)/shard_map/nfhwc,cd->nfhwd/dot_general | solution.py:141
  19.0 0.7 %copy-done.5 = f32[33,16,256]{2,1,0:T(8,128)S(1)} copy-done((f32[33,16,256]{2,1,0:T(8,128)S(1)}, f32[33,16,256]{2,1,0:T(8,128)}, u32[]{:S(2)}) %copy-start.5) | copy-done | bytes 540696
  20.1 0.8 %copy-done.2 = bf16[33,2,16,256]{3,2,1,0:T(8,128)(2,1)} copy-done((bf16[33,2,16,256]{3,2,1,0:T(8,128)(2,1)}, bf16[33,2,16,256]{3,2,1,0:T(8,128)(2,1)S(1)}, u32[]{:S(2)}) %copy-start.2) | copy-done | bytes 540696
  20.9 0.4 fusion.26
  21.4 0.9 %fusion.53 = (f32[8,256]{1,0:T(8,128)S(1)}, f32[8,2,16,256]{3,2,1,0:T(8,128)}) fusion(bf16[256,256]{1,0:T(8,128)(2,1)S(1)} %copy-done, bf16[8,2,16,256]{3,0,2,1:T(8,128)(2,1)S(1)} %fusion.26), kind=kOutput, calls=%fused_computation.108 | convolution fusion | flops 34142208 | bytes 532480 | tf_op jit(solution)/shard_map/nqhwc,ce->nqhwe/dot_general | solution.py:166
  22.3 1.6 %collective-permute-start.2 = (f32[1,8,256]{2,1,0:T(8,128)S(1)}, f32[1,8,256]{2,1,0:T(8,128)S(1)}, u32[]{:S(2)}, u32[]{:S(2)}) collective-permute-start(f32[1,8,256]{2,1,0:T(8,128)S(1)} %bitcast.365), channel_id=1, source_target_pairs={{0,1},{1,0},{2,3},{3,2},{4,5},{5,4},{6,7},{7,6},{8,9},{9,8},{10,11... | collective-permute-start | bytes 24584 | tf_op jit(solution)/shard_map/ppermute | solution.py:57
  23.8 2.1 %collective-permute-done.2 = f32[1,8,256]{2,1,0:T(8,128)S(1)} collective-permute-done((f32[1,8,256]{2,1,0:T(8,128)S(1)}, f32[1,8,256]{2,1,0:T(8,128)S(1)}, u32[]{:S(2)}, u32[]{:S(2)}) %collective-permute-start.2) | collective-permute-done | bytes 8224 | tf_op jit(solution)/shard_map/ppermute | solution.py:57
  25.9 2.6 %collective-permute-start.3 = (f32[1,8,256]{2,1,0:T(8,128)S(1)}, f32[1,8,256]{2,1,0:T(8,128)S(1)}, u32[]{:S(2)}, u32[]{:S(2)}) collective-permute-start(f32[1,8,256]{2,1,0:T(8,128)S(1)} %bitcast_add_fusion.5), channel_id=1, source_target_pairs={{0,2},{1,3},{2,0},{3,1},{4,6},{5,7},{6,4},{7,5},{8,10},{9,11},{10,... | collective-permute-start | bytes 24584 | tf_op jit(solution)/shard_map/ppermute | solution.py:57
  28.5 2.0 %collective-permute-done.3 = f32[1,8,256]{2,1,0:T(8,128)S(1)} collective-permute-done((f32[1,8,256]{2,1,0:T(8,128)S(1)}, f32[1,8,256]{2,1,0:T(8,128)S(1)}, u32[]{:S(2)}, u32[]{:S(2)}) %collective-permute-start.3) | collective-permute-done | bytes 8224 | tf_op jit(solution)/shard_map/ppermute | solution.py:57
  30.7 1.1 %fusion.51 = bf16[8,2,16,256]{3,2,1,0:T(8,128)(2,1)S(1)} fusion(f32[8,2,16,256]{3,2,1,0:T(8,128)} %get-tuple-element.15, f32[8,256]{1,0:T(8,128)S(1)} %get-tuple-element.11, f32[8,256]{1,0:T(8,128)S(1)} %get-tuple-element.10), kind=kLoop, calls=%fused_computation.104 | loop fusion | flops 1245184 | bytes 409600 | tf_op jit(solution)/shard_map/convert_element_type | solution.py:173
  32.1 1.0 %fusion.14 = bf16[1,33,2,16,256]{4,1,3,2,0:T(8,128)(2,1)S(1)} fusion(f32[8,2,16,256]{3,0,2,1:T(8,128)S(1)} %fusion.61, bf16[1,33,2,16,256]{4,3,2,1,0:T(8,128)(2,1)S(1)} %copy-done.9, f32[33]{0:T(128)S(1)} %compare_select_fusion, s32[8]{0:T(128)S(1)} %bitcast.367), kind=kOutput, calls=%fused_computation.34 | convolution fusion | flops 27033864 | bytes 1343652 | tf_op jit(solution)/shard_map/nqf,nqhwc->nfhwc/dot_general | solution.py:182
  33.1 0.4 convolution_bitcast_fusion.1
  33.5 0.4 convolution_bitcast_fusion.2
  33.9 0.4 convolution_bitcast_fusion.3
  34.3 0.4 slice_bitcast_fusion
  34.7 0.6 copy-done.7
  36.0 0.9 %copy-done.12 = f32[33,2,16,256]{3,2,1,0:T(8,128)S(1)} copy-done((f32[33,2,16,256]{3,2,1,0:T(8,128)S(1)}, f32[33,2,16,256]{3,2,1,0:T(8,128)}, u32[]{:S(2)}) %copy-start.12) | copy-done | bytes 1081368
  36.8 0.6 fusion.15
  37.8 0.6 copy-done.4
  38.4 0.4 fusion.24
  38.8 0.4 fusion.23
  39.6 0.4 fusion.21
  40.0 0.4 fusion.20
  40.8 0.4 fusion.18
  41.2 0.4 fusion.17
  41.8 1.2 %copy-done.1 = f32[9,256,256]{2,1,0:T(8,128)} copy-done((f32[9,256,256]{2,1,0:T(8,128)}, f32[9,256,256]{2,1,0:T(8,128)S(1)}, u32[]{:S(2)}) %copy-start.1) | copy-done | bytes 2359320
  43.0 1.4 %fusion.8 = f32[4,1,4,96,256]{4,3,2,1,0:T(8,128)S(1)} fusion(s32[]{:T(128)S(6)} %select_n.81, f32[4,2,4,72,256]{4,3,2,1,0:T(8,128)} %bitcast.332, f32[4,2,4,24,256]{4,3,2,1,0:T(8,128)S(1)} %bitcast.334), kind=kLoop, calls=%fused_computation.14 | loop fusion | flops 393216 | bytes 4718596 | tf_op jit(solution)/shard_map/concatenate | solution.py:227
  44.4 0.9 %collective-permute-done.4 = bf16[16,96,256]{2,1,0:T(8,128)(2,1)S(1)} collective-permute-done((bf16[16,96,256]{2,1,0:T(8,128)(2,1)S(1)}, bf16[16,96,256]{2,1,0:T(8,128)(2,1)S(1)}, u32[]{:S(2)}, u32[]{:S(2)}) %collective-permute-start.4) | collective-permute-done | bytes 786464 | tf_op jit(solution)/shard_map/ppermute | solution.py:72
  45.7 1.6 %collective-permute-start.5 = (bf16[8,48,256]{2,1,0:T(8,128)(2,1)S(1)}, bf16[8,48,256]{2,1,0:T(8,128)(2,1)S(1)}, u32[]{:S(2)}, u32[]{:S(2)}) collective-permute-start(bf16[8,48,256]{2,1,0:T(8,128)(2,1)S(1)} %bitcast.357), channel_id=1, source_target_pairs={{0,8},{4,12},{8,0},{12,4},{16,24},{20,28},{24,16},{28,20},{1,9},{5... | collective-permute-start | bytes 589832 | tf_op jit(solution)/shard_map/ppermute | solution.py:72
  47.2 1.6 %collective-permute-start.7 = (bf16[8,48,256]{2,1,0:T(8,128)(2,1)S(1)}, bf16[8,48,256]{2,1,0:T(8,128)(2,1)S(1)}, u32[]{:S(2)}, u32[]{:S(2)}) collective-permute-start(bf16[8,48,256]{2,1,0:T(8,128)(2,1)S(1)} %fusion.54), channel_id=1, source_target_pairs={{0,16},{4,20},{8,24},{12,28},{16,0},{20,4},{24,8},{28,12},{1,17},{... | collective-permute-start | bytes 589832 | tf_op jit(solution)/shard_map/ppermute | solution.py:72
  48.8 3.8 %collective-permute-done.5 = bf16[8,48,256]{2,1,0:T(8,128)(2,1)S(1)} collective-permute-done((bf16[8,48,256]{2,1,0:T(8,128)(2,1)S(1)}, bf16[8,48,256]{2,1,0:T(8,128)(2,1)S(1)}, u32[]{:S(2)}, u32[]{:S(2)}) %collective-permute-start.5) | collective-permute-done | bytes 196640 | tf_op jit(solution)/shard_map/ppermute | solution.py:72
  52.7 1.6 %collective-permute-start.6 = (bf16[4,48,256]{2,1,0:T(8,128)(2,1)S(1)}, bf16[4,48,256]{2,1,0:T(8,128)(2,1)S(1)}, u32[]{:S(2)}, u32[]{:S(2)}) collective-permute-start(bf16[4,48,256]{2,1,0:T(8,128)(2,1)S(1)} %fusion.96), channel_id=1, source_target_pairs={{0,16},{4,20},{8,24},{12,28},{16,0},{20,4},{24,8},{28,12},{1,17},{... | collective-permute-start | bytes 294920 | tf_op jit(solution)/shard_map/ppermute | solution.py:72
  54.4 1.5 %collective-permute-start.8 = (bf16[4,48,256]{2,1,0:T(8,128)(2,1)S(1)}, bf16[4,48,256]{2,1,0:T(8,128)(2,1)S(1)}, u32[]{:S(2)}, u32[]{:S(2)}) collective-permute-start(bf16[4,48,256]{2,1,0:T(8,128)(2,1)S(1)} %fusion.97), channel_id=1, source_target_pairs={{0,8},{4,12},{8,0},{12,4},{16,24},{20,28},{24,16},{28,20},{1,9},{5... | collective-permute-start | bytes 294920 | tf_op jit(solution)/shard_map/ppermute | solution.py:72
  55.9 1.5 %collective-permute-done.6 = bf16[4,48,256]{2,1,0:T(8,128)(2,1)S(1)} collective-permute-done((bf16[4,48,256]{2,1,0:T(8,128)(2,1)S(1)}, bf16[4,48,256]{2,1,0:T(8,128)(2,1)S(1)}, u32[]{:S(2)}, u32[]{:S(2)}) %collective-permute-start.6) | collective-permute-done | bytes 98336 | tf_op jit(solution)/shard_map/ppermute | solution.py:72
  57.4 1.6 %collective-permute-done.8 = bf16[4,48,256]{2,1,0:T(8,128)(2,1)S(1)} collective-permute-done((bf16[4,48,256]{2,1,0:T(8,128)(2,1)S(1)}, bf16[4,48,256]{2,1,0:T(8,128)(2,1)S(1)}, u32[]{:S(2)}, u32[]{:S(2)}) %collective-permute-start.8) | collective-permute-done | bytes 98336 | tf_op jit(solution)/shard_map/ppermute | solution.py:72
  59.2 1.6 %collective-permute-start.9 = (bf16[96,256]{1,0:T(8,128)(2,1)S(1)}, bf16[96,256]{1,0:T(8,128)(2,1)S(1)}, u32[]{:S(2)}, u32[]{:S(2)}) collective-permute-start(bf16[96,256]{1,0:T(8,128)(2,1)S(1)} %get-tuple-element.7), channel_id=1, source_target_pairs={{0,1},{1,2},{2,3},{3,0},{4,5},{5,6},{6,7},{7,4},{8,9},{9,10},{10,1... | collective-permute-start | bytes 147464 | tf_op jit(solution)/shard_map/ppermute | solution.py:107
  60.8 1.1 %collective-permute-start.10 = (bf16[96,256]{1,0:T(8,128)(2,1)S(1)}, bf16[96,256]{1,0:T(8,128)(2,1)S(1)}, u32[]{:S(2)}, u32[]{:S(2)}) collective-permute-start(bf16[96,256]{1,0:T(8,128)(2,1)S(1)} %get-tuple-element.8), channel_id=1, source_target_pairs={{0,2},{1,3},{2,0},{3,1},{4,6},{5,7},{6,4},{7,5},{8,10},{9,11},{10,... | collective-permute-start | bytes 147464 | tf_op jit(solution)/shard_map/ppermute | solution.py:107
  61.9 2.9 %collective-permute-start.11 = (bf16[96,256]{1,0:T(8,128)(2,1)S(1)}, bf16[96,256]{1,0:T(8,128)(2,1)S(1)}, u32[]{:S(2)}, u32[]{:S(2)}) collective-permute-start(bf16[96,256]{1,0:T(8,128)(2,1)S(1)} %get-tuple-element.9), channel_id=1, source_target_pairs={{0,3},{1,0},{2,1},{3,2},{4,7},{5,4},{6,5},{7,6},{8,11},{9,8},{10,9... | collective-permute-start | bytes 147464 | tf_op jit(solution)/shard_map/ppermute | solution.py:107
  65.1 0.8 %collective-permute-done.10 = bf16[96,256]{1,0:T(8,128)(2,1)S(1)} collective-permute-done((bf16[96,256]{1,0:T(8,128)(2,1)S(1)}, bf16[96,256]{1,0:T(8,128)(2,1)S(1)}, u32[]{:S(2)}, u32[]{:S(2)}) %collective-permute-start.10) | collective-permute-done | bytes 49184 | tf_op jit(solution)/shard_map/ppermute | solution.py:107
  66.0 0.6 collective-permute-done.11
  66.8 0.6 add_add_fusion.1
  67.4 0.7 add_add_fusion
  (88 shorter events, 8.0 us)
Async XLA Ops:
  0.6 20.7 %copy-start = (bf16[256,256]{1,0:T(8,128)(2,1)S(1)}, bf16[256,256]{1,0:T(8,128)(2,1)}, u32[]{:S(2)}) copy-start(bf16[256,256]{1,0:T(8,128)(2,1)} %param.12) | copy-start | bytes 393220
  0.6 9.1 %collective-permute-start = (bf16[1,33,1,8,256]{4,3,2,1,0:T(8,128)(2,1)}, bf16[1,33,1,8,256]{4,3,2,1,0:T(8,128)(2,1)S(1)}, u32[]{:S(2)}, u32[]{:S(2)}) collective-permute-start(bf16[1,33,1,8,256]{4,3,2,1,0:T(8,128)(2,1)} %param.8), channel_id=1, source_target_pairs={{0,1},{1,2},{2,3},{4,5},{5,6},{6,7},{8,9},{9,10},{10,11},{12,13},{... | collective-permute-start | bytes 405512 | tf_op jit(solution)/shard_map/ppermute | solution.py:19
  5.7 7.1 %collective-permute-start.1 = (bf16[1,33,1,8,256]{4,3,2,1,0:T(8,128)(2,1)}, bf16[1,33,1,8,256]{4,3,2,1,0:T(8,128)(2,1)S(1)}, u32[]{:S(2)}, u32[]{:S(2)}) collective-permute-start(bf16[1,33,1,8,256]{4,3,2,1,0:T(8,128)(2,1)} %param.8), channel_id=1, source_target_pairs={{1,0},{2,1},{3,2},{5,4},{6,5},{7,6},{9,8},{10,9},{11,10},{13,12},{... | collective-permute-start | bytes 405512 | tf_op jit(solution)/shard_map/ppermute | solution.py:20
  10.0 4.8 %copy-start.3 = (bf16[1,33,1,16,256]{4,3,2,1,0:T(8,128)(2,1)}, bf16[1,33,1,16,256]{4,3,2,1,0:T(8,128)(2,1)S(1)}, u32[]{:S(2)}) copy-start(bf16[1,33,1,16,256]{4,3,2,1,0:T(8,128)(2,1)S(1)} %slice.130) | copy-start | bytes 811012
  13.2 1.3 %copy-start.8 = (bf16[3,3,256,256]{3,2,1,0:T(8,128)(2,1)S(1)}, bf16[3,3,256,256]{3,2,1,0:T(8,128)(2,1)}, u32[]{:S(2)}) copy-start(bf16[3,3,256,256]{3,2,1,0:T(8,128)(2,1)} %param.10) | copy-start | bytes 3538948
  17.0 1.4 %copy-start.6 = (bf16[3,256,256]{2,1,0:T(8,128)(2,1)S(1)}, bf16[3,256,256]{2,1,0:T(8,128)(2,1)}, u32[]{:S(2)}) copy-start(bf16[3,256,256]{2,1,0:T(8,128)(2,1)} %param.11) | copy-start | bytes 1179652
  18.7 1.1 %copy-start.5 = (f32[33,16,256]{2,1,0:T(8,128)S(1)}, f32[33,16,256]{2,1,0:T(8,128)}, u32[]{:S(2)}) copy-start(f32[33,16,256]{2,1,0:T(8,128)} %convert_element_type.133) | copy-start | bytes 1622020
  19.8 1.1 %copy-start.11 = (s32[1,8]{1,0:T(1,128)S(1)}, s32[1,8]{1,0:T(1,128)}, u32[]{:S(2)}) copy-start(s32[1,8]{1,0:T(1,128)} %param.14) | copy-start | bytes 100
  20.1 0.8 %copy-start.2 = (bf16[33,2,16,256]{3,2,1,0:T(8,128)(2,1)}, bf16[33,2,16,256]{3,2,1,0:T(8,128)(2,1)S(1)}, u32[]{:S(2)}) copy-start(bf16[33,2,16,256]{3,2,1,0:T(8,128)(2,1)S(1)} %fusion.16) | copy-start | bytes 1622020
  20.1 3.7 %copy-start.10 = (f32[256]{0:T(256)S(1)}, f32[256]{0:T(256)}, u32[]{:S(2)}) copy-start(f32[256]{0:T(256)} %param.13) | copy-start | bytes 3076
  22.3 3.7 %collective-permute-start.2 = (f32[1,8,256]{2,1,0:T(8,128)S(1)}, f32[1,8,256]{2,1,0:T(8,128)S(1)}, u32[]{:S(2)}, u32[]{:S(2)}) collective-permute-start(f32[1,8,256]{2,1,0:T(8,128)S(1)} %bitcast.365), channel_id=1, source_target_pairs={{0,1},{1,0},{2,3},{3,2},{4,5},{5,4},{6,7},{7,6},{8,9},{9,8},{10,11... | collective-permute-start | bytes 24584 | tf_op jit(solution)/shard_map/ppermute | solution.py:57
  25.9 4.5 %collective-permute-start.3 = (f32[1,8,256]{2,1,0:T(8,128)S(1)}, f32[1,8,256]{2,1,0:T(8,128)S(1)}, u32[]{:S(2)}, u32[]{:S(2)}) collective-permute-start(f32[1,8,256]{2,1,0:T(8,128)S(1)} %bitcast_add_fusion.5), channel_id=1, source_target_pairs={{0,2},{1,3},{2,0},{3,1},{4,6},{5,7},{6,4},{7,5},{8,10},{9,11},{10,... | collective-permute-start | bytes 24584 | tf_op jit(solution)/shard_map/ppermute | solution.py:57
  28.5 3.5 %copy-start.9 = (bf16[1,33,2,16,256]{4,3,2,1,0:T(8,128)(2,1)S(1)}, bf16[1,33,2,16,256]{4,3,2,1,0:T(8,128)(2,1)}, u32[]{:S(2)}) copy-start(bf16[1,33,2,16,256]{4,3,2,1,0:T(8,128)(2,1)} %param.15) | copy-start | bytes 1622020
  34.2 1.0 %copy-start.7 = (bf16[3,256,256]{2,1,0:T(8,128)(2,1)S(1)}, bf16[3,256,256]{2,1,0:T(8,128)(2,1)}, u32[]{:S(2)}) copy-start(bf16[3,256,256]{2,1,0:T(8,128)(2,1)} %param.11) | copy-start | bytes 1179652
  35.6 1.2 %copy-start.12 = (f32[33,2,16,256]{3,2,1,0:T(8,128)S(1)}, f32[33,2,16,256]{3,2,1,0:T(8,128)}, u32[]{:S(2)}) copy-start(f32[33,2,16,256]{3,2,1,0:T(8,128)} %get-tuple-element.13) | copy-start | bytes 3244036
  37.4 1.0 %copy-start.4 = (bf16[1,33,1,16,256]{4,3,2,1,0:T(8,128)(2,1)S(1)}, bf16[1,33,1,16,256]{4,3,2,1,0:T(8,128)(2,1)}, u32[]{:S(2)}) copy-start(bf16[1,33,1,16,256]{4,3,2,1,0:T(8,128)(2,1)} %copy-done.3) | copy-start | bytes 811012
  41.6 1.4 %copy-start.1 = (f32[9,256,256]{2,1,0:T(8,128)}, f32[9,256,256]{2,1,0:T(8,128)S(1)}, u32[]{:S(2)}) copy-start(f32[9,256,256]{2,1,0:T(8,128)S(1)} %fusion.17) | copy-start | bytes 7077892
  43.0 2.3 %collective-permute-start.4 = (bf16[16,96,256]{2,1,0:T(8,128)(2,1)S(1)}, bf16[16,96,256]{2,1,0:T(8,128)(2,1)S(1)}, u32[]{:S(2)}, u32[]{:S(2)}) collective-permute-start(bf16[16,96,256]{2,1,0:T(8,128)(2,1)S(1)} %bitcast.352), channel_id=1, source_target_pairs={{0,4},{4,0},{8,12},{12,8},{16,20},{20,16},{24,28},{28,24},{1,5},{5... | collective-permute-start | bytes 2359304 | tf_op jit(solution)/shard_map/ppermute | solution.py:72
  45.7 7.0 %collective-permute-start.5 = (bf16[8,48,256]{2,1,0:T(8,128)(2,1)S(1)}, bf16[8,48,256]{2,1,0:T(8,128)(2,1)S(1)}, u32[]{:S(2)}, u32[]{:S(2)}) collective-permute-start(bf16[8,48,256]{2,1,0:T(8,128)(2,1)S(1)} %bitcast.357), channel_id=1, source_target_pairs={{0,8},{4,12},{8,0},{12,4},{16,24},{20,28},{24,16},{28,20},{1,9},{5... | collective-permute-start | bytes 589832 | tf_op jit(solution)/shard_map/ppermute | solution.py:72
  47.2 7.1 %collective-permute-start.7 = (bf16[8,48,256]{2,1,0:T(8,128)(2,1)S(1)}, bf16[8,48,256]{2,1,0:T(8,128)(2,1)S(1)}, u32[]{:S(2)}, u32[]{:S(2)}) collective-permute-start(bf16[8,48,256]{2,1,0:T(8,128)(2,1)S(1)} %fusion.54), channel_id=1, source_target_pairs={{0,16},{4,20},{8,24},{12,28},{16,0},{20,4},{24,8},{28,12},{1,17},{... | collective-permute-start | bytes 589832 | tf_op jit(solution)/shard_map/ppermute | solution.py:72
  52.7 4.7 %collective-permute-start.6 = (bf16[4,48,256]{2,1,0:T(8,128)(2,1)S(1)}, bf16[4,48,256]{2,1,0:T(8,128)(2,1)S(1)}, u32[]{:S(2)}, u32[]{:S(2)}) collective-permute-start(bf16[4,48,256]{2,1,0:T(8,128)(2,1)S(1)} %fusion.96), channel_id=1, source_target_pairs={{0,16},{4,20},{8,24},{12,28},{16,0},{20,4},{24,8},{28,12},{1,17},{... | collective-permute-start | bytes 294920 | tf_op jit(solution)/shard_map/ppermute | solution.py:72
  54.4 4.7 %collective-permute-start.8 = (bf16[4,48,256]{2,1,0:T(8,128)(2,1)S(1)}, bf16[4,48,256]{2,1,0:T(8,128)(2,1)S(1)}, u32[]{:S(2)}, u32[]{:S(2)}) collective-permute-start(bf16[4,48,256]{2,1,0:T(8,128)(2,1)S(1)} %fusion.97), channel_id=1, source_target_pairs={{0,8},{4,12},{8,0},{12,4},{16,24},{20,28},{24,16},{28,20},{1,9},{5... | collective-permute-start | bytes 294920 | tf_op jit(solution)/shard_map/ppermute | solution.py:72
  59.2 5.9 %collective-permute-start.9 = (bf16[96,256]{1,0:T(8,128)(2,1)S(1)}, bf16[96,256]{1,0:T(8,128)(2,1)S(1)}, u32[]{:S(2)}, u32[]{:S(2)}) collective-permute-start(bf16[96,256]{1,0:T(8,128)(2,1)S(1)} %get-tuple-element.7), channel_id=1, source_target_pairs={{0,1},{1,2},{2,3},{3,0},{4,5},{5,6},{6,7},{7,4},{8,9},{9,10},{10,1... | collective-permute-start | bytes 147464 | tf_op jit(solution)/shard_map/ppermute | solution.py:107
  60.8 5.1 %collective-permute-start.10 = (bf16[96,256]{1,0:T(8,128)(2,1)S(1)}, bf16[96,256]{1,0:T(8,128)(2,1)S(1)}, u32[]{:S(2)}, u32[]{:S(2)}) collective-permute-start(bf16[96,256]{1,0:T(8,128)(2,1)S(1)} %get-tuple-element.8), channel_id=1, source_target_pairs={{0,2},{1,3},{2,0},{3,1},{4,6},{5,7},{6,4},{7,5},{8,10},{9,11},{10,... | collective-permute-start | bytes 147464 | tf_op jit(solution)/shard_map/ppermute | solution.py:107
  61.9 4.6 %collective-permute-start.11 = (bf16[96,256]{1,0:T(8,128)(2,1)S(1)}, bf16[96,256]{1,0:T(8,128)(2,1)S(1)}, u32[]{:S(2)}, u32[]{:S(2)}) collective-permute-start(bf16[96,256]{1,0:T(8,128)(2,1)S(1)} %get-tuple-element.9), channel_id=1, source_target_pairs={{0,3},{1,0},{2,1},{3,2},{4,7},{5,4},{6,5},{7,6},{8,11},{9,8},{10,9... | collective-permute-start | bytes 147464 | tf_op jit(solution)/shard_map/ppermute | solution.py:107

commit v12 on v11

--- a/solution.py
+++ b/solution.py
@@ -22,8 +22,12 @@
 
 
 def upsample(values):
-    doubled = jnp.repeat(values, 2, axis=-3)
-    return jnp.repeat(doubled, 2, axis=-2)
+    cols = values.shape[-2]
+    spread = (jnp.arange(2 * cols)[:, None] // 2 == jnp.arange(cols)[None, :]).astype(values.dtype)
+    wide = jnp.einsum(
+        "...wc,vw->...vc", values, spread, preferred_element_type=jnp.float32
+    ).astype(values.dtype)
+    return jnp.repeat(wide, 2, axis=-3)
 
 
 def silu_slope(pre_act):

time: 68.5 us -> 68.8 us (level)
  matrix products: 13.3 us -> 15.2 us
  local copies, waits for them, and re-layouts: 7.77 us -> 6.91 us
  other arithmetic: 6.36 us -> 5.51 us
    dot_general x0 -> x3, matrix products: none -> 1.74 us  [upsample(): jnp.einsum('...wc,vw->...vc', values, spread, preferred_element_type=jnp....]
    broadcast_in_dim x5 -> x0, local copies, waits for them, and re-layouts: 1.48 us -> none  [upsample(): return jnp.repeat(doubled, 2, axis=-2)]
    convert_element_type x1 -> x0, other arithmetic: 0.86 us -> none  [on_device(): upsampled.astype(jnp.float32) + mixing]
    ppermute x1, waiting for transfers between devices: 2.88 us -> 3.68 us  [exchange_rows(): below = lax.ppermute(head, axis, [(i + 1, i) for i in range(ends)])]
    convert_element_type x0 -> x1, local copies, waits for them, and re-layouts: none -> 0.8 us  [upsample(): wide = jnp.einsum('...wc,vw->...vc', values, spread, preferred_element_ty...]
    ppermute x2, waiting for transfers between devices: 4.05 us -> 3.26 us  [space_sum(): lax.ppermute(values, 'space', [(i, i ^ step) for i in range(count)])]
    unnamed x42 -> x46, local copies, waits for them, and re-layouts: 5.43 us -> 5.43 us
where the time goes in v12:
time: 68.8 us; the launch traced here: 68.3 us
  starting transfers between devices  22.4 us (33%)
  waiting for transfers between devices  16.4 us (24%)
  matrix products  15.2 us (22%)
  local copies, waits for them, and re-layouts  6.91 us (10%)
  other arithmetic  5.51 us (8%)
  between operations  1.92 us (3%)
    ppermute x5, waiting for transfers between devices, _halve(): got = lax.ppermute(send, axis, [(i, i ^ 1 << bit) for i in range(size)])  7.8 us
    ppermute x5, starting transfers between devices, _halve(): got = lax.ppermute(send, axis, [(i, i ^ 1 << bit) for i in range(size)])  6.24 us
    ppermute x3, starting transfers between devices, halving_scatter(): lax.ppermute(send.astype(jnp.bfloat16), 'space', [(i, (i + shift) % ns) f...  5.63 us
    unnamed x46, local copies, waits for them, and re-layouts  5.43 us
    ppermute x1, starting transfers between devices, exchange_rows(): above = lax.ppermute(tail, axis, [(i, i + 1) for i in range(ends)])  5.1 us
    ppermute x2, starting transfers between devices, space_sum(): lax.ppermute(values, 'space', [(i, i ^ step) for i in range(count)])  4.13 us
    dot_general x9, matrix products, on_device(): jnp.einsum('nfhwc,cd->nfhwd', window, spatial_weight[row_tap, col_tap], p...  3.88 us
    dot_general x9, matrix products, on_device(): jnp.einsum('nfhwc,nfhwd->cd', window, pre_slope, preferred_element_type=j...  3.73 us
  transfers between devices with their start and end apart: 12, of which 10 were waited for; matrix products, arithmetic and copies ran while one was open for 6% of the time, Pallas kernels for 0%

profile of v12, /device:TPU:0, one launch (start us, length us, event | category | flops | bytes accessed | tf_op | source)
XLA Modules:
  0.0 68.3 jit_solution(3380625692684247335)
XLA Ops:
  0.6 5.1 %collective-permute-start = (bf16[1,33,1,8,256]{4,3,1,2,0:T(8,128)(2,1)}, bf16[1,33,1,8,256]{4,3,1,2,0:T(8,128)(2,1)S(1)}, u32[]{:S(2)}, u32[]{:S(2)}) collective-permute-start(bf16[1,33,1,8,256]{4,3,1,2,0:T(8,128)(2,1)} %bitcast.392), channel_id=1, source_target_pairs={{0,1},{1,2},{2,3},{4,5},{5,6},{6,7},{8,9},{9,10},{10,11},{12,13},{... | collective-permute-start | bytes 405512 | tf_op jit(solution)/shard_map/ppermute | solution.py:19
  5.8 1.3 %collective-permute-start.1 = (bf16[1,33,1,8,256]{4,3,1,2,0:T(8,128)(2,1)}, bf16[1,33,1,8,256]{4,3,1,2,0:T(8,128)(2,1)S(1)}, u32[]{:S(2)}, u32[]{:S(2)}) collective-permute-start(bf16[1,33,1,8,256]{4,3,1,2,0:T(8,128)(2,1)} %bitcast.393), channel_id=1, source_target_pairs={{1,0},{2,1},{3,2},{5,4},{6,5},{7,6},{9,8},{10,9},{11,10},{13,12},{... | collective-permute-start | bytes 405512 | tf_op jit(solution)/shard_map/ppermute | solution.py:20
  7.1 1.2 %fusion.136 = (f32[33,16,256]{2,1,0:T(8,128)S(1)}, bf16[33,16,256]{2,1,0:T(8,128)(2,1)S(1)}) fusion(bf16[1,33,1,8,256]{4,3,2,1,0:T(8,128)(2,1)} %param.8, s32[16]{0:T(128)S(1)} %and_select_fusion), kind=kOutput, calls=%fused_computation.218 | convolution fusion | flops 2433152 | bytes 946240 | tf_op jit(solution)/shard_map/...wc,vw->...vc/dot_general | solution.py:27
  9.2 3.7 %collective-permute-done.1 = bf16[1,33,1,8,256]{4,3,1,2,0:T(8,128)(2,1)S(1)} collective-permute-done((bf16[1,33,1,8,256]{4,3,1,2,0:T(8,128)(2,1)}, bf16[1,33,1,8,256]{4,3,1,2,0:T(8,128)(2,1)S(1)}, u32[]{:S(2)}, u32[]{:S(2)}) %collective-permute-start.1) | collective-permute-done | bytes 135200 | tf_op jit(solution)/shard_map/ppermute | solution.py:20
  13.2 0.9 %fusion.5 = bf16[1,33,4,18,256]{4,3,2,1,0:T(8,128)(2,1)S(1)} fusion(bf16[1,33,1,16,256]{4,3,2,1,0:T(8,128)(2,1)S(1)} %fusion.19, bf16[1,33,2,16,256]{4,3,2,1,0:T(8,128)(2,1)S(1)} %reshape.434, bf16[1,33,1,16,256]{4,3,2,1,0:T(8,128)(2,1)S(1)} %fusion.18), kind=kLoop, calls=%fused_computation.11 | loop fusion | flops 7299072 | bytes 2297856 | tf_op jit(solution)/shard_map/concatenate | solution.py:135
  14.2 0.4 copy-done.9
  17.1 1.4 %multiply_convert_fusion = (bf16[33,2,16,256]{3,2,1,0:T(8,128)(2,1)S(1)}, f32[33,2,16,256]{3,2,1,0:T(8,128)}) fusion(f32[33,2,16,256]{3,2,1,0:T(8,128)S(1)} %convolution_add_fusion.5, bf16[3,3,256,256]{3,2,1,0:T(8,128)(2,1)S(1)} %copy-done.9, bf16[1,33,4,18,256]{4,3,2,1,0:T(8,128)(2,1)S(1)} %fusion.5), kind=kOutput, calls=%fused_computation.64 | convolution fusion | flops 140034048 | bytes 3375104 | tf_op jit(solution)/shard_map/nfhwc,cd->nfhwd/dot_general | solution.py:145
  19.8 0.4 fusion.29
  20.2 0.9 %fusion.57 = (f32[8,256]{1,0:T(8,128)S(1)}, f32[8,2,16,256]{3,2,1,0:T(8,128)}) fusion(bf16[256,256]{1,0:T(8,128)(2,1)S(1)} %copy-done, bf16[8,2,16,256]{3,0,2,1:T(8,128)(2,1)S(1)} %fusion.29), kind=kOutput, calls=%fused_computation.115 | convolution fusion | flops 34142208 | bytes 532480 | tf_op jit(solution)/shard_map/nqhwc,ce->nqhwe/dot_general | solution.py:170
  21.1 1.6 %collective-permute-start.2 = (f32[1,8,256]{2,1,0:T(8,128)S(1)}, f32[1,8,256]{2,1,0:T(8,128)S(1)}, u32[]{:S(2)}, u32[]{:S(2)}) collective-permute-start(f32[1,8,256]{2,1,0:T(8,128)S(1)} %bitcast.398), channel_id=1, source_target_pairs={{0,1},{1,0},{2,3},{3,2},{4,5},{5,4},{6,7},{7,6},{8,9},{9,8},{10,11... | collective-permute-start | bytes 24584 | tf_op jit(solution)/shard_map/ppermute | solution.py:61
  22.7 2.1 %collective-permute-done.2 = f32[1,8,256]{2,1,0:T(8,128)S(1)} collective-permute-done((f32[1,8,256]{2,1,0:T(8,128)S(1)}, f32[1,8,256]{2,1,0:T(8,128)S(1)}, u32[]{:S(2)}, u32[]{:S(2)}) %collective-permute-start.2) | collective-permute-done | bytes 8224 | tf_op jit(solution)/shard_map/ppermute | solution.py:61
  24.8 2.6 %collective-permute-start.3 = (f32[1,8,256]{2,1,0:T(8,128)S(1)}, f32[1,8,256]{2,1,0:T(8,128)S(1)}, u32[]{:S(2)}, u32[]{:S(2)}) collective-permute-start(f32[1,8,256]{2,1,0:T(8,128)S(1)} %bitcast_add_fusion.5), channel_id=1, source_target_pairs={{0,2},{1,3},{2,0},{3,1},{4,6},{5,7},{6,4},{7,5},{8,10},{9,11},{10,... | collective-permute-start | bytes 24584 | tf_op jit(solution)/shard_map/ppermute | solution.py:61
  27.4 0.8 %copy.48 = bf16[33,16,256]{2,0,1:T(8,128)(2,1)} copy(bf16[33,16,256]{2,1,0:T(8,128)(2,1)S(1)} %get-tuple-element.15) | data formatting | bytes 540672 | tf_op jit(solution)/shard_map/convert_element_type | solution.py:29
  28.2 1.2 %collective-permute-done.3 = f32[1,8,256]{2,1,0:T(8,128)S(1)} collective-permute-done((f32[1,8,256]{2,1,0:T(8,128)S(1)}, f32[1,8,256]{2,1,0:T(8,128)S(1)}, u32[]{:S(2)}, u32[]{:S(2)}) %collective-permute-start.3) | collective-permute-done | bytes 8224 | tf_op jit(solution)/shard_map/ppermute | solution.py:61
  29.5 1.1 %fusion.55 = bf16[8,2,16,256]{3,2,1,0:T(8,128)(2,1)S(1)} fusion(f32[8,2,16,256]{3,2,1,0:T(8,128)} %get-tuple-element.17, f32[8,256]{1,0:T(8,128)S(1)} %get-tuple-element.11, f32[8,256]{1,0:T(8,128)S(1)} %get-tuple-element.10), kind=kLoop, calls=%fused_computation.111 | loop fusion | flops 1245184 | bytes 409600 | tf_op jit(solution)/shard_map/convert_element_type | solution.py:177
  30.9 1.0 %fusion.14 = bf16[1,33,2,16,256]{4,1,3,2,0:T(8,128)(2,1)S(1)} fusion(f32[8,2,16,256]{3,0,2,1:T(8,128)S(1)} %fusion.68, bf16[1,33,2,16,256]{4,3,2,1,0:T(8,128)(2,1)S(1)} %copy-done.10, f32[33]{0:T(128)S(1)} %compare_select_fusion, s32[8]{0:T(128)S(1)} %bitcast.400), kind=kOutput, calls=%fused_computation.34 | convolution fusion | flops 27033864 | bytes 1343652 | tf_op jit(solution)/shard_map/nqf,nqhwc->nfhwc/dot_general | solution.py:186
  33.1 0.4 slice_bitcast_fusion
  33.5 0.6 copy-done.8
  34.8 0.9 %copy-done.14 = f32[33,2,16,256]{3,2,1,0:T(8,128)S(1)} copy-done((f32[33,2,16,256]{3,2,1,0:T(8,128)S(1)}, f32[33,2,16,256]{3,2,1,0:T(8,128)}, u32[]{:S(2)}) %copy-start.14) | copy-done | bytes 1081368
  35.7 0.6 fusion.15
  36.3 0.4 fusion.27
  36.7 0.6 copy-done.6
  37.2 0.4 fusion.26
  37.6 0.4 fusion.25
  38.1 0.4 fusion.24
  38.4 0.6 copy-done.11
  39.0 0.6 fusion.28
  39.6 0.4 fusion.23
  40.4 0.6 copy-done.4
  41.0 0.4 fusion.21
  41.4 0.4 fusion.20
  42.0 1.3 %copy-done.1 = f32[9,256,256]{2,1,0:T(8,128)} copy-done((f32[9,256,256]{2,1,0:T(8,128)}, f32[9,256,256]{2,1,0:T(8,128)S(1)}, u32[]{:S(2)}) %copy-start.1) | copy-done | bytes 2359320
  43.2 1.4 %fusion.8 = f32[4,1,4,96,256]{4,3,2,1,0:T(8,128)S(1)} fusion(s32[]{:T(128)S(6)} %select_n.98, f32[4,2,4,72,256]{4,3,2,1,0:T(8,128)} %bitcast.366, f32[4,2,4,24,256]{4,3,2,1,0:T(8,128)S(1)} %bitcast.368), kind=kLoop, calls=%fused_computation.14 | loop fusion | flops 393216 | bytes 4718596 | tf_op jit(solution)/shard_map/concatenate | solution.py:231
  44.6 0.9 %collective-permute-done.4 = bf16[16,96,256]{2,1,0:T(8,128)(2,1)S(1)} collective-permute-done((bf16[16,96,256]{2,1,0:T(8,128)(2,1)S(1)}, bf16[16,96,256]{2,1,0:T(8,128)(2,1)S(1)}, u32[]{:S(2)}, u32[]{:S(2)}) %collective-permute-start.4) | collective-permute-done | bytes 786464 | tf_op jit(solution)/shard_map/ppermute | solution.py:76
  45.9 1.5 %collective-permute-start.5 = (bf16[8,48,256]{2,1,0:T(8,128)(2,1)S(1)}, bf16[8,48,256]{2,1,0:T(8,128)(2,1)S(1)}, u32[]{:S(2)}, u32[]{:S(2)}) collective-permute-start(bf16[8,48,256]{2,1,0:T(8,128)(2,1)S(1)} %bitcast.391), channel_id=1, source_target_pairs={{0,8},{4,12},{8,0},{12,4},{16,24},{20,28},{24,16},{28,20},{1,9},{5... | collective-permute-start | bytes 589832 | tf_op jit(solution)/shard_map/ppermute | solution.py:76
  47.4 1.6 %collective-permute-start.7 = (bf16[8,48,256]{2,1,0:T(8,128)(2,1)S(1)}, bf16[8,48,256]{2,1,0:T(8,128)(2,1)S(1)}, u32[]{:S(2)}, u32[]{:S(2)}) collective-permute-start(bf16[8,48,256]{2,1,0:T(8,128)(2,1)S(1)} %fusion.58), channel_id=1, source_target_pairs={{0,16},{4,20},{8,24},{12,28},{16,0},{20,4},{24,8},{28,12},{1,17},{... | collective-permute-start | bytes 589832 | tf_op jit(solution)/shard_map/ppermute | solution.py:76
  49.1 3.8 %collective-permute-done.5 = bf16[8,48,256]{2,1,0:T(8,128)(2,1)S(1)} collective-permute-done((bf16[8,48,256]{2,1,0:T(8,128)(2,1)S(1)}, bf16[8,48,256]{2,1,0:T(8,128)(2,1)S(1)}, u32[]{:S(2)}, u32[]{:S(2)}) %collective-permute-start.5) | collective-permute-done | bytes 196640 | tf_op jit(solution)/shard_map/ppermute | solution.py:76
  53.0 1.6 %collective-permute-start.6 = (bf16[4,48,256]{2,1,0:T(8,128)(2,1)S(1)}, bf16[4,48,256]{2,1,0:T(8,128)(2,1)S(1)}, u32[]{:S(2)}, u32[]{:S(2)}) collective-permute-start(bf16[4,48,256]{2,1,0:T(8,128)(2,1)S(1)} %fusion.103), channel_id=1, source_target_pairs={{0,16},{4,20},{8,24},{12,28},{16,0},{20,4},{24,8},{28,12},{1,17},{... | collective-permute-start | bytes 294920 | tf_op jit(solution)/shard_map/ppermute | solution.py:76
  54.6 1.5 %collective-permute-start.8 = (bf16[4,48,256]{2,1,0:T(8,128)(2,1)S(1)}, bf16[4,48,256]{2,1,0:T(8,128)(2,1)S(1)}, u32[]{:S(2)}, u32[]{:S(2)}) collective-permute-start(bf16[4,48,256]{2,1,0:T(8,128)(2,1)S(1)} %fusion.104), channel_id=1, source_target_pairs={{0,8},{4,12},{8,0},{12,4},{16,24},{20,28},{24,16},{28,20},{1,9},{5... | collective-permute-start | bytes 294920 | tf_op jit(solution)/shard_map/ppermute | solution.py:76
  56.2 1.5 %collective-permute-done.6 = bf16[4,48,256]{2,1,0:T(8,128)(2,1)S(1)} collective-permute-done((bf16[4,48,256]{2,1,0:T(8,128)(2,1)S(1)}, bf16[4,48,256]{2,1,0:T(8,128)(2,1)S(1)}, u32[]{:S(2)}, u32[]{:S(2)}) %collective-permute-start.6) | collective-permute-done | bytes 98336 | tf_op jit(solution)/shard_map/ppermute | solution.py:76
  57.7 1.6 %collective-permute-done.8 = bf16[4,48,256]{2,1,0:T(8,128)(2,1)S(1)} collective-permute-done((bf16[4,48,256]{2,1,0:T(8,128)(2,1)S(1)}, bf16[4,48,256]{2,1,0:T(8,128)(2,1)S(1)}, u32[]{:S(2)}, u32[]{:S(2)}) %collective-permute-start.8) | collective-permute-done | bytes 98336 | tf_op jit(solution)/shard_map/ppermute | solution.py:76
  59.4 1.6 %collective-permute-start.9 = (bf16[96,256]{1,0:T(8,128)(2,1)S(1)}, bf16[96,256]{1,0:T(8,128)(2,1)S(1)}, u32[]{:S(2)}, u32[]{:S(2)}) collective-permute-start(bf16[96,256]{1,0:T(8,128)(2,1)S(1)} %get-tuple-element.7), channel_id=1, source_target_pairs={{0,1},{1,2},{2,3},{3,0},{4,5},{5,6},{6,7},{7,4},{8,9},{9,10},{10,1... | collective-permute-start | bytes 147464 | tf_op jit(solution)/shard_map/ppermute | solution.py:111
  61.0 1.1 %collective-permute-start.10 = (bf16[96,256]{1,0:T(8,128)(2,1)S(1)}, bf16[96,256]{1,0:T(8,128)(2,1)S(1)}, u32[]{:S(2)}, u32[]{:S(2)}) collective-permute-start(bf16[96,256]{1,0:T(8,128)(2,1)S(1)} %get-tuple-element.8), channel_id=1, source_target_pairs={{0,2},{1,3},{2,0},{3,1},{4,6},{5,7},{6,4},{7,5},{8,10},{9,11},{10,... | collective-permute-start | bytes 147464 | tf_op jit(solution)/shard_map/ppermute | solution.py:111
  62.1 2.9 %collective-permute-start.11 = (bf16[96,256]{1,0:T(8,128)(2,1)S(1)}, bf16[96,256]{1,0:T(8,128)(2,1)S(1)}, u32[]{:S(2)}, u32[]{:S(2)}) collective-permute-start(bf16[96,256]{1,0:T(8,128)(2,1)S(1)} %get-tuple-element.9), channel_id=1, source_target_pairs={{0,3},{1,0},{2,1},{3,2},{4,7},{5,4},{6,5},{7,6},{8,11},{9,8},{10,9... | collective-permute-start | bytes 147464 | tf_op jit(solution)/shard_map/ppermute | solution.py:111
  65.4 0.8 %collective-permute-done.10 = bf16[96,256]{1,0:T(8,128)(2,1)S(1)} collective-permute-done((bf16[96,256]{1,0:T(8,128)(2,1)S(1)}, bf16[96,256]{1,0:T(8,128)(2,1)S(1)}, u32[]{:S(2)}, u32[]{:S(2)}) %collective-permute-start.10) | collective-permute-done | bytes 49184 | tf_op jit(solution)/shard_map/ppermute | solution.py:111
  66.2 0.6 collective-permute-done.11
  67.0 0.6 add_add_fusion.1
  67.7 0.7 add_add_fusion
  (90 shorter events, 8.3 us)
Async XLA Ops:
  0.6 19.6 %copy-start = (bf16[256,256]{1,0:T(8,128)(2,1)S(1)}, bf16[256,256]{1,0:T(8,128)(2,1)}, u32[]{:S(2)}) copy-start(bf16[256,256]{1,0:T(8,128)(2,1)} %param.12) | copy-start | bytes 393220
  0.6 8.3 %collective-permute-start = (bf16[1,33,1,8,256]{4,3,1,2,0:T(8,128)(2,1)}, bf16[1,33,1,8,256]{4,3,1,2,0:T(8,128)(2,1)S(1)}, u32[]{:S(2)}, u32[]{:S(2)}) collective-permute-start(bf16[1,33,1,8,256]{4,3,1,2,0:T(8,128)(2,1)} %bitcast.392), channel_id=1, source_target_pairs={{0,1},{1,2},{2,3},{4,5},{5,6},{6,7},{8,9},{9,10},{10,11},{12,13},{... | collective-permute-start | bytes 405512 | tf_op jit(solution)/shard_map/ppermute | solution.py:19
  5.8 7.2 %collective-permute-start.1 = (bf16[1,33,1,8,256]{4,3,1,2,0:T(8,128)(2,1)}, bf16[1,33,1,8,256]{4,3,1,2,0:T(8,128)(2,1)S(1)}, u32[]{:S(2)}, u32[]{:S(2)}) collective-permute-start(bf16[1,33,1,8,256]{4,3,1,2,0:T(8,128)(2,1)} %bitcast.393), channel_id=1, source_target_pairs={{1,0},{2,1},{3,2},{5,4},{6,5},{7,6},{9,8},{10,9},{11,10},{13,12},{... | collective-permute-start | bytes 405512 | tf_op jit(solution)/shard_map/ppermute | solution.py:20
  9.2 5.7 %copy-start.5 = (bf16[1,33,1,16,256]{4,3,2,1,0:T(8,128)(2,1)}, bf16[1,33,1,16,256]{4,3,2,1,0:T(8,128)(2,1)S(1)}, u32[]{:S(2)}) copy-start(bf16[1,33,1,16,256]{4,3,2,1,0:T(8,128)(2,1)S(1)} %fusion.18) | copy-start | bytes 811012
  13.2 3.6 %copy-start.3 = (bf16[1,33,1,16,256]{4,3,2,1,0:T(8,128)(2,1)}, bf16[1,33,1,16,256]{4,3,2,1,0:T(8,128)(2,1)S(1)}, u32[]{:S(2)}) copy-start(bf16[1,33,1,16,256]{4,3,2,1,0:T(8,128)(2,1)S(1)} %fusion.19) | copy-start | bytes 811012
  13.2 1.3 %copy-start.9 = (bf16[3,3,256,256]{3,2,1,0:T(8,128)(2,1)S(1)}, bf16[3,3,256,256]{3,2,1,0:T(8,128)(2,1)}, u32[]{:S(2)}) copy-start(bf16[3,3,256,256]{3,2,1,0:T(8,128)(2,1)} %param.10) | copy-start | bytes 3538948
  17.1 1.4 %copy-start.7 = (bf16[3,256,256]{2,1,0:T(8,128)(2,1)S(1)}, bf16[3,256,256]{2,1,0:T(8,128)(2,1)}, u32[]{:S(2)}) copy-start(bf16[3,256,256]{2,1,0:T(8,128)(2,1)} %param.11) | copy-start | bytes 1179652
  19.1 0.7 copy-start.13
  19.5 11.2 %copy-start.2 = (bf16[33,2,16,256]{3,2,1,0:T(8,128)(2,1)}, bf16[33,2,16,256]{3,2,1,0:T(8,128)(2,1)S(1)}, u32[]{:S(2)}) copy-start(bf16[33,2,16,256]{3,2,1,0:T(8,128)(2,1)S(1)} %fusion.16) | copy-start | bytes 1622020
  19.5 3.2 %copy-start.12 = (f32[256]{0:T(256)S(1)}, f32[256]{0:T(256)}, u32[]{:S(2)}) copy-start(f32[256]{0:T(256)} %param.13) | copy-start | bytes 3076
  21.1 3.7 %collective-permute-start.2 = (f32[1,8,256]{2,1,0:T(8,128)S(1)}, f32[1,8,256]{2,1,0:T(8,128)S(1)}, u32[]{:S(2)}, u32[]{:S(2)}) collective-permute-start(f32[1,8,256]{2,1,0:T(8,128)S(1)} %bitcast.398), channel_id=1, source_target_pairs={{0,1},{1,0},{2,3},{3,2},{4,5},{5,4},{6,7},{7,6},{8,9},{9,8},{10,11... | collective-permute-start | bytes 24584 | tf_op jit(solution)/shard_map/ppermute | solution.py:61
  24.8 4.5 %collective-permute-start.3 = (f32[1,8,256]{2,1,0:T(8,128)S(1)}, f32[1,8,256]{2,1,0:T(8,128)S(1)}, u32[]{:S(2)}, u32[]{:S(2)}) collective-permute-start(f32[1,8,256]{2,1,0:T(8,128)S(1)} %bitcast_add_fusion.5), channel_id=1, source_target_pairs={{0,2},{1,3},{2,0},{3,1},{4,6},{5,7},{6,4},{7,5},{8,10},{9,11},{10,... | collective-permute-start | bytes 24584 | tf_op jit(solution)/shard_map/ppermute | solution.py:61
  28.2 2.8 %copy-start.10 = (bf16[1,33,2,16,256]{4,3,2,1,0:T(8,128)(2,1)S(1)}, bf16[1,33,2,16,256]{4,3,2,1,0:T(8,128)(2,1)}, u32[]{:S(2)}) copy-start(bf16[1,33,2,16,256]{4,3,2,1,0:T(8,128)(2,1)} %param.15) | copy-start | bytes 1622020
  33.1 1.0 %copy-start.8 = (bf16[3,256,256]{2,1,0:T(8,128)(2,1)S(1)}, bf16[3,256,256]{2,1,0:T(8,128)(2,1)}, u32[]{:S(2)}) copy-start(bf16[3,256,256]{2,1,0:T(8,128)(2,1)} %param.11) | copy-start | bytes 1179652
  34.5 1.2 %copy-start.14 = (f32[33,2,16,256]{3,2,1,0:T(8,128)S(1)}, f32[33,2,16,256]{3,2,1,0:T(8,128)}, u32[]{:S(2)}) copy-start(f32[33,2,16,256]{3,2,1,0:T(8,128)} %get-tuple-element.13) | copy-start | bytes 3244036
  36.3 1.0 %copy-start.6 = (bf16[1,33,1,16,256]{4,3,2,1,0:T(8,128)(2,1)S(1)}, bf16[1,33,1,16,256]{4,3,2,1,0:T(8,128)(2,1)}, u32[]{:S(2)}) copy-start(bf16[1,33,1,16,256]{4,3,2,1,0:T(8,128)(2,1)} %copy-done.5) | copy-start | bytes 811012
  38.0 1.0 %copy-start.11 = (bf16[33,16,256]{2,0,1:T(8,128)(2,1)S(1)}, bf16[33,16,256]{2,0,1:T(8,128)(2,1)}, u32[]{:S(2)}) copy-start(bf16[33,16,256]{2,0,1:T(8,128)(2,1)} %copy.48) | copy-start | bytes 811012
  40.0 1.0 %copy-start.4 = (bf16[1,33,1,16,256]{4,3,2,1,0:T(8,128)(2,1)S(1)}, bf16[1,33,1,16,256]{4,3,2,1,0:T(8,128)(2,1)}, u32[]{:S(2)}) copy-start(bf16[1,33,1,16,256]{4,3,2,1,0:T(8,128)(2,1)} %copy-done.3) | copy-start | bytes 811012
  41.8 1.4 %copy-start.1 = (f32[9,256,256]{2,1,0:T(8,128)}, f32[9,256,256]{2,1,0:T(8,128)S(1)}, u32[]{:S(2)}) copy-start(f32[9,256,256]{2,1,0:T(8,128)S(1)} %fusion.20) | copy-start | bytes 7077892
  43.2 2.3 %collective-permute-start.4 = (bf16[16,96,256]{2,1,0:T(8,128)(2,1)S(1)}, bf16[16,96,256]{2,1,0:T(8,128)(2,1)S(1)}, u32[]{:S(2)}, u32[]{:S(2)}) collective-permute-start(bf16[16,96,256]{2,1,0:T(8,128)(2,1)S(1)} %bitcast.386), channel_id=1, source_target_pairs={{0,4},{4,0},{8,12},{12,8},{16,20},{20,16},{24,28},{28,24},{1,5},{5... | collective-permute-start | bytes 2359304 | tf_op jit(solution)/shard_map/ppermute | solution.py:76
  45.9 7.0 %collective-permute-start.5 = (bf16[8,48,256]{2,1,0:T(8,128)(2,1)S(1)}, bf16[8,48,256]{2,1,0:T(8,128)(2,1)S(1)}, u32[]{:S(2)}, u32[]{:S(2)}) collective-permute-start(bf16[8,48,256]{2,1,0:T(8,128)(2,1)S(1)} %bitcast.391), channel_id=1, source_target_pairs={{0,8},{4,12},{8,0},{12,4},{16,24},{20,28},{24,16},{28,20},{1,9},{5... | collective-permute-start | bytes 589832 | tf_op jit(solution)/shard_map/ppermute | solution.py:76
  47.4 7.1 %collective-permute-start.7 = (bf16[8,48,256]{2,1,0:T(8,128)(2,1)S(1)}, bf16[8,48,256]{2,1,0:T(8,128)(2,1)S(1)}, u32[]{:S(2)}, u32[]{:S(2)}) collective-permute-start(bf16[8,48,256]{2,1,0:T(8,128)(2,1)S(1)} %fusion.58), channel_id=1, source_target_pairs={{0,16},{4,20},{8,24},{12,28},{16,0},{20,4},{24,8},{28,12},{1,17},{... | collective-permute-start | bytes 589832 | tf_op jit(solution)/shard_map/ppermute | solution.py:76
  53.0 4.7 %collective-permute-start.6 = (bf16[4,48,256]{2,1,0:T(8,128)(2,1)S(1)}, bf16[4,48,256]{2,1,0:T(8,128)(2,1)S(1)}, u32[]{:S(2)}, u32[]{:S(2)}) collective-permute-start(bf16[4,48,256]{2,1,0:T(8,128)(2,1)S(1)} %fusion.103), channel_id=1, source_target_pairs={{0,16},{4,20},{8,24},{12,28},{16,0},{20,4},{24,8},{28,12},{1,17},{... | collective-permute-start | bytes 294920 | tf_op jit(solution)/shard_map/ppermute | solution.py:76
  54.6 4.7 %collective-permute-start.8 = (bf16[4,48,256]{2,1,0:T(8,128)(2,1)S(1)}, bf16[4,48,256]{2,1,0:T(8,128)(2,1)S(1)}, u32[]{:S(2)}, u32[]{:S(2)}) collective-permute-start(bf16[4,48,256]{2,1,0:T(8,128)(2,1)S(1)} %fusion.104), channel_id=1, source_target_pairs={{0,8},{4,12},{8,0},{12,4},{16,24},{20,28},{24,16},{28,20},{1,9},{5... | collective-permute-start | bytes 294920 | tf_op jit(solution)/shard_map/ppermute | solution.py:76
  59.4 5.9 %collective-permute-start.9 = (bf16[96,256]{1,0:T(8,128)(2,1)S(1)}, bf16[96,256]{1,0:T(8,128)(2,1)S(1)}, u32[]{:S(2)}, u32[]{:S(2)}) collective-permute-start(bf16[96,256]{1,0:T(8,128)(2,1)S(1)} %get-tuple-element.7), channel_id=1, source_target_pairs={{0,1},{1,2},{2,3},{3,0},{4,5},{5,6},{6,7},{7,4},{8,9},{9,10},{10,1... | collective-permute-start | bytes 147464 | tf_op jit(solution)/shard_map/ppermute | solution.py:111
  61.0 5.1 %collective-permute-start.10 = (bf16[96,256]{1,0:T(8,128)(2,1)S(1)}, bf16[96,256]{1,0:T(8,128)(2,1)S(1)}, u32[]{:S(2)}, u32[]{:S(2)}) collective-permute-start(bf16[96,256]{1,0:T(8,128)(2,1)S(1)} %get-tuple-element.8), channel_id=1, source_target_pairs={{0,2},{1,3},{2,0},{3,1},{4,6},{5,7},{6,4},{7,5},{8,10},{9,11},{10,... | collective-permute-start | bytes 147464 | tf_op jit(solution)/shard_map/ppermute | solution.py:111
  62.1 4.6 %collective-permute-start.11 = (bf16[96,256]{1,0:T(8,128)(2,1)S(1)}, bf16[96,256]{1,0:T(8,128)(2,1)S(1)}, u32[]{:S(2)}, u32[]{:S(2)}) collective-permute-start(bf16[96,256]{1,0:T(8,128)(2,1)S(1)} %get-tuple-element.9), channel_id=1, source_target_pairs={{0,3},{1,0},{2,1},{3,2},{4,7},{5,4},{6,5},{7,6},{8,11},{9,8},{10,9... | collective-permute-start | bytes 147464 | tf_op jit(solution)/shard_map/ppermute | solution.py:111

commit v13 on v11

--- a/solution.py
+++ b/solution.py
@@ -206,15 +206,18 @@
             preferred_element_type=jnp.float32,
         )
     pre_slope = (act_grad * silu_slope(pre_act)).astype(jnp.bfloat16)
-    tap_grads = []
-    for row_tap in range(3):
-        for col_tap in range(3):
-            window = padded[:, :, row_tap : row_tap + height, col_tap : col_tap + width]
-            tap_grads.append(
-                jnp.einsum("nfhwc,nfhwd->cd", window, pre_slope, preferred_element_type=jnp.float32)
-            )
+    windows = jnp.stack(
+        [
+            padded[:, :, row_tap : row_tap + height, col_tap : col_tap + width]
+            for row_tap in range(3)
+            for col_tap in range(3)
+        ]
+    )
+    spatial_grad = jnp.einsum(
+        "tnfhwc,nfhwd->tcd", windows, pre_slope, preferred_element_type=jnp.float32
+    )
     channels = spatial_weight.shape[-1]
-    spatial_grad = jnp.stack(tap_grads).reshape(devices, -1, channels)
+    spatial_grad = spatial_grad.reshape(devices, -1, channels)
     temporal_grad = temporal_grad.reshape(devices, -1, channels)
     core, x_bit, y_bit = ("dp", 0), ("dp", 1), ("dp", 2)
     z_lo, z_hi = ("space", 0), ("space", 1)

time: 68.5 us -> 111 us (1.62)
  local copies, waits for them, and re-layouts: 7.77 us -> 51.1 us
  starting transfers between devices: 22.4 us -> 20.9 us
  matrix products: 13.3 us -> 14.5 us
    dot_general x0 -> x2, local copies, waits for them, and re-layouts: none -> 44.7 us  [on_device(): jnp.einsum('tnfhwc,nfhwd->tcd', windows, pre_slope, preferred_element_typ...]
    ppermute x2, waiting for transfers between devices: 4.05 us -> 1.35 us  [space_sum(): lax.ppermute(values, 'space', [(i, i ^ step) for i in range(count)])]
    dot_general x9 -> x1, matrix products: 3.5 us -> 5.33 us  [on_device(): jnp.einsum('tnfhwc,nfhwd->tcd', windows, pre_slope, preferred_element_typ...]
    unnamed x42 -> x44, local copies, waits for them, and re-layouts: 5.43 us -> 3.77 us
    ppermute x3, starting transfers between devices: 5.62 us -> 4 us  [halving_scatter(): lax.ppermute(send.astype(jnp.bfloat16), 'space', [(i, (i + shift) % ns) f...]
    ppermute x5, waiting for transfers between devices: 7.79 us -> 9.38 us  [_halve(): got = lax.ppermute(send, axis, [(i, i ^ 1 << bit) for i in range(size)])]
    concatenate x1, other arithmetic: 1.42 us -> 0.14 us  [on_device(): jnp.concatenate([spatial_grad, temporal_grad], axis=1)]
    add x5, other arithmetic: 0.33 us -> 1.51 us  [_halve(): return keep + got.astype(keep.dtype)]
  transfers between devices with their start and end apart: 12 -> 12, of which waited for: 10 -> 8; matrix products, arithmetic and copies ran while one was open for 6% -> 44% of each run, Pallas kernels for 0% -> 0%
where the time goes in v13:
time: 111 us
  local copies, waits for them, and re-layouts  51.1 us (46%)
  starting transfers between devices  20.9 us (19%)
  waiting for transfers between devices  16.2 us (15%)
  matrix products  14.5 us (13%)
  other arithmetic  6.16 us (6%)
  between operations  1.93 us (2%)
    dot_general x2, local copies, waits for them, and re-layouts, on_device(): jnp.einsum('tnfhwc,nfhwd->tcd', windows, pre_slope, preferred_element_typ...  44.7 us
    ppermute x5, waiting for transfers between devices, _halve(): got = lax.ppermute(send, axis, [(i, i ^ 1 << bit) for i in range(size)])  9.38 us
    ppermute x5, starting transfers between devices, _halve(): got = lax.ppermute(send, axis, [(i, i ^ 1 << bit) for i in range(size)])  6.31 us
    dot_general x1, matrix products, on_device(): jnp.einsum('tnfhwc,nfhwd->tcd', windows, pre_slope, preferred_element_typ...  5.33 us
    ppermute x1, starting transfers between devices, exchange_rows(): above = lax.ppermute(tail, axis, [(i, i + 1) for i in range(ends)])  5.1 us
    ppermute x2, starting transfers between devices, space_sum(): lax.ppermute(values, 'space', [(i, i ^ step) for i in range(count)])  4.23 us
    ppermute x3, starting transfers between devices, halving_scatter(): lax.ppermute(send.astype(jnp.bfloat16), 'space', [(i, (i + shift) % ns) f...  4 us
    dot_general x9, matrix products, on_device(): jnp.einsum('nfhwc,cd->nfhwd', window, spatial_weight[row_tap, col_tap], p...  3.9 us
  transfers between devices with their start and end apart: 12, of which 8 were waited for; matrix products, arithmetic and copies ran while one was open for 44% of the time, Pallas kernels for 0%

profile of v13, /device:TPU:0, one launch (start us, length us, event | category | flops | bytes accessed | tf_op | source)
XLA Modules:
  0.0 110.7 jit_solution(11946901137834850207)
XLA Ops:
  0.6 5.1 %collective-permute-start = (bf16[1,33,1,8,256]{4,3,2,1,0:T(8,128)(2,1)}, bf16[1,33,1,8,256]{4,3,2,1,0:T(8,128)(2,1)S(1)}, u32[]{:S(2)}, u32[]{:S(2)}) collective-permute-start(bf16[1,33,1,8,256]{4,3,2,1,0:T(8,128)(2,1)} %param.8), channel_id=1, source_target_pairs={{0,1},{1,2},{2,3},{4,5},{5,6},{6,7},{8,9},{9,10},{10,11},{12,13},{... | collective-permute-start | bytes 405512 | tf_op jit(solution)/shard_map/ppermute | solution.py:19
  5.8 1.3 %collective-permute-start.1 = (bf16[1,33,1,8,256]{4,3,2,1,0:T(8,128)(2,1)}, bf16[1,33,1,8,256]{4,3,2,1,0:T(8,128)(2,1)S(1)}, u32[]{:S(2)}, u32[]{:S(2)}) collective-permute-start(bf16[1,33,1,8,256]{4,3,2,1,0:T(8,128)(2,1)} %param.8), channel_id=1, source_target_pairs={{1,0},{2,1},{3,2},{5,4},{6,5},{7,6},{9,8},{10,9},{11,10},{13,12},{... | collective-permute-start | bytes 405512 | tf_op jit(solution)/shard_map/ppermute | solution.py:20
  7.7 0.7 broadcast_multiply_fusion.2
  8.4 1.0 broadcast_in_dim.18
  9.9 3.0 %collective-permute-done.1 = bf16[1,33,1,8,256]{4,3,2,1,0:T(8,128)(2,1)S(1)} collective-permute-done((bf16[1,33,1,8,256]{4,3,2,1,0:T(8,128)(2,1)}, bf16[1,33,1,8,256]{4,3,2,1,0:T(8,128)(2,1)S(1)}, u32[]{:S(2)}, u32[]{:S(2)}) %collective-permute-start.1) | collective-permute-done | bytes 135200 | tf_op jit(solution)/shard_map/ppermute | solution.py:20
  13.2 0.9 fusion.10
  14.2 0.3 copy-done.3
  14.8 0.3 convolution_add_fusion.11
  15.1 0.3 convolution_add_fusion.10
  15.7 0.3 convolution_add_fusion.8
  16.0 0.3 convolution_add_fusion.7
  16.4 0.3 convolution_add_fusion.6
  16.7 0.3 convolution_add_fusion.5
  17.0 1.4 %multiply_convert_fusion = (bf16[33,2,16,256]{3,2,1,0:T(8,128)(2,1)S(1)}, f32[33,2,16,256]{3,2,1,0:T(8,128)}) fusion(f32[33,2,16,256]{3,2,1,0:T(8,128)S(1)} %convolution_add_fusion.5, bf16[3,3,256,256]{3,2,1,0:T(8,128)(2,1)S(1)} %copy-done.3, bf16[1,33,4,18,256]{4,3,2,1,0:T(8,128)(2,1)S(1)} %fusion.10), kind=kOutput, calls=%fused_computation.45 | convolution fusion | flops 140034048 | bytes 3375104 | tf_op jit(solution)/shard_map/nfhwc,cd->nfhwd/dot_general | solution.py:141
  19.1 0.3 fusion.21
  19.7 0.4 convolution_convert_fusion
  20.4 1.7 %collective-permute-start.2 = (f32[1,8,256]{2,1,0:T(8,128)S(1)}, f32[1,8,256]{2,1,0:T(8,128)S(1)}, u32[]{:S(2)}, u32[]{:S(2)}) collective-permute-start(f32[1,8,256]{2,1,0:T(8,128)S(1)} %bitcast.303), channel_id=1, source_target_pairs={{0,1},{1,0},{2,3},{3,2},{4,5},{5,4},{6,7},{7,6},{8,9},{9,8},{10,11... | collective-permute-start | bytes 24584 | tf_op jit(solution)/shard_map/ppermute | solution.py:57
  22.8 1.3 %collective-permute-done.2 = f32[1,8,256]{2,1,0:T(8,128)S(1)} collective-permute-done((f32[1,8,256]{2,1,0:T(8,128)S(1)}, f32[1,8,256]{2,1,0:T(8,128)S(1)}, u32[]{:S(2)}, u32[]{:S(2)}) %collective-permute-start.2) | collective-permute-done | bytes 8224 | tf_op jit(solution)/shard_map/ppermute | solution.py:57
  24.2 2.6 %collective-permute-start.3 = (f32[1,8,256]{2,1,0:T(8,128)S(1)}, f32[1,8,256]{2,1,0:T(8,128)S(1)}, u32[]{:S(2)}, u32[]{:S(2)}) collective-permute-start(f32[1,8,256]{2,1,0:T(8,128)S(1)} %bitcast_add_fusion.5), channel_id=1, source_target_pairs={{0,2},{1,3},{2,0},{3,1},{4,6},{5,7},{6,4},{7,5},{8,10},{9,11},{10,... | collective-permute-start | bytes 24584 | tf_op jit(solution)/shard_map/ppermute | solution.py:57
  27.0 9.8 %copy.23 = bf16[9,256,33,2,16]{1,0,4,3,2:T(8,128)(2,1)} copy(bf16[9,256,33,2,16]{1,4,3,2,0:T(8,128)(2,1)S(1)} %bitcast.273) | data formatting | bytes 9732096 | tf_op jit(solution)/shard_map/tnfhwc,nfhwd->tcd/dot_general | solution.py:216
  36.7 35.0 %dot_general.88 = bf16[4,2,4,72,33,2,16]{3,2,1,0,6,5,4:T(4,128)(2,1)} reshape(bf16[9,256,33,2,16]{1,0,4,3,2:T(8,128)(2,1)} %copy.23) | data formatting | bytes 9732096 | tf_op jit(solution)/shard_map/tnfhwc,nfhwd->tcd/dot_general | solution.py:216
  72.3 0.4 copy-done.4
  72.8 1.0 fusion.19
  73.8 0.4 convolution_bitcast_fusion.1
  74.2 0.4 convolution_bitcast_fusion.2
  74.6 0.4 convolution_bitcast_fusion.3
  75.0 0.4 slice_bitcast_fusion
  75.4 0.3 fusion.61
  75.7 0.3 convolution_add_fusion.1
  76.1 1.4 %copy-done.7 = f32[33,2,16,256]{3,2,1,0:T(8,128)S(1)} copy-done((f32[33,2,16,256]{3,2,1,0:T(8,128)S(1)}, f32[33,2,16,256]{3,2,1,0:T(8,128)}, u32[]{:S(2)}) %copy-start.7) | copy-done | bytes 1081368
  77.5 0.6 fusion.22
  78.5 5.3 %fusion.6 = f32[4,2,4,72,256]{4,3,2,1,0:T(8,128)S(1)} fusion(bf16[33,2,16,256,1,1,1]{3,2,1,0,6,5,4:T(8,128)(2,1)S(1)} %fusion.22, bf16[4,2,4,72,33,2,16]{3,2,1,0,6,5,4:T(4,128)(2,1)S(1)} %bitcast.270), kind=kOutput, calls=%fused_computation.12 | convolution fusion | flops 1245708288 | bytes 7766016 | tf_op jit(solution)/shard_map/tnfhwc,nfhwd->tcd/dot_general | solution.py:216
  83.9 1.0 fusion.12
  85.1 2.5 %collective-permute-done.4 = bf16[16,96,256]{2,1,0:T(8,128)(2,1)} collective-permute-done((bf16[16,96,256]{2,1,0:T(8,128)(2,1)}, bf16[16,96,256]{2,1,0:T(8,128)(2,1)}, u32[]{:S(2)}, u32[]{:S(2)}) %collective-permute-start.4) | collective-permute-done | bytes 786464 | tf_op jit(solution)/shard_map/ppermute | solution.py:72
  87.5 1.4 %bitcast_add_fusion = f32[16,96,256]{2,1,0:T(8,128)S(1)} fusion(f32[4,1,4,96,256]{4,3,2,1,0:T(8,128)S(1)} %fusion.13, bf16[16,96,256]{2,1,0:T(8,128)(2,1)} %collective-permute-done.4), kind=kLoop, calls=%fused_computation.18 | loop fusion | flops 786432 | bytes 3932160 | tf_op jit(solution)/shard_map/add | solution.py:73
  89.1 1.6 %collective-permute-start.5 = (bf16[8,48,256]{2,1,0:T(8,128)(2,1)S(1)}, bf16[8,48,256]{2,1,0:T(8,128)(2,1)S(1)}, u32[]{:S(2)}, u32[]{:S(2)}) collective-permute-start(bf16[8,48,256]{2,1,0:T(8,128)(2,1)S(1)} %bitcast.295), channel_id=1, source_target_pairs={{0,8},{4,12},{8,0},{12,4},{16,24},{20,28},{24,16},{28,20},{1,9},{5... | collective-permute-start | bytes 589832 | tf_op jit(solution)/shard_map/ppermute | solution.py:72
  90.7 1.6 %collective-permute-start.7 = (bf16[8,48,256]{2,1,0:T(8,128)(2,1)S(1)}, bf16[8,48,256]{2,1,0:T(8,128)(2,1)S(1)}, u32[]{:S(2)}, u32[]{:S(2)}) collective-permute-start(bf16[8,48,256]{2,1,0:T(8,128)(2,1)S(1)} %fusion.57), channel_id=1, source_target_pairs={{0,16},{4,20},{8,24},{12,28},{16,0},{20,4},{24,8},{28,12},{1,17},{... | collective-permute-start | bytes 589832 | tf_op jit(solution)/shard_map/ppermute | solution.py:72
  92.3 3.8 %collective-permute-done.5 = bf16[8,48,256]{2,1,0:T(8,128)(2,1)S(1)} collective-permute-done((bf16[8,48,256]{2,1,0:T(8,128)(2,1)S(1)}, bf16[8,48,256]{2,1,0:T(8,128)(2,1)S(1)}, u32[]{:S(2)}, u32[]{:S(2)}) %collective-permute-start.5) | collective-permute-done | bytes 196640 | tf_op jit(solution)/shard_map/ppermute | solution.py:72
  96.2 1.6 %collective-permute-start.6 = (bf16[4,48,256]{2,1,0:T(8,128)(2,1)S(1)}, bf16[4,48,256]{2,1,0:T(8,128)(2,1)S(1)}, u32[]{:S(2)}, u32[]{:S(2)}) collective-permute-start(bf16[4,48,256]{2,1,0:T(8,128)(2,1)S(1)} %fusion.100), channel_id=1, source_target_pairs={{0,16},{4,20},{8,24},{12,28},{16,0},{20,4},{24,8},{28,12},{1,17},{... | collective-permute-start | bytes 294920 | tf_op jit(solution)/shard_map/ppermute | solution.py:72
  97.8 1.6 %collective-permute-start.8 = (bf16[4,48,256]{2,1,0:T(8,128)(2,1)S(1)}, bf16[4,48,256]{2,1,0:T(8,128)(2,1)S(1)}, u32[]{:S(2)}, u32[]{:S(2)}) collective-permute-start(bf16[4,48,256]{2,1,0:T(8,128)(2,1)S(1)} %fusion.101), channel_id=1, source_target_pairs={{0,8},{4,12},{8,0},{12,4},{16,24},{20,28},{24,16},{28,20},{1,9},{5... | collective-permute-start | bytes 294920 | tf_op jit(solution)/shard_map/ppermute | solution.py:72
  99.4 1.4 %collective-permute-done.6 = bf16[4,48,256]{2,1,0:T(8,128)(2,1)S(1)} collective-permute-done((bf16[4,48,256]{2,1,0:T(8,128)(2,1)S(1)}, bf16[4,48,256]{2,1,0:T(8,128)(2,1)S(1)}, u32[]{:S(2)}, u32[]{:S(2)}) %collective-permute-start.6) | collective-permute-done | bytes 98336 | tf_op jit(solution)/shard_map/ppermute | solution.py:72
  100.9 1.7 %collective-permute-done.8 = bf16[4,48,256]{2,1,0:T(8,128)(2,1)S(1)} collective-permute-done((bf16[4,48,256]{2,1,0:T(8,128)(2,1)S(1)}, bf16[4,48,256]{2,1,0:T(8,128)(2,1)S(1)}, u32[]{:S(2)}, u32[]{:S(2)}) %collective-permute-start.8) | collective-permute-done | bytes 98336 | tf_op jit(solution)/shard_map/ppermute | solution.py:72
  102.7 1.9 %collective-permute-start.10 = (bf16[96,256]{1,0:T(8,128)(2,1)S(1)}, bf16[96,256]{1,0:T(8,128)(2,1)S(1)}, u32[]{:S(2)}, u32[]{:S(2)}) collective-permute-start(bf16[96,256]{1,0:T(8,128)(2,1)S(1)} %get-tuple-element.8), channel_id=1, source_target_pairs={{0,2},{1,3},{2,0},{3,1},{4,6},{5,7},{6,4},{7,5},{8,10},{9,11},{10,... | collective-permute-start | bytes 147464 | tf_op jit(solution)/shard_map/ppermute | solution.py:107
  104.7 2.0 %collective-permute-start.11 = (bf16[96,256]{1,0:T(8,128)(2,1)S(1)}, bf16[96,256]{1,0:T(8,128)(2,1)S(1)}, u32[]{:S(2)}, u32[]{:S(2)}) collective-permute-start(bf16[96,256]{1,0:T(8,128)(2,1)S(1)} %get-tuple-element.9), channel_id=1, source_target_pairs={{0,3},{1,0},{2,1},{3,2},{4,7},{5,4},{6,5},{7,6},{8,11},{9,8},{10,9... | collective-permute-start | bytes 147464 | tf_op jit(solution)/shard_map/ppermute | solution.py:107
  106.7 1.9 %collective-permute-done.9 = bf16[96,256]{1,0:T(8,128)(2,1)S(1)} collective-permute-done((bf16[96,256]{1,0:T(8,128)(2,1)S(1)}, bf16[96,256]{1,0:T(8,128)(2,1)S(1)}, u32[]{:S(2)}, u32[]{:S(2)}) %collective-permute-start.9) | collective-permute-done | bytes 49184 | tf_op jit(solution)/shard_map/ppermute | solution.py:107
  108.6 0.6 collective-permute-done.11
  109.5 0.6 add_add_fusion.1
  110.1 0.7 add_add_fusion
  (88 shorter events, 5.4 us)
Async XLA Ops:
  0.6 19.5 %copy-start = (bf16[256,256]{1,0:T(8,128)(2,1)S(1)}, bf16[256,256]{1,0:T(8,128)(2,1)}, u32[]{:S(2)}) copy-start(bf16[256,256]{1,0:T(8,128)(2,1)} %param.12) | copy-start | bytes 393220
  0.6 9.0 %collective-permute-start = (bf16[1,33,1,8,256]{4,3,2,1,0:T(8,128)(2,1)}, bf16[1,33,1,8,256]{4,3,2,1,0:T(8,128)(2,1)S(1)}, u32[]{:S(2)}, u32[]{:S(2)}) collective-permute-start(bf16[1,33,1,8,256]{4,3,2,1,0:T(8,128)(2,1)} %param.8), channel_id=1, source_target_pairs={{0,1},{1,2},{2,3},{4,5},{5,6},{6,7},{8,9},{9,10},{10,11},{12,13},{... | collective-permute-start | bytes 405512 | tf_op jit(solution)/shard_map/ppermute | solution.py:19
  5.8 7.2 %collective-permute-start.1 = (bf16[1,33,1,8,256]{4,3,2,1,0:T(8,128)(2,1)}, bf16[1,33,1,8,256]{4,3,2,1,0:T(8,128)(2,1)S(1)}, u32[]{:S(2)}, u32[]{:S(2)}) collective-permute-start(bf16[1,33,1,8,256]{4,3,2,1,0:T(8,128)(2,1)} %param.8), channel_id=1, source_target_pairs={{1,0},{2,1},{3,2},{5,4},{6,5},{7,6},{9,8},{10,9},{11,10},{13,12},{... | collective-permute-start | bytes 405512 | tf_op jit(solution)/shard_map/ppermute | solution.py:20
  13.2 1.3 %copy-start.3 = (bf16[3,3,256,256]{3,2,1,0:T(8,128)(2,1)S(1)}, bf16[3,3,256,256]{3,2,1,0:T(8,128)(2,1)}, u32[]{:S(2)}) copy-start(bf16[3,3,256,256]{3,2,1,0:T(8,128)(2,1)} %param.10) | copy-start | bytes 3538948
  17.0 1.5 %copy-start.2 = (bf16[3,256,256]{2,1,0:T(8,128)(2,1)S(1)}, bf16[3,256,256]{2,1,0:T(8,128)(2,1)}, u32[]{:S(2)}) copy-start(bf16[3,256,256]{2,1,0:T(8,128)(2,1)} %param.11) | copy-start | bytes 1179652
  19.0 0.7 copy-start.6
  19.4 2.8 %copy-start.1 = (bf16[33,2,16,256]{3,2,1,0:T(8,128)(2,1)}, bf16[33,2,16,256]{3,2,1,0:T(8,128)(2,1)S(1)}, u32[]{:S(2)}) copy-start(bf16[33,2,16,256]{3,2,1,0:T(8,128)(2,1)S(1)} %fusion.21) | copy-start | bytes 1622020
  20.4 3.7 %collective-permute-start.2 = (f32[1,8,256]{2,1,0:T(8,128)S(1)}, f32[1,8,256]{2,1,0:T(8,128)S(1)}, u32[]{:S(2)}, u32[]{:S(2)}) collective-permute-start(f32[1,8,256]{2,1,0:T(8,128)S(1)} %bitcast.303), channel_id=1, source_target_pairs={{0,1},{1,0},{2,3},{3,2},{4,5},{5,4},{6,7},{7,6},{8,9},{9,8},{10,11... | collective-permute-start | bytes 24584 | tf_op jit(solution)/shard_map/ppermute | solution.py:57
  24.2 47.5 %collective-permute-start.3 = (f32[1,8,256]{2,1,0:T(8,128)S(1)}, f32[1,8,256]{2,1,0:T(8,128)S(1)}, u32[]{:S(2)}, u32[]{:S(2)}) collective-permute-start(f32[1,8,256]{2,1,0:T(8,128)S(1)} %bitcast_add_fusion.5), channel_id=1, source_target_pairs={{0,2},{1,3},{2,0},{3,1},{4,6},{5,7},{6,4},{7,5},{8,10},{9,11},{10,... | collective-permute-start | bytes 24584 | tf_op jit(solution)/shard_map/ppermute | solution.py:57
  36.7 35.1 %copy-start.5 = (f32[256]{0:T(256)S(1)}, f32[256]{0:T(256)}, u32[]{:S(2)}) copy-start(f32[256]{0:T(256)} %param.13) | copy-start | bytes 3076
  71.7 1.0 copy-start.4
  74.5 3.5 %slice-start = ((s8[8650752]{0:T(1024)(128)(4,1)}), s8[4194304]{0:T(1024)(128)(4,1)S(1)}, s32[]{:S(2)}) async-start(s8[8650752]{0:T(1024)(128)(4,1)} %bitcast.269), calls=%async_computation | async-start | bytes 8388608
  74.6 3.8 %slice-start.1 = ((s8[8650752]{0:T(1024)(128)(4,1)}), s8[4194304]{0:T(1024)(128)(4,1)S(1)}, s32[]{:S(2)}) async-start(s8[8650752]{0:T(1024)(128)(4,1)} %bitcast.269), calls=%async_computation.1 | async-start | bytes 8388608
  75.7 1.8 %copy-start.7 = (f32[33,2,16,256]{3,2,1,0:T(8,128)S(1)}, f32[33,2,16,256]{3,2,1,0:T(8,128)}, u32[]{:S(2)}) copy-start(f32[33,2,16,256]{3,2,1,0:T(8,128)} %get-tuple-element.13) | copy-start | bytes 3244036
  75.7 2.8 %slice-start.2 = ((s8[8650752]{0:T(1024)(128)(4,1)}), s8[262144]{0:T(1024)(128)(4,1)S(1)}, s32[]{:S(2)}) async-start(s8[8650752]{0:T(1024)(128)(4,1)} %bitcast.269), calls=%async_computation.2 | async-start | bytes 524288
  84.9 2.6 %collective-permute-start.4 = (bf16[16,96,256]{2,1,0:T(8,128)(2,1)}, bf16[16,96,256]{2,1,0:T(8,128)(2,1)}, u32[]{:S(2)}, u32[]{:S(2)}) collective-permute-start(bf16[16,96,256]{2,1,0:T(8,128)(2,1)} %bitcast.94), channel_id=1, source_target_pairs={{0,4},{4,0},{8,12},{12,8},{16,20},{20,16},{24,28},{28,24},{1,5},{5... | collective-permute-start | bytes 2359304 | tf_op jit(solution)/shard_map/ppermute | solution.py:72
  89.1 7.0 %collective-permute-start.5 = (bf16[8,48,256]{2,1,0:T(8,128)(2,1)S(1)}, bf16[8,48,256]{2,1,0:T(8,128)(2,1)S(1)}, u32[]{:S(2)}, u32[]{:S(2)}) collective-permute-start(bf16[8,48,256]{2,1,0:T(8,128)(2,1)S(1)} %bitcast.295), channel_id=1, source_target_pairs={{0,8},{4,12},{8,0},{12,4},{16,24},{20,28},{24,16},{28,20},{1,9},{5... | collective-permute-start | bytes 589832 | tf_op jit(solution)/shard_map/ppermute | solution.py:72
  90.7 7.1 %collective-permute-start.7 = (bf16[8,48,256]{2,1,0:T(8,128)(2,1)S(1)}, bf16[8,48,256]{2,1,0:T(8,128)(2,1)S(1)}, u32[]{:S(2)}, u32[]{:S(2)}) collective-permute-start(bf16[8,48,256]{2,1,0:T(8,128)(2,1)S(1)} %fusion.57), channel_id=1, source_target_pairs={{0,16},{4,20},{8,24},{12,28},{16,0},{20,4},{24,8},{28,12},{1,17},{... | collective-permute-start | bytes 589832 | tf_op jit(solution)/shard_map/ppermute | solution.py:72
  96.2 4.7 %collective-permute-start.6 = (bf16[4,48,256]{2,1,0:T(8,128)(2,1)S(1)}, bf16[4,48,256]{2,1,0:T(8,128)(2,1)S(1)}, u32[]{:S(2)}, u32[]{:S(2)}) collective-permute-start(bf16[4,48,256]{2,1,0:T(8,128)(2,1)S(1)} %fusion.100), channel_id=1, source_target_pairs={{0,16},{4,20},{8,24},{12,28},{16,0},{20,4},{24,8},{28,12},{1,17},{... | collective-permute-start | bytes 294920 | tf_op jit(solution)/shard_map/ppermute | solution.py:72
  97.8 4.7 %collective-permute-start.8 = (bf16[4,48,256]{2,1,0:T(8,128)(2,1)S(1)}, bf16[4,48,256]{2,1,0:T(8,128)(2,1)S(1)}, u32[]{:S(2)}, u32[]{:S(2)}) collective-permute-start(bf16[4,48,256]{2,1,0:T(8,128)(2,1)S(1)} %fusion.101), channel_id=1, source_target_pairs={{0,8},{4,12},{8,0},{12,4},{16,24},{20,28},{24,16},{28,20},{1,9},{5... | collective-permute-start | bytes 294920 | tf_op jit(solution)/shard_map/ppermute | solution.py:72
  102.6 5.9 %collective-permute-start.9 = (bf16[96,256]{1,0:T(8,128)(2,1)S(1)}, bf16[96,256]{1,0:T(8,128)(2,1)S(1)}, u32[]{:S(2)}, u32[]{:S(2)}) collective-permute-start(bf16[96,256]{1,0:T(8,128)(2,1)S(1)} %get-tuple-element.7), channel_id=1, source_target_pairs={{0,1},{1,2},{2,3},{3,0},{4,5},{5,6},{6,7},{7,4},{8,9},{9,10},{10,1... | collective-permute-start | bytes 147464 | tf_op jit(solution)/shard_map/ppermute | solution.py:107
  102.7 5.9 %collective-permute-start.10 = (bf16[96,256]{1,0:T(8,128)(2,1)S(1)}, bf16[96,256]{1,0:T(8,128)(2,1)S(1)}, u32[]{:S(2)}, u32[]{:S(2)}) collective-permute-start(bf16[96,256]{1,0:T(8,128)(2,1)S(1)} %get-tuple-element.8), channel_id=1, source_target_pairs={{0,2},{1,3},{2,0},{3,1},{4,6},{5,7},{6,4},{7,5},{8,10},{9,11},{10,... | collective-permute-start | bytes 147464 | tf_op jit(solution)/shard_map/ppermute | solution.py:107
  104.7 4.6 %collective-permute-start.11 = (bf16[96,256]{1,0:T(8,128)(2,1)S(1)}, bf16[96,256]{1,0:T(8,128)(2,1)S(1)}, u32[]{:S(2)}, u32[]{:S(2)}) collective-permute-start(bf16[96,256]{1,0:T(8,128)(2,1)S(1)} %get-tuple-element.9), channel_id=1, source_target_pairs={{0,3},{1,0},{2,1},{3,2},{4,7},{5,4},{6,5},{7,6},{8,11},{9,8},{10,9... | collective-permute-start | bytes 147464 | tf_op jit(solution)/shard_map/ppermute | solution.py:107

commit v14 on v11

--- a/solution.py
+++ b/solution.py
@@ -90,10 +90,14 @@
     tail = len(natural)
     while tail > shared and all(o[tail - 1] == orders[0][tail - 1] for o in orders):
         tail -= 1
-    width = cur.shape[1] // len(orders)
+    rows = cur.shape[1]
+    if len(orders) == 2 and rows % 16 == 0:
+        cuts = [0, rows // 2 + 8, rows]
+    else:
+        cuts = [p * rows // len(orders) for p in range(len(orders) + 1)]
     outs = []
     for p, order in enumerate(orders):
-        part, part_left = cur[:, p * width : (p + 1) * width], list(left)
+        part, part_left = cur[:, cuts[p] : cuts[p + 1]], list(left)
         for axis, bit in order[shared:tail]:
             part = _halve(part, part_left, axis, bit, jnp.bfloat16)
         outs.append(part)

time: 68.5 us -> 69.8 us (1.019)
  waiting for transfers between devices: 16.4 us -> 19.1 us
  starting transfers between devices: 22.4 us -> 20.9 us
    ppermute x5, waiting for transfers between devices: 7.79 us -> 10.6 us  [_halve(): got = lax.ppermute(send, axis, [(i, i ^ 1 << bit) for i in range(size)])]
    ppermute x5, starting transfers between devices: 6.26 us -> 4.76 us  [_halve(): got = lax.ppermute(send, axis, [(i, i ^ 1 << bit) for i in range(size)])]
  transfers between devices with their start and end apart: 12 -> 12, of which waited for: 10 -> 11; matrix products, arithmetic and copies ran while one was open for 6% -> 6% of each run, Pallas kernels for 0% -> 0%
where the time goes in v14:
time: 69.8 us; the launch traced here: 69.4 us
  starting transfers between devices  20.9 us (30%)
  waiting for transfers between devices  19.1 us (27%)
  matrix products  13.3 us (19%)
  local copies, waits for them, and re-layouts  7.78 us (11%)
  other arithmetic  6.37 us (9%)
  between operations  1.91 us (3%)
    ppermute x5, waiting for transfers between devices, _halve(): got = lax.ppermute(send, axis, [(i, i ^ 1 << bit) for i in range(size)])  10.6 us
    ppermute x3, starting transfers between devices, halving_scatter(): lax.ppermute(send.astype(jnp.bfloat16), 'space', [(i, (i + shift) % ns) f...  5.61 us
    unnamed x42, local copies, waits for them, and re-layouts  5.43 us
    ppermute x1, starting transfers between devices, exchange_rows(): above = lax.ppermute(tail, axis, [(i, i + 1) for i in range(ends)])  5.1 us
    ppermute x5, starting transfers between devices, _halve(): got = lax.ppermute(send, axis, [(i, i ^ 1 << bit) for i in range(size)])  4.76 us
    ppermute x2, starting transfers between devices, space_sum(): lax.ppermute(values, 'space', [(i, i ^ step) for i in range(count)])  4.14 us
    ppermute x2, waiting for transfers between devices, space_sum(): lax.ppermute(values, 'space', [(i, i ^ step) for i in range(count)])  4.05 us
    dot_general x9, matrix products, on_device(): jnp.einsum('nfhwc,cd->nfhwd', window, spatial_weight[row_tap, col_tap], p...  3.9 us
  transfers between devices with their start and end apart: 12, of which 11 were waited for; matrix products, arithmetic and copies ran while one was open for 6% of the time, Pallas kernels for 0%

profile of v14, /device:TPU:0, one launch (start us, length us, event | category | flops | bytes accessed | tf_op | source)
XLA Modules:
  0.0 69.4 jit_solution(18061074085341352537)
XLA Ops:
  0.6 5.1 %collective-permute-start = (bf16[1,33,1,8,256]{4,3,2,1,0:T(8,128)(2,1)}, bf16[1,33,1,8,256]{4,3,2,1,0:T(8,128)(2,1)S(1)}, u32[]{:S(2)}, u32[]{:S(2)}) collective-permute-start(bf16[1,33,1,8,256]{4,3,2,1,0:T(8,128)(2,1)} %param.8), channel_id=1, source_target_pairs={{0,1},{1,2},{2,3},{4,5},{5,6},{6,7},{8,9},{9,10},{10,11},{12,13},{... | collective-permute-start | bytes 405512 | tf_op jit(solution)/shard_map/ppermute | solution.py:19
  5.7 1.3 %collective-permute-start.1 = (bf16[1,33,1,8,256]{4,3,2,1,0:T(8,128)(2,1)}, bf16[1,33,1,8,256]{4,3,2,1,0:T(8,128)(2,1)S(1)}, u32[]{:S(2)}, u32[]{:S(2)}) collective-permute-start(bf16[1,33,1,8,256]{4,3,2,1,0:T(8,128)(2,1)} %param.8), channel_id=1, source_target_pairs={{1,0},{2,1},{3,2},{5,4},{6,5},{7,6},{9,8},{10,9},{11,10},{13,12},{... | collective-permute-start | bytes 405512 | tf_op jit(solution)/shard_map/ppermute | solution.py:20
  7.0 1.1 %broadcast_in_dim.16 = bf16[33,8,2,256]{3,2,1,0:T(2,128)(2,1)S(1)} broadcast(bf16[33,8,256]{2,1,0:T(8,128)(2,1)} %bitcast.358), dimensions={0,1,3} | broadcast | bytes 405504 | tf_op jit(solution)/shard_map/broadcast_in_dim | solution.py:26
  8.2 0.9 %convert_element_type.133 = f32[33,16,256]{2,1,0:T(8,128)} convert(bf16[33,16,256]{2,1,0:T(8,128)(2,1)S(1)} %broadcast_in_dim.17) | non-fusion elementwise | flops 135168 | bytes 811008 | tf_op jit(solution)/shard_map/convert_element_type | solution.py:163
  10.0 2.9 %collective-permute-done.1 = bf16[1,33,1,8,256]{4,3,2,1,0:T(8,128)(2,1)S(1)} collective-permute-done((bf16[1,33,1,8,256]{4,3,2,1,0:T(8,128)(2,1)}, bf16[1,33,1,8,256]{4,3,2,1,0:T(8,128)(2,1)S(1)}, u32[]{:S(2)}, u32[]{:S(2)}) %collective-permute-start.1) | collective-permute-done | bytes 135200 | tf_op jit(solution)/shard_map/ppermute | solution.py:20
  13.2 0.9 %fusion.5 = bf16[1,33,4,18,256]{4,3,2,1,0:T(8,128)(2,1)S(1)} fusion(bf16[1,33,1,16,256]{4,3,2,1,0:T(8,128)(2,1)S(1)} %slice.131, bf16[1,33,2,16,256]{4,3,2,1,0:T(8,128)(2,1)S(1)} %broadcast_in_dim.40, bf16[1,33,1,16,256]{4,3,2,1,0:T(8,128)(2,1)S(1)} %slice.130), kind=kLoop, calls=%fused_computation.11 | loop fusion | flops 7299072 | bytes 2297856 | tf_op jit(solution)/shard_map/concatenate | solution.py:135
  17.0 1.4 %multiply_convert_fusion = (bf16[33,2,16,256]{3,2,1,0:T(8,128)(2,1)S(1)}, f32[33,2,16,256]{3,2,1,0:T(8,128)}) fusion(f32[33,2,16,256]{3,2,1,0:T(8,128)S(1)} %convolution_add_fusion.5, bf16[3,3,256,256]{3,2,1,0:T(8,128)(2,1)S(1)} %copy-done.8, bf16[1,33,4,18,256]{4,3,2,1,0:T(8,128)(2,1)S(1)} %fusion.5), kind=kOutput, calls=%fused_computation.58 | convolution fusion | flops 140034048 | bytes 3375104 | tf_op jit(solution)/shard_map/nfhwc,cd->nfhwd/dot_general | solution.py:145
  19.1 0.7 %copy-done.5 = f32[33,16,256]{2,1,0:T(8,128)S(1)} copy-done((f32[33,16,256]{2,1,0:T(8,128)S(1)}, f32[33,16,256]{2,1,0:T(8,128)}, u32[]{:S(2)}) %copy-start.5) | copy-done | bytes 540696
  20.1 0.8 %copy-done.2 = bf16[33,2,16,256]{3,2,1,0:T(8,128)(2,1)} copy-done((bf16[33,2,16,256]{3,2,1,0:T(8,128)(2,1)}, bf16[33,2,16,256]{3,2,1,0:T(8,128)(2,1)S(1)}, u32[]{:S(2)}) %copy-start.2) | copy-done | bytes 540696
  20.9 0.4 fusion.26
  21.4 0.9 %fusion.53 = (f32[8,256]{1,0:T(8,128)S(1)}, f32[8,2,16,256]{3,2,1,0:T(8,128)}) fusion(bf16[256,256]{1,0:T(8,128)(2,1)S(1)} %copy-done, bf16[8,2,16,256]{3,0,2,1:T(8,128)(2,1)S(1)} %fusion.26), kind=kOutput, calls=%fused_computation.108 | convolution fusion | flops 34142208 | bytes 532480 | tf_op jit(solution)/shard_map/nqhwc,ce->nqhwe/dot_general | solution.py:170
  22.3 1.6 %collective-permute-start.2 = (f32[1,8,256]{2,1,0:T(8,128)S(1)}, f32[1,8,256]{2,1,0:T(8,128)S(1)}, u32[]{:S(2)}, u32[]{:S(2)}) collective-permute-start(f32[1,8,256]{2,1,0:T(8,128)S(1)} %bitcast.365), channel_id=1, source_target_pairs={{0,1},{1,0},{2,3},{3,2},{4,5},{5,4},{6,7},{7,6},{8,9},{9,8},{10,11... | collective-permute-start | bytes 24584 | tf_op jit(solution)/shard_map/ppermute | solution.py:57
  23.8 2.1 %collective-permute-done.2 = f32[1,8,256]{2,1,0:T(8,128)S(1)} collective-permute-done((f32[1,8,256]{2,1,0:T(8,128)S(1)}, f32[1,8,256]{2,1,0:T(8,128)S(1)}, u32[]{:S(2)}, u32[]{:S(2)}) %collective-permute-start.2) | collective-permute-done | bytes 8224 | tf_op jit(solution)/shard_map/ppermute | solution.py:57
  25.9 2.6 %collective-permute-start.3 = (f32[1,8,256]{2,1,0:T(8,128)S(1)}, f32[1,8,256]{2,1,0:T(8,128)S(1)}, u32[]{:S(2)}, u32[]{:S(2)}) collective-permute-start(f32[1,8,256]{2,1,0:T(8,128)S(1)} %bitcast_add_fusion.5), channel_id=1, source_target_pairs={{0,2},{1,3},{2,0},{3,1},{4,6},{5,7},{6,4},{7,5},{8,10},{9,11},{10,... | collective-permute-start | bytes 24584 | tf_op jit(solution)/shard_map/ppermute | solution.py:57
  28.5 2.0 %collective-permute-done.3 = f32[1,8,256]{2,1,0:T(8,128)S(1)} collective-permute-done((f32[1,8,256]{2,1,0:T(8,128)S(1)}, f32[1,8,256]{2,1,0:T(8,128)S(1)}, u32[]{:S(2)}, u32[]{:S(2)}) %collective-permute-start.3) | collective-permute-done | bytes 8224 | tf_op jit(solution)/shard_map/ppermute | solution.py:57
  30.7 1.1 %fusion.51 = bf16[8,2,16,256]{3,2,1,0:T(8,128)(2,1)S(1)} fusion(f32[8,2,16,256]{3,2,1,0:T(8,128)} %get-tuple-element.13, f32[8,256]{1,0:T(8,128)S(1)} %get-tuple-element.9, f32[8,256]{1,0:T(8,128)S(1)} %get-tuple-element.8), kind=kLoop, calls=%fused_computation.104 | loop fusion | flops 1245184 | bytes 409600 | tf_op jit(solution)/shard_map/convert_element_type | solution.py:177
  32.0 1.0 %fusion.14 = bf16[1,33,2,16,256]{4,1,3,2,0:T(8,128)(2,1)S(1)} fusion(f32[8,2,16,256]{3,0,2,1:T(8,128)S(1)} %fusion.61, bf16[1,33,2,16,256]{4,3,2,1,0:T(8,128)(2,1)S(1)} %copy-done.9, f32[33]{0:T(128)S(1)} %compare_select_fusion, s32[8]{0:T(128)S(1)} %bitcast.367), kind=kOutput, calls=%fused_computation.34 | convolution fusion | flops 27033864 | bytes 1343652 | tf_op jit(solution)/shard_map/nqf,nqhwc->nfhwc/dot_general | solution.py:186
  33.1 0.4 convolution_bitcast_fusion.1
  33.5 0.4 convolution_bitcast_fusion.2
  34.2 0.4 slice_bitcast_fusion
  34.7 0.6 copy-done.7
  36.0 0.9 %copy-done.12 = f32[33,2,16,256]{3,2,1,0:T(8,128)S(1)} copy-done((f32[33,2,16,256]{3,2,1,0:T(8,128)S(1)}, f32[33,2,16,256]{3,2,1,0:T(8,128)}, u32[]{:S(2)}) %copy-start.12) | copy-done | bytes 1081368
  36.8 0.6 fusion.15
  37.8 0.6 copy-done.4
  38.4 0.4 fusion.24
  38.8 0.4 fusion.23
  39.2 0.4 fusion.22
  39.6 0.4 fusion.21
  40.0 0.4 fusion.20
  40.7 0.4 fusion.18
  41.2 0.4 fusion.17
  41.7 1.3 %copy-done.1 = f32[9,256,256]{2,1,0:T(8,128)} copy-done((f32[9,256,256]{2,1,0:T(8,128)}, f32[9,256,256]{2,1,0:T(8,128)S(1)}, u32[]{:S(2)}) %copy-start.1) | copy-done | bytes 2359320
  43.0 1.4 %fusion.8 = f32[4,1,4,96,256]{4,3,2,1,0:T(8,128)S(1)} fusion(s32[]{:T(128)S(6)} %select_n.82, f32[4,2,4,72,256]{4,3,2,1,0:T(8,128)} %bitcast.332, f32[4,2,4,24,256]{4,3,2,1,0:T(8,128)S(1)} %bitcast.334), kind=kLoop, calls=%fused_computation.14 | loop fusion | flops 393216 | bytes 4718596 | tf_op jit(solution)/shard_map/concatenate | solution.py:231
  44.4 0.9 %collective-permute-done.4 = bf16[16,96,256]{2,1,0:T(8,128)(2,1)S(1)} collective-permute-done((bf16[16,96,256]{2,1,0:T(8,128)(2,1)S(1)}, bf16[16,96,256]{2,1,0:T(8,128)(2,1)S(1)}, u32[]{:S(2)}, u32[]{:S(2)}) %collective-permute-start.4) | collective-permute-done | bytes 786464 | tf_op jit(solution)/shard_map/ppermute | solution.py:72
  45.7 1.6 %collective-permute-start.7 = (bf16[8,40,256]{2,1,0:T(8,128)(2,1)S(1)}, bf16[8,40,256]{2,1,0:T(8,128)(2,1)S(1)}, u32[]{:S(2)}, u32[]{:S(2)}) collective-permute-start(bf16[8,40,256]{2,1,0:T(8,128)(2,1)S(1)} %fusion.59), channel_id=1, source_target_pairs={{0,16},{4,20},{8,24},{12,28},{16,0},{20,4},{24,8},{28,12},{1,17},{... | collective-permute-start | bytes 491528 | tf_op jit(solution)/shard_map/ppermute | solution.py:72
  47.3 1.5 %collective-permute-start.5 = (bf16[8,56,256]{2,1,0:T(8,128)(2,1)S(1)}, bf16[8,56,256]{2,1,0:T(8,128)(2,1)S(1)}, u32[]{:S(2)}, u32[]{:S(2)}) collective-permute-start(bf16[8,56,256]{2,1,0:T(8,128)(2,1)S(1)} %bitcast.357), channel_id=1, source_target_pairs={{0,8},{4,12},{8,0},{12,4},{16,24},{20,28},{24,16},{28,20},{1,9},{5... | collective-permute-start | bytes 688136 | tf_op jit(solution)/shard_map/ppermute | solution.py:72
  48.9 3.1 %collective-permute-done.7 = bf16[8,40,256]{2,1,0:T(8,128)(2,1)S(1)} collective-permute-done((bf16[8,40,256]{2,1,0:T(8,128)(2,1)S(1)}, bf16[8,40,256]{2,1,0:T(8,128)(2,1)S(1)}, u32[]{:S(2)}, u32[]{:S(2)}) %collective-permute-start.7) | collective-permute-done | bytes 163872 | tf_op jit(solution)/shard_map/ppermute | solution.py:72
  52.0 1.6 %collective-permute-start.8 = (bf16[4,40,256]{2,1,0:T(8,128)(2,1)S(1)}, bf16[4,40,256]{2,1,0:T(8,128)(2,1)S(1)}, u32[]{:S(2)}, u32[]{:S(2)}) collective-permute-start(bf16[4,40,256]{2,1,0:T(8,128)(2,1)S(1)} %fusion.104), channel_id=1, source_target_pairs={{0,8},{4,12},{8,0},{12,4},{16,24},{20,28},{24,16},{28,20},{1,9},{5... | collective-permute-start | bytes 245768 | tf_op jit(solution)/shard_map/ppermute | solution.py:72
  53.6 1.8 %collective-permute-done.5 = bf16[8,56,256]{2,1,0:T(8,128)(2,1)S(1)} collective-permute-done((bf16[8,56,256]{2,1,0:T(8,128)(2,1)S(1)}, bf16[8,56,256]{2,1,0:T(8,128)(2,1)S(1)}, u32[]{:S(2)}, u32[]{:S(2)}) %collective-permute-start.5) | collective-permute-done | bytes 229408 | tf_op jit(solution)/shard_map/ppermute | solution.py:72
  55.6 0.9 %collective-permute-done.8 = bf16[4,40,256]{2,1,0:T(8,128)(2,1)S(1)} collective-permute-done((bf16[4,40,256]{2,1,0:T(8,128)(2,1)S(1)}, bf16[4,40,256]{2,1,0:T(8,128)(2,1)S(1)}, u32[]{:S(2)}, u32[]{:S(2)}) %collective-permute-start.8) | collective-permute-done | bytes 81952 | tf_op jit(solution)/shard_map/ppermute | solution.py:72
  56.6 3.8 %collective-permute-done.6 = bf16[4,56,256]{2,1,0:T(8,128)(2,1)S(1)} collective-permute-done((bf16[4,56,256]{2,1,0:T(8,128)(2,1)S(1)}, bf16[4,56,256]{2,1,0:T(8,128)(2,1)S(1)}, u32[]{:S(2)}, u32[]{:S(2)}) %collective-permute-start.6) | collective-permute-done | bytes 114720 | tf_op jit(solution)/shard_map/ppermute | solution.py:72
  60.5 1.7 %collective-permute-start.9 = (bf16[96,256]{1,0:T(8,128)(2,1)S(1)}, bf16[96,256]{1,0:T(8,128)(2,1)S(1)}, u32[]{:S(2)}, u32[]{:S(2)}) collective-permute-start(bf16[96,256]{1,0:T(8,128)(2,1)S(1)} %get-tuple-element.5), channel_id=1, source_target_pairs={{0,1},{1,2},{2,3},{3,0},{4,5},{5,6},{6,7},{7,4},{8,9},{9,10},{10,1... | collective-permute-start | bytes 147464 | tf_op jit(solution)/shard_map/ppermute | solution.py:111
  62.2 1.0 %collective-permute-start.10 = (bf16[96,256]{1,0:T(8,128)(2,1)S(1)}, bf16[96,256]{1,0:T(8,128)(2,1)S(1)}, u32[]{:S(2)}, u32[]{:S(2)}) collective-permute-start(bf16[96,256]{1,0:T(8,128)(2,1)S(1)} %get-tuple-element.6), channel_id=1, source_target_pairs={{0,2},{1,3},{2,0},{3,1},{4,6},{5,7},{6,4},{7,5},{8,10},{9,11},{10,... | collective-permute-start | bytes 147464 | tf_op jit(solution)/shard_map/ppermute | solution.py:111
  63.2 2.9 %collective-permute-start.11 = (bf16[96,256]{1,0:T(8,128)(2,1)S(1)}, bf16[96,256]{1,0:T(8,128)(2,1)S(1)}, u32[]{:S(2)}, u32[]{:S(2)}) collective-permute-start(bf16[96,256]{1,0:T(8,128)(2,1)S(1)} %get-tuple-element.7), channel_id=1, source_target_pairs={{0,3},{1,0},{2,1},{3,2},{4,7},{5,4},{6,5},{7,6},{8,11},{9,8},{10,9... | collective-permute-start | bytes 147464 | tf_op jit(solution)/shard_map/ppermute | solution.py:111
  66.4 0.8 %collective-permute-done.10 = bf16[96,256]{1,0:T(8,128)(2,1)S(1)} collective-permute-done((bf16[96,256]{1,0:T(8,128)(2,1)S(1)}, bf16[96,256]{1,0:T(8,128)(2,1)S(1)}, u32[]{:S(2)}, u32[]{:S(2)}) %collective-permute-start.10) | collective-permute-done | bytes 49184 | tf_op jit(solution)/shard_map/ppermute | solution.py:111
  67.3 0.6 collective-permute-done.11
  68.1 0.6 add_add_fusion.1
  68.7 0.7 add_add_fusion
  (89 shorter events, 8.1 us)
Async XLA Ops:
  0.6 20.7 %copy-start = (bf16[256,256]{1,0:T(8,128)(2,1)S(1)}, bf16[256,256]{1,0:T(8,128)(2,1)}, u32[]{:S(2)}) copy-start(bf16[256,256]{1,0:T(8,128)(2,1)} %param.12) | copy-start | bytes 393220
  0.6 9.1 %collective-permute-start = (bf16[1,33,1,8,256]{4,3,2,1,0:T(8,128)(2,1)}, bf16[1,33,1,8,256]{4,3,2,1,0:T(8,128)(2,1)S(1)}, u32[]{:S(2)}, u32[]{:S(2)}) collective-permute-start(bf16[1,33,1,8,256]{4,3,2,1,0:T(8,128)(2,1)} %param.8), channel_id=1, source_target_pairs={{0,1},{1,2},{2,3},{4,5},{5,6},{6,7},{8,9},{9,10},{10,11},{12,13},{... | collective-permute-start | bytes 405512 | tf_op jit(solution)/shard_map/ppermute | solution.py:19
  5.7 7.1 %collective-permute-start.1 = (bf16[1,33,1,8,256]{4,3,2,1,0:T(8,128)(2,1)}, bf16[1,33,1,8,256]{4,3,2,1,0:T(8,128)(2,1)S(1)}, u32[]{:S(2)}, u32[]{:S(2)}) collective-permute-start(bf16[1,33,1,8,256]{4,3,2,1,0:T(8,128)(2,1)} %param.8), channel_id=1, source_target_pairs={{1,0},{2,1},{3,2},{5,4},{6,5},{7,6},{9,8},{10,9},{11,10},{13,12},{... | collective-permute-start | bytes 405512 | tf_op jit(solution)/shard_map/ppermute | solution.py:20
  10.0 4.8 %copy-start.3 = (bf16[1,33,1,16,256]{4,3,2,1,0:T(8,128)(2,1)}, bf16[1,33,1,16,256]{4,3,2,1,0:T(8,128)(2,1)S(1)}, u32[]{:S(2)}) copy-start(bf16[1,33,1,16,256]{4,3,2,1,0:T(8,128)(2,1)S(1)} %slice.130) | copy-start | bytes 811012
  13.2 1.3 %copy-start.8 = (bf16[3,3,256,256]{3,2,1,0:T(8,128)(2,1)S(1)}, bf16[3,3,256,256]{3,2,1,0:T(8,128)(2,1)}, u32[]{:S(2)}) copy-start(bf16[3,3,256,256]{3,2,1,0:T(8,128)(2,1)} %param.10) | copy-start | bytes 3538948
  17.0 1.5 %copy-start.6 = (bf16[3,256,256]{2,1,0:T(8,128)(2,1)S(1)}, bf16[3,256,256]{2,1,0:T(8,128)(2,1)}, u32[]{:S(2)}) copy-start(bf16[3,256,256]{2,1,0:T(8,128)(2,1)} %param.11) | copy-start | bytes 1179652
  18.7 1.1 %copy-start.5 = (f32[33,16,256]{2,1,0:T(8,128)S(1)}, f32[33,16,256]{2,1,0:T(8,128)}, u32[]{:S(2)}) copy-start(f32[33,16,256]{2,1,0:T(8,128)} %convert_element_type.133) | copy-start | bytes 1622020
  19.8 1.1 %copy-start.11 = (s32[1,8]{1,0:T(1,128)S(1)}, s32[1,8]{1,0:T(1,128)}, u32[]{:S(2)}) copy-start(s32[1,8]{1,0:T(1,128)} %param.14) | copy-start | bytes 100
  20.1 0.8 %copy-start.2 = (bf16[33,2,16,256]{3,2,1,0:T(8,128)(2,1)}, bf16[33,2,16,256]{3,2,1,0:T(8,128)(2,1)S(1)}, u32[]{:S(2)}) copy-start(bf16[33,2,16,256]{3,2,1,0:T(8,128)(2,1)S(1)} %fusion.16) | copy-start | bytes 1622020
  20.1 3.7 %copy-start.10 = (f32[256]{0:T(256)S(1)}, f32[256]{0:T(256)}, u32[]{:S(2)}) copy-start(f32[256]{0:T(256)} %param.13) | copy-start | bytes 3076
  22.3 3.7 %collective-permute-start.2 = (f32[1,8,256]{2,1,0:T(8,128)S(1)}, f32[1,8,256]{2,1,0:T(8,128)S(1)}, u32[]{:S(2)}, u32[]{:S(2)}) collective-permute-start(f32[1,8,256]{2,1,0:T(8,128)S(1)} %bitcast.365), channel_id=1, source_target_pairs={{0,1},{1,0},{2,3},{3,2},{4,5},{5,4},{6,7},{7,6},{8,9},{9,8},{10,11... | collective-permute-start | bytes 24584 | tf_op jit(solution)/shard_map/ppermute | solution.py:57
  25.9 4.5 %collective-permute-start.3 = (f32[1,8,256]{2,1,0:T(8,128)S(1)}, f32[1,8,256]{2,1,0:T(8,128)S(1)}, u32[]{:S(2)}, u32[]{:S(2)}) collective-permute-start(f32[1,8,256]{2,1,0:T(8,128)S(1)} %bitcast_add_fusion.5), channel_id=1, source_target_pairs={{0,2},{1,3},{2,0},{3,1},{4,6},{5,7},{6,4},{7,5},{8,10},{9,11},{10,... | collective-permute-start | bytes 24584 | tf_op jit(solution)/shard_map/ppermute | solution.py:57
  28.5 3.5 %copy-start.9 = (bf16[1,33,2,16,256]{4,3,2,1,0:T(8,128)(2,1)S(1)}, bf16[1,33,2,16,256]{4,3,2,1,0:T(8,128)(2,1)}, u32[]{:S(2)}) copy-start(bf16[1,33,2,16,256]{4,3,2,1,0:T(8,128)(2,1)} %param.15) | copy-start | bytes 1622020
  34.2 1.0 %copy-start.7 = (bf16[3,256,256]{2,1,0:T(8,128)(2,1)S(1)}, bf16[3,256,256]{2,1,0:T(8,128)(2,1)}, u32[]{:S(2)}) copy-start(bf16[3,256,256]{2,1,0:T(8,128)(2,1)} %param.11) | copy-start | bytes 1179652
  35.6 1.2 %copy-start.12 = (f32[33,2,16,256]{3,2,1,0:T(8,128)S(1)}, f32[33,2,16,256]{3,2,1,0:T(8,128)}, u32[]{:S(2)}) copy-start(f32[33,2,16,256]{3,2,1,0:T(8,128)} %get-tuple-element.11) | copy-start | bytes 3244036
  37.4 1.0 %copy-start.4 = (bf16[1,33,1,16,256]{4,3,2,1,0:T(8,128)(2,1)S(1)}, bf16[1,33,1,16,256]{4,3,2,1,0:T(8,128)(2,1)}, u32[]{:S(2)}) copy-start(bf16[1,33,1,16,256]{4,3,2,1,0:T(8,128)(2,1)} %copy-done.3) | copy-start | bytes 811012
  41.5 1.4 %copy-start.1 = (f32[9,256,256]{2,1,0:T(8,128)}, f32[9,256,256]{2,1,0:T(8,128)S(1)}, u32[]{:S(2)}) copy-start(f32[9,256,256]{2,1,0:T(8,128)S(1)} %fusion.17) | copy-start | bytes 7077892
  43.0 2.3 %collective-permute-start.4 = (bf16[16,96,256]{2,1,0:T(8,128)(2,1)S(1)}, bf16[16,96,256]{2,1,0:T(8,128)(2,1)S(1)}, u32[]{:S(2)}, u32[]{:S(2)}) collective-permute-start(bf16[16,96,256]{2,1,0:T(8,128)(2,1)S(1)} %bitcast.352), channel_id=1, source_target_pairs={{0,4},{4,0},{8,12},{12,8},{16,20},{20,16},{24,28},{28,24},{1,5},{5... | collective-permute-start | bytes 2359304 | tf_op jit(solution)/shard_map/ppermute | solution.py:72
  45.7 6.3 %collective-permute-start.7 = (bf16[8,40,256]{2,1,0:T(8,128)(2,1)S(1)}, bf16[8,40,256]{2,1,0:T(8,128)(2,1)S(1)}, u32[]{:S(2)}, u32[]{:S(2)}) collective-permute-start(bf16[8,40,256]{2,1,0:T(8,128)(2,1)S(1)} %fusion.59), channel_id=1, source_target_pairs={{0,16},{4,20},{8,24},{12,28},{16,0},{20,4},{24,8},{28,12},{1,17},{... | collective-permute-start | bytes 491528 | tf_op jit(solution)/shard_map/ppermute | solution.py:72
  47.3 8.2 %collective-permute-start.5 = (bf16[8,56,256]{2,1,0:T(8,128)(2,1)S(1)}, bf16[8,56,256]{2,1,0:T(8,128)(2,1)S(1)}, u32[]{:S(2)}, u32[]{:S(2)}) collective-permute-start(bf16[8,56,256]{2,1,0:T(8,128)(2,1)S(1)} %bitcast.357), channel_id=1, source_target_pairs={{0,8},{4,12},{8,0},{12,4},{16,24},{20,28},{24,16},{28,20},{1,9},{5... | collective-permute-start | bytes 688136 | tf_op jit(solution)/shard_map/ppermute | solution.py:72
  52.0 4.5 %collective-permute-start.8 = (bf16[4,40,256]{2,1,0:T(8,128)(2,1)S(1)}, bf16[4,40,256]{2,1,0:T(8,128)(2,1)S(1)}, u32[]{:S(2)}, u32[]{:S(2)}) collective-permute-start(bf16[4,40,256]{2,1,0:T(8,128)(2,1)S(1)} %fusion.104), channel_id=1, source_target_pairs={{0,8},{4,12},{8,0},{12,4},{16,24},{20,28},{24,16},{28,20},{1,9},{5... | collective-permute-start | bytes 245768 | tf_op jit(solution)/shard_map/ppermute | solution.py:72
  55.5 4.9 %collective-permute-start.6 = (bf16[4,56,256]{2,1,0:T(8,128)(2,1)S(1)}, bf16[4,56,256]{2,1,0:T(8,128)(2,1)S(1)}, u32[]{:S(2)}, u32[]{:S(2)}) collective-permute-start(bf16[4,56,256]{2,1,0:T(8,128)(2,1)S(1)} %fusion.96), channel_id=1, source_target_pairs={{0,16},{4,20},{8,24},{12,28},{16,0},{20,4},{24,8},{28,12},{1,17},{... | collective-permute-start | bytes 344072 | tf_op jit(solution)/shard_map/ppermute | solution.py:72
  60.5 5.9 %collective-permute-start.9 = (bf16[96,256]{1,0:T(8,128)(2,1)S(1)}, bf16[96,256]{1,0:T(8,128)(2,1)S(1)}, u32[]{:S(2)}, u32[]{:S(2)}) collective-permute-start(bf16[96,256]{1,0:T(8,128)(2,1)S(1)} %get-tuple-element.5), channel_id=1, source_target_pairs={{0,1},{1,2},{2,3},{3,0},{4,5},{5,6},{6,7},{7,4},{8,9},{9,10},{10,1... | collective-permute-start | bytes 147464 | tf_op jit(solution)/shard_map/ppermute | solution.py:111
  62.2 5.1 %collective-permute-start.10 = (bf16[96,256]{1,0:T(8,128)(2,1)S(1)}, bf16[96,256]{1,0:T(8,128)(2,1)S(1)}, u32[]{:S(2)}, u32[]{:S(2)}) collective-permute-start(bf16[96,256]{1,0:T(8,128)(2,1)S(1)} %get-tuple-element.6), channel_id=1, source_target_pairs={{0,2},{1,3},{2,0},{3,1},{4,6},{5,7},{6,4},{7,5},{8,10},{9,11},{10,... | collective-permute-start | bytes 147464 | tf_op jit(solution)/shard_map/ppermute | solution.py:111
  63.2 4.6 %collective-permute-start.11 = (bf16[96,256]{1,0:T(8,128)(2,1)S(1)}, bf16[96,256]{1,0:T(8,128)(2,1)S(1)}, u32[]{:S(2)}, u32[]{:S(2)}) collective-permute-start(bf16[96,256]{1,0:T(8,128)(2,1)S(1)} %get-tuple-element.7), channel_id=1, source_target_pairs={{0,3},{1,0},{2,1},{3,2},{4,7},{5,4},{6,5},{7,6},{8,11},{9,8},{10,9... | collective-permute-start | bytes 147464 | tf_op jit(solution)/shard_map/ppermute | solution.py:111

commit v15 on v14

--- a/solution.py
+++ b/solution.py
@@ -92,7 +92,7 @@
         tail -= 1
     rows = cur.shape[1]
     if len(orders) == 2 and rows % 16 == 0:
-        cuts = [0, rows // 2 + 8, rows]
+        cuts = [0, rows // 2 - 8, rows]
     else:
         cuts = [p * rows // len(orders) for p in range(len(orders) + 1)]
     outs = []

time: 69.8 us -> 69.8 us (level)
  no operation moved by 1% of the time
where the time goes in v15:
time: 69.8 us; the launch traced here: 69.4 us
  starting transfers between devices  21 us (30%)
  waiting for transfers between devices  19.1 us (27%)
  matrix products  13.3 us (19%)
  local copies, waits for them, and re-layouts  7.76 us (11%)
  other arithmetic  6.37 us (9%)
  between operations  1.91 us (3%)
    ppermute x5, waiting for transfers between devices, _halve(): got = lax.ppermute(send, axis, [(i, i ^ 1 << bit) for i in range(size)])  10.5 us
    ppermute x3, starting transfers between devices, halving_scatter(): lax.ppermute(send.astype(jnp.bfloat16), 'space', [(i, (i + shift) % ns) f...  5.66 us
    unnamed x42, local copies, waits for them, and re-layouts  5.43 us
    ppermute x1, starting transfers between devices, exchange_rows(): above = lax.ppermute(tail, axis, [(i, i + 1) for i in range(ends)])  5.1 us
    ppermute x5, starting transfers between devices, _halve(): got = lax.ppermute(send, axis, [(i, i ^ 1 << bit) for i in range(size)])  4.79 us
    ppermute x2, starting transfers between devices, space_sum(): lax.ppermute(values, 'space', [(i, i ^ step) for i in range(count)])  4.14 us
    ppermute x2, waiting for transfers between devices, space_sum(): lax.ppermute(values, 'space', [(i, i ^ step) for i in range(count)])  4.05 us
    dot_general x9, matrix products, on_device(): jnp.einsum('nfhwc,cd->nfhwd', window, spatial_weight[row_tap, col_tap], p...  3.9 us
  transfers between devices with their start and end apart: 12, of which 11 were waited for; matrix products, arithmetic and copies ran while one was open for 6% of the time, Pallas kernels for 0%

profile of v15, /device:TPU:0, one launch (start us, length us, event | category | flops | bytes accessed | tf_op | source)
XLA Modules:
  0.0 69.4 jit_solution(4387035327798605275)
XLA Ops:
  0.6 5.1 %collective-permute-start = (bf16[1,33,1,8,256]{4,3,2,1,0:T(8,128)(2,1)}, bf16[1,33,1,8,256]{4,3,2,1,0:T(8,128)(2,1)S(1)}, u32[]{:S(2)}, u32[]{:S(2)}) collective-permute-start(bf16[1,33,1,8,256]{4,3,2,1,0:T(8,128)(2,1)} %param.8), channel_id=1, source_target_pairs={{0,1},{1,2},{2,3},{4,5},{5,6},{6,7},{8,9},{9,10},{10,11},{12,13},{... | collective-permute-start | bytes 405512 | tf_op jit(solution)/shard_map/ppermute | solution.py:19
  5.7 1.3 %collective-permute-start.1 = (bf16[1,33,1,8,256]{4,3,2,1,0:T(8,128)(2,1)}, bf16[1,33,1,8,256]{4,3,2,1,0:T(8,128)(2,1)S(1)}, u32[]{:S(2)}, u32[]{:S(2)}) collective-permute-start(bf16[1,33,1,8,256]{4,3,2,1,0:T(8,128)(2,1)} %param.8), channel_id=1, source_target_pairs={{1,0},{2,1},{3,2},{5,4},{6,5},{7,6},{9,8},{10,9},{11,10},{13,12},{... | collective-permute-start | bytes 405512 | tf_op jit(solution)/shard_map/ppermute | solution.py:20
  7.0 1.1 %broadcast_in_dim.16 = bf16[33,8,2,256]{3,2,1,0:T(2,128)(2,1)S(1)} broadcast(bf16[33,8,256]{2,1,0:T(8,128)(2,1)} %bitcast.358), dimensions={0,1,3} | broadcast | bytes 405504 | tf_op jit(solution)/shard_map/broadcast_in_dim | solution.py:26
  8.2 0.9 %convert_element_type.133 = f32[33,16,256]{2,1,0:T(8,128)} convert(bf16[33,16,256]{2,1,0:T(8,128)(2,1)S(1)} %broadcast_in_dim.17) | non-fusion elementwise | flops 135168 | bytes 811008 | tf_op jit(solution)/shard_map/convert_element_type | solution.py:163
  10.0 2.9 %collective-permute-done.1 = bf16[1,33,1,8,256]{4,3,2,1,0:T(8,128)(2,1)S(1)} collective-permute-done((bf16[1,33,1,8,256]{4,3,2,1,0:T(8,128)(2,1)}, bf16[1,33,1,8,256]{4,3,2,1,0:T(8,128)(2,1)S(1)}, u32[]{:S(2)}, u32[]{:S(2)}) %collective-permute-start.1) | collective-permute-done | bytes 135200 | tf_op jit(solution)/shard_map/ppermute | solution.py:20
  13.2 0.9 %fusion.5 = bf16[1,33,4,18,256]{4,3,2,1,0:T(8,128)(2,1)S(1)} fusion(bf16[1,33,1,16,256]{4,3,2,1,0:T(8,128)(2,1)S(1)} %slice.131, bf16[1,33,2,16,256]{4,3,2,1,0:T(8,128)(2,1)S(1)} %broadcast_in_dim.40, bf16[1,33,1,16,256]{4,3,2,1,0:T(8,128)(2,1)S(1)} %slice.130), kind=kLoop, calls=%fused_computation.11 | loop fusion | flops 7299072 | bytes 2297856 | tf_op jit(solution)/shard_map/concatenate | solution.py:135
  17.0 1.4 %multiply_convert_fusion = (bf16[33,2,16,256]{3,2,1,0:T(8,128)(2,1)S(1)}, f32[33,2,16,256]{3,2,1,0:T(8,128)}) fusion(f32[33,2,16,256]{3,2,1,0:T(8,128)S(1)} %convolution_add_fusion.5, bf16[3,3,256,256]{3,2,1,0:T(8,128)(2,1)S(1)} %copy-done.8, bf16[1,33,4,18,256]{4,3,2,1,0:T(8,128)(2,1)S(1)} %fusion.5), kind=kOutput, calls=%fused_computation.58 | convolution fusion | flops 140034048 | bytes 3375104 | tf_op jit(solution)/shard_map/nfhwc,cd->nfhwd/dot_general | solution.py:145
  19.1 0.7 %copy-done.5 = f32[33,16,256]{2,1,0:T(8,128)S(1)} copy-done((f32[33,16,256]{2,1,0:T(8,128)S(1)}, f32[33,16,256]{2,1,0:T(8,128)}, u32[]{:S(2)}) %copy-start.5) | copy-done | bytes 540696
  20.1 0.8 %copy-done.2 = bf16[33,2,16,256]{3,2,1,0:T(8,128)(2,1)} copy-done((bf16[33,2,16,256]{3,2,1,0:T(8,128)(2,1)}, bf16[33,2,16,256]{3,2,1,0:T(8,128)(2,1)S(1)}, u32[]{:S(2)}) %copy-start.2) | copy-done | bytes 540696
  20.9 0.4 fusion.26
  21.4 0.9 %fusion.53 = (f32[8,256]{1,0:T(8,128)S(1)}, f32[8,2,16,256]{3,2,1,0:T(8,128)}) fusion(bf16[256,256]{1,0:T(8,128)(2,1)S(1)} %copy-done, bf16[8,2,16,256]{3,0,2,1:T(8,128)(2,1)S(1)} %fusion.26), kind=kOutput, calls=%fused_computation.108 | convolution fusion | flops 34142208 | bytes 532480 | tf_op jit(solution)/shard_map/nqhwc,ce->nqhwe/dot_general | solution.py:170
  22.3 1.6 %collective-permute-start.2 = (f32[1,8,256]{2,1,0:T(8,128)S(1)}, f32[1,8,256]{2,1,0:T(8,128)S(1)}, u32[]{:S(2)}, u32[]{:S(2)}) collective-permute-start(f32[1,8,256]{2,1,0:T(8,128)S(1)} %bitcast.365), channel_id=1, source_target_pairs={{0,1},{1,0},{2,3},{3,2},{4,5},{5,4},{6,7},{7,6},{8,9},{9,8},{10,11... | collective-permute-start | bytes 24584 | tf_op jit(solution)/shard_map/ppermute | solution.py:57
  23.8 2.1 %collective-permute-done.2 = f32[1,8,256]{2,1,0:T(8,128)S(1)} collective-permute-done((f32[1,8,256]{2,1,0:T(8,128)S(1)}, f32[1,8,256]{2,1,0:T(8,128)S(1)}, u32[]{:S(2)}, u32[]{:S(2)}) %collective-permute-start.2) | collective-permute-done | bytes 8224 | tf_op jit(solution)/shard_map/ppermute | solution.py:57
  25.9 2.6 %collective-permute-start.3 = (f32[1,8,256]{2,1,0:T(8,128)S(1)}, f32[1,8,256]{2,1,0:T(8,128)S(1)}, u32[]{:S(2)}, u32[]{:S(2)}) collective-permute-start(f32[1,8,256]{2,1,0:T(8,128)S(1)} %bitcast_add_fusion.5), channel_id=1, source_target_pairs={{0,2},{1,3},{2,0},{3,1},{4,6},{5,7},{6,4},{7,5},{8,10},{9,11},{10,... | collective-permute-start | bytes 24584 | tf_op jit(solution)/shard_map/ppermute | solution.py:57
  28.5 2.0 %collective-permute-done.3 = f32[1,8,256]{2,1,0:T(8,128)S(1)} collective-permute-done((f32[1,8,256]{2,1,0:T(8,128)S(1)}, f32[1,8,256]{2,1,0:T(8,128)S(1)}, u32[]{:S(2)}, u32[]{:S(2)}) %collective-permute-start.3) | collective-permute-done | bytes 8224 | tf_op jit(solution)/shard_map/ppermute | solution.py:57
  30.7 1.1 %fusion.51 = bf16[8,2,16,256]{3,2,1,0:T(8,128)(2,1)S(1)} fusion(f32[8,2,16,256]{3,2,1,0:T(8,128)} %get-tuple-element.13, f32[8,256]{1,0:T(8,128)S(1)} %get-tuple-element.9, f32[8,256]{1,0:T(8,128)S(1)} %get-tuple-element.8), kind=kLoop, calls=%fused_computation.104 | loop fusion | flops 1245184 | bytes 409600 | tf_op jit(solution)/shard_map/convert_element_type | solution.py:177
  32.0 1.0 %fusion.14 = bf16[1,33,2,16,256]{4,1,3,2,0:T(8,128)(2,1)S(1)} fusion(f32[8,2,16,256]{3,0,2,1:T(8,128)S(1)} %fusion.61, bf16[1,33,2,16,256]{4,3,2,1,0:T(8,128)(2,1)S(1)} %copy-done.9, f32[33]{0:T(128)S(1)} %compare_select_fusion, s32[8]{0:T(128)S(1)} %bitcast.367), kind=kOutput, calls=%fused_computation.34 | convolution fusion | flops 27033864 | bytes 1343652 | tf_op jit(solution)/shard_map/nqf,nqhwc->nfhwc/dot_general | solution.py:186
  33.1 0.4 convolution_bitcast_fusion.1
  33.5 0.4 convolution_bitcast_fusion.2
  34.2 0.4 slice_bitcast_fusion
  34.7 0.6 copy-done.7
  36.0 0.9 %copy-done.12 = f32[33,2,16,256]{3,2,1,0:T(8,128)S(1)} copy-done((f32[33,2,16,256]{3,2,1,0:T(8,128)S(1)}, f32[33,2,16,256]{3,2,1,0:T(8,128)}, u32[]{:S(2)}) %copy-start.12) | copy-done | bytes 1081368
  36.8 0.6 fusion.15
  37.8 0.6 copy-done.4
  38.4 0.4 fusion.24
  38.8 0.4 fusion.23
  39.2 0.4 fusion.22
  39.6 0.4 fusion.21
  40.0 0.4 fusion.20
  40.7 0.4 fusion.18
  41.2 0.4 fusion.17
  41.7 1.3 %copy-done.1 = f32[9,256,256]{2,1,0:T(8,128)} copy-done((f32[9,256,256]{2,1,0:T(8,128)}, f32[9,256,256]{2,1,0:T(8,128)S(1)}, u32[]{:S(2)}) %copy-start.1) | copy-done | bytes 2359320
  43.0 1.4 %fusion.8 = f32[4,1,4,96,256]{4,3,2,1,0:T(8,128)S(1)} fusion(s32[]{:T(128)S(6)} %select_n.82, f32[4,2,4,72,256]{4,3,2,1,0:T(8,128)} %bitcast.332, f32[4,2,4,24,256]{4,3,2,1,0:T(8,128)S(1)} %bitcast.334), kind=kLoop, calls=%fused_computation.14 | loop fusion | flops 393216 | bytes 4718596 | tf_op jit(solution)/shard_map/concatenate | solution.py:231
  44.4 0.9 %collective-permute-done.4 = bf16[16,96,256]{2,1,0:T(8,128)(2,1)S(1)} collective-permute-done((bf16[16,96,256]{2,1,0:T(8,128)(2,1)S(1)}, bf16[16,96,256]{2,1,0:T(8,128)(2,1)S(1)}, u32[]{:S(2)}, u32[]{:S(2)}) %collective-permute-start.4) | collective-permute-done | bytes 786464 | tf_op jit(solution)/shard_map/ppermute | solution.py:72
  45.7 1.6 %collective-permute-start.5 = (bf16[8,40,256]{2,1,0:T(8,128)(2,1)S(1)}, bf16[8,40,256]{2,1,0:T(8,128)(2,1)S(1)}, u32[]{:S(2)}, u32[]{:S(2)}) collective-permute-start(bf16[8,40,256]{2,1,0:T(8,128)(2,1)S(1)} %bitcast.357), channel_id=1, source_target_pairs={{0,8},{4,12},{8,0},{12,4},{16,24},{20,28},{24,16},{28,20},{1,9},{5... | collective-permute-start | bytes 491528 | tf_op jit(solution)/shard_map/ppermute | solution.py:72
  47.2 1.6 %collective-permute-start.7 = (bf16[8,56,256]{2,1,0:T(8,128)(2,1)S(1)}, bf16[8,56,256]{2,1,0:T(8,128)(2,1)S(1)}, u32[]{:S(2)}, u32[]{:S(2)}) collective-permute-start(bf16[8,56,256]{2,1,0:T(8,128)(2,1)S(1)} %fusion.54), channel_id=1, source_target_pairs={{0,16},{4,20},{8,24},{12,28},{16,0},{20,4},{24,8},{28,12},{1,17},{... | collective-permute-start | bytes 688136 | tf_op jit(solution)/shard_map/ppermute | solution.py:72
  48.8 3.1 %collective-permute-done.5 = bf16[8,40,256]{2,1,0:T(8,128)(2,1)S(1)} collective-permute-done((bf16[8,40,256]{2,1,0:T(8,128)(2,1)S(1)}, bf16[8,40,256]{2,1,0:T(8,128)(2,1)S(1)}, u32[]{:S(2)}, u32[]{:S(2)}) %collective-permute-start.5) | collective-permute-done | bytes 163872 | tf_op jit(solution)/shard_map/ppermute | solution.py:72
  52.0 1.6 %collective-permute-start.6 = (bf16[4,40,256]{2,1,0:T(8,128)(2,1)S(1)}, bf16[4,40,256]{2,1,0:T(8,128)(2,1)S(1)}, u32[]{:S(2)}, u32[]{:S(2)}) collective-permute-start(bf16[4,40,256]{2,1,0:T(8,128)(2,1)S(1)} %fusion.104), channel_id=1, source_target_pairs={{0,16},{4,20},{8,24},{12,28},{16,0},{20,4},{24,8},{28,12},{1,17},{... | collective-permute-start | bytes 245768 | tf_op jit(solution)/shard_map/ppermute | solution.py:72
  53.6 1.8 %collective-permute-done.7 = bf16[8,56,256]{2,1,0:T(8,128)(2,1)S(1)} collective-permute-done((bf16[8,56,256]{2,1,0:T(8,128)(2,1)S(1)}, bf16[8,56,256]{2,1,0:T(8,128)(2,1)S(1)}, u32[]{:S(2)}, u32[]{:S(2)}) %collective-permute-start.7) | collective-permute-done | bytes 229408 | tf_op jit(solution)/shard_map/ppermute | solution.py:72
  55.5 1.0 %collective-permute-done.6 = bf16[4,40,256]{2,1,0:T(8,128)(2,1)S(1)} collective-permute-done((bf16[4,40,256]{2,1,0:T(8,128)(2,1)S(1)}, bf16[4,40,256]{2,1,0:T(8,128)(2,1)S(1)}, u32[]{:S(2)}, u32[]{:S(2)}) %collective-permute-start.6) | collective-permute-done | bytes 81952 | tf_op jit(solution)/shard_map/ppermute | solution.py:72
  56.5 3.8 %collective-permute-done.8 = bf16[4,56,256]{2,1,0:T(8,128)(2,1)S(1)} collective-permute-done((bf16[4,56,256]{2,1,0:T(8,128)(2,1)S(1)}, bf16[4,56,256]{2,1,0:T(8,128)(2,1)S(1)}, u32[]{:S(2)}, u32[]{:S(2)}) %collective-permute-start.8) | collective-permute-done | bytes 114720 | tf_op jit(solution)/shard_map/ppermute | solution.py:72
  60.4 1.6 %collective-permute-start.9 = (bf16[96,256]{1,0:T(8,128)(2,1)S(1)}, bf16[96,256]{1,0:T(8,128)(2,1)S(1)}, u32[]{:S(2)}, u32[]{:S(2)}) collective-permute-start(bf16[96,256]{1,0:T(8,128)(2,1)S(1)} %get-tuple-element.5), channel_id=1, source_target_pairs={{0,1},{1,2},{2,3},{3,0},{4,5},{5,6},{6,7},{7,4},{8,9},{9,10},{10,1... | collective-permute-start | bytes 147464 | tf_op jit(solution)/shard_map/ppermute | solution.py:111
  62.1 1.1 %collective-permute-start.10 = (bf16[96,256]{1,0:T(8,128)(2,1)S(1)}, bf16[96,256]{1,0:T(8,128)(2,1)S(1)}, u32[]{:S(2)}, u32[]{:S(2)}) collective-permute-start(bf16[96,256]{1,0:T(8,128)(2,1)S(1)} %get-tuple-element.6), channel_id=1, source_target_pairs={{0,2},{1,3},{2,0},{3,1},{4,6},{5,7},{6,4},{7,5},{8,10},{9,11},{10,... | collective-permute-start | bytes 147464 | tf_op jit(solution)/shard_map/ppermute | solution.py:111
  63.2 2.9 %collective-permute-start.11 = (bf16[96,256]{1,0:T(8,128)(2,1)S(1)}, bf16[96,256]{1,0:T(8,128)(2,1)S(1)}, u32[]{:S(2)}, u32[]{:S(2)}) collective-permute-start(bf16[96,256]{1,0:T(8,128)(2,1)S(1)} %get-tuple-element.7), channel_id=1, source_target_pairs={{0,3},{1,0},{2,1},{3,2},{4,7},{5,4},{6,5},{7,6},{8,11},{9,8},{10,9... | collective-permute-start | bytes 147464 | tf_op jit(solution)/shard_map/ppermute | solution.py:111
  66.4 0.8 %collective-permute-done.10 = bf16[96,256]{1,0:T(8,128)(2,1)S(1)} collective-permute-done((bf16[96,256]{1,0:T(8,128)(2,1)S(1)}, bf16[96,256]{1,0:T(8,128)(2,1)S(1)}, u32[]{:S(2)}, u32[]{:S(2)}) %collective-permute-start.10) | collective-permute-done | bytes 49184 | tf_op jit(solution)/shard_map/ppermute | solution.py:111
  67.2 0.6 collective-permute-done.11
  68.1 0.6 add_add_fusion.1
  68.7 0.7 add_add_fusion
  (89 shorter events, 8.0 us)
Async XLA Ops:
  0.6 20.7 %copy-start = (bf16[256,256]{1,0:T(8,128)(2,1)S(1)}, bf16[256,256]{1,0:T(8,128)(2,1)}, u32[]{:S(2)}) copy-start(bf16[256,256]{1,0:T(8,128)(2,1)} %param.12) | copy-start | bytes 393220
  0.6 9.1 %collective-permute-start = (bf16[1,33,1,8,256]{4,3,2,1,0:T(8,128)(2,1)}, bf16[1,33,1,8,256]{4,3,2,1,0:T(8,128)(2,1)S(1)}, u32[]{:S(2)}, u32[]{:S(2)}) collective-permute-start(bf16[1,33,1,8,256]{4,3,2,1,0:T(8,128)(2,1)} %param.8), channel_id=1, source_target_pairs={{0,1},{1,2},{2,3},{4,5},{5,6},{6,7},{8,9},{9,10},{10,11},{12,13},{... | collective-permute-start | bytes 405512 | tf_op jit(solution)/shard_map/ppermute | solution.py:19
  5.7 7.1 %collective-permute-start.1 = (bf16[1,33,1,8,256]{4,3,2,1,0:T(8,128)(2,1)}, bf16[1,33,1,8,256]{4,3,2,1,0:T(8,128)(2,1)S(1)}, u32[]{:S(2)}, u32[]{:S(2)}) collective-permute-start(bf16[1,33,1,8,256]{4,3,2,1,0:T(8,128)(2,1)} %param.8), channel_id=1, source_target_pairs={{1,0},{2,1},{3,2},{5,4},{6,5},{7,6},{9,8},{10,9},{11,10},{13,12},{... | collective-permute-start | bytes 405512 | tf_op jit(solution)/shard_map/ppermute | solution.py:20
  10.0 4.8 %copy-start.3 = (bf16[1,33,1,16,256]{4,3,2,1,0:T(8,128)(2,1)}, bf16[1,33,1,16,256]{4,3,2,1,0:T(8,128)(2,1)S(1)}, u32[]{:S(2)}) copy-start(bf16[1,33,1,16,256]{4,3,2,1,0:T(8,128)(2,1)S(1)} %slice.130) | copy-start | bytes 811012
  13.2 1.3 %copy-start.8 = (bf16[3,3,256,256]{3,2,1,0:T(8,128)(2,1)S(1)}, bf16[3,3,256,256]{3,2,1,0:T(8,128)(2,1)}, u32[]{:S(2)}) copy-start(bf16[3,3,256,256]{3,2,1,0:T(8,128)(2,1)} %param.10) | copy-start | bytes 3538948
  17.0 1.5 %copy-start.6 = (bf16[3,256,256]{2,1,0:T(8,128)(2,1)S(1)}, bf16[3,256,256]{2,1,0:T(8,128)(2,1)}, u32[]{:S(2)}) copy-start(bf16[3,256,256]{2,1,0:T(8,128)(2,1)} %param.11) | copy-start | bytes 1179652
  18.7 1.1 %copy-start.5 = (f32[33,16,256]{2,1,0:T(8,128)S(1)}, f32[33,16,256]{2,1,0:T(8,128)}, u32[]{:S(2)}) copy-start(f32[33,16,256]{2,1,0:T(8,128)} %convert_element_type.133) | copy-start | bytes 1622020
  19.8 1.1 %copy-start.11 = (s32[1,8]{1,0:T(1,128)S(1)}, s32[1,8]{1,0:T(1,128)}, u32[]{:S(2)}) copy-start(s32[1,8]{1,0:T(1,128)} %param.14) | copy-start | bytes 100
  20.1 0.8 %copy-start.2 = (bf16[33,2,16,256]{3,2,1,0:T(8,128)(2,1)}, bf16[33,2,16,256]{3,2,1,0:T(8,128)(2,1)S(1)}, u32[]{:S(2)}) copy-start(bf16[33,2,16,256]{3,2,1,0:T(8,128)(2,1)S(1)} %fusion.16) | copy-start | bytes 1622020
  20.1 3.7 %copy-start.10 = (f32[256]{0:T(256)S(1)}, f32[256]{0:T(256)}, u32[]{:S(2)}) copy-start(f32[256]{0:T(256)} %param.13) | copy-start | bytes 3076
  22.3 3.7 %collective-permute-start.2 = (f32[1,8,256]{2,1,0:T(8,128)S(1)}, f32[1,8,256]{2,1,0:T(8,128)S(1)}, u32[]{:S(2)}, u32[]{:S(2)}) collective-permute-start(f32[1,8,256]{2,1,0:T(8,128)S(1)} %bitcast.365), channel_id=1, source_target_pairs={{0,1},{1,0},{2,3},{3,2},{4,5},{5,4},{6,7},{7,6},{8,9},{9,8},{10,11... | collective-permute-start | bytes 24584 | tf_op jit(solution)/shard_map/ppermute | solution.py:57
  25.9 4.5 %collective-permute-start.3 = (f32[1,8,256]{2,1,0:T(8,128)S(1)}, f32[1,8,256]{2,1,0:T(8,128)S(1)}, u32[]{:S(2)}, u32[]{:S(2)}) collective-permute-start(f32[1,8,256]{2,1,0:T(8,128)S(1)} %bitcast_add_fusion.5), channel_id=1, source_target_pairs={{0,2},{1,3},{2,0},{3,1},{4,6},{5,7},{6,4},{7,5},{8,10},{9,11},{10,... | collective-permute-start | bytes 24584 | tf_op jit(solution)/shard_map/ppermute | solution.py:57
  28.5 3.5 %copy-start.9 = (bf16[1,33,2,16,256]{4,3,2,1,0:T(8,128)(2,1)S(1)}, bf16[1,33,2,16,256]{4,3,2,1,0:T(8,128)(2,1)}, u32[]{:S(2)}) copy-start(bf16[1,33,2,16,256]{4,3,2,1,0:T(8,128)(2,1)} %param.15) | copy-start | bytes 1622020
  34.2 1.0 %copy-start.7 = (bf16[3,256,256]{2,1,0:T(8,128)(2,1)S(1)}, bf16[3,256,256]{2,1,0:T(8,128)(2,1)}, u32[]{:S(2)}) copy-start(bf16[3,256,256]{2,1,0:T(8,128)(2,1)} %param.11) | copy-start | bytes 1179652
  35.6 1.2 %copy-start.12 = (f32[33,2,16,256]{3,2,1,0:T(8,128)S(1)}, f32[33,2,16,256]{3,2,1,0:T(8,128)}, u32[]{:S(2)}) copy-start(f32[33,2,16,256]{3,2,1,0:T(8,128)} %get-tuple-element.11) | copy-start | bytes 3244036
  37.4 1.0 %copy-start.4 = (bf16[1,33,1,16,256]{4,3,2,1,0:T(8,128)(2,1)S(1)}, bf16[1,33,1,16,256]{4,3,2,1,0:T(8,128)(2,1)}, u32[]{:S(2)}) copy-start(bf16[1,33,1,16,256]{4,3,2,1,0:T(8,128)(2,1)} %copy-done.3) | copy-start | bytes 811012
  41.5 1.4 %copy-start.1 = (f32[9,256,256]{2,1,0:T(8,128)}, f32[9,256,256]{2,1,0:T(8,128)S(1)}, u32[]{:S(2)}) copy-start(f32[9,256,256]{2,1,0:T(8,128)S(1)} %fusion.17) | copy-start | bytes 7077892
  43.0 2.3 %collective-permute-start.4 = (bf16[16,96,256]{2,1,0:T(8,128)(2,1)S(1)}, bf16[16,96,256]{2,1,0:T(8,128)(2,1)S(1)}, u32[]{:S(2)}, u32[]{:S(2)}) collective-permute-start(bf16[16,96,256]{2,1,0:T(8,128)(2,1)S(1)} %bitcast.352), channel_id=1, source_target_pairs={{0,4},{4,0},{8,12},{12,8},{16,20},{20,16},{24,28},{28,24},{1,5},{5... | collective-permute-start | bytes 2359304 | tf_op jit(solution)/shard_map/ppermute | solution.py:72
  45.7 6.3 %collective-permute-start.5 = (bf16[8,40,256]{2,1,0:T(8,128)(2,1)S(1)}, bf16[8,40,256]{2,1,0:T(8,128)(2,1)S(1)}, u32[]{:S(2)}, u32[]{:S(2)}) collective-permute-start(bf16[8,40,256]{2,1,0:T(8,128)(2,1)S(1)} %bitcast.357), channel_id=1, source_target_pairs={{0,8},{4,12},{8,0},{12,4},{16,24},{20,28},{24,16},{28,20},{1,9},{5... | collective-permute-start | bytes 491528 | tf_op jit(solution)/shard_map/ppermute | solution.py:72
  47.2 8.1 %collective-permute-start.7 = (bf16[8,56,256]{2,1,0:T(8,128)(2,1)S(1)}, bf16[8,56,256]{2,1,0:T(8,128)(2,1)S(1)}, u32[]{:S(2)}, u32[]{:S(2)}) collective-permute-start(bf16[8,56,256]{2,1,0:T(8,128)(2,1)S(1)} %fusion.54), channel_id=1, source_target_pairs={{0,16},{4,20},{8,24},{12,28},{16,0},{20,4},{24,8},{28,12},{1,17},{... | collective-permute-start | bytes 688136 | tf_op jit(solution)/shard_map/ppermute | solution.py:72
  52.0 4.5 %collective-permute-start.6 = (bf16[4,40,256]{2,1,0:T(8,128)(2,1)S(1)}, bf16[4,40,256]{2,1,0:T(8,128)(2,1)S(1)}, u32[]{:S(2)}, u32[]{:S(2)}) collective-permute-start(bf16[4,40,256]{2,1,0:T(8,128)(2,1)S(1)} %fusion.104), channel_id=1, source_target_pairs={{0,16},{4,20},{8,24},{12,28},{16,0},{20,4},{24,8},{28,12},{1,17},{... | collective-permute-start | bytes 245768 | tf_op jit(solution)/shard_map/ppermute | solution.py:72
  55.4 4.9 %collective-permute-start.8 = (bf16[4,56,256]{2,1,0:T(8,128)(2,1)S(1)}, bf16[4,56,256]{2,1,0:T(8,128)(2,1)S(1)}, u32[]{:S(2)}, u32[]{:S(2)}) collective-permute-start(bf16[4,56,256]{2,1,0:T(8,128)(2,1)S(1)} %fusion.96), channel_id=1, source_target_pairs={{0,8},{4,12},{8,0},{12,4},{16,24},{20,28},{24,16},{28,20},{1,9},{5... | collective-permute-start | bytes 344072 | tf_op jit(solution)/shard_map/ppermute | solution.py:72
  60.4 5.9 %collective-permute-start.9 = (bf16[96,256]{1,0:T(8,128)(2,1)S(1)}, bf16[96,256]{1,0:T(8,128)(2,1)S(1)}, u32[]{:S(2)}, u32[]{:S(2)}) collective-permute-start(bf16[96,256]{1,0:T(8,128)(2,1)S(1)} %get-tuple-element.5), channel_id=1, source_target_pairs={{0,1},{1,2},{2,3},{3,0},{4,5},{5,6},{6,7},{7,4},{8,9},{9,10},{10,1... | collective-permute-start | bytes 147464 | tf_op jit(solution)/shard_map/ppermute | solution.py:111
  62.1 5.1 %collective-permute-start.10 = (bf16[96,256]{1,0:T(8,128)(2,1)S(1)}, bf16[96,256]{1,0:T(8,128)(2,1)S(1)}, u32[]{:S(2)}, u32[]{:S(2)}) collective-permute-start(bf16[96,256]{1,0:T(8,128)(2,1)S(1)} %get-tuple-element.6), channel_id=1, source_target_pairs={{0,2},{1,3},{2,0},{3,1},{4,6},{5,7},{6,4},{7,5},{8,10},{9,11},{10,... | collective-permute-start | bytes 147464 | tf_op jit(solution)/shard_map/ppermute | solution.py:111
  63.2 4.6 %collective-permute-start.11 = (bf16[96,256]{1,0:T(8,128)(2,1)S(1)}, bf16[96,256]{1,0:T(8,128)(2,1)S(1)}, u32[]{:S(2)}, u32[]{:S(2)}) collective-permute-start(bf16[96,256]{1,0:T(8,128)(2,1)S(1)} %get-tuple-element.7), channel_id=1, source_target_pairs={{0,3},{1,0},{2,1},{3,2},{4,7},{5,4},{6,5},{7,6},{8,11},{9,8},{10,9... | collective-permute-start | bytes 147464 | tf_op jit(solution)/shard_map/ppermute | solution.py:111
